TPU v7x, 32 devices: a whole 2x2x4 slice. The times are simulated.
32 devices in a mesh: leaf: 4 (over y, x), src: 8 (over z, core).
Axes of the slice: x: 2, y: 2, z: 4, core: 2. Of those that a mesh axis runs over, the one named last changes fastest.
Arguments:
- src_cells: int32 [1024], P('src'), may hold values from 0 to 2047
- rec_cells: int32 [512], P('leaf'), may hold values from 0 to 511
- residual: float32 [1024, 512], P('src', 'leaf'), may hold values from -6 to 6
- pattern: int32 [12, 2], P('leaf'), may hold values 0 or 1
- leaf_lower: bfloat16 [2048, 512], P('leaf'), may hold values from -0.1875 to 0.1875
- leaf_upper: bfloat16 [2048, 512], P('leaf'), may hold values from -0.1875 to 0.1875
- leaf_inv: bfloat16 [16, 128, 128], P('leaf'), may hold values from -0.5 to 0.5
- anc_lower: bfloat16 [1024, 512], P('leaf'), may hold values from -0.125 to 0.125
- anc_upper: bfloat16 [2048, 256], P('leaf'), may hold values from -0.375 to 0.375
- sep_inv: bfloat16 [8, 128, 128], P('leaf'), may hold values from -0.5 to 0.5
- sep_lower: bfloat16 [8, 256, 128], P('leaf'), may hold values from -0.25 to 0.25
- sep_upper: bfloat16 [8, 128, 256], P('leaf'), may hold values from -0.375 to 0.375
Outputs:
- forward_field: float32 [1024, 2048], P('src', 'leaf')
- adjoint_field: float32 [1024, 2048], P('src', 'leaf')
- gradient: float32 [2048], P(('leaf', 'src'))
Inputs may be any that keep to these rules, and one draw needn't show every extreme that they name: src_cells holds 512 d + c for a source in interior cell c of subdomain d. rec_cells holds a receiver's cell within the subdomain of its block of 128 entries.
All inputs are finite; a program needn't handle non-finite values. No bound on the sum of `pattern` on one device may be relied on, other than what follows from the above.
Results may differ from a plain program's by a relative error of at most 0.0068.
Values may be sent and summed in bfloat16 or wider, within the bound.
No kernel may reach another device: no remote copies, remote signals or barrier semaphores. Data moves between devices by JAX's collectives and lax.ppermute only.
A program may use at most 64 MiB of HBM per device.

v0:
```python
import math

import jax
import jax.numpy as jnp
from jax import lax
from jax.sharding import PartitionSpec as P


def across(former, latter):
    return lax.dot_general(
        former, latter, (((1,), (1,)), ((), ())), preferred_element_type=jnp.float32
    )


def plain_dot(former, latter):
    return jnp.dot(former, latter, preferred_element_type=jnp.float32)


def as_half(values):
    return values.astype(jnp.bfloat16)


def lower_solve(right_side, lower, block_size, block_count):
    solved = []
    for index in range(block_count):
        segment = right_side[:, index * block_size : (index + 1) * block_size]
        if index:
            earlier = as_half(jnp.concatenate(solved, axis=1))
            segment = segment - across(
                earlier, lower[index * block_size : (index + 1) * block_size, : index * block_size]
            )
        solved.append(segment)
    return jnp.concatenate(solved, axis=1)


def upper_solve(right_side, upper, inverse, block_size, block_count):
    behind = []
    for index in reversed(range(block_count)):
        segment = right_side[:, index * block_size : (index + 1) * block_size]
        if behind:
            segment = segment - across(
                as_half(jnp.concatenate(behind, axis=1)),
                upper[index * block_size : (index + 1) * block_size, (index + 1) * block_size :],
            )
        behind.insert(0, across(as_half(segment), inverse[index]))
    return jnp.concatenate(behind, axis=1)


def upper_t_solve(right_side, upper, inverse, block_size, block_count):
    solved = []
    for index in range(block_count):
        segment = right_side[:, index * block_size : (index + 1) * block_size]
        if index:
            earlier = as_half(jnp.concatenate(solved, axis=1))
            segment = segment - plain_dot(
                earlier, upper[: index * block_size, index * block_size : (index + 1) * block_size]
            )
        solved.append(plain_dot(as_half(segment), inverse[index]))
    return jnp.concatenate(solved, axis=1)


def lower_t_solve(right_side, lower, block_size, block_count):
    behind = []
    for index in reversed(range(block_count)):
        segment = right_side[:, index * block_size : (index + 1) * block_size]
        if behind:
            segment = segment - plain_dot(
                as_half(jnp.concatenate(behind, axis=1)),
                lower[(index + 1) * block_size :, index * block_size : (index + 1) * block_size],
            )
        behind.insert(0, segment)
    return jnp.concatenate(behind, axis=1)


def climb(starts, handlers, levels, block_size, device):
    contributions = list(starts)
    results = [[] for member in starts]
    for height in range(1, levels + 1):
        lowest = (height - 1) * block_size
        piece = jnp.stack([summed[:, lowest : lowest + block_size] for summed in contributions])
        gathered = lax.all_gather(piece[None], "leaf", axis=0, tiled=True)
        first = device >> height << height
        total = jnp.sum(lax.dynamic_slice_in_dim(gathered, first, 1 << height, 0), axis=0)
        owner = device % (1 << height) == 0
        member = 0
        node_value, coupling = handlers[member](height, total[member])
        results[member].append(node_value)
        contributions[member] = contributions[member] + jnp.where(
            owner, coupling, jnp.zeros_like(coupling)
        )
    return results


def descend(node_values, handlers, levels, block_size, device, sources):
    known = [jnp.zeros((sources, levels * block_size), jnp.float32) for member in node_values]
    for height in range(levels, 0, -1):
        outgoing = jnp.stack([as_half(handlers[0](height, known[0], node_values[0][height - 1]))])
        gathered = lax.all_gather(outgoing[None], "leaf", axis=0, tiled=True)
        owner_index = device >> height << height
        piece = lax.dynamic_index_in_dim(gathered, owner_index, 0, keepdims=False).astype(
            jnp.float32
        )
        known = [lax.dynamic_update_slice_in_dim(known[0], piece[0], (height - 1) * block_size, 1)]
    return known


def shards(
    src_cells,
    rec_cells,
    residual,
    pattern,
    leaf_lower,
    leaf_upper,
    leaf_inv,
    anc_lower,
    anc_upper,
    sep_inv,
    sep_lower,
    sep_upper,
):
    levels = lax.axis_size("leaf").bit_length() - 1
    device = lax.axis_index("leaf")
    block_size = leaf_inv.shape[1]
    block_count = leaf_inv.shape[0]
    cell_count = leaf_lower.shape[1]
    source_count = src_cells.shape[0]
    factor = 1.0 / math.sqrt(source_count * lax.axis_size("src"))
    present = pattern.astype(jnp.float32)

    def level_mask(height):
        level_row = present[height] * (jnp.arange(1, levels + 1) > height).astype(jnp.float32)
        return jnp.repeat(level_row, block_size)

    columns = lax.broadcasted_iota(jnp.int32, (source_count, cell_count), 1)
    forcing = (src_cells[:, None] - device * cell_count == columns).astype(jnp.float32)
    receiver_hits = (
        rec_cells[:, None] == lax.broadcasted_iota(jnp.int32, (rec_cells.shape[0], cell_count), 1)
    ).astype(jnp.float32)
    adjoint_rhs = jnp.dot(residual, receiver_hits, precision=lax.Precision.HIGHEST)

    def forward_up(height, summed):
        node_value = -summed
        return (node_value, across(as_half(node_value), sep_lower[height - 1]) * level_mask(height))

    def adjoint_up(height, summed):
        node_value = plain_dot(as_half(-summed), sep_inv[height - 1])
        return (
            node_value,
            plain_dot(as_half(node_value), sep_upper[height - 1]) * level_mask(height),
        )

    def forward_down(height, above, node_value):
        right_side = node_value - across(as_half(above * level_mask(height)), sep_upper[height - 1])
        return across(as_half(right_side), sep_inv[height - 1])

    def adjoint_down(height, above, node_value):
        return node_value - plain_dot(as_half(above * level_mask(height)), sep_lower[height - 1])

    base_mask = level_mask(0)
    y_leaf = lower_solve(forcing, leaf_lower, block_size, block_count)
    forward_start = across(as_half(y_leaf), anc_lower) * base_mask
    z_leaf = upper_t_solve(adjoint_rhs, leaf_upper, leaf_inv, block_size, block_count)
    adjoint_start = plain_dot(as_half(z_leaf), anc_upper) * base_mask
    forward_values = climb([forward_start], [forward_up], levels, block_size, device)
    forward_above = descend(
        forward_values, [forward_down], levels, block_size, device, source_count
    )[0]
    adjoint_values = climb([adjoint_start], [adjoint_up], levels, block_size, device)
    adjoint_above = descend(
        adjoint_values, [adjoint_down], levels, block_size, device, source_count
    )[0]
    forward_remain = y_leaf - across(as_half(forward_above * base_mask), anc_upper)
    forward_field = upper_solve(forward_remain, leaf_upper, leaf_inv, block_size, block_count)
    adjoint_remain = z_leaf - plain_dot(as_half(adjoint_above * base_mask), anc_lower)
    adjoint_field = lower_t_solve(adjoint_remain, leaf_lower, block_size, block_count)
    partial_gradient = jnp.sum(forward_field * adjoint_field, axis=0)
    gradient = lax.psum_scatter(partial_gradient, "src", scatter_dimension=0, tiled=True) * factor
    return (forward_field, adjoint_field, gradient)


def solution(mesh):
    in_specs = (
        P("src"),
        P("leaf"),
        P("src", "leaf"),
        P("leaf", None),
        P("leaf", None),
        P("leaf", None),
        P("leaf", None, None),
        P("leaf", None),
        P("leaf", None),
        P("leaf", None, None),
        P("leaf", None, None),
        P("leaf", None, None),
    )
    out_specs = (P("src", "leaf"), P("src", "leaf"), P(("leaf", "src")))
    return jax.shard_map(shards, mesh=mesh, in_specs=in_specs, out_specs=out_specs, check_vma=False)
```

profile of v0, /device:TPU:0, one launch (start us, length us, event | category | flops | bytes accessed | tf_op | source)
XLA Modules:
  0.0 98.7 jit_solution(13294854775724279794)
XLA Ops:
  0.6 0.0 copy-start
  0.6 0.0 copy-start.7
  0.7 0.7 broadcast_subtract_fusion
  1.4 0.9 fusion.189
  2.3 0.0 copy-done.7
  2.4 0.1 fusion.190
  2.5 0.0 copy-start.5
  2.5 0.2 convolution_subtract_fusion.5
  2.7 0.0 copy-start.9
  2.7 0.7 copy-done.9
  3.4 0.2 slice_reduce_fusion
  3.6 0.1 broadcast_bitcast_fusion.1
  3.7 0.0 copy-done.5
  3.7 0.2 convolution_multiply_fusion.1
  3.9 0.0 copy-start.6
  4.0 10.6 %all-gather = f32[512,128]{1,0:T(8,128)S(1)} all-gather(f32[128,128]{1,0:T(8,128)S(1)} %slice.198), channel_id=2, replica_groups=mesh['leaf'=4,'src'=8] {'leaf'}, dimensions={0}, use_global_device_ids=true | all-gather | bytes 327680 | tf_op jit(solution)/shard_map/all_gather | solution.py:81
  14.5 0.0 copy-done.8
  14.5 0.0 copy-done.10
  14.6 0.0 copy-start.3
  14.6 0.4 convolution_bitcast_fusion
  15.0 0.5 copy-done.3
  15.5 0.2 fusion.180
  15.7 0.0 copy-done.6
  15.7 0.3 fusion.181
  16.0 0.4 fusion.184
  16.4 0.4 fusion.13
  16.8 0.2 convolution_multiply_fusion
  17.0 9.0 %all-gather.4 = f32[512,128]{1,0:T(8,128)S(1)} all-gather(f32[128,128]{1,0:T(8,128)S(1)} %slice.210), channel_id=6, replica_groups=mesh['leaf'=4,'src'=8] {'leaf'}, dimensions={0}, use_global_device_ids=true | all-gather | bytes 327680 | tf_op jit(solution)/shard_map/all_gather | solution.py:81
  26.0 0.0 copy-start.2
  26.0 0.8 copy-done.4
  26.8 0.1 fusion.121
  27.0 0.0 copy-start.1
  27.0 0.1 fusion.91
  27.1 0.8 copy-done.1
  27.9 0.2 fusion.98
  28.1 0.1 broadcast_bitcast_fusion
  28.2 8.1 %all-gather.1 = f32[512,128]{1,0:T(8,128)S(1)} all-gather(f32[128,128]{1,0:T(8,128)S(1)} %get-tuple-element.16), channel_id=3, replica_groups=mesh['leaf'=4,'src'=8] {'leaf'}, dimensions={0}, use_global_device_ids=true | all-gather | bytes 327680 | tf_op jit(solution)/shard_map/all_gather | solution.py:81
  36.3 0.1 broadcast_bitcast_fusion.2
  36.4 0.3 convolution_convert_fusion.1
  36.6 8.7 %all-gather.2 = bf16[512,128]{1,0:T(8,128)(2,1)S(1)} all-gather(bf16[128,128]{1,0:T(8,128)(2,1)S(1)} %convolution_convert_fusion.1), channel_id=4, replica_groups=mesh['leaf'=4,'src'=8] {'leaf'}, dimensions={0}, use_global_device_ids=true | all-gather | bytes 163840 | tf_op jit(solution)/shard_map/all_gather | solution.py:98
  45.4 0.3 convolution_convert_fusion
  45.7 7.3 %all-gather.3 = bf16[512,128]{1,0:T(8,128)(2,1)S(1)} all-gather(bf16[128,128]{1,0:T(8,128)(2,1)S(1)} %convolution_convert_fusion), channel_id=5, replica_groups=mesh['leaf'=4,'src'=8] {'leaf'}, dimensions={0}, use_global_device_ids=true | all-gather | bytes 163840 | tf_op jit(solution)/shard_map/all_gather | solution.py:98
  53.0 0.2 convolution_subtract_fusion.1
  53.2 0.1 fusion.193
  53.3 0.3 fusion.194
  53.6 0.3 fusion.197
  53.9 0.3 fusion.10
  54.2 9.2 %all-gather.5 = f32[512,128]{1,0:T(8,128)S(1)} all-gather(f32[128,128]{1,0:T(8,128)S(1)} %get-tuple-element.15), channel_id=7, replica_groups=mesh['leaf'=4,'src'=8] {'leaf'}, dimensions={0}, use_global_device_ids=true | all-gather | bytes 327680 | tf_op jit(solution)/shard_map/all_gather | solution.py:81
  63.5 0.1 fusion.122
  63.6 0.2 fusion.5
  63.7 7.3 %all-gather.6 = bf16[512,128]{1,0:T(8,128)(2,1)S(1)} all-gather(bf16[128,128]{1,0:T(8,128)(2,1)S(1)} %fusion.5), channel_id=8, replica_groups=mesh['leaf'=4,'src'=8] {'leaf'}, dimensions={0}, use_global_device_ids=true | all-gather | bytes 163840 | tf_op jit(solution)/shard_map/all_gather | solution.py:98
  71.1 0.1 fusion.6
  71.2 8.6 %all-gather.7 = bf16[512,128]{1,0:T(8,128)(2,1)S(1)} all-gather(bf16[128,128]{1,0:T(8,128)(2,1)S(1)} %fusion.6), channel_id=9, replica_groups=mesh['leaf'=4,'src'=8] {'leaf'}, dimensions={0}, use_global_device_ids=true | all-gather | bytes 163840 | tf_op jit(solution)/shard_map/all_gather | solution.py:98
  79.9 0.3 convolution_subtract_fusion
  80.1 0.2 fusion.191
  80.4 0.2 fusion.192
  80.6 0.2 convolution_subtract_fusion.8
  80.8 0.1 multiply_reduce_fusion
  81.0 0.8 copy.21
  81.8 0.8 copy.22
  82.7 13.6 %all-reduce.2 = f32[512]{0:T(512)S(1)} all-reduce(f32[512]{0:T(512)S(1)} %get-tuple-element.12), channel_id=10, replica_groups=mesh['leaf'=4,'src'=8] {'src'}, use_global_device_ids=true, to_apply=%region_5.6.clone | all-reduce | flops 512 | bytes 4096
  96.3 0.7 copy-done.11
  96.9 0.6 dynamic-slice
  98.1 0.6 dynamic-slice_multiply_fusion
  (26 shorter events, 0.2 us)
Async XLA Ops:
  0.6 16.1 %copy-start = (bf16[512,256]{1,0:T(8,128)(2,1)S(1)}, bf16[512,256]{1,0:T(8,128)(2,1)}, u32[]{:S(2)}) copy-start(bf16[512,256]{1,0:T(8,128)(2,1)} %param.20) | copy-start | bytes 786436
  0.6 1.7 %copy-start.7 = (bf16[512,512]{1,0:T(8,128)(2,1)S(1)}, bf16[512,512]{1,0:T(8,128)(2,1)}, u32[]{:S(2)}) copy-start(bf16[512,512]{1,0:T(8,128)(2,1)} %param.16) | copy-start | bytes 1572868
  2.5 1.2 %copy-start.5 = (bf16[256,512]{1,0:T(8,128)(2,1)S(1)}, bf16[256,512]{1,0:T(8,128)(2,1)}, u32[]{:S(2)}) copy-start(bf16[256,512]{1,0:T(8,128)(2,1)} %param.19) | copy-start | bytes 786436
  2.7 0.7 copy-start.9
  3.7 10.9 %copy-start.8 = (f32[128,128]{1,0:T(8,128)S(1)}, f32[128,128]{1,0:T(8,128)}, u32[]{:S(2)}) copy-start(f32[128,128]{1,0:T(8,128)} %param.14) | copy-start | bytes 196612
  3.7 10.9 %copy-start.10 = (s32[128]{0:T(128)S(1)}, s32[128]{0:T(128)}, u32[]{:S(2)}) copy-start(s32[128]{0:T(128)} %param.13) | copy-start | bytes 1540
  3.9 11.7 %copy-start.6 = (bf16[512,512]{1,0:T(8,128)(2,1)S(1)}, bf16[512,512]{1,0:T(8,128)(2,1)}, u32[]{:S(2)}) copy-start(bf16[512,512]{1,0:T(8,128)(2,1)} %param.17) | copy-start | bytes 1572868
  14.6 0.9 copy-start.3
  26.0 0.8 copy-start.4
  26.0 0.9 copy-start.2
  27.0 0.9 copy-start.1
  96.2 0.7 copy-start.11
where the time goes:
time: 99.2 us; the launch traced here: 98.7 us
  blocking collectives  82.3 us (83%)
  matrix products  6.91 us (7%)
  local copies, waits for them, and re-layouts  6.16 us (6%)
  between operations  1.7 us (2%)
  other arithmetic  1.61 us (2%)
    all_gather x4, blocking collectives, climb(): gathered = lax.all_gather(piece[None], 'leaf', axis=0, tiled=True)  36.8 us
    all_gather x4, blocking collectives, descend(): gathered = lax.all_gather(outgoing[None], 'leaf', axis=0, tiled=True)  31.9 us
    unnamed x1, blocking collectives  13.6 us
    unnamed x27, local copies, waits for them, and re-layouts  5.69 us
    dot_general x12, matrix products, across(): lax.dot_general(former, latter, (((1,), (1,)), ((), ())), preferred_eleme...  3.42 us
    dot_general x14, matrix products, plain_dot(): return jnp.dot(former, latter, preferred_element_type=jnp.float32)  3.11 us

commit v1 on v0

--- a/solution.py
+++ b/solution.py
@@ -70,38 +70,6 @@
             )
         behind.insert(0, segment)
     return jnp.concatenate(behind, axis=1)
-
-
-def climb(starts, handlers, levels, block_size, device):
-    contributions = list(starts)
-    results = [[] for member in starts]
-    for height in range(1, levels + 1):
-        lowest = (height - 1) * block_size
-        piece = jnp.stack([summed[:, lowest : lowest + block_size] for summed in contributions])
-        gathered = lax.all_gather(piece[None], "leaf", axis=0, tiled=True)
-        first = device >> height << height
-        total = jnp.sum(lax.dynamic_slice_in_dim(gathered, first, 1 << height, 0), axis=0)
-        owner = device % (1 << height) == 0
-        member = 0
-        node_value, coupling = handlers[member](height, total[member])
-        results[member].append(node_value)
-        contributions[member] = contributions[member] + jnp.where(
-            owner, coupling, jnp.zeros_like(coupling)
-        )
-    return results
-
-
-def descend(node_values, handlers, levels, block_size, device, sources):
-    known = [jnp.zeros((sources, levels * block_size), jnp.float32) for member in node_values]
-    for height in range(levels, 0, -1):
-        outgoing = jnp.stack([as_half(handlers[0](height, known[0], node_values[0][height - 1]))])
-        gathered = lax.all_gather(outgoing[None], "leaf", axis=0, tiled=True)
-        owner_index = device >> height << height
-        piece = lax.dynamic_index_in_dim(gathered, owner_index, 0, keepdims=False).astype(
-            jnp.float32
-        )
-        known = [lax.dynamic_update_slice_in_dim(known[0], piece[0], (height - 1) * block_size, 1)]
-    return known
 
 
 def shards(
@@ -118,7 +86,8 @@
     sep_lower,
     sep_upper,
 ):
-    levels = lax.axis_size("leaf").bit_length() - 1
+    leaves = lax.axis_size("leaf")
+    levels = leaves.bit_length() - 1
     device = lax.axis_index("leaf")
     block_size = leaf_inv.shape[1]
     block_count = leaf_inv.shape[0]
@@ -131,6 +100,9 @@
         level_row = present[height] * (jnp.arange(1, levels + 1) > height).astype(jnp.float32)
         return jnp.repeat(level_row, block_size)
 
+    def blocks_of(values):
+        return [values[:, k * block_size : (k + 1) * block_size] for k in range(values.shape[1] // block_size)]
+
     columns = lax.broadcasted_iota(jnp.int32, (source_count, cell_count), 1)
     forcing = (src_cells[:, None] - device * cell_count == columns).astype(jnp.float32)
     receiver_hits = (
@@ -138,37 +110,75 @@
     ).astype(jnp.float32)
     adjoint_rhs = jnp.dot(residual, receiver_hits, precision=lax.Precision.HIGHEST)
 
-    def forward_up(height, summed):
-        node_value = -summed
-        return (node_value, across(as_half(node_value), sep_lower[height - 1]) * level_mask(height))
-
-    def adjoint_up(height, summed):
-        node_value = plain_dot(as_half(-summed), sep_inv[height - 1])
-        return (
-            node_value,
-            plain_dot(as_half(node_value), sep_upper[height - 1]) * level_mask(height),
-        )
-
-    def forward_down(height, above, node_value):
-        right_side = node_value - across(as_half(above * level_mask(height)), sep_upper[height - 1])
-        return across(as_half(right_side), sep_inv[height - 1])
-
-    def adjoint_down(height, above, node_value):
-        return node_value - plain_dot(as_half(above * level_mask(height)), sep_lower[height - 1])
-
     base_mask = level_mask(0)
     y_leaf = lower_solve(forcing, leaf_lower, block_size, block_count)
-    forward_start = across(as_half(y_leaf), anc_lower) * base_mask
     z_leaf = upper_t_solve(adjoint_rhs, leaf_upper, leaf_inv, block_size, block_count)
-    adjoint_start = plain_dot(as_half(z_leaf), anc_upper) * base_mask
-    forward_values = climb([forward_start], [forward_up], levels, block_size, device)
-    forward_above = descend(
-        forward_values, [forward_down], levels, block_size, device, source_count
-    )[0]
-    adjoint_values = climb([adjoint_start], [adjoint_up], levels, block_size, device)
-    adjoint_above = descend(
-        adjoint_values, [adjoint_down], levels, block_size, device, source_count
-    )[0]
+    forward_sums = blocks_of(across(as_half(y_leaf), anc_lower) * base_mask)
+    adjoint_sums = blocks_of(plain_dot(as_half(z_leaf), anc_upper) * base_mask)
+
+    lower_panels, upper_panels, inverse_panels = [], [], []
+    for height in range(1, levels + 1):
+        mask = level_mask(height)[height * block_size :]
+        lower_panels.append(sep_lower[height - 1, height * block_size :, :] * mask[:, None].astype(jnp.bfloat16))
+        upper_panels.append(sep_upper[height - 1, :, height * block_size :] * mask[None, :].astype(jnp.bfloat16))
+        inverse_panels.append(sep_inv[height - 1])
+
+    forward_nodes, adjoint_nodes = [], []
+    for height in range(1, levels + 1):
+        stride = 1 << (height - 1)
+        pairs = [(index, index ^ stride) for index in range(leaves)]
+        pieces = list(forward_sums) + list(adjoint_sums)
+        for upper_level in range(height, levels + 1):
+            pieces.append(lower_panels[upper_level - 1].astype(jnp.float32))
+            pieces.extend(block.astype(jnp.float32) for block in blocks_of(upper_panels[upper_level - 1]))
+            pieces.append(inverse_panels[upper_level - 1].astype(jnp.float32))
+        incoming = lax.ppermute(jnp.concatenate(pieces, axis=0), "leaf", pairs)
+        received, row = [], 0
+        for piece in pieces:
+            received.append(incoming[row : row + piece.shape[0]])
+            row += piece.shape[0]
+        count = len(forward_sums)
+        forward_sums = [mine + theirs for mine, theirs in zip(forward_sums, received[:count])]
+        adjoint_sums = [mine + theirs for mine, theirs in zip(adjoint_sums, received[count : 2 * count])]
+        received = received[2 * count :]
+        for upper_level in range(height, levels + 1):
+            place = device % (1 << upper_level)
+            take = jnp.logical_and(place >= stride, place < 2 * stride)
+            width = levels - upper_level
+            lower_in = received[0].astype(jnp.bfloat16)
+            upper_in = jnp.concatenate([block.astype(jnp.bfloat16) for block in received[1 : 1 + width]] or [upper_panels[upper_level - 1]], axis=1)
+            inverse_in = received[1 + width].astype(jnp.bfloat16)
+            received = received[2 + width :]
+            lower_panels[upper_level - 1] = jnp.where(take, lower_in, lower_panels[upper_level - 1])
+            upper_panels[upper_level - 1] = jnp.where(take, upper_in, upper_panels[upper_level - 1])
+            inverse_panels[upper_level - 1] = jnp.where(take, inverse_in, inverse_panels[upper_level - 1])
+        forward_node = -forward_sums[0]
+        adjoint_node = plain_dot(as_half(-adjoint_sums[0]), inverse_panels[height - 1])
+        forward_nodes.append(forward_node)
+        adjoint_nodes.append(adjoint_node)
+        forward_sums, adjoint_sums = forward_sums[1:], adjoint_sums[1:]
+        if forward_sums:
+            forward_coupling = blocks_of(across(as_half(forward_node), lower_panels[height - 1]))
+            adjoint_coupling = blocks_of(plain_dot(as_half(adjoint_node), upper_panels[height - 1]))
+            forward_sums = [total + extra for total, extra in zip(forward_sums, forward_coupling)]
+            adjoint_sums = [total + extra for total, extra in zip(adjoint_sums, adjoint_coupling)]
+
+    forward_above, adjoint_above = [], []
+    for height in range(levels, 0, -1):
+        right_side = forward_nodes[height - 1]
+        adjoint_value = adjoint_nodes[height - 1]
+        if forward_above:
+            right_side = right_side - across(
+                as_half(jnp.concatenate(forward_above, axis=1)), upper_panels[height - 1]
+            )
+            adjoint_value = adjoint_value - plain_dot(
+                as_half(jnp.concatenate(adjoint_above, axis=1)), lower_panels[height - 1]
+            )
+        forward_above.insert(0, across(as_half(right_side), inverse_panels[height - 1]))
+        adjoint_above.insert(0, adjoint_value)
+    forward_above = jnp.concatenate(forward_above, axis=1)
+    adjoint_above = jnp.concatenate(adjoint_above, axis=1)
+
     forward_remain = y_leaf - across(as_half(forward_above * base_mask), anc_upper)
     forward_field = upper_solve(forward_remain, leaf_upper, leaf_inv, block_size, block_count)
     adjoint_remain = z_leaf - plain_dot(as_half(adjoint_above * base_mask), anc_lower)

time: 99.2 us -> 63.9 us (0.64)
  blocking collectives: 82.3 us -> 14.8 us
  waiting for transfers between devices: 0 us -> 14.3 us
  matrix products: 6.91 us -> 18.7 us
  starting transfers between devices: 0 us -> 4.83 us
    all_gather x8 -> x0, blocking collectives: 68.8 us -> none  [the longest x4 36.8 us: climb(): gathered = lax.all_gather(piece[None], 'leaf', axis=0, tiled=True)]
    ppermute x0 -> x2, waiting for transfers between devices: none -> 14.3 us  [shards(): incoming = lax.ppermute(jnp.concatenate(pieces, axis=0), 'leaf', pairs)]
    dot_general x14 -> x13, matrix products: 3.11 us -> 9.55 us  [plain_dot(): return jnp.dot(former, latter, preferred_element_type=jnp.float32)]
    dot_general x12, matrix products: 3.42 us -> 8.82 us  [across(): lax.dot_general(former, latter, (((1,), (1,)), ((), ())), preferred_eleme...]
    ppermute x0 -> x2, starting transfers between devices: none -> 4.83 us  [shards(): incoming = lax.ppermute(jnp.concatenate(pieces, axis=0), 'leaf', pairs)]
    unnamed x0 -> x3, other arithmetic: none -> 1.34 us
    unnamed x1, blocking collectives: 13.6 us -> 14.8 us
    unnamed x27 -> x29, local copies, waits for them, and re-layouts: 5.69 us -> 5.39 us
  transfers between devices with their start and end apart: 0 -> 2, of which waited for: 0 -> 2; matrix products, arithmetic and copies ran while one was open for 0% -> 1% of each run, Pallas kernels for 0% -> 0%
where the time goes in v1:
time: 63.9 us; the launch traced here: 63 us
  matrix products  18.7 us (29%)
  blocking collectives  14.8 us (23%)
  waiting for transfers between devices  14.3 us (22%)
  local copies, waits for them, and re-layouts  6.55 us (10%)
  starting transfers between devices  4.83 us (8%)
  other arithmetic  2.21 us (3%)
  between operations  1.68 us (3%)
    unnamed x1, blocking collectives  14.8 us
    ppermute x2, waiting for transfers between devices, shards(): incoming = lax.ppermute(jnp.concatenate(pieces, axis=0), 'leaf', pairs)  14.3 us
    dot_general x13, matrix products, plain_dot(): return jnp.dot(former, latter, preferred_element_type=jnp.float32)  9.55 us
    dot_general x12, matrix products, across(): lax.dot_general(former, latter, (((1,), (1,)), ((), ())), preferred_eleme...  8.82 us
    unnamed x29, local copies, waits for them, and re-layouts  5.39 us
    ppermute x2, starting transfers between devices, shards(): incoming = lax.ppermute(jnp.concatenate(pieces, axis=0), 'leaf', pairs)  4.83 us
    unnamed x3, other arithmetic  1.34 us
  transfers between devices with their start and end apart: 2, of which 2 were waited for; matrix products, arithmetic and copies ran while one was open for 1% of the time, Pallas kernels for 0%

profile of v1, /device:TPU:0, one launch (start us, length us, event | category | flops | bytes accessed | tf_op | source)
XLA Modules:
  0.0 63.0 jit_solution(222626306581348558)
XLA Ops:
  0.6 0.0 copy-start
  0.6 0.0 copy-start.9
  0.7 0.7 %copy-done.9 = s32[128]{0:T(128)S(1)} copy-done((s32[128]{0:T(128)S(1)}, s32[128]{0:T(128)}, u32[]{:S(2)}) %copy-start.9) | copy-done | bytes 536
  1.4 0.9 %fusion.174 = (bf16[128,128]{0,1:T(8,128)(2,1)S(1)}, f32[128,128]{0,1:T(8,128)S(1)}) fusion(bf16[512,512]{1,0:T(8,128)(2,1)} %param.16, f32[128,512]{0,1:T(8,128)S(1)} %fusion.14), kind=kOutput, calls=%fused_computation.188 | convolution fusion | flops 4227072 | bytes 229376 | tf_op jit(solution)/shard_map/dot_general | solution.py:10
  2.3 1.0 %fusion.175 = (bf16[128,128]{0,1:T(8,128)(2,1)S(1)}, f32[128,128]{0,1:T(8,128)S(1)}) fusion(bf16[128,128]{0,1:T(8,128)(2,1)S(1)} %get-tuple-element.20, bf16[128,128]{0,1:T(8,128)(2,1)S(1)} %slice.452, bf16[512,512]{1,0:T(8,128)(2,1)} %param.16, f32[128,512]{0,1:T(8,128)S(1)} %fusion.14), kind=kOutput, calls=%fused_computation.189 | convolution fusion | flops 8552448 | bytes 294912 | tf_op jit(solution)/shard_map/dot_general | solution.py:10
  3.3 0.0 copy-start.7
  3.3 1.1 %convolution_subtract_fusion.5 = f32[128,128]{0,1:T(8,128)S(1)} fusion(bf16[128,128]{0,1:T(8,128)(2,1)S(1)} %get-tuple-element.22, bf16[128,128]{0,1:T(8,128)(2,1)S(1)} %get-tuple-element.20, bf16[128,128]{0,1:T(8,128)(2,1)S(1)} %slice.452, bf16[512,512]{1,0:T(8,128)(2,1)} %param.16, f32[128,512]{0,1:T(8,128)S(1)} %fusion.14), kind=kOutput, calls=%fused_computation.8 | convolution fusion | flops 12894208 | bytes 327680 | tf_op jit(solution)/shard_map/dot_general | solution.py:10
  4.4 0.0 copy-done.7
  4.4 0.2 slice_reduce_fusion
  4.6 0.1 broadcast_bitcast_fusion
  4.7 0.0 copy-done
  4.7 0.2 convolution_multiply_fusion.1
  4.9 0.0 copy-start.6
  5.0 0.0 copy-start.8
  5.0 0.8 %copy-done.6 = f32[128,128]{1,0:T(8,128)S(1)} copy-done((f32[128,128]{1,0:T(8,128)S(1)}, f32[128,128]{1,0:T(8,128)}, u32[]{:S(2)}) %copy-start.6) | copy-done | bytes 65560
  5.8 0.0 copy-done.8
  5.8 0.4 convolution_bitcast_fusion
  6.2 0.5 copy-done.3
  6.7 0.2 fusion.165
  6.9 1.1 %fusion.166 = (bf16[128,128]{0,1:T(8,128)(2,1)S(1)}, f32[128,128]{0,1:T(8,128)S(1)}) fusion(bf16[4,128,128]{2,1,0:T(8,128)(2,1)S(1)} %copy-done.3, bf16[128,128]{0,1:T(8,128)(2,1)S(1)} %get-tuple-element.14, f32[128,512]{0,1:T(8,128)S(1)} %convolution_bitcast_fusion, bf16[512,512]{1,0:T(8,128)(2,1)} %param.17), kind=kOutput, calls=%fused_computation.186 | convolution fusion | flops 8437760 | bytes 262144 | tf_op jit(solution)/shard_map/dot_general | solution.py:16
  8.0 1.2 %fusion.169 = (bf16[128,128]{0,1:T(8,128)(2,1)S(1)}, f32[128,128]{0,1:T(8,128)S(1)}) fusion(bf16[4,128,128]{2,1,0:T(8,128)(2,1)S(1)} %copy-done.3, f32[128,512]{0,1:T(8,128)S(1)} %convolution_bitcast_fusion, bf16[128,128]{0,1:T(8,128)(2,1)S(1)} %get-tuple-element.16, bf16[128,128]{0,1:T(8,128)(2,1)S(1)} %get-tuple-element.14, bf16[512,512]{1,0:T(8,128)(2,1)} %param.17), kind=kOutput, calls=%fused_computation.187 | convolution fusion | flops 12763136 | bytes 327680 | tf_op jit(solution)/shard_map/dot_general | solution.py:16
  9.2 0.0 copy-start.1
  9.2 1.3 %fusion.11 = f32[128,128]{0,1:T(8,128)S(1)} fusion(bf16[128,128]{0,1:T(8,128)(2,1)S(1)} %get-tuple-element.18, bf16[128,128]{0,1:T(8,128)(2,1)S(1)} %get-tuple-element.16, bf16[128,128]{0,1:T(8,128)(2,1)S(1)} %get-tuple-element.14, bf16[512,512]{1,0:T(8,128)(2,1)} %param.17, f32[128,512]{0,1:T(8,128)S(1)} %convolution_bitcast_fusion, ...), kind=kOutput, calls=%fused_computation.29 | convolution fusion | flops 17104896 | bytes 360448 | tf_op jit(solution)/shard_map/dot_general | solution.py:16
  10.5 0.0 copy-done.1
  10.5 0.2 convolution_multiply_fusion
  10.8 0.0 copy-start.5
  10.8 0.0 copy-start.4
  10.8 0.6 slice.200
  11.4 0.3 copy-done.5
  11.7 0.7 %convert_dynamic-update-slice_fusion.3 = f32[1024,128]{1,0:T(8,128)S(1)} fusion(f32[1024,128]{1,0:T(8,128)S(1)} %slice_dynamic-update-slice_fusion, bf16[2,256,128]{2,1,0:T(8,128)(2,1)S(1)} %copy-done.5, bf16[]{:T(256)} %bitcast.6), kind=kLoop, calls=%fused_computation.114 | loop fusion | flops 81920 | bytes 98306
  12.3 0.0 copy-done.4
  12.4 0.0 copy-start.2
  12.4 0.7 %convert_dynamic-update-slice_fusion.2 = f32[1024,128]{1,0:T(8,128)S(1)} fusion(f32[1024,128]{1,0:T(8,128)S(1)} %convert_dynamic-update-slice_fusion.3, bf16[2,128,256]{2,1,0:T(8,128)(2,1)S(1)} %copy-done.4, bf16[]{:T(256)} %bitcast.6), kind=kLoop, calls=%fused_computation.113 | loop fusion | flops 81920 | bytes 98306
  13.1 0.1 copy-done.2
  13.2 3.0 %collective-permute-start = (f32[1024,128]{1,0:T(8,128)S(1)}, f32[1024,128]{1,0:T(8,128)S(1)}, u32[]{:S(2)}, u32[]{:S(2)}) collective-permute-start(f32[1024,128]{1,0:T(8,128)S(1)} %convert_dynamic-update-slice_fusion), channel_id=1, source_target_pairs={{0,8},{8,0},{16,24},{24,16},{1,9},{9,1},{17,25},{25,17},{2,10},{10... | collective-permute-start | bytes 1572872 | tf_op jit(solution)/shard_map/ppermute | solution.py:135
  16.2 11.9 %collective-permute-done = f32[1024,128]{1,0:T(8,128)S(1)} collective-permute-done((f32[1024,128]{1,0:T(8,128)S(1)}, f32[1024,128]{1,0:T(8,128)S(1)}, u32[]{:S(2)}, u32[]{:S(2)}) %collective-permute-start) | collective-permute-done | bytes 524320 | tf_op jit(solution)/shard_map/ppermute | solution.py:135
  28.2 0.8 %fusion.72 = f32[128,128]{1,0:T(8,128)S(1)} fusion(f32[1024,128]{1,0:T(8,128)S(1)} %collective-permute-done, f32[128,256]{1,0:T(8,128)S(1)} %convolution_multiply_fusion.1, bf16[1024,128]{1,0:T(8,128)(2,1)S(1)} %convert.56, pred[]{:T(512)S(6)} %and.21, bf16[2,256,128]{2,1,0:T(8,128)(2,1)S(1)} %copy-done.5, bf16[]{:T(256)} %bitcast.6), kind=kOutput, calls=%fused_computation.90 | convolution fusion | flops 4308992 | bytes 393219 | tf_op jit(solution)/shard_map/dot_general | solution.py:10
  29.0 0.2 fusion.104
  29.2 0.8 %fusion.71 = f32[128,128]{1,0:T(8,128)S(1)} fusion(f32[1024,128]{1,0:T(8,128)S(1)} %collective-permute-done, f32[128,256]{1,0:T(8,128)S(1)} %convolution_multiply_fusion, f32[128,128]{0,1:T(8,128)S(1)} %fusion.104, bf16[1024,128]{1,0:T(8,128)(2,1)S(1)} %convert.56, pred[]{:T(512)S(6)} %and.21, bf16[2,128,256]{2,1,0:T(8,128)(2,1)S(1)} %copy-done.4, bf16[]{:T(256)} %bitcast.6), kind=kOutput, calls=%fused_computation.88 | convolution fusion | flops 4276224 | bytes 327683 | tf_op jit(solution)/shard_map/dot_general | solution.py:16
  30.1 1.8 %collective-permute-start.1 = (f32[384,128]{1,0:T(8,128)S(1)}, f32[384,128]{1,0:T(8,128)S(1)}, u32[]{:S(2)}, u32[]{:S(2)}) collective-permute-start(f32[384,128]{1,0:T(8,128)S(1)} %pad_maximum_fusion.4), channel_id=1, source_target_pairs={{0,16},{8,24},{16,0},{24,8},{1,17},{9,25},{17,1},{25,9},{2,18},{10... | collective-permute-start | bytes 589832 | tf_op jit(solution)/shard_map/ppermute | solution.py:135
  31.9 0.7 %copy-done.10 = u32[32]{0:T(128)S(1)} copy-done((u32[32]{0:T(128)S(1)}, u32[32]{0:T(128)}, u32[]{:S(2)}) %copy-start.10) | copy-done | bytes 152
  32.6 0.6 dynamic-slice
  33.8 0.1 copy.24
  33.9 2.3 %collective-permute-done.1 = f32[384,128]{1,0:T(8,128)S(1)} collective-permute-done((f32[384,128]{1,0:T(8,128)S(1)}, f32[384,128]{1,0:T(8,128)S(1)}, u32[]{:S(2)}, u32[]{:S(2)}) %collective-permute-start.1) | collective-permute-done | bytes 196640 | tf_op jit(solution)/shard_map/ppermute | solution.py:135
  36.2 0.2 fusion.110
  36.4 0.8 %fusion.121 = f32[128,128]{1,0:T(8,128)S(1)} fusion(f32[128,128]{0,1:T(8,128)S(1)} %fusion.110, bf16[1024,128]{1,0:T(8,128)(2,1)S(1)} %convert.56, pred[]{:T(512)S(6)} %and.21, bf16[2,256,128]{2,1,0:T(8,128)(2,1)S(1)} %copy-done.5, bf16[]{:T(256)} %bitcast.6), kind=kOutput, calls=%fused_computation.142 | convolution fusion | flops 4243456 | bytes 196611 | tf_op jit(solution)/shard_map/dot_general | solution.py:16
  37.3 0.1 copy.25
  37.4 0.3 convolution_subtract_fusion
  37.7 1.0 %fusion.176 = (bf16[128,128]{0,1:T(8,128)(2,1)S(1)}, f32[128,128]{0,1:T(8,128)S(1)}) fusion(bf16[512,512]{1,0:T(8,128)(2,1)} %param.16, f32[128,512]{0,1:T(8,128)S(1)} %convolution_subtract_fusion), kind=kOutput, calls=%fused_computation.190 | convolution fusion | flops 4227072 | bytes 229376 | tf_op jit(solution)/shard_map/dot_general | solution.py:16
  38.7 0.1 fusion.106
  38.8 0.1 copy.22
  39.0 0.9 %fusion.10 = f32[128,128]{1,0:T(8,128)S(1)} fusion(f32[128,128]{0,1:T(8,128)S(1)} %fusion.106, f32[1024,128]{1,0:T(8,128)S(1)} %collective-permute-done, f32[128,256]{1,0:T(8,128)S(1)} %convolution_multiply_fusion.1, bf16[1024,128]{1,0:T(8,128)(2,1)S(1)} %convert.56, pred[]{:T(512)S(6)} %and.21, bf16[2,128,128]{2,1,0:T(8,128)(2,1)S(1)} %copy-done.2, ...), kind=kOutput, calls=%fused_computation.28 | convolution fusion | flops 8519680 | bytes 394242 | tf_op jit(solution)/shard_map/dot_general | solution.py:10
  39.9 0.2 convolution_subtract_fusion.1
  40.1 0.1 fusion.178
  40.3 1.0 %fusion.179 = (bf16[128,128]{0,1:T(8,128)(2,1)S(1)}, f32[128,128]{0,1:T(8,128)S(1)}) fusion(bf16[128,128]{0,1:T(8,128)(2,1)S(1)} %get-tuple-element.28, f32[128,512]{0,1:T(8,128)S(1)} %convolution_subtract_fusion.1, bf16[512,512]{1,0:T(8,128)(2,1)} %param.17, bf16[4,128,128]{2,1,0:T(8,128)(2,1)S(1)} %copy-done.3), kind=kOutput, calls=%fused_computation.193 | convolution fusion | flops 8437760 | bytes 262144 | tf_op jit(solution)/shard_map/dot_general | solution.py:10
  41.3 1.1 %fusion.182 = (bf16[128,128]{0,1:T(8,128)(2,1)S(1)}, f32[128,128]{0,1:T(8,128)S(1)}) fusion(f32[128,512]{0,1:T(8,128)S(1)} %convolution_subtract_fusion.1, bf16[128,128]{0,1:T(8,128)(2,1)S(1)} %get-tuple-element.28, bf16[128,128]{0,1:T(8,128)(2,1)S(1)} %get-tuple-element.30, bf16[512,512]{1,0:T(8,128)(2,1)} %param.17, bf16[4,128,128]{2,1,0:T(8,128)(2,1)S(1)} %copy-done.3), kind=kOutput, calls=%fused_computation.194 | convolution fusion | flops 12763136 | bytes 327680 | tf_op jit(solution)/shard_map/dot_general | solution.py:10
  42.5 1.2 %fusion.7 = f32[128,128]{0,1:T(8,128)S(1)} fusion(bf16[128,128]{0,1:T(8,128)(2,1)S(1)} %get-tuple-element.28, bf16[128,128]{0,1:T(8,128)(2,1)S(1)} %get-tuple-element.30, bf16[128,128]{0,1:T(8,128)(2,1)S(1)} %get-tuple-element.32, bf16[512,512]{1,0:T(8,128)(2,1)} %param.17, f32[128,512]{0,1:T(8,128)S(1)} %convolution_subtract_fusion.1, ...), kind=kOutput, calls=%fused_computation.25 | convolution fusion | flops 17104896 | bytes 360448 | tf_op jit(solution)/shard_map/dot_general | solution.py:10
  43.7 1.1 %fusion.177 = (bf16[128,128]{0,1:T(8,128)(2,1)S(1)}, f32[128,128]{0,1:T(8,128)S(1)}) fusion(bf16[512,512]{1,0:T(8,128)(2,1)} %param.16, bf16[128,128]{0,1:T(8,128)(2,1)S(1)} %slice.451, bf16[128,128]{0,1:T(8,128)(2,1)S(1)} %get-tuple-element.24, f32[128,512]{0,1:T(8,128)S(1)} %convolution_subtract_fusion), kind=kOutput, calls=%fused_computation.191 | convolution fusion | flops 8552448 | bytes 294912 | tf_op jit(solution)/shard_map/dot_general | solution.py:16
  44.7 1.1 %convolution_subtract_fusion.8 = f32[128,128]{0,1:T(8,128)S(1)} fusion(bf16[128,128]{0,1:T(8,128)(2,1)S(1)} %slice.451, bf16[128,128]{0,1:T(8,128)(2,1)S(1)} %get-tuple-element.24, bf16[128,128]{0,1:T(8,128)(2,1)S(1)} %get-tuple-element.26, bf16[512,512]{1,0:T(8,128)(2,1)} %param.16, f32[128,512]{0,1:T(8,128)S(1)} %convolution_subtract_fusion), kind=kOutput, calls=%fused_computation.11 | convolution fusion | flops 12894208 | bytes 327680 | tf_op jit(solution)/shard_map/dot_general | solution.py:16
  45.9 0.1 multiply_reduce_fusion
  46.0 0.8 %copy.27 = f32[128,512]{1,0:T(8,128)} copy(f32[128,512]{0,1:T(8,128)S(1)} %get-tuple-element.12) | data formatting | bytes 524288
  46.9 0.8 %copy.28 = f32[128,512]{1,0:T(8,128)} copy(f32[128,512]{0,1:T(8,128)S(1)} %get-tuple-element.13) | data formatting | bytes 524288
  47.7 14.8 %all-reduce = f32[512]{0:T(512)S(1)} all-reduce(f32[512]{0:T(512)S(1)} %get-tuple-element.11), channel_id=2, replica_groups=mesh['leaf'=4,'src'=8] {'src'}, use_global_device_ids=true, to_apply=%region_1.2.clone | all-reduce | flops 512 | bytes 4096
  62.4 0.6 dynamic-slice_multiply_fusion
  (22 shorter events, 0.2 us)
Async XLA Ops:
  0.6 4.1 %copy-start = (bf16[256,512]{1,0:T(8,128)(2,1)S(1)}, bf16[256,512]{1,0:T(8,128)(2,1)}, u32[]{:S(2)}) copy-start(bf16[256,512]{1,0:T(8,128)(2,1)} %param.19) | copy-start | bytes 786436
  0.6 0.7 %copy-start.9 = (s32[128]{0:T(128)S(1)}, s32[128]{0:T(128)}, u32[]{:S(2)}) copy-start(s32[128]{0:T(128)} %param.12) | copy-start | bytes 1540
  3.3 1.1 %copy-start.7 = (s32[3,2]{0,1:T(2,128)S(1)}, s32[3,2]{0,1:T(2,128)}, u32[]{:S(2)}) copy-start(s32[3,2]{0,1:T(2,128)} %param.15) | copy-start | bytes 76
  4.9 0.8 %copy-start.6 = (f32[128,128]{1,0:T(8,128)S(1)}, f32[128,128]{1,0:T(8,128)}, u32[]{:S(2)}) copy-start(f32[128,128]{1,0:T(8,128)} %param.14) | copy-start | bytes 196612
  5.0 0.8 %copy-start.8 = (s32[128]{0:T(128)S(1)}, s32[128]{0:T(128)}, u32[]{:S(2)}) copy-start(s32[128]{0:T(128)} %param.13) | copy-start | bytes 1540
  5.8 0.9 %copy-start.3 = (bf16[4,128,128]{2,1,0:T(8,128)(2,1)S(1)}, bf16[4,128,128]{2,1,0:T(8,128)(2,1)}, u32[]{:S(2)}) copy-start(bf16[4,128,128]{2,1,0:T(8,128)(2,1)} %param.18) | copy-start | bytes 393220
  9.2 1.3 %copy-start.1 = (bf16[512,256]{1,0:T(8,128)(2,1)S(1)}, bf16[512,256]{1,0:T(8,128)(2,1)}, u32[]{:S(2)}) copy-start(bf16[512,256]{1,0:T(8,128)(2,1)} %param.20) | copy-start | bytes 786436
  10.8 0.9 %copy-start.5 = (bf16[2,256,128]{2,1,0:T(8,128)(2,1)S(1)}, bf16[2,256,128]{2,1,0:T(8,128)(2,1)}, u32[]{:S(2)}) copy-start(bf16[2,256,128]{2,1,0:T(8,128)(2,1)} %param.22) | copy-start | bytes 393220
  10.8 1.5 %copy-start.4 = (bf16[2,128,256]{2,1,0:T(8,128)(2,1)S(1)}, bf16[2,128,256]{2,1,0:T(8,128)(2,1)}, u32[]{:S(2)}) copy-start(bf16[2,128,256]{2,1,0:T(8,128)(2,1)} %param.23) | copy-start | bytes 393220
  12.4 0.8 %copy-start.2 = (bf16[2,128,128]{2,1,0:T(8,128)(2,1)S(1)}, bf16[2,128,128]{2,1,0:T(8,128)(2,1)}, u32[]{:S(2)}) copy-start(bf16[2,128,128]{2,1,0:T(8,128)(2,1)} %param.21) | copy-start | bytes 196612
  13.2 14.9 %collective-permute-start = (f32[1024,128]{1,0:T(8,128)S(1)}, f32[1024,128]{1,0:T(8,128)S(1)}, u32[]{:S(2)}, u32[]{:S(2)}) collective-permute-start(f32[1024,128]{1,0:T(8,128)S(1)} %convert_dynamic-update-slice_fusion), channel_id=1, source_target_pairs={{0,8},{8,0},{16,24},{24,16},{1,9},{9,1},{17,25},{25,17},{2,10},{10... | collective-permute-start | bytes 1572872 | tf_op jit(solution)/shard_map/ppermute | solution.py:135
  30.1 6.2 %collective-permute-start.1 = (f32[384,128]{1,0:T(8,128)S(1)}, f32[384,128]{1,0:T(8,128)S(1)}, u32[]{:S(2)}, u32[]{:S(2)}) collective-permute-start(f32[384,128]{1,0:T(8,128)S(1)} %pad_maximum_fusion.4), channel_id=1, source_target_pairs={{0,16},{8,24},{16,0},{24,8},{1,17},{9,25},{17,1},{25,9},{2,18},{10... | collective-permute-start | bytes 589832 | tf_op jit(solution)/shard_map/ppermute | solution.py:135
  31.9 0.7 %copy-start.10 = (u32[32]{0:T(128)S(1)}, u32[32]{0:T(128)}, u32[]{:S(2)}) copy-start(u32[32]{0:T(128)} %constant.48) | copy-start | bytes 388

commit v2 on v1

--- a/solution.py
+++ b/solution.py
@@ -123,44 +123,53 @@
         upper_panels.append(sep_upper[height - 1, :, height * block_size :] * mask[None, :].astype(jnp.bfloat16))
         inverse_panels.append(sep_inv[height - 1])
 
-    forward_nodes, adjoint_nodes = [], []
-    for height in range(1, levels + 1):
-        stride = 1 << (height - 1)
-        pairs = [(index, index ^ stride) for index in range(leaves)]
-        pieces = list(forward_sums) + list(adjoint_sums)
-        for upper_level in range(height, levels + 1):
-            pieces.append(lower_panels[upper_level - 1].astype(jnp.float32))
-            pieces.extend(block.astype(jnp.float32) for block in blocks_of(upper_panels[upper_level - 1]))
-            pieces.append(inverse_panels[upper_level - 1].astype(jnp.float32))
+    def exchange(values, pairs):
+        pieces = [piece for piece in values]
         incoming = lax.ppermute(jnp.concatenate(pieces, axis=0), "leaf", pairs)
         received, row = [], 0
         for piece in pieces:
             received.append(incoming[row : row + piece.shape[0]])
             row += piece.shape[0]
-        count = len(forward_sums)
-        forward_sums = [mine + theirs for mine, theirs in zip(forward_sums, received[:count])]
-        adjoint_sums = [mine + theirs for mine, theirs in zip(adjoint_sums, received[count : 2 * count])]
-        received = received[2 * count :]
+        return received
+
+    for height in range(1, levels + 1):
+        stride = 1 << (height - 1)
+        pairs = [(index, index ^ stride) for index in range(leaves)]
+        pieces = []
+        for upper_level in range(height, levels + 1):
+            pieces.append(lower_panels[upper_level - 1])
+            pieces.extend(blocks_of(upper_panels[upper_level - 1]))
+            pieces.append(inverse_panels[upper_level - 1])
+        received = exchange(pieces, pairs)
         for upper_level in range(height, levels + 1):
             place = device % (1 << upper_level)
             take = jnp.logical_and(place >= stride, place < 2 * stride)
             width = levels - upper_level
-            lower_in = received[0].astype(jnp.bfloat16)
-            upper_in = jnp.concatenate([block.astype(jnp.bfloat16) for block in received[1 : 1 + width]] or [upper_panels[upper_level - 1]], axis=1)
-            inverse_in = received[1 + width].astype(jnp.bfloat16)
+            lower_in = received[0]
+            upper_in = jnp.concatenate(received[1 : 1 + width] or [upper_panels[upper_level - 1]], axis=1)
+            inverse_in = received[1 + width]
             received = received[2 + width :]
             lower_panels[upper_level - 1] = jnp.where(take, lower_in, lower_panels[upper_level - 1])
             upper_panels[upper_level - 1] = jnp.where(take, upper_in, upper_panels[upper_level - 1])
             inverse_panels[upper_level - 1] = jnp.where(take, inverse_in, inverse_panels[upper_level - 1])
+
+    forward_nodes, adjoint_nodes = [], []
+    for height in range(1, levels + 1):
+        stride = 1 << (height - 1)
+        pairs = [(index, index ^ stride) for index in range(leaves)]
+        forward_sums = [mine + theirs for mine, theirs in zip(forward_sums, exchange(forward_sums, pairs))]
         forward_node = -forward_sums[0]
-        adjoint_node = plain_dot(as_half(-adjoint_sums[0]), inverse_panels[height - 1])
         forward_nodes.append(forward_node)
-        adjoint_nodes.append(adjoint_node)
-        forward_sums, adjoint_sums = forward_sums[1:], adjoint_sums[1:]
+        forward_sums = forward_sums[1:]
         if forward_sums:
             forward_coupling = blocks_of(across(as_half(forward_node), lower_panels[height - 1]))
+            forward_sums = [total + extra for total, extra in zip(forward_sums, forward_coupling)]
+        adjoint_sums = [mine + theirs for mine, theirs in zip(adjoint_sums, exchange(adjoint_sums, pairs))]
+        adjoint_node = plain_dot(as_half(-adjoint_sums[0]), inverse_panels[height - 1])
+        adjoint_nodes.append(adjoint_node)
+        adjoint_sums = adjoint_sums[1:]
+        if adjoint_sums:
             adjoint_coupling = blocks_of(plain_dot(as_half(adjoint_node), upper_panels[height - 1]))
-            forward_sums = [total + extra for total, extra in zip(forward_sums, forward_coupling)]
             adjoint_sums = [total + extra for total, extra in zip(adjoint_sums, adjoint_coupling)]
 
     forward_above, adjoint_above = [], []
@@ -184,7 +193,9 @@
     adjoint_remain = z_leaf - plain_dot(as_half(adjoint_above * base_mask), anc_lower)
     adjoint_field = lower_t_solve(adjoint_remain, leaf_lower, block_size, block_count)
     partial_gradient = jnp.sum(forward_field * adjoint_field, axis=0)
-    gradient = lax.psum_scatter(partial_gradient, "src", scatter_dimension=0, tiled=True) * factor
+    spread = lax.axis_size("src")
+    gathered = lax.all_to_all(partial_gradient.reshape(spread, -1), "src", 0, 0, tiled=True)
+    gradient = jnp.sum(gathered, axis=0) * factor
     return (forward_field, adjoint_field, gradient)
 
 

time: 63.9 us -> 38.4 us (0.60)
  blocking collectives: 14.8 us -> 0 us
  matrix products: 18.7 us -> 6.11 us
  starting transfers between devices: 4.83 us -> 13.2 us
  waiting for transfers between devices: 14.3 us -> 8.53 us
  other arithmetic: 2.21 us -> 2.96 us
  between operations: 1.68 us -> 0.99 us
    unnamed x1 -> x0, blocking collectives: 14.8 us -> none
    ppermute x2 -> x6, waiting for transfers between devices: 14.3 us -> 4.64 us  [exchange(): incoming = lax.ppermute(jnp.concatenate(pieces, axis=0), 'leaf', pairs)]
    dot_general x13, matrix products: 9.55 us -> 3.21 us  [plain_dot(): return jnp.dot(former, latter, preferred_element_type=jnp.float32)]
    dot_general x12, matrix products: 8.82 us -> 2.52 us  [across(): lax.dot_general(former, latter, (((1,), (1,)), ((), ())), preferred_eleme...]
    all_to_all x0 -> x1, starting transfers between devices: none -> 4.88 us  [shards(): lax.all_to_all(partial_gradient.reshape(spread, -1), 'src', 0, 0, tiled=T...]
    all_to_all x0 -> x1, waiting for transfers between devices: none -> 3.89 us  [shards(): lax.all_to_all(partial_gradient.reshape(spread, -1), 'src', 0, 0, tiled=T...]
    ppermute x2 -> x6, starting transfers between devices: 4.83 us -> 8.33 us  [exchange(): incoming = lax.ppermute(jnp.concatenate(pieces, axis=0), 'leaf', pairs)]
    unnamed x29 -> x20, local copies, waits for them, and re-layouts: 5.39 us -> 3.53 us
  transfers between devices with their start and end apart: 2 -> 7, of which waited for: 2 -> 4; matrix products, arithmetic and copies ran while one was open for 1% -> 16% of each run, Pallas kernels for 0% -> 0%
where the time goes in v2:
time: 38.4 us; the launch traced here: 38 us
  starting transfers between devices  13.2 us (34%)
  waiting for transfers between devices  8.53 us (22%)
  local copies, waits for them, and re-layouts  6.18 us (16%)
  matrix products  6.11 us (16%)
  other arithmetic  2.96 us (8%)
  between operations  0.99 us (3%)
    ppermute x6, starting transfers between devices, exchange(): incoming = lax.ppermute(jnp.concatenate(pieces, axis=0), 'leaf', pairs)  8.33 us
    all_to_all x1, starting transfers between devices, shards(): lax.all_to_all(partial_gradient.reshape(spread, -1), 'src', 0, 0, tiled=T...  4.88 us
    ppermute x6, waiting for transfers between devices, exchange(): incoming = lax.ppermute(jnp.concatenate(pieces, axis=0), 'leaf', pairs)  4.64 us
    all_to_all x1, waiting for transfers between devices, shards(): lax.all_to_all(partial_gradient.reshape(spread, -1), 'src', 0, 0, tiled=T...  3.89 us
    unnamed x20, local copies, waits for them, and re-layouts  3.53 us
    dot_general x13, matrix products, plain_dot(): return jnp.dot(former, latter, preferred_element_type=jnp.float32)  3.21 us
    dot_general x12, matrix products, across(): lax.dot_general(former, latter, (((1,), (1,)), ((), ())), preferred_eleme...  2.52 us
    mul x1, other arithmetic, shards(): sep_upper[height - 1, :, height * block_size:]  1.43 us
  transfers between devices with their start and end apart: 7, of which 4 were waited for; matrix products, arithmetic and copies ran while one was open for 16% of the time, Pallas kernels for 0%

profile of v2, /device:TPU:0, one launch (start us, length us, event | category | flops | bytes accessed | tf_op | source)
XLA Modules:
  0.0 38.0 jit_solution(6434293224536512428)
XLA Ops:
  0.6 0.0 copy-start
  0.7 0.8 %convert_element_type.101 = f32[3,2]{0,1:T(2,128)S(1)} convert(s32[3,2]{0,1:T(2,128)} %param.15) | non-fusion elementwise | flops 6 | bytes 48 | tf_op jit(solution)/shard_map/convert_element_type | solution.py:97
  1.4 0.2 slice_reduce_fusion
  1.6 0.6 %slice.175 = bf16[1]{0:T(256)(128)(2,1)} slice(bf16[2]{0:T(256)(128)(2,1)S(1)} %compare_select_fusion), slice={[1:2]} | slice | bytes 4 | tf_op jit(solution)/shard_map/slice | solution.py:121
  2.2 0.8 %slice_bitcast_fusion.1 = (bf16[128,128]{1,0:T(8,128)(2,1)S(1)}, bf16[128,128]{1,0:T(8,128)(2,1)S(1)}) fusion(bf16[2,128,128]{2,1,0:T(8,128)(2,1)} %param.21), kind=kLoop, calls=%fused_computation.138 | loop fusion | bytes 131072 | tf_op jit(solution)/shard_map/squeeze | solution.py:124
  3.0 1.4 %multiply_bitcast_fusion = (bf16[128,128]{1,0:T(8,128)(2,1)S(1)}, bf16[128,128]{1,0:T(8,128)(2,1)S(1)}) fusion(bf16[2,128,256]{2,1,0:T(8,128)(2,1)} %param.23, bf16[]{:T(256)} %bitcast.1, bf16[2,256,128]{2,1,0:T(8,128)(2,1)} %param.22), kind=kLoop, calls=%fused_computation.139 | loop fusion | flops 32768 | bytes 131074 | tf_op jit(solution)/shard_map/mul | solution.py:123
  4.4 3.0 %collective-permute-start.1 = (bf16[512,128]{1,0:T(8,128)(2,1)S(1)}, bf16[512,128]{1,0:T(8,128)(2,1)S(1)}, u32[]{:S(2)}, u32[]{:S(2)}) collective-permute-start(bf16[512,128]{1,0:T(8,128)(2,1)S(1)} %pad_maximum_fusion.5), channel_id=1, source_target_pairs={{0,8},{8,0},{16,24},{24,16},{1,9},{9,1},{17,25},{25,17},{2,10},{10... | collective-permute-start | bytes 393224 | tf_op jit(solution)/shard_map/ppermute | solution.py:128
  7.4 0.7 %copy-done.8 = s32[128]{0:T(128)S(1)} copy-done((s32[128]{0:T(128)S(1)}, s32[128]{0:T(128)}, u32[]{:S(2)}) %copy-start.8) | copy-done | bytes 536
  8.2 0.1 broadcast_bitcast_fusion
  8.2 0.1 fusion.173
  8.4 0.1 fusion.174
  8.5 0.2 convolution_subtract_fusion.5
  8.7 0.0 copy-start.6
  8.7 0.2 convolution_multiply_fusion.1
  9.0 0.0 copy-start.4
  9.0 0.0 copy-start.7
  9.0 0.0 copy-start.3
  9.0 0.1 collective-permute-start
  9.1 0.4 %copy-done.6 = f32[128,128]{1,0:T(8,128)S(1)} copy-done((f32[128,128]{1,0:T(8,128)S(1)}, f32[128,128]{1,0:T(8,128)}, u32[]{:S(2)}) %copy-start.6) | copy-done | bytes 65560
  9.6 0.2 copy-done.7
  9.7 0.4 convolution_bitcast_fusion
  10.1 0.2 fusion.162
  10.3 0.3 fusion.163
  10.7 0.4 fusion.166
  11.0 0.0 copy-start.1
  11.1 0.4 fusion.10
  11.4 0.6 %copy-done.1 = bf16[512,256]{1,0:T(8,128)(2,1)S(1)} copy-done((bf16[512,256]{1,0:T(8,128)(2,1)S(1)}, bf16[512,256]{1,0:T(8,128)(2,1)}, u32[]{:S(2)}) %copy-start.1) | copy-done | bytes 262168
  12.0 0.2 convolution_multiply_fusion
  12.2 0.0 copy-start.2
  12.3 1.5 %collective-permute-start.4 = (f32[256,128]{1,0:T(8,128)S(1)}, f32[256,128]{1,0:T(8,128)S(1)}, u32[]{:S(2)}, u32[]{:S(2)}) collective-permute-start(f32[256,128]{1,0:T(8,128)S(1)} %pad_maximum_fusion.6), channel_id=1, source_target_pairs={{0,8},{8,0},{16,24},{24,16},{1,9},{9,1},{17,25},{25,17},{2,10},{10... | collective-permute-start | bytes 393224 | tf_op jit(solution)/shard_map/ppermute | solution.py:128
  13.8 0.0 collective-permute-done.1
  13.8 1.6 %collective-permute-start.3 = (bf16[128,128]{1,0:T(8,128)(2,1)S(1)}, bf16[128,128]{1,0:T(8,128)(2,1)S(1)}, u32[]{:S(2)}, u32[]{:S(2)}) collective-permute-start(bf16[128,128]{1,0:T(8,128)(2,1)S(1)} %slice_select_fusion.2), channel_id=1, source_target_pairs={{0,16},{8,24},{16,0},{24,8},{1,17},{9,25},{17,1},{25,9},{2,18},{10... | collective-permute-start | bytes 98312 | tf_op jit(solution)/shard_map/ppermute | solution.py:128
  15.4 1.9 %collective-permute-done.4 = f32[256,128]{1,0:T(8,128)S(1)} collective-permute-done((f32[256,128]{1,0:T(8,128)S(1)}, f32[256,128]{1,0:T(8,128)S(1)}, u32[]{:S(2)}, u32[]{:S(2)}) %collective-permute-start.4) | collective-permute-done | bytes 131104 | tf_op jit(solution)/shard_map/ppermute | solution.py:128
  17.3 0.2 fusion.103
  17.5 0.2 fusion.62
  17.7 1.6 %collective-permute-start.5 = (f32[128,128]{1,0:T(8,128)S(1)}, f32[128,128]{1,0:T(8,128)S(1)}, u32[]{:S(2)}, u32[]{:S(2)}) collective-permute-start(f32[128,128]{1,0:T(8,128)S(1)} %fusion.62), channel_id=1, source_target_pairs={{0,16},{8,24},{16,0},{24,8},{1,17},{9,25},{17,1},{25,9},{2,18},{10... | collective-permute-start | bytes 196616 | tf_op jit(solution)/shard_map/ppermute | solution.py:128
  19.3 0.0 collective-permute-done
  19.3 0.2 fusion.71
  19.5 0.1 copy.38
  19.6 0.6 %collective-permute-start.2 = (f32[128,128]{1,0:T(8,128)S(1)}, f32[128,128]{1,0:T(8,128)S(1)}, u32[]{:S(2)}, u32[]{:S(2)}) collective-permute-start(f32[128,128]{1,0:T(8,128)S(1)} %fusion.71), channel_id=1, source_target_pairs={{0,16},{8,24},{16,0},{24,8},{1,17},{9,25},{17,1},{25,9},{2,18},{10... | collective-permute-start | bytes 196616 | tf_op jit(solution)/shard_map/ppermute | solution.py:128
  20.1 1.9 %collective-permute-done.5 = f32[128,128]{1,0:T(8,128)S(1)} collective-permute-done((f32[128,128]{1,0:T(8,128)S(1)}, f32[128,128]{1,0:T(8,128)S(1)}, u32[]{:S(2)}, u32[]{:S(2)}) %collective-permute-start.5) | collective-permute-done | bytes 65568 | tf_op jit(solution)/shard_map/ppermute | solution.py:128
  22.0 0.2 fusion.100
  22.3 0.1 copy.40
  22.4 0.2 fusion.114
  22.6 0.3 convolution_subtract_fusion
  22.9 0.2 fusion.171
  23.1 0.8 %collective-permute-done.2 = f32[128,128]{1,0:T(8,128)S(1)} collective-permute-done((f32[128,128]{1,0:T(8,128)S(1)}, f32[128,128]{1,0:T(8,128)S(1)}, u32[]{:S(2)}, u32[]{:S(2)}) %collective-permute-start.2) | collective-permute-done | bytes 65568 | tf_op jit(solution)/shard_map/ppermute | solution.py:128
  23.9 0.1 fusion.99
  24.0 0.1 copy.30
  24.1 0.3 fusion.13
  24.5 0.2 convolution_subtract_fusion.1
  24.7 0.1 fusion.175
  24.8 0.3 fusion.176
  25.1 0.3 fusion.179
  25.4 0.3 fusion.7
  25.7 0.2 fusion.172
  25.9 0.2 convolution_subtract_fusion.8
  26.2 0.1 multiply_reduce_fusion
  26.3 0.7 %all_to_all.6 = f32[8,1,64]{2,1,0:T(1,128)} reshape(f32[512]{0:T(512)S(1)} %get-tuple-element.14) | data formatting | bytes 4096 | tf_op jit(solution)/shard_map/all_to_all | solution.py:197
  27.0 4.9 %all-to-all-start = ((f32[8,1,64]{2,1,0:T(1,128)}), f32[8,1,64]{2,1,0:T(1,128)S(1)}, u32[]{:S(2)}, u32[]{:S(2)}) async-start(f32[8,1,64]{2,1,0:T(1,128)} %all_to_all.6), calls=%async_computation | async-start | bytes 8192 | tf_op jit(solution)/shard_map/all_to_all | solution.py:197
  31.9 0.8 %copy.43 = f32[128,512]{1,0:T(8,128)} copy(f32[128,512]{0,1:T(8,128)S(1)} %get-tuple-element.15) | data formatting | bytes 524288
  32.7 0.8 %copy.44 = f32[128,512]{1,0:T(8,128)} copy(f32[128,512]{0,1:T(8,128)S(1)} %get-tuple-element.16) | data formatting | bytes 524288
  33.6 3.9 %all-to-all-done = f32[8,1,64]{2,1,0:T(1,128)S(1)} async-done(((f32[8,1,64]{2,1,0:T(1,128)}), f32[8,1,64]{2,1,0:T(1,128)S(1)}, u32[]{:S(2)}, u32[]{:S(2)}) %all-to-all-start) | async-done | bytes 2080 | tf_op jit(solution)/shard_map/all_to_all | solution.py:197
  37.5 0.5 %broadcast_multiply_fusion = f32[64]{0:T(128)} fusion(f32[64]{0:T(128)S(1)} %reduce_sum.19), kind=kLoop, calls=%fused_computation.159 | loop fusion | flops 64 | bytes 512 | tf_op jit(solution)/shard_map/mul | solution.py:198
  (24 shorter events, 0.2 us)
Async XLA Ops:
  0.6 8.1 %copy-start = (bf16[256,512]{1,0:T(8,128)(2,1)S(1)}, bf16[256,512]{1,0:T(8,128)(2,1)}, u32[]{:S(2)}) copy-start(bf16[256,512]{1,0:T(8,128)(2,1)} %param.19) | copy-start | bytes 786436
  0.6 7.6 %copy-start.5 = (bf16[512,512]{1,0:T(8,128)(2,1)S(1)}, bf16[512,512]{1,0:T(8,128)(2,1)}, u32[]{:S(2)}) copy-start(bf16[512,512]{1,0:T(8,128)(2,1)} %param.16) | copy-start | bytes 1572868
  4.4 9.4 %collective-permute-start.1 = (bf16[512,128]{1,0:T(8,128)(2,1)S(1)}, bf16[512,128]{1,0:T(8,128)(2,1)S(1)}, u32[]{:S(2)}, u32[]{:S(2)}) collective-permute-start(bf16[512,128]{1,0:T(8,128)(2,1)S(1)} %pad_maximum_fusion.5), channel_id=1, source_target_pairs={{0,8},{8,0},{16,24},{24,16},{1,9},{9,1},{17,25},{25,17},{2,10},{10... | collective-permute-start | bytes 393224 | tf_op jit(solution)/shard_map/ppermute | solution.py:128
  7.4 0.7 %copy-start.8 = (s32[128]{0:T(128)S(1)}, s32[128]{0:T(128)}, u32[]{:S(2)}) copy-start(s32[128]{0:T(128)} %param.12) | copy-start | bytes 1540
  8.7 0.8 %copy-start.6 = (f32[128,128]{1,0:T(8,128)S(1)}, f32[128,128]{1,0:T(8,128)}, u32[]{:S(2)}) copy-start(f32[128,128]{1,0:T(8,128)} %param.14) | copy-start | bytes 196612
  9.0 1.4 %copy-start.4 = (bf16[512,512]{1,0:T(8,128)(2,1)S(1)}, bf16[512,512]{1,0:T(8,128)(2,1)}, u32[]{:S(2)}) copy-start(bf16[512,512]{1,0:T(8,128)(2,1)} %param.17) | copy-start | bytes 1572868
  9.0 0.7 %copy-start.7 = (s32[128]{0:T(128)S(1)}, s32[128]{0:T(128)}, u32[]{:S(2)}) copy-start(s32[128]{0:T(128)} %param.13) | copy-start | bytes 1540
  9.0 1.1 %copy-start.3 = (bf16[4,128,128]{2,1,0:T(8,128)(2,1)S(1)}, bf16[4,128,128]{2,1,0:T(8,128)(2,1)}, u32[]{:S(2)}) copy-start(bf16[4,128,128]{2,1,0:T(8,128)(2,1)} %param.18) | copy-start | bytes 393220
  9.0 10.3 %collective-permute-start = (f32[256,128]{1,0:T(8,128)S(1)}, f32[256,128]{1,0:T(8,128)S(1)}, u32[]{:S(2)}, u32[]{:S(2)}) collective-permute-start(f32[256,128]{1,0:T(8,128)S(1)} %pad_maximum_fusion.4), channel_id=1, source_target_pairs={{0,8},{8,0},{16,24},{24,16},{1,9},{9,1},{17,25},{25,17},{2,10},{10... | collective-permute-start | bytes 393224 | tf_op jit(solution)/shard_map/ppermute | solution.py:128
  11.0 1.0 %copy-start.1 = (bf16[512,256]{1,0:T(8,128)(2,1)S(1)}, bf16[512,256]{1,0:T(8,128)(2,1)}, u32[]{:S(2)}) copy-start(bf16[512,256]{1,0:T(8,128)(2,1)} %param.20) | copy-start | bytes 786436
  12.2 1.5 %copy-start.2 = (bf16[2,128,128]{2,1,0:T(8,128)(2,1)S(1)}, bf16[2,128,128]{2,1,0:T(8,128)(2,1)}, u32[]{:S(2)}) copy-start(bf16[2,128,128]{2,1,0:T(8,128)(2,1)} %param.21) | copy-start | bytes 196612
  12.3 5.0 %collective-permute-start.4 = (f32[256,128]{1,0:T(8,128)S(1)}, f32[256,128]{1,0:T(8,128)S(1)}, u32[]{:S(2)}, u32[]{:S(2)}) collective-permute-start(f32[256,128]{1,0:T(8,128)S(1)} %pad_maximum_fusion.6), channel_id=1, source_target_pairs={{0,8},{8,0},{16,24},{24,16},{1,9},{9,1},{17,25},{25,17},{2,10},{10... | collective-permute-start | bytes 393224 | tf_op jit(solution)/shard_map/ppermute | solution.py:128
  13.8 6.3 %collective-permute-start.3 = (bf16[128,128]{1,0:T(8,128)(2,1)S(1)}, bf16[128,128]{1,0:T(8,128)(2,1)S(1)}, u32[]{:S(2)}, u32[]{:S(2)}) collective-permute-start(bf16[128,128]{1,0:T(8,128)(2,1)S(1)} %slice_select_fusion.2), channel_id=1, source_target_pairs={{0,16},{8,24},{16,0},{24,8},{1,17},{9,25},{17,1},{25,9},{2,18},{10... | collective-permute-start | bytes 98312 | tf_op jit(solution)/shard_map/ppermute | solution.py:128
  17.7 4.3 %collective-permute-start.5 = (f32[128,128]{1,0:T(8,128)S(1)}, f32[128,128]{1,0:T(8,128)S(1)}, u32[]{:S(2)}, u32[]{:S(2)}) collective-permute-start(f32[128,128]{1,0:T(8,128)S(1)} %fusion.62), channel_id=1, source_target_pairs={{0,16},{8,24},{16,0},{24,8},{1,17},{9,25},{17,1},{25,9},{2,18},{10... | collective-permute-start | bytes 196616 | tf_op jit(solution)/shard_map/ppermute | solution.py:128
  19.6 4.3 %collective-permute-start.2 = (f32[128,128]{1,0:T(8,128)S(1)}, f32[128,128]{1,0:T(8,128)S(1)}, u32[]{:S(2)}, u32[]{:S(2)}) collective-permute-start(f32[128,128]{1,0:T(8,128)S(1)} %fusion.71), channel_id=1, source_target_pairs={{0,16},{8,24},{16,0},{24,8},{1,17},{9,25},{17,1},{25,9},{2,18},{10... | collective-permute-start | bytes 196616 | tf_op jit(solution)/shard_map/ppermute | solution.py:128
  27.0 10.4 %all-to-all-start = ((f32[8,1,64]{2,1,0:T(1,128)}), f32[8,1,64]{2,1,0:T(1,128)S(1)}, u32[]{:S(2)}, u32[]{:S(2)}) async-start(f32[8,1,64]{2,1,0:T(1,128)} %all_to_all.6), calls=%async_computation | async-start | bytes 8192 | tf_op jit(solution)/shard_map/all_to_all | solution.py:197

commit v3 on v2

--- a/solution.py
+++ b/solution.py
@@ -116,12 +116,18 @@
     forward_sums = blocks_of(across(as_half(y_leaf), anc_lower) * base_mask)
     adjoint_sums = blocks_of(plain_dot(as_half(z_leaf), anc_upper) * base_mask)
 
-    lower_panels, upper_panels, inverse_panels = [], [], []
+    lower_panels, upper_panels, inverse_panels, pattern_rows = [], [], [], []
     for height in range(1, levels + 1):
-        mask = level_mask(height)[height * block_size :]
-        lower_panels.append(sep_lower[height - 1, height * block_size :, :] * mask[:, None].astype(jnp.bfloat16))
-        upper_panels.append(sep_upper[height - 1, :, height * block_size :] * mask[None, :].astype(jnp.bfloat16))
+        lower_panels.append(sep_lower[height - 1, height * block_size :, :])
+        upper_panels.append(sep_upper[height - 1, :, height * block_size :])
         inverse_panels.append(sep_inv[height - 1])
+        row = pattern[height].astype(jnp.bfloat16)[None, :]
+        pattern_rows.append(jnp.pad(row, ((0, 7), (0, block_size - levels))))
+
+    def chain_mask(height):
+        level_row = pattern_rows[height - 1][0, :levels].astype(jnp.float32)
+        level_row = level_row * (jnp.arange(1, levels + 1) > height).astype(jnp.float32)
+        return jnp.repeat(level_row, block_size)[height * block_size :]
 
     def exchange(values, pairs):
         pieces = [piece for piece in values]
@@ -140,6 +146,7 @@
             pieces.append(lower_panels[upper_level - 1])
             pieces.extend(blocks_of(upper_panels[upper_level - 1]))
             pieces.append(inverse_panels[upper_level - 1])
+            pieces.append(pattern_rows[upper_level - 1])
         received = exchange(pieces, pairs)
         for upper_level in range(height, levels + 1):
             place = device % (1 << upper_level)
@@ -148,7 +155,9 @@
             lower_in = received[0]
             upper_in = jnp.concatenate(received[1 : 1 + width] or [upper_panels[upper_level - 1]], axis=1)
             inverse_in = received[1 + width]
-            received = received[2 + width :]
+            pattern_in = received[2 + width]
+            received = received[3 + width :]
+            pattern_rows[upper_level - 1] = jnp.where(take, pattern_in, pattern_rows[upper_level - 1])
             lower_panels[upper_level - 1] = jnp.where(take, lower_in, lower_panels[upper_level - 1])
             upper_panels[upper_level - 1] = jnp.where(take, upper_in, upper_panels[upper_level - 1])
             inverse_panels[upper_level - 1] = jnp.where(take, inverse_in, inverse_panels[upper_level - 1])
@@ -162,14 +171,18 @@
         forward_nodes.append(forward_node)
         forward_sums = forward_sums[1:]
         if forward_sums:
-            forward_coupling = blocks_of(across(as_half(forward_node), lower_panels[height - 1]))
+            forward_coupling = blocks_of(
+                across(as_half(forward_node), lower_panels[height - 1]) * chain_mask(height)
+            )
             forward_sums = [total + extra for total, extra in zip(forward_sums, forward_coupling)]
         adjoint_sums = [mine + theirs for mine, theirs in zip(adjoint_sums, exchange(adjoint_sums, pairs))]
         adjoint_node = plain_dot(as_half(-adjoint_sums[0]), inverse_panels[height - 1])
         adjoint_nodes.append(adjoint_node)
         adjoint_sums = adjoint_sums[1:]
         if adjoint_sums:
-            adjoint_coupling = blocks_of(plain_dot(as_half(adjoint_node), upper_panels[height - 1]))
+            adjoint_coupling = blocks_of(
+                plain_dot(as_half(adjoint_node), upper_panels[height - 1]) * chain_mask(height)
+            )
             adjoint_sums = [total + extra for total, extra in zip(adjoint_sums, adjoint_coupling)]
 
     forward_above, adjoint_above = [], []
@@ -178,10 +191,10 @@
         adjoint_value = adjoint_nodes[height - 1]
         if forward_above:
             right_side = right_side - across(
-                as_half(jnp.concatenate(forward_above, axis=1)), upper_panels[height - 1]
+                as_half(jnp.concatenate(forward_above, axis=1) * chain_mask(height)), upper_panels[height - 1]
             )
             adjoint_value = adjoint_value - plain_dot(
-                as_half(jnp.concatenate(adjoint_above, axis=1)), lower_panels[height - 1]
+                as_half(jnp.concatenate(adjoint_above, axis=1) * chain_mask(height)), lower_panels[height - 1]
             )
         forward_above.insert(0, across(as_half(right_side), inverse_panels[height - 1]))
         adjoint_above.insert(0, adjoint_value)
@@ -192,9 +205,10 @@
     forward_field = upper_solve(forward_remain, leaf_upper, leaf_inv, block_size, block_count)
     adjoint_remain = z_leaf - plain_dot(as_half(adjoint_above * base_mask), anc_lower)
     adjoint_field = lower_t_solve(adjoint_remain, leaf_lower, block_size, block_count)
-    partial_gradient = jnp.sum(forward_field * adjoint_field, axis=0)
     spread = lax.axis_size("src")
-    gathered = lax.all_to_all(partial_gradient.reshape(spread, -1), "src", 0, 0, tiled=True)
+    product_field = (forward_field * adjoint_field).reshape(source_count, spread, cell_count // spread)
+    partial_gradient = jnp.sum(product_field, axis=0)
+    gathered = lax.all_to_all(partial_gradient, "src", 0, 0, tiled=True)
     gradient = jnp.sum(gathered, axis=0) * factor
     return (forward_field, adjoint_field, gradient)
 

time: 38.4 us -> 39.1 us (1.018)
  matrix products: 6.11 us -> 8.68 us
  waiting for transfers between devices: 8.53 us -> 6.92 us
  other arithmetic: 2.96 us -> 2.04 us
  local copies, waits for them, and re-layouts: 6.18 us -> 6.85 us
    unnamed x20 -> x36, local copies, waits for them, and re-layouts: 3.53 us -> 5.92 us
    ppermute x6, waiting for transfers between devices: 4.64 us -> 3.06 us  [exchange(): incoming = lax.ppermute(jnp.concatenate(pieces, axis=0), 'leaf', pairs)]
    mul x1, other arithmetic: 1.43 us -> 0.01 us  [chain_mask(): level_row * (jnp.arange(1, levels + 1) > height).astype(jnp.float32)]
    dot_general x12, matrix products: 2.52 us -> 3.87 us  [across(): lax.dot_general(former, latter, (((1,), (1,)), ((), ())), preferred_eleme...]
    dot_general x13, matrix products: 3.21 us -> 4.43 us  [plain_dot(): return jnp.dot(former, latter, preferred_element_type=jnp.float32)]
    squeeze x1 -> x0, local copies, waits for them, and re-layouts: 0.78 us -> none  [shards(): inverse_panels.append(sep_inv[height - 1])]
    convert_element_type x1, other arithmetic: 0.75 us -> 0.01 us  [shards(): present = pattern.astype(jnp.float32)]
    all_to_all x1 -> x0, local copies, waits for them, and re-layouts: 0.68 us -> none  [shards(): lax.all_to_all(partial_gradient.reshape(spread, -1), 'src', 0, 0, tiled=T...]
  transfers between devices with their start and end apart: 7 -> 7, of which waited for: 4 -> 4; matrix products, arithmetic and copies ran while one was open for 16% -> 24% of each run, Pallas kernels for 0% -> 0%
where the time goes in v3:
time: 39.1 us; the launch traced here: 38.7 us
  starting transfers between devices  13.2 us (34%)
  matrix products  8.68 us (22%)
  waiting for transfers between devices  6.92 us (18%)
  local copies, waits for them, and re-layouts  6.85 us (18%)
  other arithmetic  2.04 us (5%)
  between operations  1.02 us (3%)
    ppermute x6, starting transfers between devices, exchange(): incoming = lax.ppermute(jnp.concatenate(pieces, axis=0), 'leaf', pairs)  8.29 us
    unnamed x36, local copies, waits for them, and re-layouts  5.92 us
    all_to_all x1, starting transfers between devices, shards(): gathered = lax.all_to_all(partial_gradient, 'src', 0, 0, tiled=True)  4.89 us
    dot_general x13, matrix products, plain_dot(): return jnp.dot(former, latter, preferred_element_type=jnp.float32)  4.43 us
    dot_general x12, matrix products, across(): lax.dot_general(former, latter, (((1,), (1,)), ((), ())), preferred_eleme...  3.87 us
    all_to_all x1, waiting for transfers between devices, shards(): gathered = lax.all_to_all(partial_gradient, 'src', 0, 0, tiled=True)  3.86 us
    ppermute x6, waiting for transfers between devices, exchange(): incoming = lax.ppermute(jnp.concatenate(pieces, axis=0), 'leaf', pairs)  3.06 us
  transfers between devices with their start and end apart: 7, of which 4 were waited for; matrix products, arithmetic and copies ran while one was open for 24% of the time, Pallas kernels for 0%

profile of v3, /device:TPU:0, one launch (start us, length us, event | category | flops | bytes accessed | tf_op | source)
XLA Modules:
  0.0 38.7 jit_solution(8218369556963222565)
XLA Ops:
  0.6 0.0 copy-start
  0.6 0.8 %copy.25 = s32[3,2]{1,0:T(4,128)S(1)} copy(s32[3,2]{0,1:T(2,128)} %param.15) | data formatting | bytes 48 | tf_op args[3]
  1.5 0.0 copy-start.2
  1.5 0.0 copy-start.6
  1.5 0.8 %bitcast_dynamic-update-slice_fusion.3 = bf16[528,128]{1,0:T(8,128)(2,1)S(1)} fusion(bf16[2,256,128]{2,1,0:T(8,128)(2,1)} %param.22), kind=kLoop, calls=%fused_computation.139 | loop fusion | bytes 65536
  2.3 0.8 %bitcast_dynamic-update-slice_fusion.2 = bf16[528,128]{1,0:T(8,128)(2,1)S(1)} fusion(bf16[528,128]{1,0:T(8,128)(2,1)S(1)} %bitcast_dynamic-update-slice_fusion.3, bf16[2,128,256]{2,1,0:T(8,128)(2,1)} %param.23), kind=kLoop, calls=%fused_computation.138 | loop fusion | bytes 65536
  3.1 3.0 %collective-permute-start.1 = (bf16[528,128]{1,0:T(8,128)(2,1)S(1)}, bf16[528,128]{1,0:T(8,128)(2,1)S(1)}, u32[]{:S(2)}, u32[]{:S(2)}) collective-permute-start(bf16[528,128]{1,0:T(8,128)(2,1)S(1)} %constant_dynamic-update-slice_fusion), channel_id=1, source_target_pairs={{0,8},{8,0},{16,24},{24,16},{1,9},{9,1},{17,25},{25,17},{2,10},{10... | collective-permute-start | bytes 405512 | tf_op jit(solution)/shard_map/ppermute | solution.py:134
  6.2 0.1 slice_reduce_fusion
  6.4 0.1 broadcast_bitcast_fusion
  6.4 0.1 fusion.160
  6.6 0.1 fusion.161
  6.7 0.2 convolution_subtract_fusion.5
  6.9 0.0 copy-start.9
  6.9 0.6 %copy-done.9 = f32[128,128]{0,1:T(8,128)} copy-done((f32[128,128]{0,1:T(8,128)}, f32[128,128]{0,1:T(8,128)S(1)}, u32[]{:S(2)}) %copy-start.9) | copy-done | bytes 65560
  7.6 0.2 convolution_multiply_fusion.1
  7.8 0.0 copy-start.5
  7.8 0.0 copy-start.12
  7.9 0.0 copy-start.3
  7.9 0.1 collective-permute-start
  8.0 0.4 %copy-done.8 = f32[128,128]{1,0:T(8,128)S(1)} copy-done((f32[128,128]{1,0:T(8,128)S(1)}, f32[128,128]{1,0:T(8,128)}, u32[]{:S(2)}) %copy-start.8) | copy-done | bytes 65560
  8.4 0.1 copy-done.12
  8.5 0.4 convolution_bitcast_fusion
  8.9 0.2 fusion.171
  9.2 0.3 fusion.172
  9.5 0.4 fusion.175
  9.9 0.0 copy-start.1
  9.9 0.4 fusion.10
  10.2 0.6 %copy-done.1 = bf16[512,256]{1,0:T(8,128)(2,1)S(1)} copy-done((bf16[512,256]{1,0:T(8,128)(2,1)S(1)}, bf16[512,256]{1,0:T(8,128)(2,1)}, u32[]{:S(2)}) %copy-start.1) | copy-done | bytes 262168
  10.8 0.2 convolution_multiply_fusion
  11.1 1.5 %collective-permute-start.4 = (f32[256,128]{1,0:T(8,128)S(1)}, f32[256,128]{1,0:T(8,128)S(1)}, u32[]{:S(2)}, u32[]{:S(2)}) collective-permute-start(f32[256,128]{1,0:T(8,128)S(1)} %pad_maximum_fusion.5), channel_id=1, source_target_pairs={{0,8},{8,0},{16,24},{24,16},{1,9},{9,1},{17,25},{25,17},{2,10},{10... | collective-permute-start | bytes 393224 | tf_op jit(solution)/shard_map/ppermute | solution.py:134
  12.6 0.0 collective-permute-done.1
  12.6 0.6 %slice.207 = f32[1]{0:T(128)} slice(f32[2]{0:T(128)S(1)} %compare_select_fusion), slice={[1:2]} | slice | bytes 8 | tf_op jit(solution)/shard_map/slice | solution.py:130
  13.2 0.6 %pad_maximum_fusion.6 = bf16[136,128]{1,0:T(8,128)(2,1)} fusion(bf16[8,128]{1,0:T(8,128)(2,1)S(1)} %get-tuple-element.9, bf16[128,128]{1,0:T(8,128)(2,1)S(1)} %slice_select_fusion.3), kind=kLoop, calls=%fused_computation.116 | loop fusion | flops 69632 | bytes 69632 | tf_op jit(solution)/shard_map/concatenate | solution.py:134
  13.8 1.5 %collective-permute-start.3 = (bf16[136,128]{1,0:T(8,128)(2,1)}, bf16[136,128]{1,0:T(8,128)(2,1)S(1)}, u32[]{:S(2)}, u32[]{:S(2)}) collective-permute-start(bf16[136,128]{1,0:T(8,128)(2,1)} %pad_maximum_fusion.6), channel_id=1, source_target_pairs={{0,16},{8,24},{16,0},{24,8},{1,17},{9,25},{17,1},{25,9},{2,18},{10... | collective-permute-start | bytes 104456 | tf_op jit(solution)/shard_map/ppermute | solution.py:134
  15.4 0.8 %collective-permute-done.4 = f32[256,128]{1,0:T(8,128)S(1)} collective-permute-done((f32[256,128]{1,0:T(8,128)S(1)}, f32[256,128]{1,0:T(8,128)S(1)}, u32[]{:S(2)}, u32[]{:S(2)}) %collective-permute-start.4) | collective-permute-done | bytes 131104 | tf_op jit(solution)/shard_map/ppermute | solution.py:134
  16.1 0.2 fusion.105
  16.3 0.0 copy-start.7
  16.4 0.9 %fusion.63 = f32[128,128]{1,0:T(8,128)S(1)} fusion(f32[256,128]{1,0:T(8,128)S(1)} %collective-permute-done.4, f32[128,128]{0,1:T(8,128)S(1)} %fusion.105, f32[]{:T(128)} %bitcast.6, bf16[528,128]{1,0:T(8,128)(2,1)S(1)} %collective-permute-done.1, pred[]{:T(512)S(6)} %and.21, bf16[2,128,256]{2,1,0:T(8,128)(2,1)S(1)} %copy-done.4, ...), kind=kOutput, calls=%fused_computation.78 | convolution fusion | flops 4276224 | bytes 327685 | tf_op jit(solution)/shard_map/dot_general | solution.py:16
  17.2 1.6 %collective-permute-start.5 = (f32[128,128]{1,0:T(8,128)S(1)}, f32[128,128]{1,0:T(8,128)S(1)}, u32[]{:S(2)}, u32[]{:S(2)}) collective-permute-start(f32[128,128]{1,0:T(8,128)S(1)} %fusion.63), channel_id=1, source_target_pairs={{0,16},{8,24},{16,0},{24,8},{1,17},{9,25},{17,1},{25,9},{2,18},{10... | collective-permute-start | bytes 196616 | tf_op jit(solution)/shard_map/ppermute | solution.py:134
  18.8 0.0 collective-permute-done
  18.8 0.8 %fusion.72 = f32[128,128]{1,0:T(8,128)S(1)} fusion(f32[256,128]{1,0:T(8,128)S(1)} %collective-permute-done, f32[]{:T(128)} %bitcast.6, bf16[528,128]{1,0:T(8,128)(2,1)S(1)} %collective-permute-done.1, pred[]{:T(512)S(6)} %and.21, bf16[2,256,128]{2,1,0:T(8,128)(2,1)S(1)} %copy-done.7, f32[128,256]{1,0:T(8,128)S(1)} %convolution_multiply_fusion.1), kind=kOutput, calls=%fused_computation.91 | convolution fusion | flops 4308992 | bytes 393221 | tf_op jit(solution)/shard_map/dot_general | solution.py:10
  19.6 0.1 copy.30
  19.7 0.6 %collective-permute-start.2 = (f32[128,128]{1,0:T(8,128)S(1)}, f32[128,128]{1,0:T(8,128)S(1)}, u32[]{:S(2)}, u32[]{:S(2)}) collective-permute-start(f32[128,128]{1,0:T(8,128)S(1)} %fusion.72), channel_id=1, source_target_pairs={{0,16},{8,24},{16,0},{24,8},{1,17},{9,25},{17,1},{25,9},{2,18},{10... | collective-permute-start | bytes 196616 | tf_op jit(solution)/shard_map/ppermute | solution.py:134
  20.3 1.6 %collective-permute-done.5 = f32[128,128]{1,0:T(8,128)S(1)} collective-permute-done((f32[128,128]{1,0:T(8,128)S(1)}, f32[128,128]{1,0:T(8,128)S(1)}, u32[]{:S(2)}, u32[]{:S(2)}) %collective-permute-start.5) | collective-permute-done | bytes 65568 | tf_op jit(solution)/shard_map/ppermute | solution.py:134
  21.9 0.1 fusion.101
  22.1 0.8 %fusion.102 = f32[128,128]{1,0:T(8,128)S(1)} fusion(f32[128,128]{1,0:T(8,128)S(1)} %fusion.101, f32[]{:T(128)} %bitcast.6, bf16[528,128]{1,0:T(8,128)(2,1)S(1)} %collective-permute-done.1, pred[]{:T(512)S(6)} %and.21, bf16[2,256,128]{2,1,0:T(8,128)(2,1)S(1)} %copy-done.7), kind=kOutput, calls=%fused_computation.119 | convolution fusion | flops 4243456 | bytes 196613 | tf_op jit(solution)/shard_map/dot_general | solution.py:16
  22.9 0.3 convolution_subtract_fusion
  23.1 0.2 fusion.180
  23.4 0.7 %collective-permute-done.2 = f32[128,128]{1,0:T(8,128)S(1)} collective-permute-done((f32[128,128]{1,0:T(8,128)S(1)}, f32[128,128]{1,0:T(8,128)S(1)}, u32[]{:S(2)}, u32[]{:S(2)}) %collective-permute-start.2) | collective-permute-done | bytes 65568 | tf_op jit(solution)/shard_map/ppermute | solution.py:134
  24.1 0.1 fusion.100
  24.2 1.0 %fusion.13 = f32[128,128]{1,0:T(8,128)S(1)} fusion(f32[128,128]{1,0:T(8,128)S(1)} %fusion.100, f32[]{:T(128)} %bitcast.6, f32[256,128]{1,0:T(8,128)S(1)} %collective-permute-done, bf16[528,128]{1,0:T(8,128)(2,1)S(1)} %collective-permute-done.1, pred[]{:T(512)S(6)} %and.21, bf16[2,128,256]{2,1,0:T(8,128)(2,1)S(1)} %copy-done.4, ...), kind=kOutput, calls=%fused_computation.33 | convolution fusion | flops 8519680 | bytes 394244 | tf_op jit(solution)/shard_map/dot_general | solution.py:10
  25.2 0.2 convolution_subtract_fusion.1
  25.4 0.1 fusion.162
  25.6 0.3 fusion.163
  25.9 0.3 fusion.166
  26.2 0.3 fusion.7
  26.5 0.2 fusion.181
  26.7 0.2 convolution_subtract_fusion.8
  27.0 0.7 %fusion.14 = f32[8,64]{1,0:T(8,128)} fusion(f32[128,2,64]{0,2,1:T(8,128)S(1)} %bitcast.76, f32[128,2,64]{0,2,1:T(8,128)S(1)} %bitcast.79, f32[128,2,64]{0,2,1:T(8,128)S(1)} %bitcast.77, f32[128,2,64]{0,2,1:T(8,128)S(1)} %bitcast.81, f32[128,2,64]{0,2,1:T(8,128)S(1)} %bitcast.78, f32[128,2,64]{0,2,1:T(8,128)S(1)} %bitcast.75, f32[128,2,64]{0,2,1:T(8,128)S(1)} %bitcast.80, ...), kind=kLoop, calls=%fused_computation.39 | loop fusion | flops 523776 | bytes 526336 | tf_op jit(solution)/shard_map/reduce_sum | solution.py:210
  27.7 4.9 %all-to-all-start = ((f32[8,1,64]{2,1,0:T(1,128)}), f32[8,1,64]{2,1,0:T(1,128)S(1)}, u32[]{:S(2)}, u32[]{:S(2)}) async-start(f32[8,1,64]{2,1,0:T(1,128)} %bitcast.20), calls=%async_computation | async-start | bytes 8192 | tf_op jit(solution)/shard_map/all_to_all | solution.py:211
  32.6 0.8 %copy.34 = f32[128,512]{1,0:T(8,128)} copy(f32[128,512]{0,1:T(8,128)S(1)} %pad_maximum_fusion.3) | data formatting | bytes 524288
  33.4 0.8 %copy.33 = f32[128,512]{1,0:T(8,128)} copy(f32[128,512]{0,1:T(8,128)S(1)} %pad_maximum_fusion.1) | data formatting | bytes 524288
  34.3 3.9 %all-to-all-done = f32[8,1,64]{2,1,0:T(1,128)S(1)} async-done(((f32[8,1,64]{2,1,0:T(1,128)}), f32[8,1,64]{2,1,0:T(1,128)S(1)}, u32[]{:S(2)}, u32[]{:S(2)}) %all-to-all-start) | async-done | bytes 2080 | tf_op jit(solution)/shard_map/all_to_all | solution.py:211
  38.2 0.5 %broadcast_multiply_fusion = f32[64]{0:T(128)} fusion(f32[64]{0:T(128)S(1)} %reduce_sum.19), kind=kLoop, calls=%fused_computation.165 | loop fusion | flops 64 | bytes 512 | tf_op jit(solution)/shard_map/mul | solution.py:212
  (41 shorter events, 0.3 us)
Async XLA Ops:
  0.6 6.9 %copy-start = (bf16[256,512]{1,0:T(8,128)(2,1)S(1)}, bf16[256,512]{1,0:T(8,128)(2,1)}, u32[]{:S(2)}) copy-start(bf16[256,512]{1,0:T(8,128)(2,1)} %param.19) | copy-start | bytes 786436
  1.5 4.7 %copy-start.11 = (s32[3,2]{0,1:T(2,128)S(1)}, s32[3,2]{0,1:T(2,128)}, u32[]{:S(2)}) copy-start(s32[3,2]{0,1:T(2,128)} %param.15) | copy-start | bytes 76
  1.5 4.7 %copy-start.13 = (s32[128]{0:T(128)S(1)}, s32[128]{0:T(128)}, u32[]{:S(2)}) copy-start(s32[128]{0:T(128)} %param.12) | copy-start | bytes 1540
  1.5 1.6 %copy-start.2 = (bf16[2,128,128]{2,1,0:T(8,128)(2,1)S(1)}, bf16[2,128,128]{2,1,0:T(8,128)(2,1)}, u32[]{:S(2)}) copy-start(bf16[2,128,128]{2,1,0:T(8,128)(2,1)} %param.21) | copy-start | bytes 196612
  1.5 4.9 %copy-start.6 = (bf16[512,512]{1,0:T(8,128)(2,1)S(1)}, bf16[512,512]{1,0:T(8,128)(2,1)}, u32[]{:S(2)}) copy-start(bf16[512,512]{1,0:T(8,128)(2,1)} %param.16) | copy-start | bytes 1572868
  3.1 9.4 %collective-permute-start.1 = (bf16[528,128]{1,0:T(8,128)(2,1)S(1)}, bf16[528,128]{1,0:T(8,128)(2,1)S(1)}, u32[]{:S(2)}, u32[]{:S(2)}) collective-permute-start(bf16[528,128]{1,0:T(8,128)(2,1)S(1)} %constant_dynamic-update-slice_fusion), channel_id=1, source_target_pairs={{0,8},{8,0},{16,24},{24,16},{1,9},{9,1},{17,25},{25,17},{2,10},{10... | collective-permute-start | bytes 405512 | tf_op jit(solution)/shard_map/ppermute | solution.py:134
  6.9 0.6 %copy-start.9 = (f32[128,128]{0,1:T(8,128)}, f32[128,128]{0,1:T(8,128)S(1)}, u32[]{:S(2)}) copy-start(f32[128,128]{0,1:T(8,128)S(1)} %convolution_subtract_fusion.5) | copy-start | bytes 196612
  7.5 0.8 %copy-start.8 = (f32[128,128]{1,0:T(8,128)S(1)}, f32[128,128]{1,0:T(8,128)}, u32[]{:S(2)}) copy-start(f32[128,128]{1,0:T(8,128)} %param.14) | copy-start | bytes 196612
  7.8 1.4 %copy-start.5 = (bf16[512,512]{1,0:T(8,128)(2,1)S(1)}, bf16[512,512]{1,0:T(8,128)(2,1)}, u32[]{:S(2)}) copy-start(bf16[512,512]{1,0:T(8,128)(2,1)} %param.17) | copy-start | bytes 1572868
  7.8 0.7 %copy-start.12 = (s32[128]{0:T(128)S(1)}, s32[128]{0:T(128)}, u32[]{:S(2)}) copy-start(s32[128]{0:T(128)} %param.13) | copy-start | bytes 1540
  7.9 1.1 %copy-start.3 = (bf16[4,128,128]{2,1,0:T(8,128)(2,1)S(1)}, bf16[4,128,128]{2,1,0:T(8,128)(2,1)}, u32[]{:S(2)}) copy-start(bf16[4,128,128]{2,1,0:T(8,128)(2,1)} %param.18) | copy-start | bytes 393220
  7.9 11.0 %collective-permute-start = (f32[256,128]{1,0:T(8,128)S(1)}, f32[256,128]{1,0:T(8,128)S(1)}, u32[]{:S(2)}, u32[]{:S(2)}) collective-permute-start(f32[256,128]{1,0:T(8,128)S(1)} %pad_maximum_fusion.4), channel_id=1, source_target_pairs={{0,8},{8,0},{16,24},{24,16},{1,9},{9,1},{17,25},{25,17},{2,10},{10... | collective-permute-start | bytes 393224 | tf_op jit(solution)/shard_map/ppermute | solution.py:134
  9.9 1.0 %copy-start.1 = (bf16[512,256]{1,0:T(8,128)(2,1)S(1)}, bf16[512,256]{1,0:T(8,128)(2,1)}, u32[]{:S(2)}) copy-start(bf16[512,256]{1,0:T(8,128)(2,1)} %param.20) | copy-start | bytes 786436
  11.1 5.0 %collective-permute-start.4 = (f32[256,128]{1,0:T(8,128)S(1)}, f32[256,128]{1,0:T(8,128)S(1)}, u32[]{:S(2)}, u32[]{:S(2)}) collective-permute-start(f32[256,128]{1,0:T(8,128)S(1)} %pad_maximum_fusion.5), channel_id=1, source_target_pairs={{0,8},{8,0},{16,24},{24,16},{1,9},{9,1},{17,25},{25,17},{2,10},{10... | collective-permute-start | bytes 393224 | tf_op jit(solution)/shard_map/ppermute | solution.py:134
  13.8 2.5 %copy-start.4 = (bf16[2,128,256]{2,1,0:T(8,128)(2,1)S(1)}, bf16[2,128,256]{2,1,0:T(8,128)(2,1)}, u32[]{:S(2)}) copy-start(bf16[2,128,256]{2,1,0:T(8,128)(2,1)} %param.23) | copy-start | bytes 393220
  13.8 6.5 %collective-permute-start.3 = (bf16[136,128]{1,0:T(8,128)(2,1)}, bf16[136,128]{1,0:T(8,128)(2,1)S(1)}, u32[]{:S(2)}, u32[]{:S(2)}) collective-permute-start(bf16[136,128]{1,0:T(8,128)(2,1)} %pad_maximum_fusion.6), channel_id=1, source_target_pairs={{0,16},{8,24},{16,0},{24,8},{1,17},{9,25},{17,1},{25,9},{2,18},{10... | collective-permute-start | bytes 104456 | tf_op jit(solution)/shard_map/ppermute | solution.py:134
  16.3 2.5 %copy-start.7 = (bf16[2,256,128]{2,1,0:T(8,128)(2,1)S(1)}, bf16[2,256,128]{2,1,0:T(8,128)(2,1)}, u32[]{:S(2)}) copy-start(bf16[2,256,128]{2,1,0:T(8,128)(2,1)} %param.22) | copy-start | bytes 393220
  17.2 4.7 %collective-permute-start.5 = (f32[128,128]{1,0:T(8,128)S(1)}, f32[128,128]{1,0:T(8,128)S(1)}, u32[]{:S(2)}, u32[]{:S(2)}) collective-permute-start(f32[128,128]{1,0:T(8,128)S(1)} %fusion.63), channel_id=1, source_target_pairs={{0,16},{8,24},{16,0},{24,8},{1,17},{9,25},{17,1},{25,9},{2,18},{10... | collective-permute-start | bytes 196616 | tf_op jit(solution)/shard_map/ppermute | solution.py:134
  19.7 4.3 %collective-permute-start.2 = (f32[128,128]{1,0:T(8,128)S(1)}, f32[128,128]{1,0:T(8,128)S(1)}, u32[]{:S(2)}, u32[]{:S(2)}) collective-permute-start(f32[128,128]{1,0:T(8,128)S(1)} %fusion.72), channel_id=1, source_target_pairs={{0,16},{8,24},{16,0},{24,8},{1,17},{9,25},{17,1},{25,9},{2,18},{10... | collective-permute-start | bytes 196616 | tf_op jit(solution)/shard_map/ppermute | solution.py:134
  24.2 1.0 %copy-start.10 = (f32[128,128]{0,1:T(8,128)S(1)}, f32[128,128]{0,1:T(8,128)}, u32[]{:S(2)}) copy-start(f32[128,128]{0,1:T(8,128)} %copy-done.9) | copy-start | bytes 196612
  27.7 10.4 %all-to-all-start = ((f32[8,1,64]{2,1,0:T(1,128)}), f32[8,1,64]{2,1,0:T(1,128)S(1)}, u32[]{:S(2)}, u32[]{:S(2)}) async-start(f32[8,1,64]{2,1,0:T(1,128)} %bitcast.20), calls=%async_computation | async-start | bytes 8192 | tf_op jit(solution)/shard_map/all_to_all | solution.py:211

commit v4 on v3

--- a/solution.py
+++ b/solution.py
@@ -1,6 +1,7 @@
 import math
 
 import jax
+import numpy as np
 import jax.numpy as jnp
 from jax import lax
 from jax.sharding import PartitionSpec as P
@@ -138,48 +139,62 @@
             row += piece.shape[0]
         return received
 
+    pieces, piece_levels = [], []
+    for height in range(1, levels + 1):
+        node_pieces = [lower_panels[height - 1]] + blocks_of(upper_panels[height - 1])
+        node_pieces += [inverse_panels[height - 1], pattern_rows[height - 1]]
+        pieces += node_pieces
+        piece_levels += [height] * len(node_pieces)
+    row_levels = np.concatenate([np.full(piece.shape[0], height) for piece, height in zip(pieces, piece_levels)])
+    panel_buffer = jnp.concatenate(pieces, axis=0)
     for height in range(1, levels + 1):
         stride = 1 << (height - 1)
         pairs = [(index, index ^ stride) for index in range(leaves)]
-        pieces = []
-        for upper_level in range(height, levels + 1):
-            pieces.append(lower_panels[upper_level - 1])
-            pieces.extend(blocks_of(upper_panels[upper_level - 1]))
-            pieces.append(inverse_panels[upper_level - 1])
-            pieces.append(pattern_rows[upper_level - 1])
-        received = exchange(pieces, pairs)
-        for upper_level in range(height, levels + 1):
+        received = lax.ppermute(panel_buffer, "leaf", pairs)
+        takes = [jnp.zeros((), jnp.bool_)]
+        for upper_level in range(1, levels + 1):
             place = device % (1 << upper_level)
-            take = jnp.logical_and(place >= stride, place < 2 * stride)
-            width = levels - upper_level
-            lower_in = received[0]
-            upper_in = jnp.concatenate(received[1 : 1 + width] or [upper_panels[upper_level - 1]], axis=1)
-            inverse_in = received[1 + width]
-            pattern_in = received[2 + width]
-            received = received[3 + width :]
-            pattern_rows[upper_level - 1] = jnp.where(take, pattern_in, pattern_rows[upper_level - 1])
-            lower_panels[upper_level - 1] = jnp.where(take, lower_in, lower_panels[upper_level - 1])
-            upper_panels[upper_level - 1] = jnp.where(take, upper_in, upper_panels[upper_level - 1])
-            inverse_panels[upper_level - 1] = jnp.where(take, inverse_in, inverse_panels[upper_level - 1])
+            takes.append(jnp.logical_and(upper_level >= height, jnp.logical_and(place >= stride, place < 2 * stride)))
+        take_rows = jnp.stack(takes)[row_levels]
+        panel_buffer = jnp.where(take_rows[:, None], received, panel_buffer)
+    row = 0
+    for height in range(1, levels + 1):
+        width = levels - height
+        lower_panels[height - 1] = panel_buffer[row : row + width * block_size]
+        row += width * block_size
+        if width:
+            upper_panels[height - 1] = jnp.concatenate(
+                [panel_buffer[row + k * block_size : row + (k + 1) * block_size] for k in range(width)], axis=1
+            )
+        row += width * block_size
+        inverse_panels[height - 1] = panel_buffer[row : row + block_size]
+        row += block_size
+        pattern_rows[height - 1] = panel_buffer[row : row + 8]
+        row += 8
+
+    def exchange(values, pairs):
+        incoming = lax.ppermute(jnp.concatenate(values, axis=0), "leaf", pairs)
+        return [incoming[k * source_count : (k + 1) * source_count] for k in range(len(values))]
 
     forward_nodes, adjoint_nodes = [], []
     for height in range(1, levels + 1):
         stride = 1 << (height - 1)
         pairs = [(index, index ^ stride) for index in range(leaves)]
-        forward_sums = [mine + theirs for mine, theirs in zip(forward_sums, exchange(forward_sums, pairs))]
+        count = len(forward_sums)
+        received = exchange(forward_sums + adjoint_sums, pairs)
+        forward_sums = [mine + theirs for mine, theirs in zip(forward_sums, received[:count])]
+        adjoint_sums = [mine + theirs for mine, theirs in zip(adjoint_sums, received[count:])]
         forward_node = -forward_sums[0]
         forward_nodes.append(forward_node)
         forward_sums = forward_sums[1:]
+        adjoint_node = plain_dot(as_half(-adjoint_sums[0]), inverse_panels[height - 1])
+        adjoint_nodes.append(adjoint_node)
+        adjoint_sums = adjoint_sums[1:]
         if forward_sums:
             forward_coupling = blocks_of(
                 across(as_half(forward_node), lower_panels[height - 1]) * chain_mask(height)
             )
             forward_sums = [total + extra for total, extra in zip(forward_sums, forward_coupling)]
-        adjoint_sums = [mine + theirs for mine, theirs in zip(adjoint_sums, exchange(adjoint_sums, pairs))]
-        adjoint_node = plain_dot(as_half(-adjoint_sums[0]), inverse_panels[height - 1])
-        adjoint_nodes.append(adjoint_node)
-        adjoint_sums = adjoint_sums[1:]
-        if adjoint_sums:
             adjoint_coupling = blocks_of(
                 plain_dot(as_half(adjoint_node), upper_panels[height - 1]) * chain_mask(height)
             )

time: 39.1 us -> 46.9 us (1.20)
  waiting for transfers between devices: 6.92 us -> 14.4 us
  starting transfers between devices: 13.2 us -> 10.6 us
  local copies, waits for them, and re-layouts: 6.85 us -> 8.66 us
  other arithmetic: 2.04 us -> 3.04 us
    ppermute x6 -> x4, waiting for transfers between devices: 3.06 us -> 10.6 us  [the longest x2 7.7 us: exchange(): incoming = lax.ppermute(jnp.concatenate(values, axis=0), 'leaf', pairs)]
    ppermute x6 -> x4, starting transfers between devices: 8.29 us -> 5.76 us  [the longest x2 4.59 us: shards(): received = lax.ppermute(panel_buffer, 'leaf', pairs)]
    unnamed x36 -> x24, local copies, waits for them, and re-layouts: 5.92 us -> 7.74 us
    convert_element_type x1, other arithmetic: 0.01 us -> 0.68 us  [shards(): present = pattern.astype(jnp.float32)]
    sub x1, other arithmetic: 0.01 us -> 0.66 us  [shards(): src_cells[:, None] - device * cell_count == columns]
    concatenate x3 -> x2, other arithmetic: 0.64 us -> 0.03 us  [exchange(): incoming = lax.ppermute(jnp.concatenate(values, axis=0), 'leaf', pairs)]
  transfers between devices with their start and end apart: 7 -> 5, of which waited for: 4 -> 4; matrix products, arithmetic and copies ran while one was open for 24% -> 14% of each run, Pallas kernels for 0% -> 0%
where the time goes in v4:
time: 46.9 us; the launch traced here: 46.3 us
  waiting for transfers between devices  14.4 us (31%)
  starting transfers between devices  10.6 us (23%)
  local copies, waits for them, and re-layouts  8.66 us (18%)
  matrix products  8.6 us (18%)
  other arithmetic  3.04 us (6%)
  between operations  0.96 us (2%)
    unnamed x24, local copies, waits for them, and re-layouts  7.74 us
    ppermute x2, waiting for transfers between devices, exchange(): incoming = lax.ppermute(jnp.concatenate(values, axis=0), 'leaf', pairs)  7.7 us
    all_to_all x1, starting transfers between devices, shards(): gathered = lax.all_to_all(partial_gradient, 'src', 0, 0, tiled=True)  4.89 us
    ppermute x2, starting transfers between devices, shards(): received = lax.ppermute(panel_buffer, 'leaf', pairs)  4.59 us
    dot_general x13, matrix products, plain_dot(): return jnp.dot(former, latter, preferred_element_type=jnp.float32)  4.38 us
    all_to_all x1, waiting for transfers between devices, shards(): gathered = lax.all_to_all(partial_gradient, 'src', 0, 0, tiled=True)  3.86 us
    dot_general x12, matrix products, across(): lax.dot_general(former, latter, (((1,), (1,)), ((), ())), preferred_eleme...  3.83 us
    ppermute x2, waiting for transfers between devices, shards(): received = lax.ppermute(panel_buffer, 'leaf', pairs)  2.88 us
  transfers between devices with their start and end apart: 5, of which 4 were waited for; matrix products, arithmetic and copies ran while one was open for 14% of the time, Pallas kernels for 0%

profile of v4, /device:TPU:0, one launch (start us, length us, event | category | flops | bytes accessed | tf_op | source)
XLA Modules:
  0.0 46.3 jit_solution(12293225893332282855)
XLA Ops:
  0.6 0.0 copy-start
  0.6 0.0 copy-start.4
  0.7 0.8 %copy.28 = s32[3,2]{1,0:T(4,128)S(1)} copy(s32[3,2]{0,1:T(2,128)} %param.18) | data formatting | bytes 48 | tf_op args[3]
  1.5 0.8 %bitcast_dynamic-update-slice_fusion.3 = bf16[528,128]{1,0:T(8,128)(2,1)S(1)} fusion(bf16[2,256,128]{2,1,0:T(8,128)(2,1)} %param.25), kind=kLoop, calls=%fused_computation.131 | loop fusion | bytes 65536
  2.3 0.8 %bitcast_dynamic-update-slice_fusion.2 = bf16[528,128]{1,0:T(8,128)(2,1)S(1)} fusion(bf16[528,128]{1,0:T(8,128)(2,1)S(1)} %bitcast_dynamic-update-slice_fusion.3, bf16[2,128,256]{2,1,0:T(8,128)(2,1)} %param.26), kind=kLoop, calls=%fused_computation.130 | loop fusion | bytes 65536
  3.0 0.8 %bitcast_dynamic-update-slice_fusion.1 = bf16[528,128]{1,0:T(8,128)(2,1)S(1)} fusion(bf16[528,128]{1,0:T(8,128)(2,1)S(1)} %bitcast_dynamic-update-slice_fusion.2, bf16[2,128,128]{2,1,0:T(8,128)(2,1)} %param.24), kind=kLoop, calls=%fused_computation.129 | loop fusion | bytes 65536
  3.8 0.8 %bitcast_dynamic-update-slice_fusion = bf16[528,128]{1,0:T(8,128)(2,1)S(1)} fusion(bf16[528,128]{1,0:T(8,128)(2,1)S(1)} %constant_dynamic-update-slice_fusion.1, bf16[2,128,128]{2,1,0:T(8,128)(2,1)} %param.24), kind=kLoop, calls=%fused_computation.128 | loop fusion | bytes 65536
  4.6 3.0 %collective-permute-start.1 = (bf16[528,128]{1,0:T(8,128)(2,1)S(1)}, bf16[528,128]{1,0:T(8,128)(2,1)S(1)}, u32[]{:S(2)}, u32[]{:S(2)}) collective-permute-start(bf16[528,128]{1,0:T(8,128)(2,1)S(1)} %constant_dynamic-update-slice_fusion), channel_id=1, source_target_pairs={{0,8},{8,0},{16,24},{24,16},{1,9},{9,1},{17,25},{25,17},{2,10},{10... | collective-permute-start | bytes 405512 | tf_op jit(solution)/shard_map/ppermute | solution.py:153
  7.6 0.7 %convert_element_type.107 = f32[3,2]{0,1:T(2,128)S(1)} convert(s32[3,2]{0,1:T(2,128)} %param.18) | non-fusion elementwise | flops 6 | bytes 48 | tf_op jit(solution)/shard_map/convert_element_type | solution.py:98
  8.3 0.7 %broadcast_subtract_fusion = s32[128]{0:T(128)S(1)} fusion(s32[128]{0:T(128)} %param.15, s32[]{:T(128)S(6)} %mul.35), kind=kLoop, calls=%fused_computation.176 | loop fusion | flops 128 | bytes 1028 | tf_op jit(solution)/shard_map/sub | solution.py:108
  9.0 0.1 slice_reduce_fusion
  9.1 0.1 broadcast_bitcast_fusion
  9.2 0.1 fusion.176
  9.3 0.0 copy-start.5
  9.4 0.0 copy-start.7
  9.4 0.2 fusion.177
  9.5 0.0 copy-start.3
  9.5 0.2 convolution_subtract_fusion.5
  9.7 0.5 %copy-done.5 = f32[128,128]{1,0:T(8,128)S(1)} copy-done((f32[128,128]{1,0:T(8,128)S(1)}, f32[128,128]{1,0:T(8,128)}, u32[]{:S(2)}) %copy-start.5) | copy-done | bytes 65560
  10.2 0.0 copy-done.7
  10.2 0.4 convolution_bitcast_fusion
  10.6 0.5 %copy-done.2 = bf16[4,128,128]{2,1,0:T(8,128)(2,1)S(1)} copy-done((bf16[4,128,128]{2,1,0:T(8,128)(2,1)S(1)}, bf16[4,128,128]{2,1,0:T(8,128)(2,1)}, u32[]{:S(2)}) %copy-start.2) | copy-done | bytes 131096
  11.1 0.2 fusion.178
  11.3 0.3 fusion.179
  11.7 0.4 fusion.182
  12.0 0.4 fusion.11
  12.4 0.0 copy-start.1
  12.4 0.2 convolution_multiply_fusion.1
  12.7 0.7 %copy-done.1 = bf16[512,256]{1,0:T(8,128)(2,1)S(1)} copy-done((bf16[512,256]{1,0:T(8,128)(2,1)S(1)}, bf16[512,256]{1,0:T(8,128)(2,1)}, u32[]{:S(2)}) %copy-start.1) | copy-done | bytes 262168
  13.4 0.2 convolution_multiply_fusion
  13.6 0.4 copy-done.6
  14.1 0.0 collective-permute-done.1
  14.1 0.1 broadcast_select_fusion
  14.2 1.6 %collective-permute-start.2 = (bf16[528,128]{1,0:T(8,128)(2,1)S(1)}, bf16[528,128]{1,0:T(8,128)(2,1)S(1)}, u32[]{:S(2)}, u32[]{:S(2)}) collective-permute-start(bf16[528,128]{1,0:T(8,128)(2,1)S(1)} %broadcast_select_fusion), channel_id=1, source_target_pairs={{0,16},{8,24},{16,0},{24,8},{1,17},{9,25},{17,1},{25,9},{2,18},{10... | collective-permute-start | bytes 405512 | tf_op jit(solution)/shard_map/ppermute | solution.py:153
  15.8 0.6 %collective-permute-start = (f32[512,128]{1,0:T(8,128)S(1)}, f32[512,128]{1,0:T(8,128)S(1)}, u32[]{:S(2)}, u32[]{:S(2)}) collective-permute-start(f32[512,128]{1,0:T(8,128)S(1)} %pad_maximum_fusion.2), channel_id=1, source_target_pairs={{0,8},{8,0},{16,24},{24,16},{1,9},{9,1},{17,25},{25,17},{2,10},{10... | collective-permute-start | bytes 786440 | tf_op jit(solution)/shard_map/ppermute | solution.py:176
  16.4 2.9 %collective-permute-done.2 = bf16[528,128]{1,0:T(8,128)(2,1)S(1)} collective-permute-done((bf16[528,128]{1,0:T(8,128)(2,1)S(1)}, bf16[528,128]{1,0:T(8,128)(2,1)S(1)}, u32[]{:S(2)}, u32[]{:S(2)}) %collective-permute-start.2) | collective-permute-done | bytes 135200 | tf_op jit(solution)/shard_map/ppermute | solution.py:153
  19.3 0.1 broadcast_select_fusion.1
  19.5 0.6 %slice.218 = f32[1]{0:T(128)} slice(f32[2]{0:T(128)S(1)} %compare_select_fusion), slice={[1:2]} | slice | bytes 8 | tf_op jit(solution)/shard_map/slice | solution.py:131
  20.1 3.3 %collective-permute-done = f32[512,128]{1,0:T(8,128)S(1)} collective-permute-done((f32[512,128]{1,0:T(8,128)S(1)}, f32[512,128]{1,0:T(8,128)S(1)}, u32[]{:S(2)}, u32[]{:S(2)}) %collective-permute-start) | collective-permute-done | bytes 262176 | tf_op jit(solution)/shard_map/ppermute | solution.py:176
  23.4 0.2 fusion.106
  23.6 0.8 %fusion.73 = f32[128,128]{1,0:T(8,128)S(1)} fusion(f32[512,128]{1,0:T(8,128)S(1)} %collective-permute-done, f32[]{:T(128)} %bitcast.11, bf16[528,128]{1,0:T(8,128)(2,1)S(1)} %broadcast_select_fusion.1, f32[128,256]{1,0:T(8,128)S(1)} %convolution_multiply_fusion.1), kind=kOutput, calls=%fused_computation.95 | convolution fusion | flops 4292608 | bytes 360452 | tf_op jit(solution)/shard_map/dot_general | solution.py:11
  24.4 0.8 %fusion.72 = f32[128,128]{1,0:T(8,128)S(1)} fusion(f32[512,128]{1,0:T(8,128)S(1)} %collective-permute-done, f32[128,128]{0,1:T(8,128)S(1)} %fusion.106, f32[]{:T(128)} %bitcast.11, bf16[528,128]{1,0:T(8,128)(2,1)S(1)} %broadcast_select_fusion.1, f32[128,256]{1,0:T(8,128)S(1)} %convolution_multiply_fusion), kind=kOutput, calls=%fused_computation.93 | convolution fusion | flops 4259840 | bytes 294916 | tf_op jit(solution)/shard_map/dot_general | solution.py:17
  25.3 0.6 %collective-permute-start.3 = (f32[256,128]{1,0:T(8,128)S(1)}, f32[256,128]{1,0:T(8,128)S(1)}, u32[]{:S(2)}, u32[]{:S(2)}) collective-permute-start(f32[256,128]{1,0:T(8,128)S(1)} %pad_maximum_fusion.5), channel_id=1, source_target_pairs={{0,16},{8,24},{16,0},{24,8},{1,17},{9,25},{17,1},{25,9},{2,18},{10... | collective-permute-start | bytes 393224 | tf_op jit(solution)/shard_map/ppermute | solution.py:176
  25.8 0.1 copy.33
  25.9 4.4 %collective-permute-done.3 = f32[256,128]{1,0:T(8,128)S(1)} collective-permute-done((f32[256,128]{1,0:T(8,128)S(1)}, f32[256,128]{1,0:T(8,128)S(1)}, u32[]{:S(2)}, u32[]{:S(2)}) %collective-permute-start.3) | collective-permute-done | bytes 131104 | tf_op jit(solution)/shard_map/ppermute | solution.py:176
  30.3 0.1 fusion.111
  30.4 0.8 %fusion.104 = f32[128,128]{1,0:T(8,128)S(1)} fusion(f32[128,128]{1,0:T(8,128)S(1)} %fusion.111, f32[]{:T(128)} %bitcast.11, bf16[528,128]{1,0:T(8,128)(2,1)S(1)} %broadcast_select_fusion.1), kind=kOutput, calls=%fused_computation.122 | convolution fusion | flops 4227072 | bytes 163844 | tf_op jit(solution)/shard_map/dot_general | solution.py:17
  31.2 0.3 convolution_subtract_fusion
  31.6 0.2 fusion.196
  31.8 0.1 fusion.108
  31.9 0.9 %fusion.10 = f32[128,128]{1,0:T(8,128)S(1)} fusion(f32[128,128]{1,0:T(8,128)S(1)} %fusion.108, f32[]{:T(128)} %bitcast.11, bf16[528,128]{1,0:T(8,128)(2,1)S(1)} %broadcast_select_fusion.1, f32[512,128]{1,0:T(8,128)S(1)} %collective-permute-done, f32[128,256]{1,0:T(8,128)S(1)} %convolution_multiply_fusion.1), kind=kOutput, calls=%fused_computation.30 | convolution fusion | flops 8486912 | bytes 327684 | tf_op jit(solution)/shard_map/dot_general | solution.py:11
  32.9 0.2 convolution_subtract_fusion.1
  33.1 0.2 fusion.197
  33.3 0.2 convolution_subtract_fusion.8
  33.5 0.1 fusion.187
  33.7 0.3 fusion.188
  34.0 0.3 fusion.191
  34.3 0.3 fusion.7
  34.6 0.7 %fusion.14 = f32[8,64]{1,0:T(8,128)} fusion(f32[128,2,64]{0,2,1:T(8,128)S(1)} %bitcast.69, f32[128,2,64]{0,2,1:T(8,128)S(1)} %bitcast.73, f32[128,2,64]{0,2,1:T(8,128)S(1)} %bitcast.70, f32[128,2,64]{0,2,1:T(8,128)S(1)} %bitcast.75, f32[128,2,64]{0,2,1:T(8,128)S(1)} %bitcast.71, f32[128,2,64]{0,2,1:T(8,128)S(1)} %bitcast.68, f32[128,2,64]{0,2,1:T(8,128)S(1)} %bitcast.72, ...), kind=kLoop, calls=%fused_computation.40 | loop fusion | flops 523776 | bytes 526336 | tf_op jit(solution)/shard_map/reduce_sum | solution.py:225
  35.3 4.9 %all-to-all-start = ((f32[8,1,64]{2,1,0:T(1,128)}), f32[8,1,64]{2,1,0:T(1,128)S(1)}, u32[]{:S(2)}, u32[]{:S(2)}) async-start(f32[8,1,64]{2,1,0:T(1,128)} %bitcast.20), calls=%async_computation | async-start | bytes 8192 | tf_op jit(solution)/shard_map/all_to_all | solution.py:226
  40.3 0.8 %copy.36 = f32[128,512]{1,0:T(8,128)} copy(f32[128,512]{0,1:T(8,128)S(1)} %pad_maximum_fusion.3) | data formatting | bytes 524288
  41.1 0.8 %copy.37 = f32[128,512]{1,0:T(8,128)} copy(f32[128,512]{0,1:T(8,128)S(1)} %pad_maximum_fusion.4) | data formatting | bytes 524288
  41.9 3.9 %all-to-all-done = f32[8,1,64]{2,1,0:T(1,128)S(1)} async-done(((f32[8,1,64]{2,1,0:T(1,128)}), f32[8,1,64]{2,1,0:T(1,128)S(1)}, u32[]{:S(2)}, u32[]{:S(2)}) %all-to-all-start) | async-done | bytes 2080 | tf_op jit(solution)/shard_map/all_to_all | solution.py:226
  45.8 0.5 %broadcast_multiply_fusion = f32[64]{0:T(128)} fusion(f32[64]{0:T(128)S(1)} %reduce_sum.19), kind=kLoop, calls=%fused_computation.175 | loop fusion | flops 64 | bytes 512 | tf_op jit(solution)/shard_map/mul | solution.py:227
  (24 shorter events, 0.2 us)
Async XLA Ops:
  0.6 11.8 %copy-start = (bf16[256,512]{1,0:T(8,128)(2,1)S(1)}, bf16[256,512]{1,0:T(8,128)(2,1)}, u32[]{:S(2)}) copy-start(bf16[256,512]{1,0:T(8,128)(2,1)} %param.22) | copy-start | bytes 786436
  0.6 8.5 %copy-start.4 = (bf16[512,512]{1,0:T(8,128)(2,1)S(1)}, bf16[512,512]{1,0:T(8,128)(2,1)}, u32[]{:S(2)}) copy-start(bf16[512,512]{1,0:T(8,128)(2,1)} %param.19) | copy-start | bytes 1572868
  4.6 9.5 %collective-permute-start.1 = (bf16[528,128]{1,0:T(8,128)(2,1)S(1)}, bf16[528,128]{1,0:T(8,128)(2,1)S(1)}, u32[]{:S(2)}, u32[]{:S(2)}) collective-permute-start(bf16[528,128]{1,0:T(8,128)(2,1)S(1)} %constant_dynamic-update-slice_fusion), channel_id=1, source_target_pairs={{0,8},{8,0},{16,24},{24,16},{1,9},{9,1},{17,25},{25,17},{2,10},{10... | collective-permute-start | bytes 405512 | tf_op jit(solution)/shard_map/ppermute | solution.py:153
  9.3 0.8 %copy-start.5 = (f32[128,128]{1,0:T(8,128)S(1)}, f32[128,128]{1,0:T(8,128)}, u32[]{:S(2)}) copy-start(f32[128,128]{1,0:T(8,128)} %param.17) | copy-start | bytes 196612
  9.4 0.8 %copy-start.7 = (s32[128]{0:T(128)S(1)}, s32[128]{0:T(128)}, u32[]{:S(2)}) copy-start(s32[128]{0:T(128)} %param.16) | copy-start | bytes 1540
  9.5 1.8 %copy-start.3 = (bf16[512,512]{1,0:T(8,128)(2,1)S(1)}, bf16[512,512]{1,0:T(8,128)(2,1)}, u32[]{:S(2)}) copy-start(bf16[512,512]{1,0:T(8,128)(2,1)} %param.20) | copy-start | bytes 1572868
  10.2 0.9 %copy-start.2 = (bf16[4,128,128]{2,1,0:T(8,128)(2,1)S(1)}, bf16[4,128,128]{2,1,0:T(8,128)(2,1)}, u32[]{:S(2)}) copy-start(bf16[4,128,128]{2,1,0:T(8,128)(2,1)} %param.21) | copy-start | bytes 393220
  12.4 1.0 %copy-start.1 = (bf16[512,256]{1,0:T(8,128)(2,1)S(1)}, bf16[512,256]{1,0:T(8,128)(2,1)}, u32[]{:S(2)}) copy-start(bf16[512,256]{1,0:T(8,128)(2,1)} %param.23) | copy-start | bytes 786436
  13.4 0.7 %copy-start.6 = (pred[528]{0:T(1024)(128)(4,1)S(1)}, pred[528]{0:T(1024)(128)(4,1)}, u32[]{:S(2)}) copy-start(pred[528]{0:T(1024)(128)(4,1)} %constant.73) | copy-start | bytes 1588
  14.2 5.1 %collective-permute-start.2 = (bf16[528,128]{1,0:T(8,128)(2,1)S(1)}, bf16[528,128]{1,0:T(8,128)(2,1)S(1)}, u32[]{:S(2)}, u32[]{:S(2)}) collective-permute-start(bf16[528,128]{1,0:T(8,128)(2,1)S(1)} %broadcast_select_fusion), channel_id=1, source_target_pairs={{0,16},{8,24},{16,0},{24,8},{1,17},{9,25},{17,1},{25,9},{2,18},{10... | collective-permute-start | bytes 405512 | tf_op jit(solution)/shard_map/ppermute | solution.py:153
  15.8 7.5 %collective-permute-start = (f32[512,128]{1,0:T(8,128)S(1)}, f32[512,128]{1,0:T(8,128)S(1)}, u32[]{:S(2)}, u32[]{:S(2)}) collective-permute-start(f32[512,128]{1,0:T(8,128)S(1)} %pad_maximum_fusion.2), channel_id=1, source_target_pairs={{0,8},{8,0},{16,24},{24,16},{1,9},{9,1},{17,25},{25,17},{2,10},{10... | collective-permute-start | bytes 786440 | tf_op jit(solution)/shard_map/ppermute | solution.py:176
  25.3 5.0 %collective-permute-start.3 = (f32[256,128]{1,0:T(8,128)S(1)}, f32[256,128]{1,0:T(8,128)S(1)}, u32[]{:S(2)}, u32[]{:S(2)}) collective-permute-start(f32[256,128]{1,0:T(8,128)S(1)} %pad_maximum_fusion.5), channel_id=1, source_target_pairs={{0,16},{8,24},{16,0},{24,8},{1,17},{9,25},{17,1},{25,9},{2,18},{10... | collective-permute-start | bytes 393224 | tf_op jit(solution)/shard_map/ppermute | solution.py:176
  35.3 10.4 %all-to-all-start = ((f32[8,1,64]{2,1,0:T(1,128)}), f32[8,1,64]{2,1,0:T(1,128)S(1)}, u32[]{:S(2)}, u32[]{:S(2)}) async-start(f32[8,1,64]{2,1,0:T(1,128)} %bitcast.20), calls=%async_computation | async-start | bytes 8192 | tf_op jit(solution)/shard_map/all_to_all | solution.py:226

commit v5 on v3

--- a/solution.py
+++ b/solution.py
@@ -116,6 +116,9 @@
     forward_sums = blocks_of(across(as_half(y_leaf), anc_lower) * base_mask)
     adjoint_sums = blocks_of(plain_dot(as_half(z_leaf), anc_upper) * base_mask)
 
+    forward_sums, sep_lower, sep_upper, sep_inv, pattern = lax.optimization_barrier(
+        (forward_sums, sep_lower, sep_upper, sep_inv, pattern)
+    )
     lower_panels, upper_panels, inverse_panels, pattern_rows = [], [], [], []
     for height in range(1, levels + 1):
         lower_panels.append(sep_lower[height - 1, height * block_size :, :])

time: 39.1 us -> 43 us (1.100)
  matrix products: 8.68 us -> 13.6 us
  local copies, waits for them, and re-layouts: 6.85 us -> 5.51 us
  starting transfers between devices: 13.2 us -> 14 us
  other arithmetic: 2.04 us -> 1.42 us
    dot_general x12, matrix products: 3.87 us -> 6.33 us  [across(): lax.dot_general(former, latter, (((1,), (1,)), ((), ())), preferred_eleme...]
    dot_general x13, matrix products: 4.43 us -> 6.89 us  [plain_dot(): return jnp.dot(former, latter, preferred_element_type=jnp.float32)]
    unnamed x36 -> x29, local copies, waits for them, and re-layouts: 5.92 us -> 4.49 us
    ppermute x6, starting transfers between devices: 8.29 us -> 9.09 us  [exchange(): incoming = lax.ppermute(jnp.concatenate(pieces, axis=0), 'leaf', pairs)]
    concatenate x3, other arithmetic: 0.64 us -> 0.03 us  [exchange(): incoming = lax.ppermute(jnp.concatenate(pieces, axis=0), 'leaf', pairs)]
  transfers between devices with their start and end apart: 7 -> 7, of which waited for: 4 -> 4; matrix products, arithmetic and copies ran while one was open for 24% -> 20% of each run, Pallas kernels for 0% -> 0%
where the time goes in v5:
time: 43 us; the launch traced here: 42.3 us
  starting transfers between devices  14 us (33%)
  matrix products  13.6 us (32%)
  waiting for transfers between devices  6.79 us (16%)
  local copies, waits for them, and re-layouts  5.51 us (13%)
  other arithmetic  1.42 us (3%)
  between operations  1.04 us (2%)
    ppermute x6, starting transfers between devices, exchange(): incoming = lax.ppermute(jnp.concatenate(pieces, axis=0), 'leaf', pairs)  9.09 us
    dot_general x13, matrix products, plain_dot(): return jnp.dot(former, latter, preferred_element_type=jnp.float32)  6.89 us
    dot_general x12, matrix products, across(): lax.dot_general(former, latter, (((1,), (1,)), ((), ())), preferred_eleme...  6.33 us
    all_to_all x1, starting transfers between devices, shards(): gathered = lax.all_to_all(partial_gradient, 'src', 0, 0, tiled=True)  4.88 us
    unnamed x29, local copies, waits for them, and re-layouts  4.49 us
    all_to_all x1, waiting for transfers between devices, shards(): gathered = lax.all_to_all(partial_gradient, 'src', 0, 0, tiled=True)  3.86 us
    ppermute x6, waiting for transfers between devices, exchange(): incoming = lax.ppermute(jnp.concatenate(pieces, axis=0), 'leaf', pairs)  2.93 us
  transfers between devices with their start and end apart: 7, of which 4 were waited for; matrix products, arithmetic and copies ran while one was open for 20% of the time, Pallas kernels for 0%

profile of v5, /device:TPU:0, one launch (start us, length us, event | category | flops | bytes accessed | tf_op | source)
XLA Modules:
  0.0 42.3 jit_solution(5387180274744288099)
XLA Ops:
  0.6 0.0 copy-start
  0.7 0.7 %copy-done.10 = s32[128]{0:T(128)S(1)} copy-done((s32[128]{0:T(128)S(1)}, s32[128]{0:T(128)}, u32[]{:S(2)}) %copy-start.10) | copy-done | bytes 536
  1.4 0.0 copy-start.8
  1.4 0.7 %copy-done.8 = s32[3,2]{0,1:T(2,128)S(1)} copy-done((s32[3,2]{0,1:T(2,128)S(1)}, s32[3,2]{0,1:T(2,128)}, u32[]{:S(2)}) %copy-start.8) | copy-done | bytes 48
  2.1 0.1 slice_reduce_fusion
  2.2 0.1 broadcast_bitcast_fusion
  2.3 0.9 %fusion.158 = (bf16[128,128]{0,1:T(8,128)(2,1)S(1)}, f32[128,128]{0,1:T(8,128)S(1)}) fusion(bf16[512,512]{1,0:T(8,128)(2,1)} %param.16, f32[128,512]{0,1:T(8,128)S(1)} %fusion.15), kind=kOutput, calls=%fused_computation.185 | convolution fusion | flops 4227072 | bytes 229376 | tf_op jit(solution)/shard_map/dot_general | solution.py:10
  3.2 1.0 %fusion.159 = (bf16[128,128]{0,1:T(8,128)(2,1)S(1)}, f32[128,128]{0,1:T(8,128)S(1)}) fusion(bf16[128,128]{0,1:T(8,128)(2,1)S(1)} %get-tuple-element.29, bf16[128,128]{0,1:T(8,128)(2,1)S(1)} %slice.432, bf16[512,512]{1,0:T(8,128)(2,1)} %param.16, f32[128,512]{0,1:T(8,128)S(1)} %fusion.15), kind=kOutput, calls=%fused_computation.186 | convolution fusion | flops 8552448 | bytes 294912 | tf_op jit(solution)/shard_map/dot_general | solution.py:10
  4.2 1.1 %convolution_subtract_fusion.5 = f32[128,128]{0,1:T(8,128)S(1)} fusion(bf16[128,128]{0,1:T(8,128)(2,1)S(1)} %get-tuple-element.31, bf16[128,128]{0,1:T(8,128)(2,1)S(1)} %get-tuple-element.29, bf16[128,128]{0,1:T(8,128)(2,1)S(1)} %slice.432, bf16[512,512]{1,0:T(8,128)(2,1)} %param.16, f32[128,512]{0,1:T(8,128)S(1)} %fusion.15), kind=kOutput, calls=%fused_computation.8 | convolution fusion | flops 12894208 | bytes 327680 | tf_op jit(solution)/shard_map/dot_general | solution.py:10
  5.3 0.0 copy-done
  5.3 0.0 copy-start.6
  5.3 0.2 convolution_multiply_fusion.1
  5.5 0.0 copy-start.5
  5.6 0.0 copy-start.4
  5.6 3.0 %collective-permute-start = (f32[256,128]{1,0:T(8,128)S(1)}, f32[256,128]{1,0:T(8,128)S(1)}, u32[]{:S(2)}, u32[]{:S(2)}) collective-permute-start(f32[256,128]{1,0:T(8,128)S(1)} %pad_maximum_fusion.4), channel_id=1, source_target_pairs={{0,8},{8,0},{16,24},{24,16},{1,9},{9,1},{17,25},{25,17},{2,10},{10... | collective-permute-start | bytes 393224 | tf_op jit(solution)/shard_map/ppermute | solution.py:137
  8.6 0.1 copy.25
  8.8 0.8 %copy-done.2 = bf16[2,128,128]{2,1,0:T(8,128)(2,1)S(1)} copy-done((bf16[2,128,128]{2,1,0:T(8,128)(2,1)S(1)}, bf16[2,128,128]{2,1,0:T(8,128)(2,1)}, u32[]{:S(2)}) %copy-start.2) | copy-done | bytes 65560
  9.6 0.0 copy-start.9
  9.6 0.0 copy-start.3
  9.6 0.8 %collective-permute-start.1 = (bf16[528,128]{1,0:T(8,128)(2,1)S(1)}, bf16[528,128]{1,0:T(8,128)(2,1)S(1)}, u32[]{:S(2)}, u32[]{:S(2)}) collective-permute-start(bf16[528,128]{1,0:T(8,128)(2,1)S(1)} %constant_dynamic-update-slice_fusion), channel_id=1, source_target_pairs={{0,8},{8,0},{16,24},{24,16},{1,9},{9,1},{17,25},{25,17},{2,10},{10... | collective-permute-start | bytes 405512 | tf_op jit(solution)/shard_map/ppermute | solution.py:137
  10.4 0.0 copy-done.9
  10.4 0.4 convolution_bitcast_fusion
  10.8 0.0 copy-done.3
  10.8 0.2 fusion.169
  11.0 0.3 fusion.170
  11.4 0.4 fusion.173
  11.7 0.0 copy-start.1
  11.8 0.4 fusion.10
  12.1 0.6 %copy-done.1 = bf16[512,256]{1,0:T(8,128)(2,1)S(1)} copy-done((bf16[512,256]{1,0:T(8,128)(2,1)S(1)}, bf16[512,256]{1,0:T(8,128)(2,1)}, u32[]{:S(2)}) %copy-start.1) | copy-done | bytes 262168
  12.7 0.2 convolution_multiply_fusion
  13.0 1.4 %collective-permute-start.4 = (f32[256,128]{1,0:T(8,128)S(1)}, f32[256,128]{1,0:T(8,128)S(1)}, u32[]{:S(2)}, u32[]{:S(2)}) collective-permute-start(f32[256,128]{1,0:T(8,128)S(1)} %pad_maximum_fusion.5), channel_id=1, source_target_pairs={{0,8},{8,0},{16,24},{24,16},{1,9},{9,1},{17,25},{25,17},{2,10},{10... | collective-permute-start | bytes 393224 | tf_op jit(solution)/shard_map/ppermute | solution.py:137
  14.4 0.6 %collective-permute-done.1 = bf16[528,128]{1,0:T(8,128)(2,1)S(1)} collective-permute-done((bf16[528,128]{1,0:T(8,128)(2,1)S(1)}, bf16[528,128]{1,0:T(8,128)(2,1)S(1)}, u32[]{:S(2)}, u32[]{:S(2)}) %collective-permute-start.1) | collective-permute-done | bytes 135200 | tf_op jit(solution)/shard_map/ppermute | solution.py:137
  15.0 0.6 %slice.207 = f32[1]{0:T(128)} slice(f32[2]{0:T(128)S(1)} %compare_select_fusion), slice={[1:2]} | slice | bytes 8 | tf_op jit(solution)/shard_map/slice | solution.py:133
  15.6 1.8 %collective-permute-start.3 = (bf16[136,128]{1,0:T(8,128)(2,1)S(1)}, bf16[136,128]{1,0:T(8,128)(2,1)S(1)}, u32[]{:S(2)}, u32[]{:S(2)}) collective-permute-start(bf16[136,128]{1,0:T(8,128)(2,1)S(1)} %pad_maximum_fusion.6), channel_id=1, source_target_pairs={{0,16},{8,24},{16,0},{24,8},{1,17},{9,25},{17,1},{25,9},{2,18},{10... | collective-permute-start | bytes 104456 | tf_op jit(solution)/shard_map/ppermute | solution.py:137
  17.4 0.6 %collective-permute-done.4 = f32[256,128]{1,0:T(8,128)S(1)} collective-permute-done((f32[256,128]{1,0:T(8,128)S(1)}, f32[256,128]{1,0:T(8,128)S(1)}, u32[]{:S(2)}, u32[]{:S(2)}) %collective-permute-start.4) | collective-permute-done | bytes 131104 | tf_op jit(solution)/shard_map/ppermute | solution.py:137
  18.0 0.2 fusion.105
  18.2 0.8 %fusion.63 = f32[128,128]{1,0:T(8,128)S(1)} fusion(f32[256,128]{1,0:T(8,128)S(1)} %collective-permute-done.4, f32[128,128]{0,1:T(8,128)S(1)} %fusion.105, f32[]{:T(128)} %bitcast.6, bf16[528,128]{1,0:T(8,128)(2,1)S(1)} %collective-permute-done.1, pred[]{:T(512)S(6)} %and.21, bf16[2,128,256]{2,1,0:T(8,128)(2,1)S(1)} %copy-done.4, ...), kind=kOutput, calls=%fused_computation.78 | convolution fusion | flops 4276224 | bytes 327685 | tf_op jit(solution)/shard_map/dot_general | solution.py:16
  19.1 1.6 %collective-permute-start.5 = (f32[128,128]{1,0:T(8,128)S(1)}, f32[128,128]{1,0:T(8,128)S(1)}, u32[]{:S(2)}, u32[]{:S(2)}) collective-permute-start(f32[128,128]{1,0:T(8,128)S(1)} %fusion.63), channel_id=1, source_target_pairs={{0,16},{8,24},{16,0},{24,8},{1,17},{9,25},{17,1},{25,9},{2,18},{10... | collective-permute-start | bytes 196616 | tf_op jit(solution)/shard_map/ppermute | solution.py:137
  20.7 0.0 collective-permute-done
  20.7 0.8 %fusion.72 = f32[128,128]{1,0:T(8,128)S(1)} fusion(f32[128,128]{1,0:T(8,128)S(1)} %get-tuple-element.10, f32[256,128]{1,0:T(8,128)S(1)} %collective-permute-done, f32[]{:T(128)} %bitcast.6, f32[128,128]{1,0:T(8,128)S(1)} %get-tuple-element.9, bf16[528,128]{1,0:T(8,128)(2,1)S(1)} %collective-permute-done.1, pred[]{:T(512)S(6)} %and.21, ...), kind=kOutput, calls=%fused_computation.91 | convolution fusion | flops 4308992 | bytes 393221 | tf_op jit(solution)/shard_map/dot_general | solution.py:10
  21.5 0.1 copy.30
  21.6 0.5 %collective-permute-start.2 = (f32[128,128]{1,0:T(8,128)S(1)}, f32[128,128]{1,0:T(8,128)S(1)}, u32[]{:S(2)}, u32[]{:S(2)}) collective-permute-start(f32[128,128]{1,0:T(8,128)S(1)} %fusion.72), channel_id=1, source_target_pairs={{0,16},{8,24},{16,0},{24,8},{1,17},{9,25},{17,1},{25,9},{2,18},{10... | collective-permute-start | bytes 196616 | tf_op jit(solution)/shard_map/ppermute | solution.py:137
  22.1 0.0 collective-permute-done.3
  22.1 1.7 %collective-permute-done.5 = f32[128,128]{1,0:T(8,128)S(1)} collective-permute-done((f32[128,128]{1,0:T(8,128)S(1)}, f32[128,128]{1,0:T(8,128)S(1)}, u32[]{:S(2)}, u32[]{:S(2)}) %collective-permute-start.5) | collective-permute-done | bytes 65568 | tf_op jit(solution)/shard_map/ppermute | solution.py:137
  23.8 0.1 fusion.101
  23.9 0.8 %fusion.102 = f32[128,128]{1,0:T(8,128)S(1)} fusion(f32[128,128]{1,0:T(8,128)S(1)} %fusion.101, f32[]{:T(128)} %bitcast.6, bf16[528,128]{1,0:T(8,128)(2,1)S(1)} %collective-permute-done.1, pred[]{:T(512)S(6)} %and.21, bf16[2,256,128]{2,1,0:T(8,128)(2,1)S(1)} %copy-done.5), kind=kOutput, calls=%fused_computation.119 | convolution fusion | flops 4243456 | bytes 196613 | tf_op jit(solution)/shard_map/dot_general | solution.py:16
  24.7 0.3 convolution_subtract_fusion
  25.0 1.0 %fusion.178 = (bf16[128,128]{0,1:T(8,128)(2,1)S(1)}, f32[128,128]{0,1:T(8,128)S(1)}) fusion(bf16[512,512]{1,0:T(8,128)(2,1)} %param.16, f32[128,512]{0,1:T(8,128)S(1)} %convolution_subtract_fusion), kind=kOutput, calls=%fused_computation.193 | convolution fusion | flops 4227072 | bytes 229376 | tf_op jit(solution)/shard_map/dot_general | solution.py:16
  26.0 0.0 collective-permute-done.2
  26.0 0.1 fusion.100
  26.2 0.9 %fusion.13 = f32[128,128]{1,0:T(8,128)S(1)} fusion(f32[128,128]{1,0:T(8,128)S(1)} %fusion.100, f32[]{:T(128)} %bitcast.6, f32[128,128]{1,0:T(8,128)S(1)} %get-tuple-element.9, f32[256,128]{1,0:T(8,128)S(1)} %collective-permute-done, bf16[528,128]{1,0:T(8,128)(2,1)S(1)} %collective-permute-done.1, pred[]{:T(512)S(6)} %and.21, ...), kind=kOutput, calls=%fused_computation.33 | convolution fusion | flops 8519680 | bytes 394244 | tf_op jit(solution)/shard_map/dot_general | solution.py:10
  27.1 0.2 convolution_subtract_fusion.1
  27.4 0.1 fusion.160
  27.5 0.3 fusion.161
  27.8 0.3 fusion.164
  28.1 0.3 fusion.7
  28.4 1.1 %fusion.179 = (bf16[128,128]{0,1:T(8,128)(2,1)S(1)}, f32[128,128]{0,1:T(8,128)S(1)}) fusion(bf16[512,512]{1,0:T(8,128)(2,1)} %param.16, bf16[128,128]{0,1:T(8,128)(2,1)S(1)} %slice.431, bf16[128,128]{0,1:T(8,128)(2,1)S(1)} %get-tuple-element.45, f32[128,512]{0,1:T(8,128)S(1)} %convolution_subtract_fusion), kind=kOutput, calls=%fused_computation.194 | convolution fusion | flops 8552448 | bytes 294912 | tf_op jit(solution)/shard_map/dot_general | solution.py:16
  29.5 1.1 %convolution_subtract_fusion.8 = f32[128,128]{0,1:T(8,128)S(1)} fusion(bf16[128,128]{0,1:T(8,128)(2,1)S(1)} %slice.431, bf16[128,128]{0,1:T(8,128)(2,1)S(1)} %get-tuple-element.45, bf16[128,128]{0,1:T(8,128)(2,1)S(1)} %get-tuple-element.47, bf16[512,512]{1,0:T(8,128)(2,1)} %param.16, f32[128,512]{0,1:T(8,128)S(1)} %convolution_subtract_fusion), kind=kOutput, calls=%fused_computation.11 | convolution fusion | flops 12894208 | bytes 327680 | tf_op jit(solution)/shard_map/dot_general | solution.py:16
  30.6 0.7 %fusion.14 = f32[8,64]{1,0:T(8,128)} fusion(f32[128,2,64]{0,2,1:T(8,128)S(1)} %bitcast.76, f32[128,2,64]{0,2,1:T(8,128)S(1)} %bitcast.79, f32[128,2,64]{0,2,1:T(8,128)S(1)} %bitcast.77, f32[128,2,64]{0,2,1:T(8,128)S(1)} %bitcast.81, f32[128,2,64]{0,2,1:T(8,128)S(1)} %bitcast.78, f32[128,2,64]{0,2,1:T(8,128)S(1)} %bitcast.75, f32[128,2,64]{0,2,1:T(8,128)S(1)} %bitcast.80, ...), kind=kLoop, calls=%fused_computation.39 | loop fusion | flops 523776 | bytes 526336 | tf_op jit(solution)/shard_map/reduce_sum | solution.py:213
  31.4 4.9 %all-to-all-start = ((f32[8,1,64]{2,1,0:T(1,128)}), f32[8,1,64]{2,1,0:T(1,128)S(1)}, u32[]{:S(2)}, u32[]{:S(2)}) async-start(f32[8,1,64]{2,1,0:T(1,128)} %bitcast.20), calls=%async_computation | async-start | bytes 8192 | tf_op jit(solution)/shard_map/all_to_all | solution.py:214
  36.3 0.8 %copy.34 = f32[128,512]{1,0:T(8,128)} copy(f32[128,512]{0,1:T(8,128)S(1)} %pad_maximum_fusion.3) | data formatting | bytes 524288
  37.1 0.8 %copy.33 = f32[128,512]{1,0:T(8,128)} copy(f32[128,512]{0,1:T(8,128)S(1)} %pad_maximum_fusion.1) | data formatting | bytes 524288
  37.9 3.9 %all-to-all-done = f32[8,1,64]{2,1,0:T(1,128)S(1)} async-done(((f32[8,1,64]{2,1,0:T(1,128)}), f32[8,1,64]{2,1,0:T(1,128)S(1)}, u32[]{:S(2)}, u32[]{:S(2)}) %all-to-all-start) | async-done | bytes 2080 | tf_op jit(solution)/shard_map/all_to_all | solution.py:214
  41.8 0.5 %broadcast_multiply_fusion = f32[64]{0:T(128)} fusion(f32[64]{0:T(128)S(1)} %reduce_sum.19), kind=kLoop, calls=%fused_computation.165 | loop fusion | flops 64 | bytes 512 | tf_op jit(solution)/shard_map/mul | solution.py:215
  (35 shorter events, 0.3 us)
Async XLA Ops:
  0.6 4.6 %copy-start = (bf16[256,512]{1,0:T(8,128)(2,1)S(1)}, bf16[256,512]{1,0:T(8,128)(2,1)}, u32[]{:S(2)}) copy-start(bf16[256,512]{1,0:T(8,128)(2,1)} %param.19) | copy-start | bytes 786436
  0.6 0.7 %copy-start.10 = (s32[128]{0:T(128)S(1)}, s32[128]{0:T(128)}, u32[]{:S(2)}) copy-start(s32[128]{0:T(128)} %param.12) | copy-start | bytes 1540
  1.4 0.7 %copy-start.8 = (s32[3,2]{0,1:T(2,128)S(1)}, s32[3,2]{0,1:T(2,128)}, u32[]{:S(2)}) copy-start(s32[3,2]{0,1:T(2,128)} %param.15) | copy-start | bytes 76
  5.3 5.7 %copy-start.6 = (bf16[512,512]{1,0:T(8,128)(2,1)S(1)}, bf16[512,512]{1,0:T(8,128)(2,1)}, u32[]{:S(2)}) copy-start(bf16[512,512]{1,0:T(8,128)(2,1)} %param.17) | copy-start | bytes 1572868
  5.5 3.2 %copy-start.5 = (bf16[2,256,128]{2,1,0:T(8,128)(2,1)S(1)}, bf16[2,256,128]{2,1,0:T(8,128)(2,1)}, u32[]{:S(2)}) copy-start(bf16[2,256,128]{2,1,0:T(8,128)(2,1)} %param.22) | copy-start | bytes 393220
  5.6 3.2 %copy-start.4 = (bf16[2,128,256]{2,1,0:T(8,128)(2,1)S(1)}, bf16[2,128,256]{2,1,0:T(8,128)(2,1)}, u32[]{:S(2)}) copy-start(bf16[2,128,256]{2,1,0:T(8,128)(2,1)} %param.23) | copy-start | bytes 393220
  5.6 15.1 %collective-permute-start = (f32[256,128]{1,0:T(8,128)S(1)}, f32[256,128]{1,0:T(8,128)S(1)}, u32[]{:S(2)}, u32[]{:S(2)}) collective-permute-start(f32[256,128]{1,0:T(8,128)S(1)} %pad_maximum_fusion.4), channel_id=1, source_target_pairs={{0,8},{8,0},{16,24},{24,16},{1,9},{9,1},{17,25},{25,17},{2,10},{10... | collective-permute-start | bytes 393224 | tf_op jit(solution)/shard_map/ppermute | solution.py:137
  8.7 0.8 %copy-start.2 = (bf16[2,128,128]{2,1,0:T(8,128)(2,1)S(1)}, bf16[2,128,128]{2,1,0:T(8,128)(2,1)}, u32[]{:S(2)}) copy-start(bf16[2,128,128]{2,1,0:T(8,128)(2,1)} %param.21) | copy-start | bytes 196612
  9.5 0.8 %copy-start.7 = (f32[128,128]{1,0:T(8,128)S(1)}, f32[128,128]{1,0:T(8,128)}, u32[]{:S(2)}) copy-start(f32[128,128]{1,0:T(8,128)} %param.14) | copy-start | bytes 196612
  9.6 0.8 %copy-start.9 = (s32[128]{0:T(128)S(1)}, s32[128]{0:T(128)}, u32[]{:S(2)}) copy-start(s32[128]{0:T(128)} %param.13) | copy-start | bytes 1540
  9.6 1.2 %copy-start.3 = (bf16[4,128,128]{2,1,0:T(8,128)(2,1)S(1)}, bf16[4,128,128]{2,1,0:T(8,128)(2,1)}, u32[]{:S(2)}) copy-start(bf16[4,128,128]{2,1,0:T(8,128)(2,1)} %param.18) | copy-start | bytes 393220
  9.6 5.4 %collective-permute-start.1 = (bf16[528,128]{1,0:T(8,128)(2,1)S(1)}, bf16[528,128]{1,0:T(8,128)(2,1)S(1)}, u32[]{:S(2)}, u32[]{:S(2)}) collective-permute-start(bf16[528,128]{1,0:T(8,128)(2,1)S(1)} %constant_dynamic-update-slice_fusion), channel_id=1, source_target_pairs={{0,8},{8,0},{16,24},{24,16},{1,9},{9,1},{17,25},{25,17},{2,10},{10... | collective-permute-start | bytes 405512 | tf_op jit(solution)/shard_map/ppermute | solution.py:137
  11.7 1.0 %copy-start.1 = (bf16[512,256]{1,0:T(8,128)(2,1)S(1)}, bf16[512,256]{1,0:T(8,128)(2,1)}, u32[]{:S(2)}) copy-start(bf16[512,256]{1,0:T(8,128)(2,1)} %param.20) | copy-start | bytes 786436
  13.0 5.0 %collective-permute-start.4 = (f32[256,128]{1,0:T(8,128)S(1)}, f32[256,128]{1,0:T(8,128)S(1)}, u32[]{:S(2)}, u32[]{:S(2)}) collective-permute-start(f32[256,128]{1,0:T(8,128)S(1)} %pad_maximum_fusion.5), channel_id=1, source_target_pairs={{0,8},{8,0},{16,24},{24,16},{1,9},{9,1},{17,25},{25,17},{2,10},{10... | collective-permute-start | bytes 393224 | tf_op jit(solution)/shard_map/ppermute | solution.py:137
  15.6 6.5 %collective-permute-start.3 = (bf16[136,128]{1,0:T(8,128)(2,1)S(1)}, bf16[136,128]{1,0:T(8,128)(2,1)S(1)}, u32[]{:S(2)}, u32[]{:S(2)}) collective-permute-start(bf16[136,128]{1,0:T(8,128)(2,1)S(1)} %pad_maximum_fusion.6), channel_id=1, source_target_pairs={{0,16},{8,24},{16,0},{24,8},{1,17},{9,25},{17,1},{25,9},{2,18},{10... | collective-permute-start | bytes 104456 | tf_op jit(solution)/shard_map/ppermute | solution.py:137
  19.1 4.7 %collective-permute-start.5 = (f32[128,128]{1,0:T(8,128)S(1)}, f32[128,128]{1,0:T(8,128)S(1)}, u32[]{:S(2)}, u32[]{:S(2)}) collective-permute-start(f32[128,128]{1,0:T(8,128)S(1)} %fusion.63), channel_id=1, source_target_pairs={{0,16},{8,24},{16,0},{24,8},{1,17},{9,25},{17,1},{25,9},{2,18},{10... | collective-permute-start | bytes 196616 | tf_op jit(solution)/shard_map/ppermute | solution.py:137
  21.6 4.4 %collective-permute-start.2 = (f32[128,128]{1,0:T(8,128)S(1)}, f32[128,128]{1,0:T(8,128)S(1)}, u32[]{:S(2)}, u32[]{:S(2)}) collective-permute-start(f32[128,128]{1,0:T(8,128)S(1)} %fusion.72), channel_id=1, source_target_pairs={{0,16},{8,24},{16,0},{24,8},{1,17},{9,25},{17,1},{25,9},{2,18},{10... | collective-permute-start | bytes 196616 | tf_op jit(solution)/shard_map/ppermute | solution.py:137
  31.4 10.4 %all-to-all-start = ((f32[8,1,64]{2,1,0:T(1,128)}), f32[8,1,64]{2,1,0:T(1,128)S(1)}, u32[]{:S(2)}, u32[]{:S(2)}) async-start(f32[8,1,64]{2,1,0:T(1,128)} %bitcast.20), calls=%async_computation | async-start | bytes 8192 | tf_op jit(solution)/shard_map/all_to_all | solution.py:214

commit v6 on v3

--- a/solution.py
+++ b/solution.py
@@ -3,6 +3,7 @@
 import jax
 import jax.numpy as jnp
 from jax import lax
+from jax.experimental import pallas as pl
 from jax.sharding import PartitionSpec as P
 
 
@@ -18,6 +19,40 @@
 
 def as_half(values):
     return values.astype(jnp.bfloat16)
+
+
+def transposed_dot(former, latter):
+    return lax.dot_general(
+        former, latter, (((1,), (1,)), ((), ())), preferred_element_type=jnp.float32
+    )
+
+
+def back_kernel(
+    y_ref, fa_ref, z_ref, aa_ref, mask_ref, anc_up_ref, anc_lo_ref, up_ref, lo_ref, inv_ref,
+    forward_out, adjoint_out, gradient_out,
+):
+    block_size = inv_ref.shape[1]
+    block_count = inv_ref.shape[0]
+    mask = mask_ref[...]
+    forward_remain = y_ref[...] - transposed_dot(as_half(fa_ref[...] * mask), anc_up_ref[...])
+    adjoint_remain = z_ref[...] - plain_dot(as_half(aa_ref[...] * mask), anc_lo_ref[...])
+    forward_blocks = [None] * block_count
+    adjoint_blocks = [None] * block_count
+    for index in reversed(range(block_count)):
+        here = slice(index * block_size, (index + 1) * block_size)
+        segment = forward_remain[:, here]
+        if index < block_count - 1:
+            later = jnp.concatenate([as_half(block) for block in forward_blocks[index + 1 :]], axis=1)
+            segment = segment - transposed_dot(later, up_ref[here, (index + 1) * block_size :])
+        forward_blocks[index] = transposed_dot(as_half(segment), inv_ref[index])
+        forward_out[:, here] = forward_blocks[index]
+        segment = adjoint_remain[:, here]
+        if index < block_count - 1:
+            later = jnp.concatenate([as_half(block) for block in adjoint_blocks[index + 1 :]], axis=1)
+            segment = segment - plain_dot(later, lo_ref[(index + 1) * block_size :, here])
+        adjoint_blocks[index] = segment
+        adjoint_out[:, here] = segment
+        gradient_out[:, here] = jnp.sum(forward_blocks[index] * segment, axis=0, keepdims=True)
 
 
 def lower_solve(right_side, lower, block_size, block_count):
@@ -201,13 +236,19 @@
     forward_above = jnp.concatenate(forward_above, axis=1)
     adjoint_above = jnp.concatenate(adjoint_above, axis=1)
 
-    forward_remain = y_leaf - across(as_half(forward_above * base_mask), anc_upper)
-    forward_field = upper_solve(forward_remain, leaf_upper, leaf_inv, block_size, block_count)
-    adjoint_remain = z_leaf - plain_dot(as_half(adjoint_above * base_mask), anc_lower)
-    adjoint_field = lower_t_solve(adjoint_remain, leaf_lower, block_size, block_count)
     spread = lax.axis_size("src")
-    product_field = (forward_field * adjoint_field).reshape(source_count, spread, cell_count // spread)
-    partial_gradient = jnp.sum(product_field, axis=0)
+    forward_field, adjoint_field, partial_gradient = pl.pallas_call(
+        back_kernel,
+        out_shape=(
+            jax.ShapeDtypeStruct((source_count, cell_count), jnp.float32),
+            jax.ShapeDtypeStruct((source_count, cell_count), jnp.float32),
+            jax.ShapeDtypeStruct((1, cell_count), jnp.float32),
+        ),
+    )(
+        y_leaf, forward_above, z_leaf, adjoint_above, base_mask[None, :],
+        anc_upper, anc_lower, leaf_upper, leaf_lower, leaf_inv,
+    )
+    partial_gradient = partial_gradient.reshape(spread, cell_count // spread)
     gathered = lax.all_to_all(partial_gradient, "src", 0, 0, tiled=True)
     gradient = jnp.sum(gathered, axis=0) * factor
     return (forward_field, adjoint_field, gradient)

time: 39.1 us -> 46.7 us (1.19)
  blocking collectives: 0 us -> 10.2 us
  waiting for transfers between devices: 6.92 us -> 1.13 us
  starting transfers between devices: 13.2 us -> 8.9 us
  Pallas kernels: 0 us -> 3.52 us
  matrix products: 8.68 us -> 12.2 us
  other arithmetic: 2.04 us -> 3.55 us
  local copies, waits for them, and re-layouts: 6.85 us -> 5.61 us
    all_to_all x0 -> x1, blocking collectives: none -> 10.2 us  [shards(): gathered = lax.all_to_all(partial_gradient, 'src', 0, 0, tiled=True)]
    all_to_all x1 -> x0, starting transfers between devices: 4.89 us -> none  [shards(): gathered = lax.all_to_all(partial_gradient, 'src', 0, 0, tiled=True)]
    all_to_all x1 -> x0, waiting for transfers between devices: 3.86 us -> none  [shards(): gathered = lax.all_to_all(partial_gradient, 'src', 0, 0, tiled=True)]
    pallas_call x0 -> x1, Pallas kernels: none -> 3.52 us  [shards(): pl.pallas_call(back_kernel, out_shape=(jax.ShapeDtypeStruct((source_count...]
    unnamed x36 -> x26, local copies, waits for them, and re-layouts: 5.92 us -> 3.18 us
    concatenate x2 -> x3, other arithmetic: 0.04 us -> 2.17 us  [the longest x1 0.84 us: lower_solve(): return jnp.concatenate(solved, axis=1)]
    ppermute x6, waiting for transfers between devices: 3.06 us -> 1.13 us  [exchange(): incoming = lax.ppermute(jnp.concatenate(pieces, axis=0), 'leaf', pairs)]
    dot_general x13 -> x9, matrix products: 4.43 us -> 5.96 us  [plain_dot(): return jnp.dot(former, latter, preferred_element_type=jnp.float32)]
  transfers between devices with their start and end apart: 7 -> 6, of which waited for: 4 -> 2; matrix products, arithmetic and copies ran while one was open for 24% -> 19% of each run, Pallas kernels for 0% -> 0%
where the time goes in v6:
time: 46.7 us; the launch traced here: 46 us
  matrix products  12.2 us (26%)
  blocking collectives  10.2 us (22%)
  starting transfers between devices  8.9 us (19%)
  local copies, waits for them, and re-layouts  5.61 us (12%)
  other arithmetic  3.55 us (8%)
  Pallas kernels  3.52 us (8%)
  waiting for transfers between devices  1.13 us (2%)
  between operations  0.95 us (2%)
    all_to_all x1, blocking collectives, shards(): gathered = lax.all_to_all(partial_gradient, 'src', 0, 0, tiled=True)  10.2 us
    ppermute x6, starting transfers between devices, exchange(): incoming = lax.ppermute(jnp.concatenate(pieces, axis=0), 'leaf', pairs)  8.9 us
    dot_general x9, matrix products, plain_dot(): return jnp.dot(former, latter, preferred_element_type=jnp.float32)  5.96 us
    dot_general x7, matrix products, across(): lax.dot_general(former, latter, (((1,), (1,)), ((), ())), preferred_eleme...  5.15 us
    pallas_call x1, Pallas kernels, shards(): pl.pallas_call(back_kernel, out_shape=(jax.ShapeDtypeStruct((source_count...  3.52 us
    unnamed x26, local copies, waits for them, and re-layouts  3.18 us
    ppermute x6, waiting for transfers between devices, exchange(): incoming = lax.ppermute(jnp.concatenate(pieces, axis=0), 'leaf', pairs)  1.13 us
    dot_general x1, matrix products, shards(): jnp.dot(residual, receiver_hits, precision=lax.Precision.HIGHEST)  1.03 us
  transfers between devices with their start and end apart: 6, of which 2 were waited for; matrix products, arithmetic and copies ran while one was open for 19% of the time, Pallas kernels for 0%

profile of v6, /device:TPU:0, one launch (start us, length us, event | category | flops | bytes accessed | tf_op | source)
XLA Modules:
  0.0 46.0 jit_solution(5918732320426998209)
XLA Ops:
  0.6 0.0 copy-start
  0.6 0.0 copy-start.2
  0.7 0.8 %copy-done = f32[128,128]{1,0:T(8,128)S(1)} copy-done((f32[128,128]{1,0:T(8,128)S(1)}, f32[128,128]{1,0:T(8,128)}, u32[]{:S(2)}) %copy-start) | copy-done | bytes 65560
  1.5 1.0 %convolution_bitcast_fusion = f32[128,512]{0,1:T(8,128)S(1)} fusion(f32[128,128]{1,0:T(8,128)S(1)} %copy-done, s32[128]{0:T(128)} %param.13), kind=kOutput, calls=%fused_computation | convolution fusion | flops 100794368 | bytes 328192 | tf_op jit(solution)/shard_map/dot_general | solution.py:146
  2.5 0.0 copy-done.2
  2.5 0.2 fusion.92
  2.7 1.1 %fusion.93 = (bf16[128,128]{0,1:T(8,128)(2,1)S(1)}, f32[128,128]{0,1:T(8,128)S(1)}) fusion(bf16[4,128,128]{2,1,0:T(8,128)(2,1)S(1)} %copy-done.2, bf16[128,128]{0,1:T(8,128)(2,1)S(1)} %get-tuple-element.21, f32[128,512]{0,1:T(8,128)S(1)} %convolution_bitcast_fusion, bf16[512,512]{1,0:T(8,128)(2,1)} %up_ref.1), kind=kOutput, calls=%fused_computation.124 | convolution fusion | flops 8437760 | bytes 262144 | tf_op jit(solution)/shard_map/dot_general | solution.py:17
  3.9 1.2 %fusion.96 = (bf16[128,128]{0,1:T(8,128)(2,1)S(1)}, f32[128,128]{0,1:T(8,128)S(1)}) fusion(bf16[4,128,128]{2,1,0:T(8,128)(2,1)S(1)} %copy-done.2, f32[128,512]{0,1:T(8,128)S(1)} %convolution_bitcast_fusion, bf16[128,128]{0,1:T(8,128)(2,1)S(1)} %get-tuple-element.23, bf16[128,128]{0,1:T(8,128)(2,1)S(1)} %get-tuple-element.21, bf16[512,512]{1,0:T(8,128)(2,1)} %up_ref.1), kind=kOutput, calls=%fused_computation.125 | convolution fusion | flops 12763136 | bytes 327680 | tf_op jit(solution)/shard_map/dot_general | solution.py:17
  5.1 1.3 %fusion.4 = f32[128,128]{1,0:T(8,128)S(1)} fusion(bf16[128,128]{0,1:T(8,128)(2,1)S(1)} %get-tuple-element.25, bf16[128,128]{0,1:T(8,128)(2,1)S(1)} %get-tuple-element.23, bf16[128,128]{0,1:T(8,128)(2,1)S(1)} %get-tuple-element.21, bf16[512,512]{1,0:T(8,128)(2,1)} %up_ref.1, f32[128,512]{0,1:T(8,128)S(1)} %convolution_bitcast_fusion, ...), kind=kOutput, calls=%fused_computation.16 | convolution fusion | flops 17104896 | bytes 360448 | tf_op jit(solution)/shard_map/dot_general | solution.py:17
  6.4 0.0 copy-start.4
  6.4 0.1 copy.39
  6.5 0.1 copy.38
  6.6 0.0 copy-start.7
  6.6 0.1 copy.37
  6.7 0.6 %copy-done.7 = s32[3,2]{0,1:T(2,128)S(1)} copy-done((s32[3,2]{0,1:T(2,128)S(1)}, s32[3,2]{0,1:T(2,128)}, u32[]{:S(2)}) %copy-start.7) | copy-done | bytes 48
  7.3 0.1 slice_reduce_fusion
  7.4 0.1 broadcast_bitcast_fusion
  7.4 0.0 copy-done.4
  7.5 0.2 convolution_multiply_fusion
  7.7 0.0 copy-start.6
  7.7 0.0 copy-start.5
  7.7 3.0 %collective-permute-start.4 = (f32[256,128]{1,0:T(8,128)S(1)}, f32[256,128]{1,0:T(8,128)S(1)}, u32[]{:S(2)}, u32[]{:S(2)}) collective-permute-start(f32[256,128]{1,0:T(8,128)S(1)} %pad_maximum_fusion.4), channel_id=1, source_target_pairs={{0,8},{8,0},{16,24},{24,16},{1,9},{9,1},{17,25},{25,17},{2,10},{10... | collective-permute-start | bytes 393224 | tf_op jit(solution)/shard_map/ppermute | solution.py:169
  10.7 0.1 copy.33
  10.8 0.0 copy-done.6
  10.8 0.0 copy-done.5
  10.9 0.8 %copy-done.1 = bf16[2,128,128]{2,1,0:T(8,128)(2,1)S(1)} copy-done((bf16[2,128,128]{2,1,0:T(8,128)(2,1)S(1)}, bf16[2,128,128]{2,1,0:T(8,128)(2,1)}, u32[]{:S(2)}) %copy-start.1) | copy-done | bytes 65560
  11.7 0.8 %collective-permute-start.1 = (bf16[528,128]{1,0:T(8,128)(2,1)S(1)}, bf16[528,128]{1,0:T(8,128)(2,1)S(1)}, u32[]{:S(2)}, u32[]{:S(2)}) collective-permute-start(bf16[528,128]{1,0:T(8,128)(2,1)S(1)} %constant_dynamic-update-slice_fusion), channel_id=1, source_target_pairs={{0,8},{8,0},{16,24},{24,16},{1,9},{9,1},{17,25},{25,17},{2,10},{10... | collective-permute-start | bytes 405512 | tf_op jit(solution)/shard_map/ppermute | solution.py:169
  12.5 0.7 %copy-done.9 = s32[128]{0:T(128)S(1)} copy-done((s32[128]{0:T(128)S(1)}, s32[128]{0:T(128)}, u32[]{:S(2)}) %copy-start.9) | copy-done | bytes 536
  13.1 0.1 fusion.8
  13.3 0.9 %fusion.90 = (bf16[128,128]{1,0:T(8,128)(2,1)S(1)}, f32[128,128]{1,0:T(8,128)S(1)}) fusion(bf16[512,512]{1,0:T(8,128)(2,1)} %lo_ref.1, f32[128,512]{1,0:T(8,128)S(1)} %fusion.8), kind=kOutput, calls=%fused_computation.121 | convolution fusion | flops 4227072 | bytes 229376 | tf_op jit(solution)/shard_map/dot_general | solution.py:11
  14.2 1.0 %fusion.91 = (bf16[128,128]{1,0:T(8,128)(2,1)S(1)}, f32[128,128]{1,0:T(8,128)S(1)}) fusion(bf16[512,512]{1,0:T(8,128)(2,1)} %lo_ref.1, bf16[128,128]{1,0:T(8,128)(2,1)S(1)} %get-tuple-element.17, bf16[128,128]{1,0:T(8,128)(2,1)S(1)} %slice.322, f32[128,512]{1,0:T(8,128)S(1)} %fusion.8), kind=kOutput, calls=%fused_computation.122 | convolution fusion | flops 8552448 | bytes 294912 | tf_op jit(solution)/shard_map/dot_general | solution.py:11
  15.2 0.0 copy-start.3
  15.2 1.1 %convolution_subtract_fusion.4 = f32[128,128]{1,0:T(8,128)S(1)} fusion(bf16[128,128]{1,0:T(8,128)(2,1)S(1)} %get-tuple-element.19, bf16[128,128]{1,0:T(8,128)(2,1)S(1)} %get-tuple-element.17, bf16[128,128]{1,0:T(8,128)(2,1)S(1)} %slice.322, bf16[512,512]{1,0:T(8,128)(2,1)} %lo_ref.1, f32[128,512]{1,0:T(8,128)S(1)} %fusion.8), kind=kOutput, calls=%fused_computation.9 | convolution fusion | flops 12894208 | bytes 327680 | tf_op jit(solution)/shard_map/dot_general | solution.py:11
  16.4 0.2 convolution_multiply_fusion.1
  16.6 1.4 %collective-permute-start = (f32[256,128]{1,0:T(8,128)S(1)}, f32[256,128]{1,0:T(8,128)S(1)}, u32[]{:S(2)}, u32[]{:S(2)}) collective-permute-start(f32[256,128]{1,0:T(8,128)S(1)} %pad_maximum_fusion.2), channel_id=1, source_target_pairs={{0,8},{8,0},{16,24},{24,16},{1,9},{9,1},{17,25},{25,17},{2,10},{10... | collective-permute-start | bytes 393224 | tf_op jit(solution)/shard_map/ppermute | solution.py:169
  18.0 0.8 %pad_maximum_fusion = (f32[128,512]{1,0:T(8,128)}, f32[128,512]{1,0:T(8,128)}) fusion(f32[128,128]{1,0:T(8,128)S(1)} %convolution_subtract_fusion.4, f32[128,128]{1,0:T(8,128)S(1)} %get-tuple-element.20, f32[128,128]{1,0:T(8,128)S(1)} %get-tuple-element.18, f32[128,128]{1,0:T(8,128)S(1)} %slice.182, f32[128,128]{1,0:T(8,128)S(1)} %fusion.4, ...), kind=kLoop, calls=%fused_computation.20 | loop fusion | flops 393216 | bytes 1048576 | tf_op jit(solution)/shard_map/concatenate | solution.py:68
  18.9 0.0 collective-permute-done.1
  18.9 0.6 %slice.160 = f32[1]{0:T(128)} slice(f32[2]{0:T(128)S(1)} %compare_select_fusion), slice={[1:2]} | slice | bytes 8 | tf_op jit(solution)/shard_map/slice | solution.py:165
  19.5 0.0 collective-permute-done.4
  19.5 0.2 fusion.56
  19.7 0.8 %fusion.32 = f32[128,128]{1,0:T(8,128)S(1)} fusion(f32[256,128]{1,0:T(8,128)S(1)} %collective-permute-done.4, f32[128,128]{0,1:T(8,128)S(1)} %fusion.56, f32[]{:T(128)} %bitcast.6, bf16[528,128]{1,0:T(8,128)(2,1)S(1)} %collective-permute-done.1, pred[]{:T(512)S(6)} %and.21, bf16[2,128,256]{2,1,0:T(8,128)(2,1)S(1)} %copy-done.5, ...), kind=kOutput, calls=%fused_computation.46 | convolution fusion | flops 4276224 | bytes 327685 | tf_op jit(solution)/shard_map/dot_general | solution.py:17
  20.5 1.6 %collective-permute-start.5 = (f32[128,128]{1,0:T(8,128)S(1)}, f32[128,128]{1,0:T(8,128)S(1)}, u32[]{:S(2)}, u32[]{:S(2)}) collective-permute-start(f32[128,128]{1,0:T(8,128)S(1)} %fusion.32), channel_id=1, source_target_pairs={{0,16},{8,24},{16,0},{24,8},{1,17},{9,25},{17,1},{25,9},{2,18},{10... | collective-permute-start | bytes 196616 | tf_op jit(solution)/shard_map/ppermute | solution.py:169
  22.1 0.6 %collective-permute-start.3 = (bf16[136,128]{1,0:T(8,128)(2,1)S(1)}, bf16[136,128]{1,0:T(8,128)(2,1)S(1)}, u32[]{:S(2)}, u32[]{:S(2)}) collective-permute-start(bf16[136,128]{1,0:T(8,128)(2,1)S(1)} %pad_maximum_fusion.6), channel_id=1, source_target_pairs={{0,16},{8,24},{16,0},{24,8},{1,17},{9,25},{17,1},{25,9},{2,18},{10... | collective-permute-start | bytes 104456 | tf_op jit(solution)/shard_map/ppermute | solution.py:169
  22.7 0.0 collective-permute-done
  22.7 0.8 %fusion.38 = f32[128,128]{1,0:T(8,128)S(1)} fusion(f32[256,128]{1,0:T(8,128)S(1)} %collective-permute-done, f32[]{:T(128)} %bitcast.6, bf16[528,128]{1,0:T(8,128)(2,1)S(1)} %collective-permute-done.1, pred[]{:T(512)S(6)} %and.21, bf16[2,256,128]{2,1,0:T(8,128)(2,1)S(1)} %copy-done.6, f32[128,256]{1,0:T(8,128)S(1)} %convolution_multiply_fusion.1), kind=kOutput, calls=%fused_computation.55 | convolution fusion | flops 4308992 | bytes 393221 | tf_op jit(solution)/shard_map/dot_general | solution.py:11
  23.5 0.1 copy.42
  23.6 1.6 %collective-permute-start.2 = (f32[128,128]{1,0:T(8,128)S(1)}, f32[128,128]{1,0:T(8,128)S(1)}, u32[]{:S(2)}, u32[]{:S(2)}) collective-permute-start(f32[128,128]{1,0:T(8,128)S(1)} %fusion.38), channel_id=1, source_target_pairs={{0,16},{8,24},{16,0},{24,8},{1,17},{9,25},{17,1},{25,9},{2,18},{10... | collective-permute-start | bytes 196616 | tf_op jit(solution)/shard_map/ppermute | solution.py:169
  25.2 0.9 %collective-permute-done.3 = bf16[136,128]{1,0:T(8,128)(2,1)S(1)} collective-permute-done((bf16[136,128]{1,0:T(8,128)(2,1)S(1)}, bf16[136,128]{1,0:T(8,128)(2,1)S(1)}, u32[]{:S(2)}, u32[]{:S(2)}) %collective-permute-start.3) | collective-permute-done | bytes 34848 | tf_op jit(solution)/shard_map/ppermute | solution.py:169
  26.1 0.0 collective-permute-done.5
  26.1 0.1 fusion.53
  26.3 0.8 %fusion.54 = f32[128,128]{1,0:T(8,128)S(1)} fusion(f32[128,128]{1,0:T(8,128)S(1)} %fusion.53, f32[]{:T(128)} %bitcast.6, bf16[528,128]{1,0:T(8,128)(2,1)S(1)} %collective-permute-done.1, pred[]{:T(512)S(6)} %and.21, bf16[2,256,128]{2,1,0:T(8,128)(2,1)S(1)} %copy-done.6), kind=kOutput, calls=%fused_computation.73 | convolution fusion | flops 4243456 | bytes 196613 | tf_op jit(solution)/shard_map/dot_general | solution.py:17
  27.1 0.7 %pad_maximum_fusion.5.aa_ref = f32[128,256]{1,0:T(8,128)} fusion(f32[128,128]{1,0:T(8,128)S(1)} %fusion.53, f32[128,128]{1,0:T(8,128)S(1)} %sub.40), kind=kLoop, calls=%fused_computation.29 | loop fusion | flops 32768 | bytes 262144 | tf_op jit(solution)/shard_map/concatenate | solution.py:237
  27.8 0.2 collective-permute-done.2
  27.9 0.1 fusion.52
  28.1 0.9 %fusion.7 = f32[128,128]{1,0:T(8,128)S(1)} fusion(f32[128,128]{1,0:T(8,128)S(1)} %fusion.52, f32[]{:T(128)} %bitcast.6, f32[256,128]{1,0:T(8,128)S(1)} %collective-permute-done, bf16[528,128]{1,0:T(8,128)(2,1)S(1)} %collective-permute-done.1, pred[]{:T(512)S(6)} %and.21, bf16[2,128,256]{2,1,0:T(8,128)(2,1)S(1)} %copy-done.5, ...), kind=kOutput, calls=%fused_computation.19 | convolution fusion | flops 8519680 | bytes 394244 | tf_op jit(solution)/shard_map/dot_general | solution.py:11
  29.0 0.7 %pad_maximum_fusion.3.fa_ref = f32[128,256]{1,0:T(8,128)} fusion(f32[128,128]{1,0:T(8,128)S(1)} %fusion.52, f32[128,128]{1,0:T(8,128)S(1)} %fusion.7), kind=kLoop, calls=%fused_computation.27 | loop fusion | flops 32768 | bytes 262144 | tf_op jit(solution)/shard_map/concatenate | solution.py:236
  29.7 0.6 %broadcast_in_dim.2 = f32[2,128]{1,0:T(2,128)} broadcast(f32[2]{0:T(128)S(1)} %compare_select_fusion.1), dimensions={0} | broadcast | bytes 1032 | tf_op jit(solution)/shard_map/broadcast_in_dim | solution.py:136
  30.3 3.5 %shard_map.139 = (f32[128,512]{1,0:T(8,128)}, f32[128,512]{1,0:T(8,128)}, f32[1,512]{1,0:T(1,128)}) custom-call(f32[128,512]{1,0:T(8,128)} %get-tuple-element.27.y_ref, f32[128,256]{1,0:T(8,128)} %pad_maximum_fusion.3.fa_ref, f32[128,512]{1,0:T(8,128)} %get-tuple-element.28.z_ref, f32[128,256]{1,0:T(8,128)} %pad_maximum_fusion.5.aa_ref, f32[1,256]{1,0:T(1,128)} %bitcast.52, ...), custom_call_target="tpu_custom_call" | custom-call | tf_op jit(solution)/shard_map/pallas_call | solution.py:240
  33.9 0.5 %broadcast.35 = f32[]{:T(128)} broadcast(f32[]{:T(128)} %constant.165), dimensions={} | broadcast | bytes 8 | tf_op jit(solution)/shard_map/pallas_call | solution.py:240
  34.4 0.2 copy-done.8
  34.5 0.7 %reduce.6 = f32[512]{0:T(512)S(1)} reduce(f32[1,512]{1,0:T(1,128)S(1)} %copy-done.8, f32[]{:T(128)} %broadcast.35), dimensions={0}, to_apply=%get-tuple-element.8.reduce_sub_computation.3 | reduce | bytes 4100 | tf_op jit(solution)/shard_map/pallas_call | solution.py:240
  35.2 0.1 all_to_all.6
  35.3 10.2 %all_to_all.9 = f32[8,1,64]{2,1,0:T(1,128)S(1)} all-to-all(f32[8,1,64]{2,1,0:T(1,128)S(1)} %bitcast.51), channel_id=1, replica_groups=mesh['leaf'=4,'src'=8] {'src'}, dimensions={0} | all-to-all | bytes 4096 | tf_op jit(solution)/shard_map/all_to_all | solution.py:252
  45.5 0.5 %broadcast_multiply_fusion = f32[64]{0:T(128)} fusion(f32[64]{0:T(128)S(1)} %reduce_sum.9), kind=kLoop, calls=%fused_computation.108 | loop fusion | flops 64 | bytes 512 | tf_op jit(solution)/shard_map/mul | solution.py:253
  (27 shorter events, 0.2 us)
Async XLA Ops:
  0.6 0.8 %copy-start = (f32[128,128]{1,0:T(8,128)S(1)}, f32[128,128]{1,0:T(8,128)}, u32[]{:S(2)}) copy-start(f32[128,128]{1,0:T(8,128)} %param.14) | copy-start | bytes 196612
  0.6 1.9 %copy-start.2 = (bf16[4,128,128]{2,1,0:T(8,128)(2,1)S(1)}, bf16[4,128,128]{2,1,0:T(8,128)(2,1)}, u32[]{:S(2)}) copy-start(bf16[4,128,128]{2,1,0:T(8,128)(2,1)} %inv_ref.1) | copy-start | bytes 393220
  6.4 1.1 %copy-start.4 = (bf16[512,256]{1,0:T(8,128)(2,1)S(1)}, bf16[512,256]{1,0:T(8,128)(2,1)}, u32[]{:S(2)}) copy-start(bf16[512,256]{1,0:T(8,128)(2,1)} %anc_up_ref.1) | copy-start | bytes 786436
  6.6 0.7 %copy-start.7 = (s32[3,2]{0,1:T(2,128)S(1)}, s32[3,2]{0,1:T(2,128)}, u32[]{:S(2)}) copy-start(s32[3,2]{0,1:T(2,128)} %param.15) | copy-start | bytes 76
  7.7 3.2 %copy-start.6 = (bf16[2,256,128]{2,1,0:T(8,128)(2,1)S(1)}, bf16[2,256,128]{2,1,0:T(8,128)(2,1)}, u32[]{:S(2)}) copy-start(bf16[2,256,128]{2,1,0:T(8,128)(2,1)} %param.22) | copy-start | bytes 393220
  7.7 3.2 %copy-start.5 = (bf16[2,128,256]{2,1,0:T(8,128)(2,1)S(1)}, bf16[2,128,256]{2,1,0:T(8,128)(2,1)}, u32[]{:S(2)}) copy-start(bf16[2,128,256]{2,1,0:T(8,128)(2,1)} %param.23) | copy-start | bytes 393220
  7.7 11.8 %collective-permute-start.4 = (f32[256,128]{1,0:T(8,128)S(1)}, f32[256,128]{1,0:T(8,128)S(1)}, u32[]{:S(2)}, u32[]{:S(2)}) collective-permute-start(f32[256,128]{1,0:T(8,128)S(1)} %pad_maximum_fusion.4), channel_id=1, source_target_pairs={{0,8},{8,0},{16,24},{24,16},{1,9},{9,1},{17,25},{25,17},{2,10},{10... | collective-permute-start | bytes 393224 | tf_op jit(solution)/shard_map/ppermute | solution.py:169
  10.8 0.8 %copy-start.1 = (bf16[2,128,128]{2,1,0:T(8,128)(2,1)S(1)}, bf16[2,128,128]{2,1,0:T(8,128)(2,1)}, u32[]{:S(2)}) copy-start(bf16[2,128,128]{2,1,0:T(8,128)(2,1)} %param.21) | copy-start | bytes 196612
  11.7 7.2 %collective-permute-start.1 = (bf16[528,128]{1,0:T(8,128)(2,1)S(1)}, bf16[528,128]{1,0:T(8,128)(2,1)S(1)}, u32[]{:S(2)}, u32[]{:S(2)}) collective-permute-start(bf16[528,128]{1,0:T(8,128)(2,1)S(1)} %constant_dynamic-update-slice_fusion), channel_id=1, source_target_pairs={{0,8},{8,0},{16,24},{24,16},{1,9},{9,1},{17,25},{25,17},{2,10},{10... | collective-permute-start | bytes 405512 | tf_op jit(solution)/shard_map/ppermute | solution.py:169
  12.5 0.7 %copy-start.9 = (s32[128]{0:T(128)S(1)}, s32[128]{0:T(128)}, u32[]{:S(2)}) copy-start(s32[128]{0:T(128)} %param.12) | copy-start | bytes 1540
  15.2 1.1 %copy-start.3 = (bf16[256,512]{1,0:T(8,128)(2,1)S(1)}, bf16[256,512]{1,0:T(8,128)(2,1)}, u32[]{:S(2)}) copy-start(bf16[256,512]{1,0:T(8,128)(2,1)} %anc_lo_ref.1) | copy-start | bytes 786436
  16.6 6.1 %collective-permute-start = (f32[256,128]{1,0:T(8,128)S(1)}, f32[256,128]{1,0:T(8,128)S(1)}, u32[]{:S(2)}, u32[]{:S(2)}) collective-permute-start(f32[256,128]{1,0:T(8,128)S(1)} %pad_maximum_fusion.2), channel_id=1, source_target_pairs={{0,8},{8,0},{16,24},{24,16},{1,9},{9,1},{17,25},{25,17},{2,10},{10... | collective-permute-start | bytes 393224 | tf_op jit(solution)/shard_map/ppermute | solution.py:169
  20.5 5.6 %collective-permute-start.5 = (f32[128,128]{1,0:T(8,128)S(1)}, f32[128,128]{1,0:T(8,128)S(1)}, u32[]{:S(2)}, u32[]{:S(2)}) collective-permute-start(f32[128,128]{1,0:T(8,128)S(1)} %fusion.32), channel_id=1, source_target_pairs={{0,16},{8,24},{16,0},{24,8},{1,17},{9,25},{17,1},{25,9},{2,18},{10... | collective-permute-start | bytes 196616 | tf_op jit(solution)/shard_map/ppermute | solution.py:169
  22.1 4.0 %collective-permute-start.3 = (bf16[136,128]{1,0:T(8,128)(2,1)S(1)}, bf16[136,128]{1,0:T(8,128)(2,1)S(1)}, u32[]{:S(2)}, u32[]{:S(2)}) collective-permute-start(bf16[136,128]{1,0:T(8,128)(2,1)S(1)} %pad_maximum_fusion.6), channel_id=1, source_target_pairs={{0,16},{8,24},{16,0},{24,8},{1,17},{9,25},{17,1},{25,9},{2,18},{10... | collective-permute-start | bytes 104456 | tf_op jit(solution)/shard_map/ppermute | solution.py:169
  23.6 4.3 %collective-permute-start.2 = (f32[128,128]{1,0:T(8,128)S(1)}, f32[128,128]{1,0:T(8,128)S(1)}, u32[]{:S(2)}, u32[]{:S(2)}) collective-permute-start(f32[128,128]{1,0:T(8,128)S(1)} %fusion.38), channel_id=1, source_target_pairs={{0,16},{8,24},{16,0},{24,8},{1,17},{9,25},{17,1},{25,9},{2,18},{10... | collective-permute-start | bytes 196616 | tf_op jit(solution)/shard_map/ppermute | solution.py:169
  33.9 0.7 %copy-start.8 = (f32[1,512]{1,0:T(1,128)S(1)}, f32[1,512]{1,0:T(1,128)}, u32[]{:S(2)}) copy-start(f32[1,512]{1,0:T(1,128)} %get-tuple-element.8) | copy-start | bytes 6148

commit v7 on v3

--- a/solution.py
+++ b/solution.py
@@ -138,29 +138,36 @@
             row += piece.shape[0]
         return received
 
-    for height in range(1, levels + 1):
-        stride = 1 << (height - 1)
-        pairs = [(index, index ^ stride) for index in range(leaves)]
-        pieces = []
-        for upper_level in range(height, levels + 1):
-            pieces.append(lower_panels[upper_level - 1])
-            pieces.extend(blocks_of(upper_panels[upper_level - 1]))
-            pieces.append(inverse_panels[upper_level - 1])
-            pieces.append(pattern_rows[upper_level - 1])
-        received = exchange(pieces, pairs)
-        for upper_level in range(height, levels + 1):
-            place = device % (1 << upper_level)
-            take = jnp.logical_and(place >= stride, place < 2 * stride)
-            width = levels - upper_level
-            lower_in = received[0]
-            upper_in = jnp.concatenate(received[1 : 1 + width] or [upper_panels[upper_level - 1]], axis=1)
-            inverse_in = received[1 + width]
-            pattern_in = received[2 + width]
-            received = received[3 + width :]
-            pattern_rows[upper_level - 1] = jnp.where(take, pattern_in, pattern_rows[upper_level - 1])
-            lower_panels[upper_level - 1] = jnp.where(take, lower_in, lower_panels[upper_level - 1])
-            upper_panels[upper_level - 1] = jnp.where(take, upper_in, upper_panels[upper_level - 1])
-            inverse_panels[upper_level - 1] = jnp.where(take, inverse_in, inverse_panels[upper_level - 1])
+    level_pieces, level_rows = [], [0]
+    for height in range(1, levels + 1):
+        node_pieces = [lower_panels[height - 1]] + blocks_of(upper_panels[height - 1])
+        node_pieces += [inverse_panels[height - 1], pattern_rows[height - 1]]
+        level_pieces.append(node_pieces)
+        level_rows.append(level_rows[-1] + sum(piece.shape[0] for piece in node_pieces))
+    panel_buffer = jnp.concatenate([piece for node_pieces in level_pieces for piece in node_pieces], axis=0)
+    received = {}
+    for offset in range(1, leaves):
+        first = level_rows[offset.bit_length() - 1]
+        pairs = [(index, index ^ offset) for index in range(leaves)]
+        received[offset] = (first, lax.ppermute(panel_buffer[first:], "leaf", pairs))
+    for height in range(1, levels + 1):
+        rows = slice(level_rows[height - 1], level_rows[height])
+        value = panel_buffer[rows]
+        place = device % (1 << height)
+        for offset in range(1, 1 << height):
+            first, incoming = received[offset]
+            piece = incoming[level_rows[height - 1] - first : level_rows[height] - first]
+            value = jnp.where(place == offset, piece, value)
+        row, width = 0, levels - height
+        lower_panels[height - 1] = value[row : row + width * block_size]
+        row += width * block_size
+        if width:
+            upper_panels[height - 1] = jnp.concatenate(
+                [value[row + k * block_size : row + (k + 1) * block_size] for k in range(width)], axis=1
+            )
+        row += width * block_size
+        inverse_panels[height - 1] = value[row : row + block_size]
+        pattern_rows[height - 1] = value[row + block_size : row + block_size + 8]
 
     forward_nodes, adjoint_nodes = [], []
     for height in range(1, levels + 1):

time: 39.1 us -> 45.2 us (1.16)
  local copies, waits for them, and re-layouts: 6.85 us -> 11.2 us
  starting transfers between devices: 13.2 us -> 15.7 us
  waiting for transfers between devices: 6.92 us -> 5.87 us
    ppermute x0 -> x3, starting transfers between devices: none -> 4.46 us  [shards(): lax.ppermute(panel_buffer[first:], 'leaf', pairs)]
    ppermute x6 -> x4, starting transfers between devices: 8.29 us -> 6.36 us  [exchange(): incoming = lax.ppermute(jnp.concatenate(pieces, axis=0), 'leaf', pairs)]
    unnamed x36 -> x31, local copies, waits for them, and re-layouts: 5.92 us -> 7.52 us
    squeeze x0 -> x2, local copies, waits for them, and re-layouts: none -> 1.57 us  [the longest x1 0.79 us: shards(): inverse_panels.append(sep_inv[height - 1])]
    ppermute x6 -> x4, waiting for transfers between devices: 3.06 us -> 1.99 us  [exchange(): incoming = lax.ppermute(jnp.concatenate(pieces, axis=0), 'leaf', pairs)]
    select_n x2, other arithmetic: 0.02 us -> 0.83 us  [shards(): value = jnp.where(place == offset, piece, value)]
    concatenate x3 -> x2, other arithmetic: 0.64 us -> 0.02 us  [exchange(): incoming = lax.ppermute(jnp.concatenate(pieces, axis=0), 'leaf', pairs)]
    pad x0 -> x1, local copies, waits for them, and re-layouts: none -> 0.58 us  [shards(): pattern_rows.append(jnp.pad(row, ((0, 7), (0, block_size - levels))))]
  transfers between devices with their start and end apart: 7 -> 8, of which waited for: 4 -> 3; matrix products, arithmetic and copies ran while one was open for 24% -> 23% of each run, Pallas kernels for 0% -> 0%
where the time goes in v7:
time: 45.2 us; the launch traced here: 44.7 us
  starting transfers between devices  15.7 us (35%)
  local copies, waits for them, and re-layouts  11.2 us (25%)
  matrix products  8.65 us (19%)
  waiting for transfers between devices  5.87 us (13%)
  other arithmetic  2.24 us (5%)
  between operations  1.01 us (2%)
    unnamed x31, local copies, waits for them, and re-layouts  7.52 us
    ppermute x4, starting transfers between devices, exchange(): incoming = lax.ppermute(jnp.concatenate(pieces, axis=0), 'leaf', pairs)  6.36 us
    all_to_all x1, starting transfers between devices, shards(): gathered = lax.all_to_all(partial_gradient, 'src', 0, 0, tiled=True)  4.88 us
    ppermute x3, starting transfers between devices, shards(): lax.ppermute(panel_buffer[first:], 'leaf', pairs)  4.46 us
    dot_general x13, matrix products, plain_dot(): return jnp.dot(former, latter, preferred_element_type=jnp.float32)  4.4 us
    all_to_all x1, waiting for transfers between devices, shards(): gathered = lax.all_to_all(partial_gradient, 'src', 0, 0, tiled=True)  3.86 us
    dot_general x12, matrix products, across(): lax.dot_general(former, latter, (((1,), (1,)), ((), ())), preferred_eleme...  3.86 us
    ppermute x4, waiting for transfers between devices, exchange(): incoming = lax.ppermute(jnp.concatenate(pieces, axis=0), 'leaf', pairs)  1.99 us
  transfers between devices with their start and end apart: 8, of which 3 were waited for; matrix products, arithmetic and copies ran while one was open for 23% of the time, Pallas kernels for 0%

profile of v7, /device:TPU:0, one launch (start us, length us, event | category | flops | bytes accessed | tf_op | source)
XLA Modules:
  0.0 44.7 jit_solution(13111932253957763673)
XLA Ops:
  0.6 0.0 copy-start
  0.6 0.8 %copy.25 = s32[3,2]{1,0:T(4,128)S(1)} copy(s32[3,2]{0,1:T(2,128)} %param.15) | data formatting | bytes 48 | tf_op args[3]
  1.5 0.0 copy-start.11
  1.5 0.8 %slice_bitcast_fusion.1 = (bf16[128,128]{1,0:T(8,128)(2,1)S(1)}, bf16[128,128]{1,0:T(8,128)(2,1)S(1)}) fusion(bf16[2,128,128]{2,1,0:T(8,128)(2,1)} %param.21), kind=kLoop, calls=%fused_computation.144 | loop fusion | bytes 131072 | tf_op jit(solution)/shard_map/squeeze | solution.py:123
  2.3 1.4 %constant_dynamic-update-slice_fusion.5 = bf16[528,128]{1,0:T(8,128)(2,1)} fusion(bf16[2,256,128]{2,1,0:T(8,128)(2,1)} %param.22), kind=kLoop, calls=%fused_computation.168 | loop fusion | bytes 65536
  3.7 1.4 %constant_dynamic-update-slice_fusion.4 = bf16[528,128]{1,0:T(8,128)(2,1)} fusion(bf16[528,128]{1,0:T(8,128)(2,1)} %constant_dynamic-update-slice_fusion.5, bf16[2,128,256]{2,1,0:T(8,128)(2,1)} %param.23), kind=kLoop, calls=%fused_computation.167 | loop fusion | bytes 65536
  5.1 0.6 %constant_dynamic-update-slice_fusion.3 = bf16[528,128]{1,0:T(8,128)(2,1)} fusion(bf16[528,128]{1,0:T(8,128)(2,1)} %constant_dynamic-update-slice_fusion.4, bf16[2,128,128]{2,1,0:T(8,128)(2,1)S(1)} %copy-done.3), kind=kLoop, calls=%fused_computation.166 | loop fusion | bytes 65536
  5.7 0.6 %fusion.172 = (bf16[8,128]{1,0:T(8,128)(2,1)S(1)}, bf16[528,128]{1,0:T(8,128)(2,1)}) fusion(bf16[1,2]{1,0:T(2,128)(2,1)S(1)} %get-tuple-element.15, bf16[528,128]{1,0:T(8,128)(2,1)} %constant_dynamic-update-slice_fusion.3), kind=kLoop, calls=%fused_computation.198 | loop fusion | bytes 4100 | tf_op jit(solution)/shard_map/jit(_pad)/pad | solution.py:125
  6.3 0.6 %constant_dynamic-update-slice_fusion.1 = bf16[528,128]{1,0:T(8,128)(2,1)} fusion(bf16[528,128]{1,0:T(8,128)(2,1)} %get-tuple-element.18, bf16[2,128,128]{2,1,0:T(8,128)(2,1)S(1)} %copy-done.3), kind=kLoop, calls=%fused_computation.164 | loop fusion | bytes 65536
  6.9 0.6 %constant_dynamic-update-slice_fusion = (bf16[528,128]{1,0:T(8,128)(2,1)}, bf16[8,128]{1,0:T(8,128)(2,1)S(1)}) fusion(bf16[528,128]{1,0:T(8,128)(2,1)} %constant_dynamic-update-slice_fusion.1, bf16[1,2]{1,0:T(2,128)(2,1)S(1)} %get-tuple-element.16), kind=kLoop, calls=%fused_computation.163 | loop fusion | bytes 4100 | tf_op jit(solution)/shard_map/concatenate | solution.py:147
  7.5 3.0 %collective-permute-start.4 = (bf16[136,128]{1,0:T(8,128)(2,1)S(1)}, bf16[136,128]{1,0:T(8,128)(2,1)}, u32[]{:S(2)}, u32[]{:S(2)}) collective-permute-start(bf16[136,128]{1,0:T(8,128)(2,1)S(1)} %pad_maximum_fusion.6), channel_id=1, source_target_pairs={{0,16},{8,24},{16,0},{24,8},{1,17},{9,25},{17,1},{25,9},{2,18},{10... | collective-permute-start | bytes 104456 | tf_op jit(solution)/shard_map/ppermute | solution.py:152
  10.5 1.4 %collective-permute-start.3 = (bf16[136,128]{1,0:T(8,128)(2,1)S(1)}, bf16[136,128]{1,0:T(8,128)(2,1)}, u32[]{:S(2)}, u32[]{:S(2)}) collective-permute-start(bf16[136,128]{1,0:T(8,128)(2,1)S(1)} %pad_maximum_fusion.6), channel_id=1, source_target_pairs={{0,24},{8,16},{16,8},{24,0},{1,25},{9,17},{17,9},{25,1},{2,26},{10... | collective-permute-start | bytes 104456 | tf_op jit(solution)/shard_map/ppermute | solution.py:152
  11.9 0.1 collective-permute-start.1
  12.1 0.1 slice_reduce_fusion
  12.2 0.1 broadcast_bitcast_fusion
  12.3 0.1 fusion.173
  12.4 0.2 fusion.174
  12.6 0.2 convolution_subtract_fusion.5
  12.7 0.0 copy-start.7
  12.8 0.0 copy-start.6
  12.8 0.2 convolution_multiply_fusion.1
  13.0 0.4 copy-done.7
  13.4 0.0 copy-start.10
  13.4 0.0 copy-start.2
  13.4 2.0 %collective-permute-start = (f32[256,128]{1,0:T(8,128)S(1)}, f32[256,128]{1,0:T(8,128)S(1)}, u32[]{:S(2)}, u32[]{:S(2)}) collective-permute-start(f32[256,128]{1,0:T(8,128)S(1)} %pad_maximum_fusion.4), channel_id=1, source_target_pairs={{0,8},{8,0},{16,24},{24,16},{1,9},{9,1},{17,25},{25,17},{2,10},{10... | collective-permute-start | bytes 393224 | tf_op jit(solution)/shard_map/ppermute | solution.py:134
  15.5 0.4 convolution_bitcast_fusion
  15.9 0.2 fusion.184
  16.1 0.3 fusion.185
  16.4 0.4 fusion.188
  16.8 0.0 copy-start.1
  16.8 0.4 fusion.10
  17.2 0.6 %copy-done.1 = bf16[512,256]{1,0:T(8,128)(2,1)S(1)} copy-done((bf16[512,256]{1,0:T(8,128)(2,1)S(1)}, bf16[512,256]{1,0:T(8,128)(2,1)}, u32[]{:S(2)}) %copy-start.1) | copy-done | bytes 262168
  17.8 0.2 convolution_multiply_fusion
  18.0 0.7 %collective-permute-start.5 = (f32[256,128]{1,0:T(8,128)S(1)}, f32[256,128]{1,0:T(8,128)S(1)}, u32[]{:S(2)}, u32[]{:S(2)}) collective-permute-start(f32[256,128]{1,0:T(8,128)S(1)} %pad_maximum_fusion.5), channel_id=1, source_target_pairs={{0,8},{8,0},{16,24},{24,16},{1,9},{9,1},{17,25},{25,17},{2,10},{10... | collective-permute-start | bytes 393224 | tf_op jit(solution)/shard_map/ppermute | solution.py:134
  18.7 0.8 %slice_bitcast_fusion.2 = (bf16[128,128]{1,0:T(8,128)(2,1)S(1)}, bf16[128,128]{1,0:T(8,128)(2,1)S(1)}) fusion(bf16[2,128,256]{2,1,0:T(8,128)(2,1)} %param.23, bf16[2,256,128]{2,1,0:T(8,128)(2,1)} %param.22), kind=kLoop, calls=%fused_computation.145 | loop fusion | bytes 131072 | tf_op jit(solution)/shard_map/squeeze | solution.py:122
  19.5 0.6 %slice.212 = f32[1]{0:T(128)} slice(f32[2]{0:T(128)S(1)} %compare_select_fusion), slice={[1:2]} | slice | bytes 8 | tf_op jit(solution)/shard_map/slice | solution.py:130
  20.1 0.8 %fusion.72 = f32[128,128]{1,0:T(8,128)S(1)} fusion(f32[256,128]{1,0:T(8,128)S(1)} %collective-permute-done, f32[]{:T(128)} %bitcast.6, bf16[392,128]{1,0:T(8,128)(2,1)S(1)} %slice_select_fusion, f32[128,256]{1,0:T(8,128)S(1)} %convolution_multiply_fusion.1), kind=kOutput, calls=%fused_computation.92 | convolution fusion | flops 4292608 | bytes 360452 | tf_op jit(solution)/shard_map/dot_general | solution.py:10
  20.9 2.1 %collective-permute-start.2 = (f32[128,128]{1,0:T(8,128)S(1)}, f32[128,128]{1,0:T(8,128)S(1)}, u32[]{:S(2)}, u32[]{:S(2)}) collective-permute-start(f32[128,128]{1,0:T(8,128)S(1)} %fusion.72), channel_id=1, source_target_pairs={{0,16},{8,24},{16,0},{24,8},{1,17},{9,25},{17,1},{25,9},{2,18},{10... | collective-permute-start | bytes 196616 | tf_op jit(solution)/shard_map/ppermute | solution.py:134
  23.0 0.1 collective-permute-done.5
  23.1 0.2 fusion.109
  23.3 0.1 copy.30
  23.4 0.8 %fusion.63 = f32[128,128]{1,0:T(8,128)S(1)} fusion(f32[256,128]{1,0:T(8,128)S(1)} %collective-permute-done.5, f32[128,128]{0,1:T(8,128)S(1)} %fusion.109, f32[]{:T(128)} %bitcast.6, bf16[392,128]{1,0:T(8,128)(2,1)S(1)} %slice_select_fusion, f32[128,256]{1,0:T(8,128)S(1)} %convolution_multiply_fusion), kind=kOutput, calls=%fused_computation.79 | convolution fusion | flops 4259840 | bytes 294916 | tf_op jit(solution)/shard_map/dot_general | solution.py:16
  24.2 1.6 %collective-permute-start.6 = (f32[128,128]{1,0:T(8,128)S(1)}, f32[128,128]{1,0:T(8,128)S(1)}, u32[]{:S(2)}, u32[]{:S(2)}) collective-permute-start(f32[128,128]{1,0:T(8,128)S(1)} %fusion.63), channel_id=1, source_target_pairs={{0,16},{8,24},{16,0},{24,8},{1,17},{9,25},{17,1},{25,9},{2,18},{10... | collective-permute-start | bytes 196616 | tf_op jit(solution)/shard_map/ppermute | solution.py:134
  25.8 0.8 %fusion.103 = bf16[128,128]{1,0:T(8,128)(2,1)S(1)} fusion(bf16[8,128]{1,0:T(8,128)(2,1)S(1)} %get-tuple-element.20, bf16[136,128]{1,0:T(8,128)(2,1)} %collective-permute-done.3, bf16[136,128]{1,0:T(8,128)(2,1)} %collective-permute-done.4, bf16[136,128]{1,0:T(8,128)(2,1)S(1)} %slice.258, pred[]{:T(512)S(6)} %eq.34, pred[]{:T(512)S(6)} %eq.35, pred[]{:T(512)S(6)} %eq.36, ...), kind=kLoop, calls=%fused_computation.122 | loop fusion | flops 114688 | bytes 165891 | tf_op jit(solution)/shard_map/jit(_where)/select_n | solution.py:160
  26.6 1.9 %collective-permute-done.6 = f32[128,128]{1,0:T(8,128)S(1)} collective-permute-done((f32[128,128]{1,0:T(8,128)S(1)}, f32[128,128]{1,0:T(8,128)S(1)}, u32[]{:S(2)}, u32[]{:S(2)}) %collective-permute-start.6) | collective-permute-done | bytes 65568 | tf_op jit(solution)/shard_map/ppermute | solution.py:134
  28.6 0.1 fusion.105
  28.7 0.8 %fusion.106 = f32[128,128]{1,0:T(8,128)S(1)} fusion(f32[128,128]{1,0:T(8,128)S(1)} %fusion.105, f32[]{:T(128)} %bitcast.6, bf16[392,128]{1,0:T(8,128)(2,1)S(1)} %slice_select_fusion), kind=kOutput, calls=%fused_computation.125 | convolution fusion | flops 4227072 | bytes 163844 | tf_op jit(solution)/shard_map/dot_general | solution.py:16
  29.5 0.3 convolution_subtract_fusion
  29.8 0.2 fusion.193
  30.0 0.1 fusion.104
  30.2 1.0 %fusion.13 = f32[128,128]{1,0:T(8,128)S(1)} fusion(f32[128,128]{1,0:T(8,128)S(1)} %fusion.104, f32[]{:T(128)} %bitcast.6, bf16[392,128]{1,0:T(8,128)(2,1)S(1)} %slice_select_fusion, f32[256,128]{1,0:T(8,128)S(1)} %collective-permute-done, f32[128,256]{1,0:T(8,128)S(1)} %convolution_multiply_fusion.1), kind=kOutput, calls=%fused_computation.33 | convolution fusion | flops 8486912 | bytes 327684 | tf_op jit(solution)/shard_map/dot_general | solution.py:10
  31.2 0.2 convolution_subtract_fusion.1
  31.4 0.1 fusion.175
  31.5 0.3 fusion.176
  31.8 0.3 fusion.179
  32.1 0.3 fusion.7
  32.4 0.2 fusion.194
  32.7 0.2 convolution_subtract_fusion.8
  32.9 0.7 %fusion.14 = f32[8,64]{1,0:T(8,128)} fusion(f32[128,2,64]{0,2,1:T(8,128)S(1)} %bitcast.79, f32[128,2,64]{0,2,1:T(8,128)S(1)} %bitcast.82, f32[128,2,64]{0,2,1:T(8,128)S(1)} %bitcast.80, f32[128,2,64]{0,2,1:T(8,128)S(1)} %bitcast.84, f32[128,2,64]{0,2,1:T(8,128)S(1)} %bitcast.81, f32[128,2,64]{0,2,1:T(8,128)S(1)} %bitcast.78, f32[128,2,64]{0,2,1:T(8,128)S(1)} %bitcast.83, ...), kind=kLoop, calls=%fused_computation.39 | loop fusion | flops 523776 | bytes 526336 | tf_op jit(solution)/shard_map/reduce_sum | solution.py:217
  33.7 4.9 %all-to-all-start = ((f32[8,1,64]{2,1,0:T(1,128)}), f32[8,1,64]{2,1,0:T(1,128)S(1)}, u32[]{:S(2)}, u32[]{:S(2)}) async-start(f32[8,1,64]{2,1,0:T(1,128)} %bitcast.20), calls=%async_computation | async-start | bytes 8192 | tf_op jit(solution)/shard_map/all_to_all | solution.py:218
  38.6 0.8 %copy.34 = f32[128,512]{1,0:T(8,128)} copy(f32[128,512]{0,1:T(8,128)S(1)} %pad_maximum_fusion.3) | data formatting | bytes 524288
  39.4 0.8 %copy.33 = f32[128,512]{1,0:T(8,128)} copy(f32[128,512]{0,1:T(8,128)S(1)} %pad_maximum_fusion.1) | data formatting | bytes 524288
  40.3 3.9 %all-to-all-done = f32[8,1,64]{2,1,0:T(1,128)S(1)} async-done(((f32[8,1,64]{2,1,0:T(1,128)}), f32[8,1,64]{2,1,0:T(1,128)S(1)}, u32[]{:S(2)}, u32[]{:S(2)}) %all-to-all-start) | async-done | bytes 2080 | tf_op jit(solution)/shard_map/all_to_all | solution.py:218
  44.1 0.5 %broadcast_multiply_fusion = f32[64]{0:T(128)} fusion(f32[64]{0:T(128)S(1)} %reduce_sum.19), kind=kLoop, calls=%fused_computation.176 | loop fusion | flops 64 | bytes 512 | tf_op jit(solution)/shard_map/mul | solution.py:219
  (42 shorter events, 0.3 us)
Async XLA Ops:
  0.6 12.1 %copy-start = (bf16[256,512]{1,0:T(8,128)(2,1)S(1)}, bf16[256,512]{1,0:T(8,128)(2,1)}, u32[]{:S(2)}) copy-start(bf16[256,512]{1,0:T(8,128)(2,1)} %param.19) | copy-start | bytes 786436
  1.5 10.5 %copy-start.9 = (s32[3,2]{0,1:T(2,128)S(1)}, s32[3,2]{0,1:T(2,128)}, u32[]{:S(2)}) copy-start(s32[3,2]{0,1:T(2,128)} %param.15) | copy-start | bytes 76
  1.5 10.5 %copy-start.11 = (s32[128]{0:T(128)S(1)}, s32[128]{0:T(128)}, u32[]{:S(2)}) copy-start(s32[128]{0:T(128)} %param.12) | copy-start | bytes 1540
  2.3 2.8 %copy-start.3 = (bf16[2,128,128]{2,1,0:T(8,128)(2,1)S(1)}, bf16[2,128,128]{2,1,0:T(8,128)(2,1)}, u32[]{:S(2)}) copy-start(bf16[2,128,128]{2,1,0:T(8,128)(2,1)} %param.21) | copy-start | bytes 196612
  2.3 10.0 %copy-start.5 = (bf16[512,512]{1,0:T(8,128)(2,1)S(1)}, bf16[512,512]{1,0:T(8,128)(2,1)}, u32[]{:S(2)}) copy-start(bf16[512,512]{1,0:T(8,128)(2,1)} %param.16) | copy-start | bytes 1572868
  7.5 18.3 %collective-permute-start.4 = (bf16[136,128]{1,0:T(8,128)(2,1)S(1)}, bf16[136,128]{1,0:T(8,128)(2,1)}, u32[]{:S(2)}, u32[]{:S(2)}) collective-permute-start(bf16[136,128]{1,0:T(8,128)(2,1)S(1)} %pad_maximum_fusion.6), channel_id=1, source_target_pairs={{0,16},{8,24},{16,0},{24,8},{1,17},{9,25},{17,1},{25,9},{2,18},{10... | collective-permute-start | bytes 104456 | tf_op jit(solution)/shard_map/ppermute | solution.py:152
  10.5 15.3 %collective-permute-start.3 = (bf16[136,128]{1,0:T(8,128)(2,1)S(1)}, bf16[136,128]{1,0:T(8,128)(2,1)}, u32[]{:S(2)}, u32[]{:S(2)}) collective-permute-start(bf16[136,128]{1,0:T(8,128)(2,1)S(1)} %pad_maximum_fusion.6), channel_id=1, source_target_pairs={{0,24},{8,16},{16,8},{24,0},{1,25},{9,17},{17,9},{25,1},{2,26},{10... | collective-permute-start | bytes 104456 | tf_op jit(solution)/shard_map/ppermute | solution.py:152
  11.9 7.6 %collective-permute-start.1 = (bf16[528,128]{1,0:T(8,128)(2,1)}, bf16[528,128]{1,0:T(8,128)(2,1)S(1)}, u32[]{:S(2)}, u32[]{:S(2)}) collective-permute-start(bf16[528,128]{1,0:T(8,128)(2,1)} %get-tuple-element.19), channel_id=1, source_target_pairs={{0,8},{8,0},{16,24},{24,16},{1,9},{9,1},{17,25},{25,17},{2,10},{10... | collective-permute-start | bytes 405512 | tf_op jit(solution)/shard_map/ppermute | solution.py:152
  12.7 0.6 %copy-start.7 = (f32[128,128]{0,1:T(8,128)}, f32[128,128]{0,1:T(8,128)S(1)}, u32[]{:S(2)}) copy-start(f32[128,128]{0,1:T(8,128)S(1)} %convolution_subtract_fusion.5) | copy-start | bytes 196612
  12.8 2.7 %copy-start.6 = (f32[128,128]{1,0:T(8,128)S(1)}, f32[128,128]{1,0:T(8,128)}, u32[]{:S(2)}) copy-start(f32[128,128]{1,0:T(8,128)} %param.14) | copy-start | bytes 196612
  13.4 2.7 %copy-start.4 = (bf16[512,512]{1,0:T(8,128)(2,1)S(1)}, bf16[512,512]{1,0:T(8,128)(2,1)}, u32[]{:S(2)}) copy-start(bf16[512,512]{1,0:T(8,128)(2,1)} %param.17) | copy-start | bytes 1572868
  13.4 2.1 %copy-start.10 = (s32[128]{0:T(128)S(1)}, s32[128]{0:T(128)}, u32[]{:S(2)}) copy-start(s32[128]{0:T(128)} %param.13) | copy-start | bytes 1540
  13.4 2.4 %copy-start.2 = (bf16[4,128,128]{2,1,0:T(8,128)(2,1)S(1)}, bf16[4,128,128]{2,1,0:T(8,128)(2,1)}, u32[]{:S(2)}) copy-start(bf16[4,128,128]{2,1,0:T(8,128)(2,1)} %param.18) | copy-start | bytes 393220
  13.4 6.7 %collective-permute-start = (f32[256,128]{1,0:T(8,128)S(1)}, f32[256,128]{1,0:T(8,128)S(1)}, u32[]{:S(2)}, u32[]{:S(2)}) collective-permute-start(f32[256,128]{1,0:T(8,128)S(1)} %pad_maximum_fusion.4), channel_id=1, source_target_pairs={{0,8},{8,0},{16,24},{24,16},{1,9},{9,1},{17,25},{25,17},{2,10},{10... | collective-permute-start | bytes 393224 | tf_op jit(solution)/shard_map/ppermute | solution.py:134
  16.8 1.0 %copy-start.1 = (bf16[512,256]{1,0:T(8,128)(2,1)S(1)}, bf16[512,256]{1,0:T(8,128)(2,1)}, u32[]{:S(2)}) copy-start(bf16[512,256]{1,0:T(8,128)(2,1)} %param.20) | copy-start | bytes 786436
  18.0 5.0 %collective-permute-start.5 = (f32[256,128]{1,0:T(8,128)S(1)}, f32[256,128]{1,0:T(8,128)S(1)}, u32[]{:S(2)}, u32[]{:S(2)}) collective-permute-start(f32[256,128]{1,0:T(8,128)S(1)} %pad_maximum_fusion.5), channel_id=1, source_target_pairs={{0,8},{8,0},{16,24},{24,16},{1,9},{9,1},{17,25},{25,17},{2,10},{10... | collective-permute-start | bytes 393224 | tf_op jit(solution)/shard_map/ppermute | solution.py:134
  20.9 9.1 %collective-permute-start.2 = (f32[128,128]{1,0:T(8,128)S(1)}, f32[128,128]{1,0:T(8,128)S(1)}, u32[]{:S(2)}, u32[]{:S(2)}) collective-permute-start(f32[128,128]{1,0:T(8,128)S(1)} %fusion.72), channel_id=1, source_target_pairs={{0,16},{8,24},{16,0},{24,8},{1,17},{9,25},{17,1},{25,9},{2,18},{10... | collective-permute-start | bytes 196616 | tf_op jit(solution)/shard_map/ppermute | solution.py:134
  24.2 4.3 %collective-permute-start.6 = (f32[128,128]{1,0:T(8,128)S(1)}, f32[128,128]{1,0:T(8,128)S(1)}, u32[]{:S(2)}, u32[]{:S(2)}) collective-permute-start(f32[128,128]{1,0:T(8,128)S(1)} %fusion.63), channel_id=1, source_target_pairs={{0,16},{8,24},{16,0},{24,8},{1,17},{9,25},{17,1},{25,9},{2,18},{10... | collective-permute-start | bytes 196616 | tf_op jit(solution)/shard_map/ppermute | solution.py:134
  30.2 1.0 %copy-start.8 = (f32[128,128]{0,1:T(8,128)S(1)}, f32[128,128]{0,1:T(8,128)}, u32[]{:S(2)}) copy-start(f32[128,128]{0,1:T(8,128)} %copy-done.7) | copy-start | bytes 196612
  33.7 10.4 %all-to-all-start = ((f32[8,1,64]{2,1,0:T(1,128)}), f32[8,1,64]{2,1,0:T(1,128)S(1)}, u32[]{:S(2)}, u32[]{:S(2)}) async-start(f32[8,1,64]{2,1,0:T(1,128)} %bitcast.20), calls=%async_computation | async-start | bytes 8192 | tf_op jit(solution)/shard_map/all_to_all | solution.py:218

commit v8 on v3

--- a/solution.py
+++ b/solution.py
@@ -208,8 +208,17 @@
     spread = lax.axis_size("src")
     product_field = (forward_field * adjoint_field).reshape(source_count, spread, cell_count // spread)
     partial_gradient = jnp.sum(product_field, axis=0)
-    gathered = lax.all_to_all(partial_gradient, "src", 0, 0, tiled=True)
-    gradient = jnp.sum(gathered, axis=0) * factor
+    place = lax.axis_index("src")
+    bit = spread // 2
+    while bit:
+        half = partial_gradient.shape[0] // 2
+        upper = (place & bit) != 0
+        outgoing = jnp.where(upper, partial_gradient[:half], partial_gradient[half:])
+        kept = jnp.where(upper, partial_gradient[half:], partial_gradient[:half])
+        pairs = [(index, index ^ bit) for index in range(spread)]
+        partial_gradient = kept + lax.ppermute(outgoing, "src", pairs)
+        bit //= 2
+    gradient = partial_gradient.reshape(-1) * factor
     return (forward_field, adjoint_field, gradient)
 
 

time: 39.1 us -> 38 us (0.972)
  other arithmetic: 2.04 us -> 1.45 us
  starting transfers between devices: 13.2 us -> 12.7 us
    all_to_all x1 -> x0, starting transfers between devices: 4.89 us -> none  [shards(): gathered = lax.all_to_all(partial_gradient, 'src', 0, 0, tiled=True)]
    ppermute x0 -> x3, starting transfers between devices: none -> 4.37 us  [shards(): partial_gradient = kept + lax.ppermute(outgoing, 'src', pairs)]
    all_to_all x1 -> x0, waiting for transfers between devices: 3.86 us -> none  [shards(): gathered = lax.all_to_all(partial_gradient, 'src', 0, 0, tiled=True)]
    ppermute x0 -> x3, waiting for transfers between devices: none -> 3.86 us  [shards(): partial_gradient = kept + lax.ppermute(outgoing, 'src', pairs)]
    reduce_sum x1, other arithmetic: 0.73 us -> 0.14 us  [shards(): partial_gradient = jnp.sum(product_field, axis=0)]
  transfers between devices with their start and end apart: 7 -> 9, of which waited for: 4 -> 5; matrix products, arithmetic and copies ran while one was open for 24% -> 24% of each run, Pallas kernels for 0% -> 0%
where the time goes in v8:
time: 38 us; the launch traced here: 37.6 us
  starting transfers between devices  12.7 us (33%)
  matrix products  8.68 us (23%)
  waiting for transfers between devices  6.92 us (18%)
  local copies, waits for them, and re-layouts  6.85 us (18%)
  other arithmetic  1.45 us (4%)
  between operations  1.04 us (3%)
    ppermute x6, starting transfers between devices, exchange(): incoming = lax.ppermute(jnp.concatenate(pieces, axis=0), 'leaf', pairs)  8.29 us
    unnamed x36, local copies, waits for them, and re-layouts  5.92 us
    dot_general x13, matrix products, plain_dot(): return jnp.dot(former, latter, preferred_element_type=jnp.float32)  4.43 us
    ppermute x3, starting transfers between devices, shards(): partial_gradient = kept + lax.ppermute(outgoing, 'src', pairs)  4.37 us
    dot_general x12, matrix products, across(): lax.dot_general(former, latter, (((1,), (1,)), ((), ())), preferred_eleme...  3.87 us
    ppermute x3, waiting for transfers between devices, shards(): partial_gradient = kept + lax.ppermute(outgoing, 'src', pairs)  3.86 us
    ppermute x6, waiting for transfers between devices, exchange(): incoming = lax.ppermute(jnp.concatenate(pieces, axis=0), 'leaf', pairs)  3.06 us
  transfers between devices with their start and end apart: 9, of which 5 were waited for; matrix products, arithmetic and copies ran while one was open for 24% of the time, Pallas kernels for 0%

profile of v8, /device:TPU:0, one launch (start us, length us, event | category | flops | bytes accessed | tf_op | source)
XLA Modules:
  0.0 37.6 jit_solution(12269758528643921520)
XLA Ops:
  0.6 0.0 copy-start
  0.6 0.8 %copy.15 = s32[3,2]{1,0:T(4,128)S(1)} copy(s32[3,2]{0,1:T(2,128)} %param.15) | data formatting | bytes 48 | tf_op args[3]
  1.5 0.0 copy-start.2
  1.5 0.0 copy-start.6
  1.5 0.8 %bitcast_dynamic-update-slice_fusion.3 = bf16[528,128]{1,0:T(8,128)(2,1)S(1)} fusion(bf16[2,256,128]{2,1,0:T(8,128)(2,1)} %param.22), kind=kLoop, calls=%fused_computation.139 | loop fusion | bytes 65536
  2.3 0.8 %bitcast_dynamic-update-slice_fusion.2 = bf16[528,128]{1,0:T(8,128)(2,1)S(1)} fusion(bf16[528,128]{1,0:T(8,128)(2,1)S(1)} %bitcast_dynamic-update-slice_fusion.3, bf16[2,128,256]{2,1,0:T(8,128)(2,1)} %param.23), kind=kLoop, calls=%fused_computation.138 | loop fusion | bytes 65536
  3.1 3.0 %collective-permute-start.1 = (bf16[528,128]{1,0:T(8,128)(2,1)S(1)}, bf16[528,128]{1,0:T(8,128)(2,1)S(1)}, u32[]{:S(2)}, u32[]{:S(2)}) collective-permute-start(bf16[528,128]{1,0:T(8,128)(2,1)S(1)} %constant_dynamic-update-slice_fusion), channel_id=1, source_target_pairs={{0,8},{8,0},{16,24},{24,16},{1,9},{9,1},{17,25},{25,17},{2,10},{10... | collective-permute-start | bytes 405512 | tf_op jit(solution)/shard_map/ppermute | solution.py:134
  6.2 0.1 slice_reduce_fusion
  6.4 0.1 broadcast_bitcast_fusion
  6.4 0.1 fusion.163
  6.6 0.1 fusion.164
  6.7 0.2 convolution_subtract_fusion.5
  6.9 0.0 copy-start.9
  6.9 0.6 %copy-done.9 = f32[128,128]{0,1:T(8,128)} copy-done((f32[128,128]{0,1:T(8,128)}, f32[128,128]{0,1:T(8,128)S(1)}, u32[]{:S(2)}) %copy-start.9) | copy-done | bytes 65560
  7.6 0.2 convolution_multiply_fusion.1
  7.8 0.0 copy-start.5
  7.8 0.0 copy-start.12
  7.9 0.0 copy-start.3
  7.9 0.1 collective-permute-start
  8.0 0.4 %copy-done.8 = f32[128,128]{1,0:T(8,128)S(1)} copy-done((f32[128,128]{1,0:T(8,128)S(1)}, f32[128,128]{1,0:T(8,128)}, u32[]{:S(2)}) %copy-start.8) | copy-done | bytes 65560
  8.4 0.1 copy-done.12
  8.5 0.4 %convolution_bitcast_fusion = f32[128,512]{0,1:T(8,128)S(1)} fusion(f32[128,128]{1,0:T(8,128)S(1)} %copy-done.8, s32[128]{0:T(128)S(1)} %copy-done.12), kind=kOutput, calls=%fused_computation.2 | convolution fusion | flops 100794368 | bytes 328192 | tf_op jit(solution)/shard_map/dot_general | solution.py:111
  8.9 0.2 fusion.174
  9.2 0.3 fusion.175
  9.5 0.4 fusion.178
  9.9 0.0 copy-start.1
  9.9 0.4 fusion.10
  10.2 0.6 %copy-done.1 = bf16[512,256]{1,0:T(8,128)(2,1)S(1)} copy-done((bf16[512,256]{1,0:T(8,128)(2,1)S(1)}, bf16[512,256]{1,0:T(8,128)(2,1)}, u32[]{:S(2)}) %copy-start.1) | copy-done | bytes 262168
  10.8 0.2 convolution_multiply_fusion
  11.1 1.5 %collective-permute-start.4 = (f32[256,128]{1,0:T(8,128)S(1)}, f32[256,128]{1,0:T(8,128)S(1)}, u32[]{:S(2)}, u32[]{:S(2)}) collective-permute-start(f32[256,128]{1,0:T(8,128)S(1)} %pad_maximum_fusion.5), channel_id=1, source_target_pairs={{0,8},{8,0},{16,24},{24,16},{1,9},{9,1},{17,25},{25,17},{2,10},{10... | collective-permute-start | bytes 393224 | tf_op jit(solution)/shard_map/ppermute | solution.py:134
  12.6 0.6 %slice.231 = f32[1]{0:T(128)} slice(f32[2]{0:T(128)S(1)} %compare_select_fusion), slice={[1:2]} | slice | bytes 8 | tf_op jit(solution)/shard_map/slice | solution.py:130
  13.2 0.6 %pad_maximum_fusion.6 = bf16[136,128]{1,0:T(8,128)(2,1)} fusion(bf16[8,128]{1,0:T(8,128)(2,1)S(1)} %get-tuple-element.6, bf16[128,128]{1,0:T(8,128)(2,1)S(1)} %slice_select_fusion.3), kind=kLoop, calls=%fused_computation.116 | loop fusion | flops 69632 | bytes 69632 | tf_op jit(solution)/shard_map/concatenate | solution.py:134
  13.8 1.5 %collective-permute-start.3 = (bf16[136,128]{1,0:T(8,128)(2,1)}, bf16[136,128]{1,0:T(8,128)(2,1)S(1)}, u32[]{:S(2)}, u32[]{:S(2)}) collective-permute-start(bf16[136,128]{1,0:T(8,128)(2,1)} %pad_maximum_fusion.6), channel_id=1, source_target_pairs={{0,16},{8,24},{16,0},{24,8},{1,17},{9,25},{17,1},{25,9},{2,18},{10... | collective-permute-start | bytes 104456 | tf_op jit(solution)/shard_map/ppermute | solution.py:134
  15.4 0.8 %collective-permute-done.4 = f32[256,128]{1,0:T(8,128)S(1)} collective-permute-done((f32[256,128]{1,0:T(8,128)S(1)}, f32[256,128]{1,0:T(8,128)S(1)}, u32[]{:S(2)}, u32[]{:S(2)}) %collective-permute-start.4) | collective-permute-done | bytes 131104 | tf_op jit(solution)/shard_map/ppermute | solution.py:134
  16.1 0.2 fusion.105
  16.4 0.9 %fusion.63 = f32[128,128]{1,0:T(8,128)S(1)} fusion(f32[256,128]{1,0:T(8,128)S(1)} %collective-permute-done.4, f32[128,128]{0,1:T(8,128)S(1)} %fusion.105, f32[]{:T(128)} %bitcast.6, bf16[528,128]{1,0:T(8,128)(2,1)S(1)} %collective-permute-done.1, pred[]{:T(512)S(6)} %and.31, bf16[2,128,256]{2,1,0:T(8,128)(2,1)S(1)} %copy-done.4, ...), kind=kOutput, calls=%fused_computation.78 | convolution fusion | flops 4276224 | bytes 327685 | tf_op jit(solution)/shard_map/dot_general | solution.py:16
  17.2 1.6 %collective-permute-start.5 = (f32[128,128]{1,0:T(8,128)S(1)}, f32[128,128]{1,0:T(8,128)S(1)}, u32[]{:S(2)}, u32[]{:S(2)}) collective-permute-start(f32[128,128]{1,0:T(8,128)S(1)} %fusion.63), channel_id=1, source_target_pairs={{0,16},{8,24},{16,0},{24,8},{1,17},{9,25},{17,1},{25,9},{2,18},{10... | collective-permute-start | bytes 196616 | tf_op jit(solution)/shard_map/ppermute | solution.py:134
  18.8 0.8 %fusion.72 = f32[128,128]{1,0:T(8,128)S(1)} fusion(f32[256,128]{1,0:T(8,128)S(1)} %collective-permute-done, f32[]{:T(128)} %bitcast.6, bf16[528,128]{1,0:T(8,128)(2,1)S(1)} %collective-permute-done.1, pred[]{:T(512)S(6)} %and.31, bf16[2,256,128]{2,1,0:T(8,128)(2,1)S(1)} %copy-done.7, f32[128,256]{1,0:T(8,128)S(1)} %convolution_multiply_fusion.1), kind=kOutput, calls=%fused_computation.91 | convolution fusion | flops 4308992 | bytes 393221 | tf_op jit(solution)/shard_map/dot_general | solution.py:10
  19.6 0.1 copy.20
  19.7 0.6 %collective-permute-start.2 = (f32[128,128]{1,0:T(8,128)S(1)}, f32[128,128]{1,0:T(8,128)S(1)}, u32[]{:S(2)}, u32[]{:S(2)}) collective-permute-start(f32[128,128]{1,0:T(8,128)S(1)} %fusion.72), channel_id=1, source_target_pairs={{0,16},{8,24},{16,0},{24,8},{1,17},{9,25},{17,1},{25,9},{2,18},{10... | collective-permute-start | bytes 196616 | tf_op jit(solution)/shard_map/ppermute | solution.py:134
  20.3 1.6 %collective-permute-done.5 = f32[128,128]{1,0:T(8,128)S(1)} collective-permute-done((f32[128,128]{1,0:T(8,128)S(1)}, f32[128,128]{1,0:T(8,128)S(1)}, u32[]{:S(2)}, u32[]{:S(2)}) %collective-permute-start.5) | collective-permute-done | bytes 65568 | tf_op jit(solution)/shard_map/ppermute | solution.py:134
  21.9 0.1 fusion.101
  22.1 0.8 %fusion.102 = f32[128,128]{1,0:T(8,128)S(1)} fusion(f32[128,128]{1,0:T(8,128)S(1)} %fusion.101, f32[]{:T(128)} %bitcast.6, bf16[528,128]{1,0:T(8,128)(2,1)S(1)} %collective-permute-done.1, pred[]{:T(512)S(6)} %and.31, bf16[2,256,128]{2,1,0:T(8,128)(2,1)S(1)} %copy-done.7), kind=kOutput, calls=%fused_computation.119 | convolution fusion | flops 4243456 | bytes 196613 | tf_op jit(solution)/shard_map/dot_general | solution.py:16
  22.9 0.3 convolution_subtract_fusion
  23.1 0.2 fusion.183
  23.4 0.7 %collective-permute-done.2 = f32[128,128]{1,0:T(8,128)S(1)} collective-permute-done((f32[128,128]{1,0:T(8,128)S(1)}, f32[128,128]{1,0:T(8,128)S(1)}, u32[]{:S(2)}, u32[]{:S(2)}) %collective-permute-start.2) | collective-permute-done | bytes 65568 | tf_op jit(solution)/shard_map/ppermute | solution.py:134
  24.1 0.1 fusion.100
  24.2 1.0 %fusion.13 = f32[128,128]{1,0:T(8,128)S(1)} fusion(f32[128,128]{1,0:T(8,128)S(1)} %fusion.100, f32[]{:T(128)} %bitcast.6, f32[256,128]{1,0:T(8,128)S(1)} %collective-permute-done, bf16[528,128]{1,0:T(8,128)(2,1)S(1)} %collective-permute-done.1, pred[]{:T(512)S(6)} %and.31, bf16[2,128,256]{2,1,0:T(8,128)(2,1)S(1)} %copy-done.4, ...), kind=kOutput, calls=%fused_computation.33 | convolution fusion | flops 8519680 | bytes 394244 | tf_op jit(solution)/shard_map/dot_general | solution.py:10
  25.2 0.2 convolution_subtract_fusion.1
  25.4 0.1 fusion.165
  25.6 0.3 fusion.166
  25.9 0.3 fusion.169
  26.2 0.3 fusion.7
  26.5 0.2 fusion.184
  26.7 0.2 convolution_subtract_fusion.8
  26.9 0.1 fusion.14
  27.1 2.7 %collective-permute-start.6 = (f32[4,64]{1,0:T(4,128)S(1)}, f32[4,64]{1,0:T(4,128)S(1)}, u32[]{:S(2)}, u32[]{:S(2)}) collective-permute-start(f32[4,64]{1,0:T(4,128)S(1)} %slice_select_fusion.14), channel_id=1, source_target_pairs={{0,4},{1,5},{2,6},{3,7},{4,0},{5,1},{6,2},{7,3},{8,12},{9,13},{10,... | collective-permute-start | bytes 3080 | tf_op jit(solution)/shard_map/ppermute | solution.py:219
  29.8 1.9 %collective-permute-done.6 = f32[4,64]{1,0:T(4,128)S(1)} collective-permute-done((f32[4,64]{1,0:T(4,128)S(1)}, f32[4,64]{1,0:T(4,128)S(1)}, u32[]{:S(2)}, u32[]{:S(2)}) %collective-permute-start.6) | collective-permute-done | bytes 1056 | tf_op jit(solution)/shard_map/ppermute | solution.py:219
  31.7 1.6 %collective-permute-start.7 = (f32[2,64]{1,0:T(2,128)S(1)}, f32[2,64]{1,0:T(2,128)S(1)}, u32[]{:S(2)}, u32[]{:S(2)}) collective-permute-start(f32[2,64]{1,0:T(2,128)S(1)} %broadcast_select_fusion), channel_id=1, source_target_pairs={{0,2},{1,3},{2,0},{3,1},{4,6},{5,7},{6,4},{7,5},{8,10},{9,11},{10,... | collective-permute-start | bytes 1544 | tf_op jit(solution)/shard_map/ppermute | solution.py:219
  33.3 2.0 %collective-permute-done.7 = f32[2,64]{1,0:T(2,128)S(1)} collective-permute-done((f32[2,64]{1,0:T(2,128)S(1)}, f32[2,64]{1,0:T(2,128)S(1)}, u32[]{:S(2)}, u32[]{:S(2)}) %collective-permute-start.7) | collective-permute-done | bytes 544 | tf_op jit(solution)/shard_map/ppermute | solution.py:219
  35.3 0.1 collective-permute-start.8
  35.4 0.8 %copy.24 = f32[128,512]{1,0:T(8,128)} copy(f32[128,512]{0,1:T(8,128)S(1)} %pad_maximum_fusion.3) | data formatting | bytes 524288
  36.2 0.8 %copy.23 = f32[128,512]{1,0:T(8,128)} copy(f32[128,512]{0,1:T(8,128)S(1)} %pad_maximum_fusion.1) | data formatting | bytes 524288
  37.1 0.5 %fusion.140 = f32[64]{0:T(128)} fusion(f32[1,64]{1,0:T(1,128)S(1)} %collective-permute-done.8, pred[]{:T(512)S(6)} %ne.23, f32[2,64]{1,0:T(2,128)S(1)} %select_add_fusion.1), kind=kLoop, calls=%fused_computation.172 | loop fusion | flops 192 | bytes 1025 | tf_op jit(solution)/shard_map/mul | solution.py:221
  (49 shorter events, 0.3 us)
Async XLA Ops:
  0.6 6.9 %copy-start = (bf16[256,512]{1,0:T(8,128)(2,1)S(1)}, bf16[256,512]{1,0:T(8,128)(2,1)}, u32[]{:S(2)}) copy-start(bf16[256,512]{1,0:T(8,128)(2,1)} %param.19) | copy-start | bytes 786436
  1.5 4.7 %copy-start.11 = (s32[3,2]{0,1:T(2,128)S(1)}, s32[3,2]{0,1:T(2,128)}, u32[]{:S(2)}) copy-start(s32[3,2]{0,1:T(2,128)} %param.15) | copy-start | bytes 76
  1.5 4.7 %copy-start.13 = (s32[128]{0:T(128)S(1)}, s32[128]{0:T(128)}, u32[]{:S(2)}) copy-start(s32[128]{0:T(128)} %param.12) | copy-start | bytes 1540
  1.5 1.6 %copy-start.2 = (bf16[2,128,128]{2,1,0:T(8,128)(2,1)S(1)}, bf16[2,128,128]{2,1,0:T(8,128)(2,1)}, u32[]{:S(2)}) copy-start(bf16[2,128,128]{2,1,0:T(8,128)(2,1)} %param.21) | copy-start | bytes 196612
  1.5 4.9 %copy-start.6 = (bf16[512,512]{1,0:T(8,128)(2,1)S(1)}, bf16[512,512]{1,0:T(8,128)(2,1)}, u32[]{:S(2)}) copy-start(bf16[512,512]{1,0:T(8,128)(2,1)} %param.16) | copy-start | bytes 1572868
  3.1 9.4 %collective-permute-start.1 = (bf16[528,128]{1,0:T(8,128)(2,1)S(1)}, bf16[528,128]{1,0:T(8,128)(2,1)S(1)}, u32[]{:S(2)}, u32[]{:S(2)}) collective-permute-start(bf16[528,128]{1,0:T(8,128)(2,1)S(1)} %constant_dynamic-update-slice_fusion), channel_id=1, source_target_pairs={{0,8},{8,0},{16,24},{24,16},{1,9},{9,1},{17,25},{25,17},{2,10},{10... | collective-permute-start | bytes 405512 | tf_op jit(solution)/shard_map/ppermute | solution.py:134
  6.9 0.6 %copy-start.9 = (f32[128,128]{0,1:T(8,128)}, f32[128,128]{0,1:T(8,128)S(1)}, u32[]{:S(2)}) copy-start(f32[128,128]{0,1:T(8,128)S(1)} %convolution_subtract_fusion.5) | copy-start | bytes 196612
  7.5 0.8 %copy-start.8 = (f32[128,128]{1,0:T(8,128)S(1)}, f32[128,128]{1,0:T(8,128)}, u32[]{:S(2)}) copy-start(f32[128,128]{1,0:T(8,128)} %param.14) | copy-start | bytes 196612
  7.8 1.4 %copy-start.5 = (bf16[512,512]{1,0:T(8,128)(2,1)S(1)}, bf16[512,512]{1,0:T(8,128)(2,1)}, u32[]{:S(2)}) copy-start(bf16[512,512]{1,0:T(8,128)(2,1)} %param.17) | copy-start | bytes 1572868
  7.8 0.7 %copy-start.12 = (s32[128]{0:T(128)S(1)}, s32[128]{0:T(128)}, u32[]{:S(2)}) copy-start(s32[128]{0:T(128)} %param.13) | copy-start | bytes 1540
  7.9 1.1 %copy-start.3 = (bf16[4,128,128]{2,1,0:T(8,128)(2,1)S(1)}, bf16[4,128,128]{2,1,0:T(8,128)(2,1)}, u32[]{:S(2)}) copy-start(bf16[4,128,128]{2,1,0:T(8,128)(2,1)} %param.18) | copy-start | bytes 393220
  7.9 11.0 %collective-permute-start = (f32[256,128]{1,0:T(8,128)S(1)}, f32[256,128]{1,0:T(8,128)S(1)}, u32[]{:S(2)}, u32[]{:S(2)}) collective-permute-start(f32[256,128]{1,0:T(8,128)S(1)} %pad_maximum_fusion.4), channel_id=1, source_target_pairs={{0,8},{8,0},{16,24},{24,16},{1,9},{9,1},{17,25},{25,17},{2,10},{10... | collective-permute-start | bytes 393224 | tf_op jit(solution)/shard_map/ppermute | solution.py:134
  9.9 1.0 %copy-start.1 = (bf16[512,256]{1,0:T(8,128)(2,1)S(1)}, bf16[512,256]{1,0:T(8,128)(2,1)}, u32[]{:S(2)}) copy-start(bf16[512,256]{1,0:T(8,128)(2,1)} %param.20) | copy-start | bytes 786436
  11.1 5.0 %collective-permute-start.4 = (f32[256,128]{1,0:T(8,128)S(1)}, f32[256,128]{1,0:T(8,128)S(1)}, u32[]{:S(2)}, u32[]{:S(2)}) collective-permute-start(f32[256,128]{1,0:T(8,128)S(1)} %pad_maximum_fusion.5), channel_id=1, source_target_pairs={{0,8},{8,0},{16,24},{24,16},{1,9},{9,1},{17,25},{25,17},{2,10},{10... | collective-permute-start | bytes 393224 | tf_op jit(solution)/shard_map/ppermute | solution.py:134
  13.8 2.5 %copy-start.4 = (bf16[2,128,256]{2,1,0:T(8,128)(2,1)S(1)}, bf16[2,128,256]{2,1,0:T(8,128)(2,1)}, u32[]{:S(2)}) copy-start(bf16[2,128,256]{2,1,0:T(8,128)(2,1)} %param.23) | copy-start | bytes 393220
  13.8 6.5 %collective-permute-start.3 = (bf16[136,128]{1,0:T(8,128)(2,1)}, bf16[136,128]{1,0:T(8,128)(2,1)S(1)}, u32[]{:S(2)}, u32[]{:S(2)}) collective-permute-start(bf16[136,128]{1,0:T(8,128)(2,1)} %pad_maximum_fusion.6), channel_id=1, source_target_pairs={{0,16},{8,24},{16,0},{24,8},{1,17},{9,25},{17,1},{25,9},{2,18},{10... | collective-permute-start | bytes 104456 | tf_op jit(solution)/shard_map/ppermute | solution.py:134
  16.3 2.5 %copy-start.7 = (bf16[2,256,128]{2,1,0:T(8,128)(2,1)S(1)}, bf16[2,256,128]{2,1,0:T(8,128)(2,1)}, u32[]{:S(2)}) copy-start(bf16[2,256,128]{2,1,0:T(8,128)(2,1)} %param.22) | copy-start | bytes 393220
  17.2 4.7 %collective-permute-start.5 = (f32[128,128]{1,0:T(8,128)S(1)}, f32[128,128]{1,0:T(8,128)S(1)}, u32[]{:S(2)}, u32[]{:S(2)}) collective-permute-start(f32[128,128]{1,0:T(8,128)S(1)} %fusion.63), channel_id=1, source_target_pairs={{0,16},{8,24},{16,0},{24,8},{1,17},{9,25},{17,1},{25,9},{2,18},{10... | collective-permute-start | bytes 196616 | tf_op jit(solution)/shard_map/ppermute | solution.py:134
  19.7 4.3 %collective-permute-start.2 = (f32[128,128]{1,0:T(8,128)S(1)}, f32[128,128]{1,0:T(8,128)S(1)}, u32[]{:S(2)}, u32[]{:S(2)}) collective-permute-start(f32[128,128]{1,0:T(8,128)S(1)} %fusion.72), channel_id=1, source_target_pairs={{0,16},{8,24},{16,0},{24,8},{1,17},{9,25},{17,1},{25,9},{2,18},{10... | collective-permute-start | bytes 196616 | tf_op jit(solution)/shard_map/ppermute | solution.py:134
  24.2 1.0 %copy-start.10 = (f32[128,128]{0,1:T(8,128)S(1)}, f32[128,128]{0,1:T(8,128)}, u32[]{:S(2)}) copy-start(f32[128,128]{0,1:T(8,128)} %copy-done.9) | copy-start | bytes 196612
  27.1 4.5 %collective-permute-start.6 = (f32[4,64]{1,0:T(4,128)S(1)}, f32[4,64]{1,0:T(4,128)S(1)}, u32[]{:S(2)}, u32[]{:S(2)}) collective-permute-start(f32[4,64]{1,0:T(4,128)S(1)} %slice_select_fusion.14), channel_id=1, source_target_pairs={{0,4},{1,5},{2,6},{3,7},{4,0},{5,1},{6,2},{7,3},{8,12},{9,13},{10,... | collective-permute-start | bytes 3080 | tf_op jit(solution)/shard_map/ppermute | solution.py:219
  31.7 3.6 %collective-permute-start.7 = (f32[2,64]{1,0:T(2,128)S(1)}, f32[2,64]{1,0:T(2,128)S(1)}, u32[]{:S(2)}, u32[]{:S(2)}) collective-permute-start(f32[2,64]{1,0:T(2,128)S(1)} %broadcast_select_fusion), channel_id=1, source_target_pairs={{0,2},{1,3},{2,0},{3,1},{4,6},{5,7},{6,4},{7,5},{8,10},{9,11},{10,... | collective-permute-start | bytes 1544 | tf_op jit(solution)/shard_map/ppermute | solution.py:219
  35.3 1.8 %collective-permute-start.8 = (f32[1,64]{1,0:T(1,128)S(1)}, f32[1,64]{1,0:T(1,128)S(1)}, u32[]{:S(2)}, u32[]{:S(2)}) collective-permute-start(f32[1,64]{1,0:T(1,128)S(1)} %broadcast_select_fusion.1), channel_id=1, source_target_pairs={{0,1},{1,0},{2,3},{3,2},{4,5},{5,4},{6,7},{7,6},{8,9},{9,8},{10,11... | collective-permute-start | bytes 776 | tf_op jit(solution)/shard_map/ppermute | solution.py:219

commit v9 on v8

--- a/solution.py
+++ b/solution.py
@@ -175,6 +175,8 @@
                 across(as_half(forward_node), lower_panels[height - 1]) * chain_mask(height)
             )
             forward_sums = [total + extra for total, extra in zip(forward_sums, forward_coupling)]
+        adjoint_sums, forward_sums, forward_node = lax.optimization_barrier((adjoint_sums, forward_sums, forward_node))
+        forward_nodes[-1] = forward_node
         adjoint_sums = [mine + theirs for mine, theirs in zip(adjoint_sums, exchange(adjoint_sums, pairs))]
         adjoint_node = plain_dot(as_half(-adjoint_sums[0]), inverse_panels[height - 1])
         adjoint_nodes.append(adjoint_node)

time: 38 us -> 41.5 us (1.092)
  waiting for transfers between devices: 6.92 us -> 9.35 us
  local copies, waits for them, and re-layouts: 6.85 us -> 8.1 us
  starting transfers between devices: 12.7 us -> 11.8 us
  matrix products: 8.68 us -> 9.39 us
    ppermute x6, waiting for transfers between devices: 3.06 us -> 6.08 us  [exchange(): incoming = lax.ppermute(jnp.concatenate(pieces, axis=0), 'leaf', pairs)]
    ppermute x6, starting transfers between devices: 8.29 us -> 7.42 us  [exchange(): incoming = lax.ppermute(jnp.concatenate(pieces, axis=0), 'leaf', pairs)]
    sub x1, other arithmetic: 0.01 us -> 0.73 us  [shards(): src_cells[:, None] - device * cell_count == columns]
    dot_general x12, matrix products: 3.87 us -> 4.59 us  [across(): lax.dot_general(former, latter, (((1,), (1,)), ((), ())), preferred_eleme...]
    unnamed x36 -> x30, local copies, waits for them, and re-layouts: 5.92 us -> 6.6 us
    concatenate x3, other arithmetic: 0.64 us -> 0.03 us  [exchange(): incoming = lax.ppermute(jnp.concatenate(pieces, axis=0), 'leaf', pairs)]
    ppermute x3, waiting for transfers between devices: 3.86 us -> 3.27 us  [shards(): partial_gradient = kept + lax.ppermute(outgoing, 'src', pairs)]
    concatenate x1, local copies, waits for them, and re-layouts: 0.01 us -> 0.58 us  [exchange(): incoming = lax.ppermute(jnp.concatenate(pieces, axis=0), 'leaf', pairs)]
  transfers between devices with their start and end apart: 9 -> 9, of which waited for: 5 -> 7; matrix products, arithmetic and copies ran while one was open for 24% -> 26% of each run, Pallas kernels for 0% -> 0%
where the time goes in v9:
time: 41.5 us; the launch traced here: 41.2 us
  starting transfers between devices  11.8 us (28%)
  matrix products  9.39 us (23%)
  waiting for transfers between devices  9.35 us (23%)
  local copies, waits for them, and re-layouts  8.1 us (20%)
  other arithmetic  1.59 us (4%)
  between operations  1.02 us (2%)
    ppermute x6, starting transfers between devices, exchange(): incoming = lax.ppermute(jnp.concatenate(pieces, axis=0), 'leaf', pairs)  7.42 us
    unnamed x30, local copies, waits for them, and re-layouts  6.6 us
    ppermute x6, waiting for transfers between devices, exchange(): incoming = lax.ppermute(jnp.concatenate(pieces, axis=0), 'leaf', pairs)  6.08 us
    dot_general x12, matrix products, across(): lax.dot_general(former, latter, (((1,), (1,)), ((), ())), preferred_eleme...  4.59 us
    dot_general x13, matrix products, plain_dot(): return jnp.dot(former, latter, preferred_element_type=jnp.float32)  4.42 us
    ppermute x3, starting transfers between devices, shards(): partial_gradient = kept + lax.ppermute(outgoing, 'src', pairs)  4.37 us
    ppermute x3, waiting for transfers between devices, shards(): partial_gradient = kept + lax.ppermute(outgoing, 'src', pairs)  3.27 us
  transfers between devices with their start and end apart: 9, of which 7 were waited for; matrix products, arithmetic and copies ran while one was open for 26% of the time, Pallas kernels for 0%

profile of v9, /device:TPU:0, one launch (start us, length us, event | category | flops | bytes accessed | tf_op | source)
XLA Modules:
  0.0 41.2 jit_solution(4712870542571107976)
XLA Ops:
  0.6 0.0 copy-start
  0.6 0.0 copy-start.7
  0.7 0.7 %broadcast_subtract_fusion = s32[128]{0:T(128)S(1)} fusion(s32[128]{0:T(128)} %param.12, s32[]{:T(128)S(6)} %mul.38), kind=kLoop, calls=%fused_computation.175 | loop fusion | flops 128 | bytes 1028 | tf_op jit(solution)/shard_map/sub | solution.py:107
  1.5 0.9 %fusion.159 = (bf16[128,128]{0,1:T(8,128)(2,1)S(1)}, f32[128,128]{0,1:T(8,128)S(1)}) fusion(bf16[512,512]{1,0:T(8,128)(2,1)} %param.16, f32[128,512]{0,1:T(8,128)S(1)} %fusion.15), kind=kOutput, calls=%fused_computation.193 | convolution fusion | flops 4227072 | bytes 229376 | tf_op jit(solution)/shard_map/dot_general | solution.py:10
  2.4 0.2 fusion.160
  2.5 0.2 convolution_subtract_fusion.5
  2.7 0.5 %copy-done.9 = s32[3,2]{0,1:T(2,128)S(1)} copy-done((s32[3,2]{0,1:T(2,128)S(1)}, s32[3,2]{0,1:T(2,128)}, u32[]{:S(2)}) %copy-start.9) | copy-done | bytes 48
  3.3 0.1 slice_reduce_fusion
  3.4 0.1 broadcast_bitcast_fusion
  3.5 0.0 copy-done.3
  3.5 0.2 convolution_multiply_fusion
  3.8 3.0 %collective-permute-start = (f32[256,128]{1,0:T(8,128)S(1)}, f32[256,128]{1,0:T(8,128)S(1)}, u32[]{:S(2)}, u32[]{:S(2)}) collective-permute-start(f32[256,128]{1,0:T(8,128)S(1)} %pad_maximum_fusion.4), channel_id=1, source_target_pairs={{0,8},{8,0},{16,24},{24,16},{1,9},{9,1},{17,25},{25,17},{2,10},{10... | collective-permute-start | bytes 393224 | tf_op jit(solution)/shard_map/ppermute | solution.py:134
  6.8 0.1 copy.15
  6.9 0.6 %bitcast_dynamic-update-slice_fusion.3 = bf16[528,128]{1,0:T(8,128)(2,1)} fusion(bf16[2,256,128]{2,1,0:T(8,128)(2,1)S(1)} %copy-done.5), kind=kLoop, calls=%fused_computation.130 | loop fusion | bytes 65536
  7.5 0.6 %bitcast_dynamic-update-slice_fusion.2 = bf16[528,128]{1,0:T(8,128)(2,1)} fusion(bf16[528,128]{1,0:T(8,128)(2,1)} %bitcast_dynamic-update-slice_fusion.3, bf16[2,128,256]{2,1,0:T(8,128)(2,1)S(1)} %copy-done.4), kind=kLoop, calls=%fused_computation.129 | loop fusion | bytes 65536
  8.2 0.6 %bitcast_dynamic-update-slice_fusion.1 = bf16[528,128]{1,0:T(8,128)(2,1)} fusion(bf16[528,128]{1,0:T(8,128)(2,1)} %bitcast_dynamic-update-slice_fusion.2, bf16[2,128,128]{2,1,0:T(8,128)(2,1)S(1)} %copy-done.1), kind=kLoop, calls=%fused_computation.128 | loop fusion | bytes 65536
  8.8 0.6 %constant_dynamic-update-slice_fusion.1 = bf16[528,128]{1,0:T(8,128)(2,1)} fusion(bf16[528,128]{1,0:T(8,128)(2,1)} %bitcast_dynamic-update-slice_fusion.1, bf16[1,2]{1,0:T(2,128)(2,1)S(1)} %get-tuple-element.25), kind=kLoop, calls=%fused_computation.158 | loop fusion | bytes 2052
  9.4 0.6 %bitcast_dynamic-update-slice_fusion = bf16[528,128]{1,0:T(8,128)(2,1)} fusion(bf16[528,128]{1,0:T(8,128)(2,1)} %constant_dynamic-update-slice_fusion.1, bf16[2,128,128]{2,1,0:T(8,128)(2,1)S(1)} %copy-done.1), kind=kLoop, calls=%fused_computation.127 | loop fusion | bytes 65536
  10.0 0.6 %constant_dynamic-update-slice_fusion = bf16[528,128]{1,0:T(8,128)(2,1)} fusion(bf16[528,128]{1,0:T(8,128)(2,1)} %bitcast_dynamic-update-slice_fusion, bf16[1,2]{1,0:T(2,128)(2,1)S(1)} %get-tuple-element.24), kind=kLoop, calls=%fused_computation.157 | loop fusion | bytes 2052 | tf_op jit(solution)/shard_map/concatenate | solution.py:134
  10.6 0.7 %collective-permute-start.1 = (bf16[528,128]{1,0:T(8,128)(2,1)}, bf16[528,128]{1,0:T(8,128)(2,1)S(1)}, u32[]{:S(2)}, u32[]{:S(2)}) collective-permute-start(bf16[528,128]{1,0:T(8,128)(2,1)} %constant_dynamic-update-slice_fusion), channel_id=1, source_target_pairs={{0,8},{8,0},{16,24},{24,16},{1,9},{9,1},{17,25},{25,17},{2,10},{10... | collective-permute-start | bytes 405512 | tf_op jit(solution)/shard_map/ppermute | solution.py:134
  11.3 0.7 %copy-done.10 = s32[128]{0:T(128)S(1)} copy-done((s32[128]{0:T(128)S(1)}, s32[128]{0:T(128)}, u32[]{:S(2)}) %copy-start.10) | copy-done | bytes 536
  11.9 0.4 convolution_bitcast_fusion
  12.3 0.5 %copy-done.2 = bf16[4,128,128]{2,1,0:T(8,128)(2,1)S(1)} copy-done((bf16[4,128,128]{2,1,0:T(8,128)(2,1)S(1)}, bf16[4,128,128]{2,1,0:T(8,128)(2,1)}, u32[]{:S(2)}) %copy-start.2) | copy-done | bytes 131096
  12.8 0.2 fusion.161
  13.0 0.3 fusion.162
  13.4 0.4 fusion.165
  13.8 0.4 fusion.11
  14.2 0.2 convolution_multiply_fusion.1
  14.4 1.4 %collective-permute-done.1 = bf16[528,128]{1,0:T(8,128)(2,1)S(1)} collective-permute-done((bf16[528,128]{1,0:T(8,128)(2,1)}, bf16[528,128]{1,0:T(8,128)(2,1)S(1)}, u32[]{:S(2)}, u32[]{:S(2)}) %collective-permute-start.1) | collective-permute-done | bytes 135200 | tf_op jit(solution)/shard_map/ppermute | solution.py:134
  15.8 0.6 %slice.244 = f32[1]{0:T(128)} slice(f32[2]{0:T(128)S(1)} %compare_select_fusion), slice={[1:2]} | slice | bytes 8 | tf_op jit(solution)/shard_map/slice | solution.py:130
  16.4 0.8 %fusion.70 = f32[128,128]{1,0:T(8,128)S(1)} fusion(f32[256,128]{1,0:T(8,128)S(1)} %collective-permute-done, f32[]{:T(128)} %bitcast.11, f32[128,128]{1,0:T(8,128)S(1)} %fusion.69, bf16[528,128]{1,0:T(8,128)(2,1)S(1)} %collective-permute-done.1, pred[]{:T(512)S(6)} %and.31, bf16[2,256,128]{2,1,0:T(8,128)(2,1)S(1)} %copy-done.5, ...), kind=kOutput, calls=%fused_computation.89 | convolution fusion | flops 4276224 | bytes 327685 | tf_op jit(solution)/shard_map/dot_general | solution.py:10
  17.2 1.6 %collective-permute-start.3 = (f32[128,128]{1,0:T(8,128)S(1)}, f32[128,128]{1,0:T(8,128)S(1)}, u32[]{:S(2)}, u32[]{:S(2)}) collective-permute-start(f32[128,128]{1,0:T(8,128)S(1)} %fusion.70), channel_id=1, source_target_pairs={{0,16},{8,24},{16,0},{24,8},{1,17},{9,25},{17,1},{25,9},{2,18},{10... | collective-permute-start | bytes 196616 | tf_op jit(solution)/shard_map/ppermute | solution.py:134
  18.8 1.0 %collective-permute-start.2 = (f32[256,128]{1,0:T(8,128)S(1)}, f32[256,128]{1,0:T(8,128)S(1)}, u32[]{:S(2)}, u32[]{:S(2)}) collective-permute-start(f32[256,128]{1,0:T(8,128)S(1)} %pad_maximum_fusion.5), channel_id=1, source_target_pairs={{0,8},{8,0},{16,24},{24,16},{1,9},{9,1},{17,25},{25,17},{2,10},{10... | collective-permute-start | bytes 393224 | tf_op jit(solution)/shard_map/ppermute | solution.py:134
  19.8 0.6 %collective-permute-start.4 = (bf16[136,128]{1,0:T(8,128)(2,1)S(1)}, bf16[136,128]{1,0:T(8,128)(2,1)S(1)}, u32[]{:S(2)}, u32[]{:S(2)}) collective-permute-start(bf16[136,128]{1,0:T(8,128)(2,1)S(1)} %pad_maximum_fusion.6), channel_id=1, source_target_pairs={{0,16},{8,24},{16,0},{24,8},{1,17},{9,25},{17,1},{25,9},{2,18},{10... | collective-permute-start | bytes 104456 | tf_op jit(solution)/shard_map/ppermute | solution.py:134
  20.4 1.5 %collective-permute-done.3 = f32[128,128]{1,0:T(8,128)S(1)} collective-permute-done((f32[128,128]{1,0:T(8,128)S(1)}, f32[128,128]{1,0:T(8,128)S(1)}, u32[]{:S(2)}, u32[]{:S(2)}) %collective-permute-start.3) | collective-permute-done | bytes 65568 | tf_op jit(solution)/shard_map/ppermute | solution.py:134
  21.9 1.9 %collective-permute-done.2 = f32[256,128]{1,0:T(8,128)S(1)} collective-permute-done((f32[256,128]{1,0:T(8,128)S(1)}, f32[256,128]{1,0:T(8,128)S(1)}, u32[]{:S(2)}, u32[]{:S(2)}) %collective-permute-start.2) | collective-permute-done | bytes 131104 | tf_op jit(solution)/shard_map/ppermute | solution.py:134
  23.8 0.2 fusion.103
  24.0 0.8 %fusion.68 = f32[128,128]{1,0:T(8,128)S(1)} fusion(f32[128,128]{1,0:T(8,128)S(1)} %get-tuple-element.10, f32[256,128]{1,0:T(8,128)S(1)} %collective-permute-done.2, f32[128,128]{0,1:T(8,128)S(1)} %fusion.103, f32[]{:T(128)} %bitcast.11, bf16[528,128]{1,0:T(8,128)(2,1)S(1)} %collective-permute-done.1, pred[]{:T(512)S(6)} %and.31, ...), kind=kOutput, calls=%fused_computation.85 | convolution fusion | flops 4276224 | bytes 327685 | tf_op jit(solution)/shard_map/dot_general | solution.py:16
  24.9 0.6 %collective-permute-start.5 = (f32[128,128]{1,0:T(8,128)S(1)}, f32[128,128]{1,0:T(8,128)S(1)}, u32[]{:S(2)}, u32[]{:S(2)}) collective-permute-start(f32[128,128]{1,0:T(8,128)S(1)} %fusion.68), channel_id=1, source_target_pairs={{0,16},{8,24},{16,0},{24,8},{1,17},{9,25},{17,1},{25,9},{2,18},{10... | collective-permute-start | bytes 196616 | tf_op jit(solution)/shard_map/ppermute | solution.py:134
  25.5 0.1 fusion.117
  25.6 1.0 %fusion.10 = f32[128,128]{1,0:T(8,128)S(1)} fusion(f32[128,128]{1,0:T(8,128)S(1)} %fusion.69, f32[128,128]{1,0:T(8,128)S(1)} %fusion.117, f32[]{:T(128)} %bitcast.11, bf16[528,128]{1,0:T(8,128)(2,1)S(1)} %collective-permute-done.1, pred[]{:T(512)S(6)} %and.31, bf16[2,128,128]{2,1,0:T(8,128)(2,1)S(1)} %copy-done.1, bf16[2,128,256]{2,1,0:T(8,128)(2,1)S(1)} %copy-done.4), kind=kOutput, calls=%fused_computation.30 | convolution fusion | flops 8486912 | bytes 328708 | tf_op jit(solution)/shard_map/dot_general | solution.py:10
  26.6 0.2 convolution_subtract_fusion.1
  26.8 0.1 fusion.170
  26.9 0.3 fusion.171
  27.2 0.3 fusion.174
  27.5 0.3 fusion.7
  27.8 0.1 copy.20
  27.9 1.3 %collective-permute-done.5 = f32[128,128]{1,0:T(8,128)S(1)} collective-permute-done((f32[128,128]{1,0:T(8,128)S(1)}, f32[128,128]{1,0:T(8,128)S(1)}, u32[]{:S(2)}, u32[]{:S(2)}) %collective-permute-start.5) | collective-permute-done | bytes 65568 | tf_op jit(solution)/shard_map/ppermute | solution.py:134
  29.2 0.1 fusion.100
  29.4 0.8 %fusion.101 = f32[128,128]{1,0:T(8,128)S(1)} fusion(f32[128,128]{1,0:T(8,128)S(1)} %fusion.100, f32[]{:T(128)} %bitcast.11, bf16[528,128]{1,0:T(8,128)(2,1)S(1)} %collective-permute-done.1, pred[]{:T(512)S(6)} %and.31, bf16[2,256,128]{2,1,0:T(8,128)(2,1)S(1)} %copy-done.5), kind=kOutput, calls=%fused_computation.118 | convolution fusion | flops 4243456 | bytes 196613 | tf_op jit(solution)/shard_map/dot_general | solution.py:16
  30.2 0.3 convolution_subtract_fusion
  30.5 0.2 fusion.179
  30.7 0.2 fusion.180
  30.9 0.2 convolution_subtract_fusion.8
  31.2 0.1 fusion.14
  31.3 2.7 %collective-permute-start.6 = (f32[4,64]{1,0:T(4,128)S(1)}, f32[4,64]{1,0:T(4,128)S(1)}, u32[]{:S(2)}, u32[]{:S(2)}) collective-permute-start(f32[4,64]{1,0:T(4,128)S(1)} %slice_select_fusion.14), channel_id=1, source_target_pairs={{0,4},{1,5},{2,6},{3,7},{4,0},{5,1},{6,2},{7,3},{8,12},{9,13},{10,... | collective-permute-start | bytes 3080 | tf_op jit(solution)/shard_map/ppermute | solution.py:221
  34.0 1.9 %collective-permute-done.6 = f32[4,64]{1,0:T(4,128)S(1)} collective-permute-done((f32[4,64]{1,0:T(4,128)S(1)}, f32[4,64]{1,0:T(4,128)S(1)}, u32[]{:S(2)}, u32[]{:S(2)}) %collective-permute-start.6) | collective-permute-done | bytes 1056 | tf_op jit(solution)/shard_map/ppermute | solution.py:221
  35.9 1.6 %collective-permute-start.7 = (f32[2,64]{1,0:T(2,128)S(1)}, f32[2,64]{1,0:T(2,128)S(1)}, u32[]{:S(2)}, u32[]{:S(2)}) collective-permute-start(f32[2,64]{1,0:T(2,128)S(1)} %broadcast_select_fusion), channel_id=1, source_target_pairs={{0,2},{1,3},{2,0},{3,1},{4,6},{5,7},{6,4},{7,5},{8,10},{9,11},{10,... | collective-permute-start | bytes 1544 | tf_op jit(solution)/shard_map/ppermute | solution.py:221
  37.6 0.8 %copy.23 = f32[128,512]{1,0:T(8,128)} copy(f32[128,512]{0,1:T(8,128)S(1)} %pad_maximum_fusion.2) | data formatting | bytes 524288
  38.4 1.1 %collective-permute-done.7 = f32[2,64]{1,0:T(2,128)S(1)} collective-permute-done((f32[2,64]{1,0:T(2,128)S(1)}, f32[2,64]{1,0:T(2,128)S(1)}, u32[]{:S(2)}, u32[]{:S(2)}) %collective-permute-start.7) | collective-permute-done | bytes 544 | tf_op jit(solution)/shard_map/ppermute | solution.py:221
  39.5 0.1 collective-permute-start.8
  39.6 0.8 %copy.24 = f32[128,512]{1,0:T(8,128)} copy(f32[128,512]{0,1:T(8,128)S(1)} %pad_maximum_fusion.3) | data formatting | bytes 524288
  40.5 0.2 collective-permute-done.8
  40.7 0.5 %fusion.139 = f32[64]{0:T(128)} fusion(f32[1,64]{1,0:T(1,128)S(1)} %collective-permute-done.8, pred[]{:T(512)S(6)} %ne.23, f32[2,64]{1,0:T(2,128)S(1)} %select_add_fusion.1), kind=kLoop, calls=%fused_computation.173 | loop fusion | flops 192 | bytes 1025 | tf_op jit(solution)/shard_map/mul | solution.py:223
  (45 shorter events, 0.3 us)
Async XLA Ops:
  0.6 13.5 %copy-start = (bf16[512,256]{1,0:T(8,128)(2,1)S(1)}, bf16[512,256]{1,0:T(8,128)(2,1)}, u32[]{:S(2)}) copy-start(bf16[512,256]{1,0:T(8,128)(2,1)} %param.20) | copy-start | bytes 786436
  0.6 1.7 %copy-start.7 = (bf16[512,512]{1,0:T(8,128)(2,1)S(1)}, bf16[512,512]{1,0:T(8,128)(2,1)}, u32[]{:S(2)}) copy-start(bf16[512,512]{1,0:T(8,128)(2,1)} %param.16) | copy-start | bytes 1572868
  2.5 1.0 %copy-start.3 = (bf16[256,512]{1,0:T(8,128)(2,1)S(1)}, bf16[256,512]{1,0:T(8,128)(2,1)}, u32[]{:S(2)}) copy-start(bf16[256,512]{1,0:T(8,128)(2,1)} %param.19) | copy-start | bytes 786436
  2.5 0.7 %copy-start.9 = (s32[3,2]{0,1:T(2,128)S(1)}, s32[3,2]{0,1:T(2,128)}, u32[]{:S(2)}) copy-start(s32[3,2]{0,1:T(2,128)} %param.15) | copy-start | bytes 76
  3.5 9.5 %copy-start.6 = (bf16[512,512]{1,0:T(8,128)(2,1)S(1)}, bf16[512,512]{1,0:T(8,128)(2,1)}, u32[]{:S(2)}) copy-start(bf16[512,512]{1,0:T(8,128)(2,1)} %param.17) | copy-start | bytes 1572868
  3.8 3.2 %copy-start.5 = (bf16[2,256,128]{2,1,0:T(8,128)(2,1)S(1)}, bf16[2,256,128]{2,1,0:T(8,128)(2,1)}, u32[]{:S(2)}) copy-start(bf16[2,256,128]{2,1,0:T(8,128)(2,1)} %param.22) | copy-start | bytes 393220
  3.8 3.8 %copy-start.4 = (bf16[2,128,256]{2,1,0:T(8,128)(2,1)S(1)}, bf16[2,128,256]{2,1,0:T(8,128)(2,1)}, u32[]{:S(2)}) copy-start(bf16[2,128,256]{2,1,0:T(8,128)(2,1)} %param.23) | copy-start | bytes 393220
  3.8 10.6 %collective-permute-start = (f32[256,128]{1,0:T(8,128)S(1)}, f32[256,128]{1,0:T(8,128)S(1)}, u32[]{:S(2)}, u32[]{:S(2)}) collective-permute-start(f32[256,128]{1,0:T(8,128)S(1)} %pad_maximum_fusion.4), channel_id=1, source_target_pairs={{0,8},{8,0},{16,24},{24,16},{1,9},{9,1},{17,25},{25,17},{2,10},{10... | collective-permute-start | bytes 393224 | tf_op jit(solution)/shard_map/ppermute | solution.py:134
  6.9 1.2 %copy-start.1 = (bf16[2,128,128]{2,1,0:T(8,128)(2,1)S(1)}, bf16[2,128,128]{2,1,0:T(8,128)(2,1)}, u32[]{:S(2)}) copy-start(bf16[2,128,128]{2,1,0:T(8,128)(2,1)} %param.21) | copy-start | bytes 196612
  8.8 2.5 %copy-start.8 = (f32[128,128]{1,0:T(8,128)S(1)}, f32[128,128]{1,0:T(8,128)}, u32[]{:S(2)}) copy-start(f32[128,128]{1,0:T(8,128)} %param.14) | copy-start | bytes 196612
  10.6 5.3 %collective-permute-start.1 = (bf16[528,128]{1,0:T(8,128)(2,1)}, bf16[528,128]{1,0:T(8,128)(2,1)S(1)}, u32[]{:S(2)}, u32[]{:S(2)}) collective-permute-start(bf16[528,128]{1,0:T(8,128)(2,1)} %constant_dynamic-update-slice_fusion), channel_id=1, source_target_pairs={{0,8},{8,0},{16,24},{24,16},{1,9},{9,1},{17,25},{25,17},{2,10},{10... | collective-permute-start | bytes 405512 | tf_op jit(solution)/shard_map/ppermute | solution.py:134
  11.2 0.7 %copy-start.10 = (s32[128]{0:T(128)S(1)}, s32[128]{0:T(128)}, u32[]{:S(2)}) copy-start(s32[128]{0:T(128)} %param.13) | copy-start | bytes 1540
  11.9 0.9 %copy-start.2 = (bf16[4,128,128]{2,1,0:T(8,128)(2,1)S(1)}, bf16[4,128,128]{2,1,0:T(8,128)(2,1)}, u32[]{:S(2)}) copy-start(bf16[4,128,128]{2,1,0:T(8,128)(2,1)} %param.18) | copy-start | bytes 393220
  17.2 4.7 %collective-permute-start.3 = (f32[128,128]{1,0:T(8,128)S(1)}, f32[128,128]{1,0:T(8,128)S(1)}, u32[]{:S(2)}, u32[]{:S(2)}) collective-permute-start(f32[128,128]{1,0:T(8,128)S(1)} %fusion.70), channel_id=1, source_target_pairs={{0,16},{8,24},{16,0},{24,8},{1,17},{9,25},{17,1},{25,9},{2,18},{10... | collective-permute-start | bytes 196616 | tf_op jit(solution)/shard_map/ppermute | solution.py:134
  18.8 5.0 %collective-permute-start.2 = (f32[256,128]{1,0:T(8,128)S(1)}, f32[256,128]{1,0:T(8,128)S(1)}, u32[]{:S(2)}, u32[]{:S(2)}) collective-permute-start(f32[256,128]{1,0:T(8,128)S(1)} %pad_maximum_fusion.5), channel_id=1, source_target_pairs={{0,8},{8,0},{16,24},{24,16},{1,9},{9,1},{17,25},{25,17},{2,10},{10... | collective-permute-start | bytes 393224 | tf_op jit(solution)/shard_map/ppermute | solution.py:134
  19.8 5.6 %collective-permute-start.4 = (bf16[136,128]{1,0:T(8,128)(2,1)S(1)}, bf16[136,128]{1,0:T(8,128)(2,1)S(1)}, u32[]{:S(2)}, u32[]{:S(2)}) collective-permute-start(bf16[136,128]{1,0:T(8,128)(2,1)S(1)} %pad_maximum_fusion.6), channel_id=1, source_target_pairs={{0,16},{8,24},{16,0},{24,8},{1,17},{9,25},{17,1},{25,9},{2,18},{10... | collective-permute-start | bytes 104456 | tf_op jit(solution)/shard_map/ppermute | solution.py:134
  24.9 4.3 %collective-permute-start.5 = (f32[128,128]{1,0:T(8,128)S(1)}, f32[128,128]{1,0:T(8,128)S(1)}, u32[]{:S(2)}, u32[]{:S(2)}) collective-permute-start(f32[128,128]{1,0:T(8,128)S(1)} %fusion.68), channel_id=1, source_target_pairs={{0,16},{8,24},{16,0},{24,8},{1,17},{9,25},{17,1},{25,9},{2,18},{10... | collective-permute-start | bytes 196616 | tf_op jit(solution)/shard_map/ppermute | solution.py:134
  31.3 4.5 %collective-permute-start.6 = (f32[4,64]{1,0:T(4,128)S(1)}, f32[4,64]{1,0:T(4,128)S(1)}, u32[]{:S(2)}, u32[]{:S(2)}) collective-permute-start(f32[4,64]{1,0:T(4,128)S(1)} %slice_select_fusion.14), channel_id=1, source_target_pairs={{0,4},{1,5},{2,6},{3,7},{4,0},{5,1},{6,2},{7,3},{8,12},{9,13},{10,... | collective-permute-start | bytes 3080 | tf_op jit(solution)/shard_map/ppermute | solution.py:221
  35.9 3.6 %collective-permute-start.7 = (f32[2,64]{1,0:T(2,128)S(1)}, f32[2,64]{1,0:T(2,128)S(1)}, u32[]{:S(2)}, u32[]{:S(2)}) collective-permute-start(f32[2,64]{1,0:T(2,128)S(1)} %broadcast_select_fusion), channel_id=1, source_target_pairs={{0,2},{1,3},{2,0},{3,1},{4,6},{5,7},{6,4},{7,5},{8,10},{9,11},{10,... | collective-permute-start | bytes 1544 | tf_op jit(solution)/shard_map/ppermute | solution.py:221
  39.5 1.2 %collective-permute-start.8 = (f32[1,64]{1,0:T(1,128)S(1)}, f32[1,64]{1,0:T(1,128)S(1)}, u32[]{:S(2)}, u32[]{:S(2)}) collective-permute-start(f32[1,64]{1,0:T(1,128)S(1)} %broadcast_select_fusion.1), channel_id=1, source_target_pairs={{0,1},{1,0},{2,3},{3,2},{4,5},{5,4},{6,7},{7,6},{8,9},{9,8},{10,11... | collective-permute-start | bytes 776 | tf_op jit(solution)/shard_map/ppermute | solution.py:221

commit v10 on v8

--- a/solution.py
+++ b/solution.py
@@ -116,51 +116,36 @@
     forward_sums = blocks_of(across(as_half(y_leaf), anc_lower) * base_mask)
     adjoint_sums = blocks_of(plain_dot(as_half(z_leaf), anc_upper) * base_mask)
 
-    lower_panels, upper_panels, inverse_panels, pattern_rows = [], [], [], []
-    for height in range(1, levels + 1):
-        lower_panels.append(sep_lower[height - 1, height * block_size :, :])
-        upper_panels.append(sep_upper[height - 1, :, height * block_size :])
-        inverse_panels.append(sep_inv[height - 1])
-        row = pattern[height].astype(jnp.bfloat16)[None, :]
-        pattern_rows.append(jnp.pad(row, ((0, 7), (0, block_size - levels))))
-
-    def chain_mask(height):
-        level_row = pattern_rows[height - 1][0, :levels].astype(jnp.float32)
-        level_row = level_row * (jnp.arange(1, levels + 1) > height).astype(jnp.float32)
-        return jnp.repeat(level_row, block_size)[height * block_size :]
-
-    def exchange(values, pairs):
-        pieces = [piece for piece in values]
-        incoming = lax.ppermute(jnp.concatenate(pieces, axis=0), "leaf", pairs)
-        received, row = [], 0
-        for piece in pieces:
-            received.append(incoming[row : row + piece.shape[0]])
-            row += piece.shape[0]
-        return received
-
+    panel_arrays = [sep_lower, sep_upper, sep_inv, pattern]
     for height in range(1, levels + 1):
         stride = 1 << (height - 1)
         pairs = [(index, index ^ stride) for index in range(leaves)]
-        pieces = []
-        for upper_level in range(height, levels + 1):
-            pieces.append(lower_panels[upper_level - 1])
-            pieces.extend(blocks_of(upper_panels[upper_level - 1]))
-            pieces.append(inverse_panels[upper_level - 1])
-            pieces.append(pattern_rows[upper_level - 1])
-        received = exchange(pieces, pairs)
-        for upper_level in range(height, levels + 1):
+        takes = []
+        for upper_level in range(1, levels + 1):
             place = device % (1 << upper_level)
-            take = jnp.logical_and(place >= stride, place < 2 * stride)
-            width = levels - upper_level
-            lower_in = received[0]
-            upper_in = jnp.concatenate(received[1 : 1 + width] or [upper_panels[upper_level - 1]], axis=1)
-            inverse_in = received[1 + width]
-            pattern_in = received[2 + width]
-            received = received[3 + width :]
-            pattern_rows[upper_level - 1] = jnp.where(take, pattern_in, pattern_rows[upper_level - 1])
-            lower_panels[upper_level - 1] = jnp.where(take, lower_in, lower_panels[upper_level - 1])
-            upper_panels[upper_level - 1] = jnp.where(take, upper_in, upper_panels[upper_level - 1])
-            inverse_panels[upper_level - 1] = jnp.where(take, inverse_in, inverse_panels[upper_level - 1])
+            takes.append(jnp.logical_and(upper_level >= height, jnp.logical_and(place >= stride, place < 2 * stride)))
+        takes = jnp.stack(takes)
+        pattern_takes = jnp.concatenate([jnp.zeros((1,), jnp.bool_), takes])
+        received = [lax.ppermute(array, "leaf", pairs) for array in panel_arrays]
+        panel_arrays = [
+            jnp.where(takes[:, None, None], received[0], panel_arrays[0]),
+            jnp.where(takes[:, None, None], received[1], panel_arrays[1]),
+            jnp.where(takes[:, None, None], received[2], panel_arrays[2]),
+            jnp.where(pattern_takes[:, None], received[3], panel_arrays[3]),
+        ]
+    chain_lower, chain_upper, chain_inverse, chain_pattern = panel_arrays
+    lower_panels = [chain_lower[height - 1, height * block_size :, :] for height in range(1, levels + 1)]
+    upper_panels = [chain_upper[height - 1, :, height * block_size :] for height in range(1, levels + 1)]
+    inverse_panels = [chain_inverse[height - 1] for height in range(1, levels + 1)]
+
+    def chain_mask(height):
+        level_row = chain_pattern[height].astype(jnp.float32)
+        level_row = level_row * (jnp.arange(1, levels + 1) > height).astype(jnp.float32)
+        return jnp.repeat(level_row, block_size)[height * block_size :]
+
+    def exchange(values, pairs):
+        incoming = lax.ppermute(jnp.concatenate(values, axis=0), "leaf", pairs)
+        return [incoming[k * source_count : (k + 1) * source_count] for k in range(len(values))]
 
     forward_nodes, adjoint_nodes = [], []
     for height in range(1, levels + 1):

time: 38 us -> 45.4 us (1.19)
  starting transfers between devices: 12.7 us -> 18.5 us
  waiting for transfers between devices: 6.92 us -> 11 us
  local copies, waits for them, and re-layouts: 6.85 us -> 4.29 us
    ppermute x6 -> x12, starting transfers between devices: 8.29 us -> 14.1 us  [the longest x8 10.8 us: shards(): received = [lax.ppermute(array, 'leaf', pairs) for array in panel_arrays]]
    ppermute x6 -> x12, waiting for transfers between devices: 3.06 us -> 7.12 us  [the longest x8 5.38 us: shards(): received = [lax.ppermute(array, 'leaf', pairs) for array in panel_arrays]]
    unnamed x36 -> x30, local copies, waits for them, and re-layouts: 5.92 us -> 3.37 us
    concatenate x3 -> x4, other arithmetic: 0.64 us -> 0.18 us  [the longest x2 0.15 us: shards(): pattern_takes = jnp.concatenate([jnp.zeros((1,), jnp.bool_), takes])]
  transfers between devices with their start and end apart: 9 -> 15, of which waited for: 5 -> 8; matrix products, arithmetic and copies ran while one was open for 24% -> 22% of each run, Pallas kernels for 0% -> 0%
where the time goes in v10:
time: 45.4 us; the launch traced here: 45.1 us
  starting transfers between devices  18.5 us (41%)
  waiting for transfers between devices  11 us (24%)
  matrix products  8.6 us (19%)
  local copies, waits for them, and re-layouts  4.29 us (9%)
  other arithmetic  1.64 us (4%)
  between operations  1.06 us (2%)
    ppermute x8, starting transfers between devices, shards(): received = [lax.ppermute(array, 'leaf', pairs) for array in panel_arrays]  10.8 us
    ppermute x8, waiting for transfers between devices, shards(): received = [lax.ppermute(array, 'leaf', pairs) for array in panel_arrays]  5.38 us
    ppermute x3, starting transfers between devices, shards(): partial_gradient = kept + lax.ppermute(outgoing, 'src', pairs)  4.39 us
    dot_general x13, matrix products, plain_dot(): return jnp.dot(former, latter, preferred_element_type=jnp.float32)  4.37 us
    dot_general x12, matrix products, across(): lax.dot_general(former, latter, (((1,), (1,)), ((), ())), preferred_eleme...  3.85 us
    ppermute x3, waiting for transfers between devices, shards(): partial_gradient = kept + lax.ppermute(outgoing, 'src', pairs)  3.84 us
    unnamed x30, local copies, waits for them, and re-layouts  3.37 us
    ppermute x4, starting transfers between devices, exchange(): incoming = lax.ppermute(jnp.concatenate(values, axis=0), 'leaf', pairs)  3.29 us
  transfers between devices with their start and end apart: 15, of which 8 were waited for; matrix products, arithmetic and copies ran while one was open for 22% of the time, Pallas kernels for 0%

profile of v10, /device:TPU:0, one launch (start us, length us, event | category | flops | bytes accessed | tf_op | source)
XLA Modules:
  0.0 45.1 jit_solution(2848139574573443075)
XLA Ops:
  0.6 3.0 %collective-permute-start.3 = (s32[3,2]{0,1:T(2,128)}, s32[3,2]{0,1:T(2,128)S(1)}, u32[]{:S(2)}, u32[]{:S(2)}) collective-permute-start(s32[3,2]{0,1:T(2,128)} %param.15), channel_id=1, source_target_pairs={{0,8},{8,0},{16,24},{24,16},{1,9},{9,1},{17,25},{25,17},{2,10},{10... | collective-permute-start | bytes 80 | tf_op jit(solution)/shard_map/ppermute | solution.py:129
  3.7 0.1 collective-permute-start.6
  3.7 1.9 %collective-permute-start.8 = (bf16[2,128,256]{2,1,0:T(8,128)(2,1)}, bf16[2,128,256]{2,1,0:T(8,128)(2,1)S(1)}, u32[]{:S(2)}, u32[]{:S(2)}) collective-permute-start(bf16[2,128,256]{2,1,0:T(8,128)(2,1)} %param.23), channel_id=1, source_target_pairs={{0,8},{8,0},{16,24},{24,16},{1,9},{9,1},{17,25},{25,17},{2,10},{10... | collective-permute-start | bytes 393224 | tf_op jit(solution)/shard_map/ppermute | solution.py:129
  5.7 0.1 collective-permute-start.1
  5.8 0.1 pad_add_fusion.3
  6.1 0.3 copy-done.13
  6.5 0.1 copy-done.7
  6.6 0.4 convolution_bitcast_fusion
  7.0 0.5 %copy-done.2 = bf16[4,128,128]{2,1,0:T(8,128)(2,1)S(1)} copy-done((bf16[4,128,128]{2,1,0:T(8,128)(2,1)S(1)}, bf16[4,128,128]{2,1,0:T(8,128)(2,1)}, u32[]{:S(2)}) %copy-start.2) | copy-done | bytes 131096
  7.5 0.2 fusion.182
  7.8 0.3 fusion.183
  8.1 0.4 fusion.186
  8.5 0.4 fusion.10
  8.8 0.1 fusion.171
  9.0 0.2 fusion.172
  9.2 0.2 convolution_subtract_fusion.5
  9.4 0.7 %copy-done.11 = s32[3,2]{0,1:T(2,128)S(1)} copy-done((s32[3,2]{0,1:T(2,128)S(1)}, s32[3,2]{0,1:T(2,128)}, u32[]{:S(2)}) %copy-start.11) | copy-done | bytes 48
  10.1 0.1 slice_reduce_fusion
  10.3 0.2 convolution_multiply_fusion
  10.5 2.0 %collective-permute-start.10 = (f32[256,128]{1,0:T(8,128)S(1)}, f32[256,128]{1,0:T(8,128)S(1)}, u32[]{:S(2)}, u32[]{:S(2)}) collective-permute-start(f32[256,128]{1,0:T(8,128)S(1)} %pad_maximum_fusion.5), channel_id=1, source_target_pairs={{0,8},{8,0},{16,24},{24,16},{1,9},{9,1},{17,25},{25,17},{2,10},{10... | collective-permute-start | bytes 393224 | tf_op jit(solution)/shard_map/ppermute | solution.py:147
  12.5 1.5 %collective-permute-start.4 = (s32[3,2]{0,1:T(2,128)S(1)}, s32[3,2]{0,1:T(2,128)S(1)}, u32[]{:S(2)}, u32[]{:S(2)}) collective-permute-start(s32[3,2]{0,1:T(2,128)S(1)} %get-tuple-element.10), channel_id=1, source_target_pairs={{0,16},{8,24},{16,0},{24,8},{1,17},{9,25},{17,1},{25,9},{2,18},{10... | collective-permute-start | bytes 80 | tf_op jit(solution)/shard_map/ppermute | solution.py:129
  14.1 0.2 convolution_multiply_fusion.1
  14.4 1.7 %collective-permute-done.4 = s32[3,2]{0,1:T(2,128)S(1)} collective-permute-done((s32[3,2]{0,1:T(2,128)S(1)}, s32[3,2]{0,1:T(2,128)S(1)}, u32[]{:S(2)}, u32[]{:S(2)}) %collective-permute-start.4) | collective-permute-done | bytes 56 | tf_op jit(solution)/shard_map/ppermute | solution.py:129
  16.1 0.1 collective-permute-start
  16.2 0.2 convert_reduce_fusion
  16.4 0.6 %slice.195 = f32[1]{0:T(128)} slice(f32[2]{0:T(128)S(1)} %compare_select_fusion), slice={[1:2]} | slice | bytes 8 | tf_op jit(solution)/shard_map/slice | solution.py:144
  17.0 0.1 broadcast_select_fusion.2
  17.1 2.0 %collective-permute-start.7 = (bf16[2,128,128]{2,1,0:T(8,128)(2,1)S(1)}, bf16[2,128,128]{2,1,0:T(8,128)(2,1)S(1)}, u32[]{:S(2)}, u32[]{:S(2)}) collective-permute-start(bf16[2,128,128]{2,1,0:T(8,128)(2,1)S(1)} %broadcast_select_fusion.2), channel_id=1, source_target_pairs={{0,16},{8,24},{16,0},{24,8},{1,17},{9,25},{17,1},{25,9},{2,18},{10... | collective-permute-start | bytes 196616 | tf_op jit(solution)/shard_map/ppermute | solution.py:129
  19.1 0.1 broadcast_select_fusion
  19.2 0.1 collective-permute-start.9
  19.3 0.1 broadcast_select_fusion.1
  19.4 2.1 %collective-permute-start.2 = (bf16[2,256,128]{2,1,0:T(8,128)(2,1)S(1)}, bf16[2,256,128]{2,1,0:T(8,128)(2,1)S(1)}, u32[]{:S(2)}, u32[]{:S(2)}) collective-permute-start(bf16[2,256,128]{2,1,0:T(8,128)(2,1)S(1)} %broadcast_select_fusion.1), channel_id=1, source_target_pairs={{0,16},{8,24},{16,0},{24,8},{1,17},{9,25},{17,1},{25,9},{2,18},{10... | collective-permute-start | bytes 393224 | tf_op jit(solution)/shard_map/ppermute | solution.py:129
  21.5 0.7 %collective-permute-done.7 = bf16[2,128,128]{2,1,0:T(8,128)(2,1)S(1)} collective-permute-done((bf16[2,128,128]{2,1,0:T(8,128)(2,1)S(1)}, bf16[2,128,128]{2,1,0:T(8,128)(2,1)S(1)}, u32[]{:S(2)}, u32[]{:S(2)}) %collective-permute-start.7) | collective-permute-done | bytes 65568 | tf_op jit(solution)/shard_map/ppermute | solution.py:129
  22.2 0.2 fusion.105
  22.5 0.1 copy.19
  22.6 2.0 %collective-permute-done.9 = bf16[2,128,256]{2,1,0:T(8,128)(2,1)S(1)} collective-permute-done((bf16[2,128,256]{2,1,0:T(8,128)(2,1)S(1)}, bf16[2,128,256]{2,1,0:T(8,128)(2,1)S(1)}, u32[]{:S(2)}, u32[]{:S(2)}) %collective-permute-start.9) | collective-permute-done | bytes 131104 | tf_op jit(solution)/shard_map/ppermute | solution.py:129
  24.6 0.8 %fusion.63 = f32[128,128]{1,0:T(8,128)S(1)} fusion(f32[256,128]{1,0:T(8,128)S(1)} %collective-permute-done.10, f32[128,128]{0,1:T(8,128)S(1)} %fusion.105, f32[]{:T(128)} %bitcast.5, bf16[2,128,256]{2,1,0:T(8,128)(2,1)S(1)} %broadcast_select_fusion, bf16[2,128,256]{2,1,0:T(8,128)(2,1)S(1)} %collective-permute-done.9, pred[1]{0:T(512)(128)(4,1)S(1)} %bitcast.83, ...), kind=kOutput, calls=%fused_computation.80 | convolution fusion | flops 4276224 | bytes 328196 | tf_op jit(solution)/shard_map/dot_general | solution.py:16
  25.4 0.6 %collective-permute-start.11 = (f32[128,128]{1,0:T(8,128)S(1)}, f32[128,128]{1,0:T(8,128)S(1)}, u32[]{:S(2)}, u32[]{:S(2)}) collective-permute-start(f32[128,128]{1,0:T(8,128)S(1)} %fusion.63), channel_id=1, source_target_pairs={{0,16},{8,24},{16,0},{24,8},{1,17},{9,25},{17,1},{25,9},{2,18},{10... | collective-permute-start | bytes 196616 | tf_op jit(solution)/shard_map/ppermute | solution.py:147
  26.0 0.9 %collective-permute-done.2 = bf16[2,256,128]{2,1,0:T(8,128)(2,1)S(1)} collective-permute-done((bf16[2,256,128]{2,1,0:T(8,128)(2,1)S(1)}, bf16[2,256,128]{2,1,0:T(8,128)(2,1)S(1)}, u32[]{:S(2)}, u32[]{:S(2)}) %collective-permute-start.2) | collective-permute-done | bytes 131104 | tf_op jit(solution)/shard_map/ppermute | solution.py:129
  26.9 0.8 %fusion.72 = f32[128,128]{1,0:T(8,128)S(1)} fusion(f32[256,128]{1,0:T(8,128)S(1)} %collective-permute-done, f32[]{:T(128)} %bitcast.5, bf16[2,256,128]{2,1,0:T(8,128)(2,1)S(1)} %broadcast_select_fusion.1, bf16[2,256,128]{2,1,0:T(8,128)(2,1)S(1)} %collective-permute-done.2, pred[1]{0:T(512)(128)(4,1)S(1)} %bitcast.84, ...), kind=kOutput, calls=%fused_computation.93 | convolution fusion | flops 4308992 | bytes 393732 | tf_op jit(solution)/shard_map/dot_general | solution.py:10
  27.7 0.6 %collective-permute-start.5 = (f32[128,128]{1,0:T(8,128)S(1)}, f32[128,128]{1,0:T(8,128)S(1)}, u32[]{:S(2)}, u32[]{:S(2)}) collective-permute-start(f32[128,128]{1,0:T(8,128)S(1)} %fusion.72), channel_id=1, source_target_pairs={{0,16},{8,24},{16,0},{24,8},{1,17},{9,25},{17,1},{25,9},{2,18},{10... | collective-permute-start | bytes 196616 | tf_op jit(solution)/shard_map/ppermute | solution.py:147
  28.3 1.4 %collective-permute-done.11 = f32[128,128]{1,0:T(8,128)S(1)} collective-permute-done((f32[128,128]{1,0:T(8,128)S(1)}, f32[128,128]{1,0:T(8,128)S(1)}, u32[]{:S(2)}, u32[]{:S(2)}) %collective-permute-start.11) | collective-permute-done | bytes 65568 | tf_op jit(solution)/shard_map/ppermute | solution.py:147
  29.7 0.1 fusion.101
  29.9 0.8 %fusion.102 = f32[128,128]{1,0:T(8,128)S(1)} fusion(f32[128,128]{1,0:T(8,128)S(1)} %fusion.101, f32[]{:T(128)} %bitcast.5, bf16[2,256,128]{2,1,0:T(8,128)(2,1)S(1)} %broadcast_select_fusion.1, bf16[2,256,128]{2,1,0:T(8,128)(2,1)S(1)} %collective-permute-done.2, pred[1]{0:T(512)(128)(4,1)S(1)} %bitcast.85), kind=kOutput, calls=%fused_computation.122 | convolution fusion | flops 4243456 | bytes 197124 | tf_op jit(solution)/shard_map/dot_general | solution.py:16
  30.7 0.3 convolution_subtract_fusion
  31.0 0.2 fusion.191
  31.2 0.2 fusion.192
  31.4 0.2 convolution_subtract_fusion.8
  31.7 0.3 collective-permute-done.5
  32.0 0.1 fusion.100
  32.1 1.0 %fusion.13 = f32[128,128]{1,0:T(8,128)S(1)} fusion(f32[128,128]{1,0:T(8,128)S(1)} %fusion.100, f32[]{:T(128)} %bitcast.5, bf16[2,128,128]{2,1,0:T(8,128)(2,1)S(1)} %broadcast_select_fusion.3, f32[256,128]{1,0:T(8,128)S(1)} %collective-permute-done, bf16[2,128,256]{2,1,0:T(8,128)(2,1)S(1)} %broadcast_select_fusion, ...), kind=kOutput, calls=%fused_computation.33 | convolution fusion | flops 8503296 | bytes 360964 | tf_op jit(solution)/shard_map/dot_general | solution.py:10
  33.1 0.2 convolution_subtract_fusion.1
  33.4 0.1 fusion.173
  33.5 0.3 fusion.174
  33.8 0.3 fusion.177
  34.1 0.3 fusion.7
  34.4 0.1 fusion.14
  34.6 2.7 %collective-permute-start.12 = (f32[4,64]{1,0:T(4,128)S(1)}, f32[4,64]{1,0:T(4,128)S(1)}, u32[]{:S(2)}, u32[]{:S(2)}) collective-permute-start(f32[4,64]{1,0:T(4,128)S(1)} %slice_select_fusion.2), channel_id=1, source_target_pairs={{0,4},{1,5},{2,6},{3,7},{4,0},{5,1},{6,2},{7,3},{8,12},{9,13},{10,... | collective-permute-start | bytes 3080 | tf_op jit(solution)/shard_map/ppermute | solution.py:204
  37.2 1.9 %collective-permute-done.12 = f32[4,64]{1,0:T(4,128)S(1)} collective-permute-done((f32[4,64]{1,0:T(4,128)S(1)}, f32[4,64]{1,0:T(4,128)S(1)}, u32[]{:S(2)}, u32[]{:S(2)}) %collective-permute-start.12) | collective-permute-done | bytes 1056 | tf_op jit(solution)/shard_map/ppermute | solution.py:204
  39.1 1.7 %collective-permute-start.13 = (f32[2,64]{1,0:T(2,128)S(1)}, f32[2,64]{1,0:T(2,128)S(1)}, u32[]{:S(2)}, u32[]{:S(2)}) collective-permute-start(f32[2,64]{1,0:T(2,128)S(1)} %broadcast_select_fusion.4), channel_id=1, source_target_pairs={{0,2},{1,3},{2,0},{3,1},{4,6},{5,7},{6,4},{7,5},{8,10},{9,11},{10,... | collective-permute-start | bytes 1544 | tf_op jit(solution)/shard_map/ppermute | solution.py:204
  40.8 2.0 %collective-permute-done.13 = f32[2,64]{1,0:T(2,128)S(1)} collective-permute-done((f32[2,64]{1,0:T(2,128)S(1)}, f32[2,64]{1,0:T(2,128)S(1)}, u32[]{:S(2)}, u32[]{:S(2)}) %collective-permute-start.13) | collective-permute-done | bytes 544 | tf_op jit(solution)/shard_map/ppermute | solution.py:204
  42.9 0.8 %copy.23 = f32[128,512]{1,0:T(8,128)} copy(f32[128,512]{0,1:T(8,128)S(1)} %pad_maximum_fusion.3) | data formatting | bytes 524288
  43.7 0.8 %copy.22 = f32[128,512]{1,0:T(8,128)} copy(f32[128,512]{0,1:T(8,128)S(1)} %pad_maximum_fusion.1) | data formatting | bytes 524288
  44.6 0.5 %fusion.149 = f32[64]{0:T(128)} fusion(f32[1,64]{1,0:T(1,128)S(1)} %collective-permute-done.14, pred[]{:T(512)S(6)} %ne.23, f32[2,64]{1,0:T(2,128)S(1)} %select_add_fusion.1), kind=kLoop, calls=%fused_computation.177 | loop fusion | flops 192 | bytes 1025 | tf_op jit(solution)/shard_map/mul | solution.py:206
  (59 shorter events, 0.7 us)
Async XLA Ops:
  0.6 13.4 %copy-start = (bf16[256,512]{1,0:T(8,128)(2,1)S(1)}, bf16[256,512]{1,0:T(8,128)(2,1)}, u32[]{:S(2)}) copy-start(bf16[256,512]{1,0:T(8,128)(2,1)} %param.19) | copy-start | bytes 786436
  0.6 8.7 %collective-permute-start.3 = (s32[3,2]{0,1:T(2,128)}, s32[3,2]{0,1:T(2,128)S(1)}, u32[]{:S(2)}, u32[]{:S(2)}) collective-permute-start(s32[3,2]{0,1:T(2,128)} %param.15), channel_id=1, source_target_pairs={{0,8},{8,0},{16,24},{24,16},{1,9},{9,1},{17,25},{25,17},{2,10},{10... | collective-permute-start | bytes 80 | tf_op jit(solution)/shard_map/ppermute | solution.py:129
  3.7 13.3 %collective-permute-start.6 = (bf16[2,128,128]{2,1,0:T(8,128)(2,1)}, bf16[2,128,128]{2,1,0:T(8,128)(2,1)S(1)}, u32[]{:S(2)}, u32[]{:S(2)}) collective-permute-start(bf16[2,128,128]{2,1,0:T(8,128)(2,1)} %param.21), channel_id=1, source_target_pairs={{0,8},{8,0},{16,24},{24,16},{1,9},{9,1},{17,25},{25,17},{2,10},{10... | collective-permute-start | bytes 196616 | tf_op jit(solution)/shard_map/ppermute | solution.py:129
  3.7 15.4 %collective-permute-start.8 = (bf16[2,128,256]{2,1,0:T(8,128)(2,1)}, bf16[2,128,256]{2,1,0:T(8,128)(2,1)S(1)}, u32[]{:S(2)}, u32[]{:S(2)}) collective-permute-start(bf16[2,128,256]{2,1,0:T(8,128)(2,1)} %param.23), channel_id=1, source_target_pairs={{0,8},{8,0},{16,24},{24,16},{1,9},{9,1},{17,25},{25,17},{2,10},{10... | collective-permute-start | bytes 393224 | tf_op jit(solution)/shard_map/ppermute | solution.py:129
  5.7 13.6 %collective-permute-start.1 = (bf16[2,256,128]{2,1,0:T(8,128)(2,1)}, bf16[2,256,128]{2,1,0:T(8,128)(2,1)S(1)}, u32[]{:S(2)}, u32[]{:S(2)}) collective-permute-start(bf16[2,256,128]{2,1,0:T(8,128)(2,1)} %param.22), channel_id=1, source_target_pairs={{0,8},{8,0},{16,24},{24,16},{1,9},{9,1},{17,25},{25,17},{2,10},{10... | collective-permute-start | bytes 393224 | tf_op jit(solution)/shard_map/ppermute | solution.py:129
  5.8 0.7 %copy-start.13 = (s32[128]{0:T(128)S(1)}, s32[128]{0:T(128)}, u32[]{:S(2)}) copy-start(s32[128]{0:T(128)} %param.12) | copy-start | bytes 1540
  5.8 0.9 %copy-start.7 = (f32[128,128]{1,0:T(8,128)S(1)}, f32[128,128]{1,0:T(8,128)}, u32[]{:S(2)}) copy-start(f32[128,128]{1,0:T(8,128)} %param.14) | copy-start | bytes 196612
  5.8 0.9 %copy-start.12 = (s32[128]{0:T(128)S(1)}, s32[128]{0:T(128)}, u32[]{:S(2)}) copy-start(s32[128]{0:T(128)} %param.13) | copy-start | bytes 1540
  5.8 2.0 %copy-start.5 = (bf16[512,512]{1,0:T(8,128)(2,1)S(1)}, bf16[512,512]{1,0:T(8,128)(2,1)}, u32[]{:S(2)}) copy-start(bf16[512,512]{1,0:T(8,128)(2,1)} %param.17) | copy-start | bytes 1572868
  6.6 0.9 %copy-start.2 = (bf16[4,128,128]{2,1,0:T(8,128)(2,1)S(1)}, bf16[4,128,128]{2,1,0:T(8,128)(2,1)}, u32[]{:S(2)}) copy-start(bf16[4,128,128]{2,1,0:T(8,128)(2,1)} %param.18) | copy-start | bytes 393220
  7.7 1.1 %copy-start.6 = (bf16[512,512]{1,0:T(8,128)(2,1)S(1)}, bf16[512,512]{1,0:T(8,128)(2,1)}, u32[]{:S(2)}) copy-start(bf16[512,512]{1,0:T(8,128)(2,1)} %param.16) | copy-start | bytes 1572868
  9.1 1.1 %copy-start.1 = (bf16[512,256]{1,0:T(8,128)(2,1)S(1)}, bf16[512,256]{1,0:T(8,128)(2,1)}, u32[]{:S(2)}) copy-start(bf16[512,256]{1,0:T(8,128)(2,1)} %param.20) | copy-start | bytes 786436
  9.3 4.7 %copy-start.9 = (f32[128,128]{0,1:T(8,128)}, f32[128,128]{0,1:T(8,128)S(1)}, u32[]{:S(2)}) copy-start(f32[128,128]{0,1:T(8,128)S(1)} %convolution_subtract_fusion.5) | copy-start | bytes 196612
  9.4 0.7 %copy-start.11 = (s32[3,2]{0,1:T(2,128)S(1)}, s32[3,2]{0,1:T(2,128)}, u32[]{:S(2)}) copy-start(s32[3,2]{0,1:T(2,128)} %param.15) | copy-start | bytes 76
  10.5 11.7 %collective-permute-start.10 = (f32[256,128]{1,0:T(8,128)S(1)}, f32[256,128]{1,0:T(8,128)S(1)}, u32[]{:S(2)}, u32[]{:S(2)}) collective-permute-start(f32[256,128]{1,0:T(8,128)S(1)} %pad_maximum_fusion.5), channel_id=1, source_target_pairs={{0,8},{8,0},{16,24},{24,16},{1,9},{9,1},{17,25},{25,17},{2,10},{10... | collective-permute-start | bytes 393224 | tf_op jit(solution)/shard_map/ppermute | solution.py:147
  12.5 3.6 %collective-permute-start.4 = (s32[3,2]{0,1:T(2,128)S(1)}, s32[3,2]{0,1:T(2,128)S(1)}, u32[]{:S(2)}, u32[]{:S(2)}) collective-permute-start(s32[3,2]{0,1:T(2,128)S(1)} %get-tuple-element.10), channel_id=1, source_target_pairs={{0,16},{8,24},{16,0},{24,8},{1,17},{9,25},{17,1},{25,9},{2,18},{10... | collective-permute-start | bytes 80 | tf_op jit(solution)/shard_map/ppermute | solution.py:129
  14.3 2.7 %copy-start.8 = (bf16[2,128,128]{2,1,0:T(8,128)(2,1)S(1)}, bf16[2,128,128]{2,1,0:T(8,128)(2,1)}, u32[]{:S(2)}) copy-start(bf16[2,128,128]{2,1,0:T(8,128)(2,1)} %param.21) | copy-start | bytes 196612
  14.4 4.8 %copy-start.3 = (bf16[2,128,256]{2,1,0:T(8,128)(2,1)S(1)}, bf16[2,128,256]{2,1,0:T(8,128)(2,1)}, u32[]{:S(2)}) copy-start(bf16[2,128,256]{2,1,0:T(8,128)(2,1)} %param.23) | copy-start | bytes 393220
  16.1 9.9 %collective-permute-start = (f32[256,128]{1,0:T(8,128)S(1)}, f32[256,128]{1,0:T(8,128)S(1)}, u32[]{:S(2)}, u32[]{:S(2)}) collective-permute-start(f32[256,128]{1,0:T(8,128)S(1)} %pad_maximum_fusion.4), channel_id=1, source_target_pairs={{0,8},{8,0},{16,24},{24,16},{1,9},{9,1},{17,25},{25,17},{2,10},{10... | collective-permute-start | bytes 393224 | tf_op jit(solution)/shard_map/ppermute | solution.py:147
  17.1 2.3 %copy-start.4 = (bf16[2,256,128]{2,1,0:T(8,128)(2,1)S(1)}, bf16[2,256,128]{2,1,0:T(8,128)(2,1)}, u32[]{:S(2)}) copy-start(bf16[2,256,128]{2,1,0:T(8,128)(2,1)} %param.22) | copy-start | bytes 393220
  17.1 5.1 %collective-permute-start.7 = (bf16[2,128,128]{2,1,0:T(8,128)(2,1)S(1)}, bf16[2,128,128]{2,1,0:T(8,128)(2,1)S(1)}, u32[]{:S(2)}, u32[]{:S(2)}) collective-permute-start(bf16[2,128,128]{2,1,0:T(8,128)(2,1)S(1)} %broadcast_select_fusion.2), channel_id=1, source_target_pairs={{0,16},{8,24},{16,0},{24,8},{1,17},{9,25},{17,1},{25,9},{2,18},{10... | collective-permute-start | bytes 196616 | tf_op jit(solution)/shard_map/ppermute | solution.py:129
  19.2 5.4 %collective-permute-start.9 = (bf16[2,128,256]{2,1,0:T(8,128)(2,1)S(1)}, bf16[2,128,256]{2,1,0:T(8,128)(2,1)S(1)}, u32[]{:S(2)}, u32[]{:S(2)}) collective-permute-start(bf16[2,128,256]{2,1,0:T(8,128)(2,1)S(1)} %broadcast_select_fusion), channel_id=1, source_target_pairs={{0,16},{8,24},{16,0},{24,8},{1,17},{9,25},{17,1},{25,9},{2,18},{10... | collective-permute-start | bytes 393224 | tf_op jit(solution)/shard_map/ppermute | solution.py:129
  19.4 7.5 %collective-permute-start.2 = (bf16[2,256,128]{2,1,0:T(8,128)(2,1)S(1)}, bf16[2,256,128]{2,1,0:T(8,128)(2,1)S(1)}, u32[]{:S(2)}, u32[]{:S(2)}) collective-permute-start(bf16[2,256,128]{2,1,0:T(8,128)(2,1)S(1)} %broadcast_select_fusion.1), channel_id=1, source_target_pairs={{0,16},{8,24},{16,0},{24,8},{1,17},{9,25},{17,1},{25,9},{2,18},{10... | collective-permute-start | bytes 393224 | tf_op jit(solution)/shard_map/ppermute | solution.py:129
  25.4 4.3 %collective-permute-start.11 = (f32[128,128]{1,0:T(8,128)S(1)}, f32[128,128]{1,0:T(8,128)S(1)}, u32[]{:S(2)}, u32[]{:S(2)}) collective-permute-start(f32[128,128]{1,0:T(8,128)S(1)} %fusion.63), channel_id=1, source_target_pairs={{0,16},{8,24},{16,0},{24,8},{1,17},{9,25},{17,1},{25,9},{2,18},{10... | collective-permute-start | bytes 196616 | tf_op jit(solution)/shard_map/ppermute | solution.py:147
  27.7 4.3 %collective-permute-start.5 = (f32[128,128]{1,0:T(8,128)S(1)}, f32[128,128]{1,0:T(8,128)S(1)}, u32[]{:S(2)}, u32[]{:S(2)}) collective-permute-start(f32[128,128]{1,0:T(8,128)S(1)} %fusion.72), channel_id=1, source_target_pairs={{0,16},{8,24},{16,0},{24,8},{1,17},{9,25},{17,1},{25,9},{2,18},{10... | collective-permute-start | bytes 196616 | tf_op jit(solution)/shard_map/ppermute | solution.py:147
  32.1 1.0 %copy-start.10 = (f32[128,128]{0,1:T(8,128)S(1)}, f32[128,128]{0,1:T(8,128)}, u32[]{:S(2)}) copy-start(f32[128,128]{0,1:T(8,128)} %copy-done.9) | copy-start | bytes 196612
  34.6 4.5 %collective-permute-start.12 = (f32[4,64]{1,0:T(4,128)S(1)}, f32[4,64]{1,0:T(4,128)S(1)}, u32[]{:S(2)}, u32[]{:S(2)}) collective-permute-start(f32[4,64]{1,0:T(4,128)S(1)} %slice_select_fusion.2), channel_id=1, source_target_pairs={{0,4},{1,5},{2,6},{3,7},{4,0},{5,1},{6,2},{7,3},{8,12},{9,13},{10,... | collective-permute-start | bytes 3080 | tf_op jit(solution)/shard_map/ppermute | solution.py:204
  39.1 3.6 %collective-permute-start.13 = (f32[2,64]{1,0:T(2,128)S(1)}, f32[2,64]{1,0:T(2,128)S(1)}, u32[]{:S(2)}, u32[]{:S(2)}) collective-permute-start(f32[2,64]{1,0:T(2,128)S(1)} %broadcast_select_fusion.4), channel_id=1, source_target_pairs={{0,2},{1,3},{2,0},{3,1},{4,6},{5,7},{6,4},{7,5},{8,10},{9,11},{10,... | collective-permute-start | bytes 1544 | tf_op jit(solution)/shard_map/ppermute | solution.py:204
  42.8 1.8 %collective-permute-start.14 = (f32[1,64]{1,0:T(1,128)S(1)}, f32[1,64]{1,0:T(1,128)S(1)}, u32[]{:S(2)}, u32[]{:S(2)}) collective-permute-start(f32[1,64]{1,0:T(1,128)S(1)} %broadcast_select_fusion.5), channel_id=1, source_target_pairs={{0,1},{1,0},{2,3},{3,2},{4,5},{5,4},{6,7},{7,6},{8,9},{9,8},{10,11... | collective-permute-start | bytes 776 | tf_op jit(solution)/shard_map/ppermute | solution.py:204

commit v11 on v8

--- a/solution.py
+++ b/solution.py
@@ -138,16 +138,27 @@
             row += piece.shape[0]
         return received
 
+    forward_nodes, adjoint_nodes = [], []
     for height in range(1, levels + 1):
         stride = 1 << (height - 1)
         pairs = [(index, index ^ stride) for index in range(leaves)]
-        pieces = []
+        panel_pieces = []
         for upper_level in range(height, levels + 1):
-            pieces.append(lower_panels[upper_level - 1])
-            pieces.extend(blocks_of(upper_panels[upper_level - 1]))
-            pieces.append(inverse_panels[upper_level - 1])
-            pieces.append(pattern_rows[upper_level - 1])
-        received = exchange(pieces, pairs)
+            panel_pieces.append(lower_panels[upper_level - 1])
+            panel_pieces.extend(blocks_of(upper_panels[upper_level - 1]))
+            panel_pieces.append(inverse_panels[upper_level - 1])
+            panel_pieces.append(pattern_rows[upper_level - 1])
+        wide_pieces = [piece.astype(jnp.float32) for piece in panel_pieces]
+        count = len(forward_sums)
+        if height == 1:
+            forward_in = exchange(forward_sums + wide_pieces, pairs)
+            adjoint_in = exchange(adjoint_sums, pairs)
+            received = forward_in[count:]
+        else:
+            forward_in = exchange(forward_sums, pairs)
+            adjoint_in = exchange(adjoint_sums + wide_pieces, pairs)
+            received = adjoint_in[count:]
+        received = [piece.astype(jnp.bfloat16) for piece in received]
         for upper_level in range(height, levels + 1):
             place = device % (1 << upper_level)
             take = jnp.logical_and(place >= stride, place < 2 * stride)
@@ -161,25 +172,19 @@
             lower_panels[upper_level - 1] = jnp.where(take, lower_in, lower_panels[upper_level - 1])
             upper_panels[upper_level - 1] = jnp.where(take, upper_in, upper_panels[upper_level - 1])
             inverse_panels[upper_level - 1] = jnp.where(take, inverse_in, inverse_panels[upper_level - 1])
-
-    forward_nodes, adjoint_nodes = [], []
-    for height in range(1, levels + 1):
-        stride = 1 << (height - 1)
-        pairs = [(index, index ^ stride) for index in range(leaves)]
-        forward_sums = [mine + theirs for mine, theirs in zip(forward_sums, exchange(forward_sums, pairs))]
+        forward_sums = [mine + theirs for mine, theirs in zip(forward_sums, forward_in[:count])]
+        adjoint_sums = [mine + theirs for mine, theirs in zip(adjoint_sums, adjoint_in[:count])]
         forward_node = -forward_sums[0]
         forward_nodes.append(forward_node)
         forward_sums = forward_sums[1:]
+        adjoint_node = plain_dot(as_half(-adjoint_sums[0]), inverse_panels[height - 1])
+        adjoint_nodes.append(adjoint_node)
+        adjoint_sums = adjoint_sums[1:]
         if forward_sums:
             forward_coupling = blocks_of(
                 across(as_half(forward_node), lower_panels[height - 1]) * chain_mask(height)
             )
             forward_sums = [total + extra for total, extra in zip(forward_sums, forward_coupling)]
-        adjoint_sums = [mine + theirs for mine, theirs in zip(adjoint_sums, exchange(adjoint_sums, pairs))]
-        adjoint_node = plain_dot(as_half(-adjoint_sums[0]), inverse_panels[height - 1])
-        adjoint_nodes.append(adjoint_node)
-        adjoint_sums = adjoint_sums[1:]
-        if adjoint_sums:
             adjoint_coupling = blocks_of(
                 plain_dot(as_half(adjoint_node), upper_panels[height - 1]) * chain_mask(height)
             )

time: 38 us -> 51.1 us (1.34)
  waiting for transfers between devices: 6.92 us -> 14.7 us
  matrix products: 8.68 us -> 13.6 us
  other arithmetic: 1.45 us -> 4.53 us
  starting transfers between devices: 12.7 us -> 10.5 us
  local copies, waits for them, and re-layouts: 6.85 us -> 6.12 us
    ppermute x6 -> x4, waiting for transfers between devices: 3.06 us -> 11.4 us  [exchange(): incoming = lax.ppermute(jnp.concatenate(pieces, axis=0), 'leaf', pairs)]
    unnamed x0 -> x5, other arithmetic: none -> 3.07 us
    ppermute x6 -> x4, starting transfers between devices: 8.29 us -> 5.63 us  [exchange(): incoming = lax.ppermute(jnp.concatenate(pieces, axis=0), 'leaf', pairs)]
    dot_general x12, matrix products: 3.87 us -> 6.35 us  [across(): lax.dot_general(former, latter, (((1,), (1,)), ((), ())), preferred_eleme...]
    dot_general x13, matrix products: 4.43 us -> 6.9 us  [plain_dot(): return jnp.dot(former, latter, preferred_element_type=jnp.float32)]
    unnamed x36 -> x27, local copies, waits for them, and re-layouts: 5.92 us -> 5.21 us
  transfers between devices with their start and end apart: 9 -> 7, of which waited for: 5 -> 5; matrix products, arithmetic and copies ran while one was open for 24% -> 19% of each run, Pallas kernels for 0% -> 0%
where the time goes in v11:
time: 51.1 us; the launch traced here: 50.5 us
  waiting for transfers between devices  14.7 us (29%)
  matrix products  13.6 us (27%)
  starting transfers between devices  10.5 us (21%)
  local copies, waits for them, and re-layouts  6.12 us (12%)
  other arithmetic  4.53 us (9%)
  between operations  0.99 us (2%)
    ppermute x4, waiting for transfers between devices, exchange(): incoming = lax.ppermute(jnp.concatenate(pieces, axis=0), 'leaf', pairs)  11.4 us
    dot_general x13, matrix products, plain_dot(): return jnp.dot(former, latter, preferred_element_type=jnp.float32)  6.9 us
    dot_general x12, matrix products, across(): lax.dot_general(former, latter, (((1,), (1,)), ((), ())), preferred_eleme...  6.35 us
    ppermute x4, starting transfers between devices, exchange(): incoming = lax.ppermute(jnp.concatenate(pieces, axis=0), 'leaf', pairs)  5.63 us
    unnamed x27, local copies, waits for them, and re-layouts  5.21 us
    ppermute x3, starting transfers between devices, shards(): partial_gradient = kept + lax.ppermute(outgoing, 'src', pairs)  4.87 us
    ppermute x3, waiting for transfers between devices, shards(): partial_gradient = kept + lax.ppermute(outgoing, 'src', pairs)  3.36 us
    unnamed x5, other arithmetic  3.07 us
  transfers between devices with their start and end apart: 7, of which 5 were waited for; matrix products, arithmetic and copies ran while one was open for 19% of the time, Pallas kernels for 0%

profile of v11, /device:TPU:0, one launch (start us, length us, event | category | flops | bytes accessed | tf_op | source)
XLA Modules:
  0.0 50.5 jit_solution(4552792563686345617)
XLA Ops:
  0.6 0.0 copy-start
  0.7 0.7 %copy-done.10 = s32[128]{0:T(128)S(1)} copy-done((s32[128]{0:T(128)S(1)}, s32[128]{0:T(128)}, u32[]{:S(2)}) %copy-start.10) | copy-done | bytes 536
  1.4 0.0 copy-start.8
  1.4 0.7 %copy-done.8 = s32[3,2]{0,1:T(2,128)S(1)} copy-done((s32[3,2]{0,1:T(2,128)S(1)}, s32[3,2]{0,1:T(2,128)}, u32[]{:S(2)}) %copy-start.8) | copy-done | bytes 48
  2.1 0.1 copy.15
  2.2 0.9 %fusion.166 = (bf16[128,128]{0,1:T(8,128)(2,1)S(1)}, f32[128,128]{0,1:T(8,128)S(1)}) fusion(bf16[512,512]{1,0:T(8,128)(2,1)} %param.16, f32[128,512]{0,1:T(8,128)S(1)} %fusion.15), kind=kOutput, calls=%fused_computation.198 | convolution fusion | flops 4227072 | bytes 229376 | tf_op jit(solution)/shard_map/dot_general | solution.py:10
  3.1 1.0 %fusion.167 = (bf16[128,128]{0,1:T(8,128)(2,1)S(1)}, f32[128,128]{0,1:T(8,128)S(1)}) fusion(bf16[128,128]{0,1:T(8,128)(2,1)S(1)} %get-tuple-element.12, bf16[128,128]{0,1:T(8,128)(2,1)S(1)} %slice.510, bf16[512,512]{1,0:T(8,128)(2,1)} %param.16, f32[128,512]{0,1:T(8,128)S(1)} %fusion.15), kind=kOutput, calls=%fused_computation.199 | convolution fusion | flops 8552448 | bytes 294912 | tf_op jit(solution)/shard_map/dot_general | solution.py:10
  4.1 1.1 %convolution_subtract_fusion.5 = f32[128,128]{0,1:T(8,128)S(1)} fusion(bf16[128,128]{0,1:T(8,128)(2,1)S(1)} %get-tuple-element.14, bf16[128,128]{0,1:T(8,128)(2,1)S(1)} %get-tuple-element.12, bf16[128,128]{0,1:T(8,128)(2,1)S(1)} %slice.510, bf16[512,512]{1,0:T(8,128)(2,1)} %param.16, f32[128,512]{0,1:T(8,128)S(1)} %fusion.15), kind=kOutput, calls=%fused_computation.8 | convolution fusion | flops 12894208 | bytes 327680 | tf_op jit(solution)/shard_map/dot_general | solution.py:10
  5.2 0.1 slice_reduce_fusion
  5.3 0.1 broadcast_bitcast_fusion
  5.3 0.2 convolution_multiply_fusion.1
  5.6 0.0 copy-start.6
  5.6 0.6 %slice_dynamic-update-slice_fusion.1 = f32[784,128]{1,0:T(8,128)} fusion(f32[128,256]{1,0:T(8,128)S(1)} %convolution_multiply_fusion.1), kind=kLoop, calls=%fused_computation.124 | loop fusion | bytes 131072
  6.2 0.6 %slice_dynamic-update-slice_fusion = f32[784,128]{1,0:T(8,128)} fusion(f32[784,128]{1,0:T(8,128)} %slice_dynamic-update-slice_fusion.1, f32[128,256]{1,0:T(8,128)S(1)} %convolution_multiply_fusion.1), kind=kLoop, calls=%fused_computation.123 | loop fusion | bytes 131072
  6.9 0.6 %convert_dynamic-update-slice_fusion.3 = f32[784,128]{1,0:T(8,128)} fusion(f32[784,128]{1,0:T(8,128)} %slice_dynamic-update-slice_fusion, bf16[2,256,128]{2,1,0:T(8,128)(2,1)S(1)} %copy-done.6), kind=kLoop, calls=%fused_computation.119 | loop fusion | flops 16384 | bytes 98304
  7.5 0.6 %convert_dynamic-update-slice_fusion.2 = f32[784,128]{1,0:T(8,128)} fusion(f32[784,128]{1,0:T(8,128)} %convert_dynamic-update-slice_fusion.3, bf16[2,128,256]{2,1,0:T(8,128)(2,1)S(1)} %copy-done.4), kind=kLoop, calls=%fused_computation.118 | loop fusion | flops 16384 | bytes 98304
  8.1 0.2 copy-done.2
  8.4 0.6 %convert_dynamic-update-slice_fusion.1 = f32[784,128]{1,0:T(8,128)} fusion(f32[784,128]{1,0:T(8,128)} %convert_dynamic-update-slice_fusion.2, bf16[2,128,128]{2,1,0:T(8,128)(2,1)S(1)} %copy-done.2), kind=kLoop, calls=%fused_computation.117 | loop fusion | flops 16384 | bytes 98304
  9.0 0.6 %constant_dynamic-update-slice_fusion.1 = f32[784,128]{1,0:T(8,128)} fusion(f32[784,128]{1,0:T(8,128)} %convert_dynamic-update-slice_fusion.1, bf16[1,2]{1,0:T(2,128)(2,1)S(1)} %get-tuple-element.10), kind=kLoop, calls=%fused_computation.161 | loop fusion | flops 1024 | bytes 4100
  9.6 0.6 %convert_dynamic-update-slice_fusion = f32[784,128]{1,0:T(8,128)} fusion(f32[784,128]{1,0:T(8,128)} %constant_dynamic-update-slice_fusion.1, bf16[2,128,128]{2,1,0:T(8,128)(2,1)S(1)} %copy-done.2), kind=kLoop, calls=%fused_computation.116 | loop fusion | flops 16384 | bytes 98304
  10.2 0.6 %constant_dynamic-update-slice_fusion = f32[784,128]{1,0:T(8,128)} fusion(f32[784,128]{1,0:T(8,128)} %convert_dynamic-update-slice_fusion, bf16[1,2]{1,0:T(2,128)(2,1)S(1)} %get-tuple-element.11), kind=kLoop, calls=%fused_computation.160 | loop fusion | flops 1024 | bytes 4100 | tf_op jit(solution)/shard_map/concatenate | solution.py:134
  10.8 2.9 %collective-permute-start = (f32[784,128]{1,0:T(8,128)}, f32[784,128]{1,0:T(8,128)S(1)}, u32[]{:S(2)}, u32[]{:S(2)}) collective-permute-start(f32[784,128]{1,0:T(8,128)} %constant_dynamic-update-slice_fusion), channel_id=1, source_target_pairs={{0,8},{8,0},{16,24},{24,16},{1,9},{9,1},{17,25},{25,17},{2,10},{10... | collective-permute-start | bytes 1204232 | tf_op jit(solution)/shard_map/ppermute | solution.py:134
  13.7 0.4 convolution_bitcast_fusion
  14.1 0.2 fusion.168
  14.4 0.3 fusion.169
  14.7 0.4 fusion.172
  15.1 0.0 copy-start.1
  15.1 0.4 fusion.11
  15.5 0.6 %copy-done.1 = bf16[512,256]{1,0:T(8,128)(2,1)S(1)} copy-done((bf16[512,256]{1,0:T(8,128)(2,1)S(1)}, bf16[512,256]{1,0:T(8,128)(2,1)}, u32[]{:S(2)}) %copy-start.1) | copy-done | bytes 262168
  16.0 0.2 convolution_multiply_fusion
  16.3 0.6 %collective-permute-start.2 = (f32[256,128]{1,0:T(8,128)S(1)}, f32[256,128]{1,0:T(8,128)S(1)}, u32[]{:S(2)}, u32[]{:S(2)}) collective-permute-start(f32[256,128]{1,0:T(8,128)S(1)} %pad_maximum_fusion.5), channel_id=1, source_target_pairs={{0,8},{8,0},{16,24},{24,16},{1,9},{9,1},{17,25},{25,17},{2,10},{10... | collective-permute-start | bytes 393224 | tf_op jit(solution)/shard_map/ppermute | solution.py:134
  16.9 7.2 %collective-permute-done = f32[784,128]{1,0:T(8,128)S(1)} collective-permute-done((f32[784,128]{1,0:T(8,128)}, f32[784,128]{1,0:T(8,128)S(1)}, u32[]{:S(2)}, u32[]{:S(2)}) %collective-permute-start) | collective-permute-done | bytes 401440 | tf_op jit(solution)/shard_map/ppermute | solution.py:134
  24.1 0.6 %slice.241 = f32[1]{0:T(128)} slice(f32[2]{0:T(128)S(1)} %compare_select_fusion), slice={[1:2]} | slice | bytes 8 | tf_op jit(solution)/shard_map/slice | solution.py:130
  24.7 1.3 %collective-permute-done.2 = f32[256,128]{1,0:T(8,128)S(1)} collective-permute-done((f32[256,128]{1,0:T(8,128)S(1)}, f32[256,128]{1,0:T(8,128)S(1)}, u32[]{:S(2)}, u32[]{:S(2)}) %collective-permute-start.2) | collective-permute-done | bytes 131104 | tf_op jit(solution)/shard_map/ppermute | solution.py:134
  26.0 0.2 fusion.105
  26.3 0.1 copy.20
  26.4 0.8 %fusion.70 = f32[128,128]{1,0:T(8,128)S(1)} fusion(f32[256,128]{1,0:T(8,128)S(1)} %collective-permute-done.2, f32[128,128]{0,1:T(8,128)S(1)} %fusion.105, f32[]{:T(128)} %bitcast.6, bf16[784,128]{1,0:T(8,128)(2,1)S(1)} %convert.61, pred[]{:T(512)S(6)} %and.31, bf16[2,128,256]{2,1,0:T(8,128)(2,1)S(1)} %copy-done.4, f32[128,256]{1,0:T(8,128)S(1)} %convolution_multiply_fusion), kind=kOutput, calls=%fused_computation.89 | convolution fusion | flops 4276224 | bytes 327685 | tf_op jit(solution)/shard_map/dot_general | solution.py:16
  27.2 1.8 %collective-permute-start.3 = (f32[264,128]{1,0:T(8,128)S(1)}, f32[264,128]{1,0:T(8,128)S(1)}, u32[]{:S(2)}, u32[]{:S(2)}) collective-permute-start(f32[264,128]{1,0:T(8,128)S(1)} %pad_maximum_fusion.4), channel_id=1, source_target_pairs={{0,16},{8,24},{16,0},{24,8},{1,17},{9,25},{17,1},{25,9},{2,18},{10... | collective-permute-start | bytes 405512 | tf_op jit(solution)/shard_map/ppermute | solution.py:134
  29.1 0.8 %fusion.74 = f32[128,128]{1,0:T(8,128)S(1)} fusion(f32[784,128]{1,0:T(8,128)S(1)} %collective-permute-done, f32[128,256]{1,0:T(8,128)S(1)} %convolution_multiply_fusion.1, f32[]{:T(128)} %bitcast.6, bf16[784,128]{1,0:T(8,128)(2,1)S(1)} %convert.61, pred[]{:T(512)S(6)} %and.31, bf16[2,256,128]{2,1,0:T(8,128)(2,1)S(1)} %copy-done.6), kind=kOutput, calls=%fused_computation.95 | convolution fusion | flops 4308992 | bytes 393221 | tf_op jit(solution)/shard_map/dot_general | solution.py:10
  29.9 0.3 collective-permute-start.1
  30.2 2.8 %collective-permute-done.3 = f32[264,128]{1,0:T(8,128)S(1)} collective-permute-done((f32[264,128]{1,0:T(8,128)S(1)}, f32[264,128]{1,0:T(8,128)S(1)}, u32[]{:S(2)}, u32[]{:S(2)}) %collective-permute-start.3) | collective-permute-done | bytes 135200 | tf_op jit(solution)/shard_map/ppermute | solution.py:134
  33.0 0.1 fusion.109
  33.1 0.8 %fusion.103 = f32[128,128]{1,0:T(8,128)S(1)} fusion(f32[128,128]{1,0:T(8,128)S(1)} %fusion.109, f32[]{:T(128)} %bitcast.6, bf16[784,128]{1,0:T(8,128)(2,1)S(1)} %convert.61, pred[]{:T(512)S(6)} %and.31, bf16[2,256,128]{2,1,0:T(8,128)(2,1)S(1)} %copy-done.6), kind=kOutput, calls=%fused_computation.126 | convolution fusion | flops 4243456 | bytes 196613 | tf_op jit(solution)/shard_map/dot_general | solution.py:16
  34.0 0.3 convolution_subtract_fusion
  34.2 1.0 %fusion.186 = (bf16[128,128]{0,1:T(8,128)(2,1)S(1)}, f32[128,128]{0,1:T(8,128)S(1)}) fusion(bf16[512,512]{1,0:T(8,128)(2,1)} %param.16, f32[128,512]{0,1:T(8,128)S(1)} %convolution_subtract_fusion), kind=kOutput, calls=%fused_computation.206 | convolution fusion | flops 4227072 | bytes 229376 | tf_op jit(solution)/shard_map/dot_general | solution.py:16
  35.2 1.1 %fusion.187 = (bf16[128,128]{0,1:T(8,128)(2,1)S(1)}, f32[128,128]{0,1:T(8,128)S(1)}) fusion(bf16[512,512]{1,0:T(8,128)(2,1)} %param.16, bf16[128,128]{0,1:T(8,128)(2,1)S(1)} %slice.509, bf16[128,128]{0,1:T(8,128)(2,1)S(1)} %get-tuple-element.28, f32[128,512]{0,1:T(8,128)S(1)} %convolution_subtract_fusion), kind=kOutput, calls=%fused_computation.207 | convolution fusion | flops 8552448 | bytes 294912 | tf_op jit(solution)/shard_map/dot_general | solution.py:16
  36.3 1.1 %convolution_subtract_fusion.8 = f32[128,128]{0,1:T(8,128)S(1)} fusion(bf16[128,128]{0,1:T(8,128)(2,1)S(1)} %slice.509, bf16[128,128]{0,1:T(8,128)(2,1)S(1)} %get-tuple-element.28, bf16[128,128]{0,1:T(8,128)(2,1)S(1)} %get-tuple-element.30, bf16[512,512]{1,0:T(8,128)(2,1)} %param.16, f32[128,512]{0,1:T(8,128)S(1)} %convolution_subtract_fusion), kind=kOutput, calls=%fused_computation.11 | convolution fusion | flops 12894208 | bytes 327680 | tf_op jit(solution)/shard_map/dot_general | solution.py:16
  37.4 0.0 collective-permute-done.1
  37.5 0.2 fusion.102
  37.6 0.9 %fusion.10 = f32[128,128]{1,0:T(8,128)S(1)} fusion(f32[128,128]{1,0:T(8,128)S(1)} %fusion.102, f32[]{:T(128)} %bitcast.6, f32[784,128]{1,0:T(8,128)S(1)} %collective-permute-done, f32[128,256]{1,0:T(8,128)S(1)} %convolution_multiply_fusion.1, bf16[784,128]{1,0:T(8,128)(2,1)S(1)} %convert.61, pred[]{:T(512)S(6)} %and.31, ...), kind=kOutput, calls=%fused_computation.30 | convolution fusion | flops 8519680 | bytes 394244 | tf_op jit(solution)/shard_map/dot_general | solution.py:10
  38.6 0.2 convolution_subtract_fusion.1
  38.8 0.1 fusion.177
  38.9 0.3 fusion.178
  39.2 0.3 fusion.181
  39.5 0.3 fusion.7
  39.8 0.1 fusion.14
  40.0 2.9 %collective-permute-start.4 = (f32[4,64]{1,0:T(4,128)S(1)}, f32[4,64]{1,0:T(4,128)S(1)}, u32[]{:S(2)}, u32[]{:S(2)}) collective-permute-start(f32[4,64]{1,0:T(4,128)S(1)} %slice_select_fusion.11), channel_id=1, source_target_pairs={{0,4},{1,5},{2,6},{3,7},{4,0},{5,1},{6,2},{7,3},{8,12},{9,13},{10,... | collective-permute-start | bytes 3080 | tf_op jit(solution)/shard_map/ppermute | solution.py:224
  42.9 1.6 %collective-permute-done.4 = f32[4,64]{1,0:T(4,128)S(1)} collective-permute-done((f32[4,64]{1,0:T(4,128)S(1)}, f32[4,64]{1,0:T(4,128)S(1)}, u32[]{:S(2)}, u32[]{:S(2)}) %collective-permute-start.4) | collective-permute-done | bytes 1056 | tf_op jit(solution)/shard_map/ppermute | solution.py:224
  44.6 1.9 %collective-permute-start.5 = (f32[2,64]{1,0:T(2,128)S(1)}, f32[2,64]{1,0:T(2,128)S(1)}, u32[]{:S(2)}, u32[]{:S(2)}) collective-permute-start(f32[2,64]{1,0:T(2,128)S(1)} %broadcast_select_fusion), channel_id=1, source_target_pairs={{0,2},{1,3},{2,0},{3,1},{4,6},{5,7},{6,4},{7,5},{8,10},{9,11},{10,... | collective-permute-start | bytes 1544 | tf_op jit(solution)/shard_map/ppermute | solution.py:224
  46.5 1.7 %collective-permute-done.5 = f32[2,64]{1,0:T(2,128)S(1)} collective-permute-done((f32[2,64]{1,0:T(2,128)S(1)}, f32[2,64]{1,0:T(2,128)S(1)}, u32[]{:S(2)}, u32[]{:S(2)}) %collective-permute-start.5) | collective-permute-done | bytes 544 | tf_op jit(solution)/shard_map/ppermute | solution.py:224
  48.2 0.1 collective-permute-start.6
  48.3 0.8 %copy.24 = f32[128,512]{1,0:T(8,128)} copy(f32[128,512]{0,1:T(8,128)S(1)} %pad_maximum_fusion.3) | data formatting | bytes 524288
  49.2 0.8 %copy.23 = f32[128,512]{1,0:T(8,128)} copy(f32[128,512]{0,1:T(8,128)S(1)} %pad_maximum_fusion.2) | data formatting | bytes 524288
  50.0 0.5 %fusion.146 = f32[64]{0:T(128)} fusion(f32[1,64]{1,0:T(1,128)S(1)} %collective-permute-done.6, pred[]{:T(512)S(6)} %ne.23, f32[2,64]{1,0:T(2,128)S(1)} %select_add_fusion.1), kind=kLoop, calls=%fused_computation.178 | loop fusion | flops 192 | bytes 1025 | tf_op jit(solution)/shard_map/mul | solution.py:226
  (40 shorter events, 0.3 us)
Async XLA Ops:
  0.6 4.7 %copy-start = (bf16[256,512]{1,0:T(8,128)(2,1)S(1)}, bf16[256,512]{1,0:T(8,128)(2,1)}, u32[]{:S(2)}) copy-start(bf16[256,512]{1,0:T(8,128)(2,1)} %param.19) | copy-start | bytes 786436
  0.7 0.7 %copy-start.10 = (s32[128]{0:T(128)S(1)}, s32[128]{0:T(128)}, u32[]{:S(2)}) copy-start(s32[128]{0:T(128)} %param.12) | copy-start | bytes 1540
  1.4 0.7 %copy-start.8 = (s32[3,2]{0,1:T(2,128)S(1)}, s32[3,2]{0,1:T(2,128)}, u32[]{:S(2)}) copy-start(s32[3,2]{0,1:T(2,128)} %param.15) | copy-start | bytes 76
  5.3 9.0 %copy-start.5 = (bf16[512,512]{1,0:T(8,128)(2,1)S(1)}, bf16[512,512]{1,0:T(8,128)(2,1)}, u32[]{:S(2)}) copy-start(bf16[512,512]{1,0:T(8,128)(2,1)} %param.17) | copy-start | bytes 1572868
  5.6 1.3 %copy-start.6 = (bf16[2,256,128]{2,1,0:T(8,128)(2,1)S(1)}, bf16[2,256,128]{2,1,0:T(8,128)(2,1)}, u32[]{:S(2)}) copy-start(bf16[2,256,128]{2,1,0:T(8,128)(2,1)} %param.22) | copy-start | bytes 393220
  6.2 1.3 %copy-start.4 = (bf16[2,128,256]{2,1,0:T(8,128)(2,1)S(1)}, bf16[2,128,256]{2,1,0:T(8,128)(2,1)}, u32[]{:S(2)}) copy-start(bf16[2,128,256]{2,1,0:T(8,128)(2,1)} %param.23) | copy-start | bytes 393220
  7.5 0.9 %copy-start.2 = (bf16[2,128,128]{2,1,0:T(8,128)(2,1)S(1)}, bf16[2,128,128]{2,1,0:T(8,128)(2,1)}, u32[]{:S(2)}) copy-start(bf16[2,128,128]{2,1,0:T(8,128)(2,1)} %param.21) | copy-start | bytes 196612
  9.0 4.7 %copy-start.7 = (f32[128,128]{1,0:T(8,128)S(1)}, f32[128,128]{1,0:T(8,128)}, u32[]{:S(2)}) copy-start(f32[128,128]{1,0:T(8,128)} %param.14) | copy-start | bytes 196612
  10.2 3.5 %copy-start.9 = (s32[128]{0:T(128)S(1)}, s32[128]{0:T(128)}, u32[]{:S(2)}) copy-start(s32[128]{0:T(128)} %param.13) | copy-start | bytes 1540
  10.8 3.3 %copy-start.3 = (bf16[4,128,128]{2,1,0:T(8,128)(2,1)S(1)}, bf16[4,128,128]{2,1,0:T(8,128)(2,1)}, u32[]{:S(2)}) copy-start(bf16[4,128,128]{2,1,0:T(8,128)(2,1)} %param.18) | copy-start | bytes 393220
  10.8 13.3 %collective-permute-start = (f32[784,128]{1,0:T(8,128)}, f32[784,128]{1,0:T(8,128)S(1)}, u32[]{:S(2)}, u32[]{:S(2)}) collective-permute-start(f32[784,128]{1,0:T(8,128)} %constant_dynamic-update-slice_fusion), channel_id=1, source_target_pairs={{0,8},{8,0},{16,24},{24,16},{1,9},{9,1},{17,25},{25,17},{2,10},{10... | collective-permute-start | bytes 1204232 | tf_op jit(solution)/shard_map/ppermute | solution.py:134
  15.1 1.0 %copy-start.1 = (bf16[512,256]{1,0:T(8,128)(2,1)S(1)}, bf16[512,256]{1,0:T(8,128)(2,1)}, u32[]{:S(2)}) copy-start(bf16[512,256]{1,0:T(8,128)(2,1)} %param.20) | copy-start | bytes 786436
  16.3 9.7 %collective-permute-start.2 = (f32[256,128]{1,0:T(8,128)S(1)}, f32[256,128]{1,0:T(8,128)S(1)}, u32[]{:S(2)}, u32[]{:S(2)}) collective-permute-start(f32[256,128]{1,0:T(8,128)S(1)} %pad_maximum_fusion.5), channel_id=1, source_target_pairs={{0,8},{8,0},{16,24},{24,16},{1,9},{9,1},{17,25},{25,17},{2,10},{10... | collective-permute-start | bytes 393224 | tf_op jit(solution)/shard_map/ppermute | solution.py:134
  27.2 5.8 %collective-permute-start.3 = (f32[264,128]{1,0:T(8,128)S(1)}, f32[264,128]{1,0:T(8,128)S(1)}, u32[]{:S(2)}, u32[]{:S(2)}) collective-permute-start(f32[264,128]{1,0:T(8,128)S(1)} %pad_maximum_fusion.4), channel_id=1, source_target_pairs={{0,16},{8,24},{16,0},{24,8},{1,17},{9,25},{17,1},{25,9},{2,18},{10... | collective-permute-start | bytes 405512 | tf_op jit(solution)/shard_map/ppermute | solution.py:134
  29.9 7.6 %collective-permute-start.1 = (f32[128,128]{1,0:T(8,128)S(1)}, f32[128,128]{1,0:T(8,128)S(1)}, u32[]{:S(2)}, u32[]{:S(2)}) collective-permute-start(f32[128,128]{1,0:T(8,128)S(1)} %fusion.74), channel_id=1, source_target_pairs={{0,16},{8,24},{16,0},{24,8},{1,17},{9,25},{17,1},{25,9},{2,18},{10... | collective-permute-start | bytes 196616 | tf_op jit(solution)/shard_map/ppermute | solution.py:134
  40.0 4.5 %collective-permute-start.4 = (f32[4,64]{1,0:T(4,128)S(1)}, f32[4,64]{1,0:T(4,128)S(1)}, u32[]{:S(2)}, u32[]{:S(2)}) collective-permute-start(f32[4,64]{1,0:T(4,128)S(1)} %slice_select_fusion.11), channel_id=1, source_target_pairs={{0,4},{1,5},{2,6},{3,7},{4,0},{5,1},{6,2},{7,3},{8,12},{9,13},{10,... | collective-permute-start | bytes 3080 | tf_op jit(solution)/shard_map/ppermute | solution.py:224
  44.6 3.6 %collective-permute-start.5 = (f32[2,64]{1,0:T(2,128)S(1)}, f32[2,64]{1,0:T(2,128)S(1)}, u32[]{:S(2)}, u32[]{:S(2)}) collective-permute-start(f32[2,64]{1,0:T(2,128)S(1)} %broadcast_select_fusion), channel_id=1, source_target_pairs={{0,2},{1,3},{2,0},{3,1},{4,6},{5,7},{6,4},{7,5},{8,10},{9,11},{10,... | collective-permute-start | bytes 1544 | tf_op jit(solution)/shard_map/ppermute | solution.py:224
  48.2 1.8 %collective-permute-start.6 = (f32[1,64]{1,0:T(1,128)S(1)}, f32[1,64]{1,0:T(1,128)S(1)}, u32[]{:S(2)}, u32[]{:S(2)}) collective-permute-start(f32[1,64]{1,0:T(1,128)S(1)} %broadcast_select_fusion.1), channel_id=1, source_target_pairs={{0,1},{1,0},{2,3},{3,2},{4,5},{5,4},{6,7},{7,6},{8,9},{9,8},{10,11... | collective-permute-start | bytes 776 | tf_op jit(solution)/shard_map/ppermute | solution.py:224

commit v12 on v8

--- a/solution.py
+++ b/solution.py
@@ -143,21 +143,20 @@
         pairs = [(index, index ^ stride) for index in range(leaves)]
         pieces = []
         for upper_level in range(height, levels + 1):
-            pieces.append(lower_panels[upper_level - 1])
+            lower = lower_panels[upper_level - 1]
+            pieces.extend(lower[k * block_size : (k + 1) * block_size] for k in range(lower.shape[0] // block_size))
             pieces.extend(blocks_of(upper_panels[upper_level - 1]))
             pieces.append(inverse_panels[upper_level - 1])
-            pieces.append(pattern_rows[upper_level - 1])
-        received = exchange(pieces, pairs)
+        stacked = lax.ppermute(jnp.stack(pieces), "leaf", pairs)
+        received = [stacked[k] for k in range(len(pieces))]
         for upper_level in range(height, levels + 1):
             place = device % (1 << upper_level)
             take = jnp.logical_and(place >= stride, place < 2 * stride)
             width = levels - upper_level
-            lower_in = received[0]
-            upper_in = jnp.concatenate(received[1 : 1 + width] or [upper_panels[upper_level - 1]], axis=1)
-            inverse_in = received[1 + width]
-            pattern_in = received[2 + width]
-            received = received[3 + width :]
-            pattern_rows[upper_level - 1] = jnp.where(take, pattern_in, pattern_rows[upper_level - 1])
+            lower_in = jnp.concatenate(received[:width] or [lower_panels[upper_level - 1]], axis=0)
+            upper_in = jnp.concatenate(received[width : 2 * width] or [upper_panels[upper_level - 1]], axis=1)
+            inverse_in = received[2 * width]
+            received = received[2 * width + 1 :]
             lower_panels[upper_level - 1] = jnp.where(take, lower_in, lower_panels[upper_level - 1])
             upper_panels[upper_level - 1] = jnp.where(take, upper_in, upper_panels[upper_level - 1])
             inverse_panels[upper_level - 1] = jnp.where(take, inverse_in, inverse_panels[upper_level - 1])
@@ -166,7 +165,16 @@
     for height in range(1, levels + 1):
         stride = 1 << (height - 1)
         pairs = [(index, index ^ stride) for index in range(leaves)]
-        forward_sums = [mine + theirs for mine, theirs in zip(forward_sums, exchange(forward_sums, pairs))]
+        count = len(forward_sums)
+        wide_rows = [pattern_rows[upper_level - 1].astype(jnp.float32) for upper_level in range(height, levels + 1)]
+        received = exchange(forward_sums + wide_rows, pairs)
+        for upper_level, pattern_in in zip(range(height, levels + 1), received[count:]):
+            place = device % (1 << upper_level)
+            take = jnp.logical_and(place >= stride, place < 2 * stride)
+            pattern_rows[upper_level - 1] = jnp.where(
+                take, pattern_in.astype(jnp.bfloat16), pattern_rows[upper_level - 1]
+            )
+        forward_sums = [mine + theirs for mine, theirs in zip(forward_sums, received[:count])]
         forward_node = -forward_sums[0]
         forward_nodes.append(forward_node)
         forward_sums = forward_sums[1:]

time: 38 us -> 40 us (1.053)
  local copies, waits for them, and re-layouts: 6.85 us -> 8.08 us
  other arithmetic: 1.45 us -> 2.2 us
    ppermute x0 -> x2, starting transfers between devices: none -> 4.59 us  [shards(): stacked = lax.ppermute(jnp.stack(pieces), 'leaf', pairs)]
    ppermute x6 -> x4, starting transfers between devices: 8.29 us -> 3.74 us  [exchange(): incoming = lax.ppermute(jnp.concatenate(pieces, axis=0), 'leaf', pairs)]
    slice x0 -> x2, local copies, waits for them, and re-layouts: none -> 1.6 us  [the longest x1 0.84 us: shards(): lower_panels.append(sep_lower[height - 1, height * block_size:, :])]
    convert_element_type x1, other arithmetic: 0.01 us -> 0.68 us  [shards(): present = pattern.astype(jnp.float32)]
    sub x1, other arithmetic: 0.01 us -> 0.66 us  [shards(): src_cells[:, None] - device * cell_count == columns]
    concatenate x3, other arithmetic: 0.64 us -> 0.03 us  [exchange(): incoming = lax.ppermute(jnp.concatenate(pieces, axis=0), 'leaf', pairs)]
    ppermute x3, waiting for transfers between devices: 3.86 us -> 3.29 us  [shards(): partial_gradient = kept + lax.ppermute(outgoing, 'src', pairs)]
    ppermute x6 -> x4, waiting for transfers between devices: 3.06 us -> 3.6 us  [exchange(): incoming = lax.ppermute(jnp.concatenate(pieces, axis=0), 'leaf', pairs)]
  transfers between devices with their start and end apart: 9 -> 9, of which waited for: 5 -> 5; matrix products, arithmetic and copies ran while one was open for 24% -> 28% of each run, Pallas kernels for 0% -> 0%
where the time goes in v12:
time: 40 us; the launch traced here: 39.6 us
  starting transfers between devices  12.7 us (32%)
  matrix products  8.68 us (22%)
  local copies, waits for them, and re-layouts  8.08 us (20%)
  waiting for transfers between devices  6.89 us (17%)
  other arithmetic  2.2 us (6%)
  between operations  1.11 us (3%)
    unnamed x39, local copies, waits for them, and re-layouts  5.56 us
    ppermute x2, starting transfers between devices, shards(): stacked = lax.ppermute(jnp.stack(pieces), 'leaf', pairs)  4.59 us
    dot_general x13, matrix products, plain_dot(): return jnp.dot(former, latter, preferred_element_type=jnp.float32)  4.42 us
    ppermute x3, starting transfers between devices, shards(): partial_gradient = kept + lax.ppermute(outgoing, 'src', pairs)  4.35 us
    dot_general x12, matrix products, across(): lax.dot_general(former, latter, (((1,), (1,)), ((), ())), preferred_eleme...  3.88 us
    ppermute x4, starting transfers between devices, exchange(): incoming = lax.ppermute(jnp.concatenate(pieces, axis=0), 'leaf', pairs)  3.74 us
    ppermute x4, waiting for transfers between devices, exchange(): incoming = lax.ppermute(jnp.concatenate(pieces, axis=0), 'leaf', pairs)  3.6 us
    ppermute x3, waiting for transfers between devices, shards(): partial_gradient = kept + lax.ppermute(outgoing, 'src', pairs)  3.29 us
  transfers between devices with their start and end apart: 9, of which 5 were waited for; matrix products, arithmetic and copies ran while one was open for 28% of the time, Pallas kernels for 0%

profile of v12, /device:TPU:0, one launch (start us, length us, event | category | flops | bytes accessed | tf_op | source)
XLA Modules:
  0.0 39.6 jit_solution(5744535593384747087)
XLA Ops:
  0.6 0.0 copy-start
  0.7 0.8 %slice.227 = bf16[1,128,128]{2,1,0:T(8,128)(2,1)S(1)} slice(bf16[2,256,128]{2,1,0:T(8,128)(2,1)} %param.22), slice={[0:1], [128:256], [0:128]} | slice | bytes 65536 | tf_op jit(solution)/shard_map/slice | solution.py:121
  1.5 0.8 %slice.228 = bf16[1,128,128]{2,1,0:T(8,128)(2,1)S(1)} slice(bf16[2,128,256]{2,1,0:T(8,128)(2,1)} %param.23), slice={[0:1], [0:128], [128:256]} | slice | bytes 65536 | tf_op jit(solution)/shard_map/slice | solution.py:122
  2.3 3.0 %collective-permute-start.1 = (bf16[4,128,128]{2,1,0:T(8,128)(2,1)S(1)}, bf16[4,128,128]{2,1,0:T(8,128)(2,1)S(1)}, u32[]{:S(2)}, u32[]{:S(2)}) collective-permute-start(bf16[4,128,128]{2,1,0:T(8,128)(2,1)S(1)} %pad_maximum_fusion.5), channel_id=1, source_target_pairs={{0,8},{8,0},{16,24},{24,16},{1,9},{9,1},{17,25},{25,17},{2,10},{10... | collective-permute-start | bytes 393224 | tf_op jit(solution)/shard_map/ppermute | solution.py:150
  5.3 0.7 %convert_element_type.118 = f32[3,2]{0,1:T(2,128)S(1)} convert(s32[3,2]{0,1:T(2,128)} %param.15) | non-fusion elementwise | flops 6 | bytes 48 | tf_op jit(solution)/shard_map/convert_element_type | solution.py:97
  6.0 0.8 %copy.15 = s32[3,2]{1,0:T(4,128)S(1)} copy(s32[3,2]{0,1:T(2,128)} %param.15) | data formatting | bytes 48 | tf_op args[3]
  6.7 0.7 %broadcast_subtract_fusion = s32[128]{0:T(128)S(1)} fusion(s32[128]{0:T(128)} %param.12, s32[]{:T(128)S(6)} %mul.38), kind=kLoop, calls=%fused_computation.179 | loop fusion | flops 128 | bytes 1028 | tf_op jit(solution)/shard_map/sub | solution.py:107
  7.5 0.1 slice_reduce_fusion
  7.6 0.1 broadcast_bitcast_fusion
  7.7 0.1 fusion.184
  7.8 0.1 fusion.185
  8.0 0.2 convolution_subtract_fusion.5
  8.2 0.0 copy-start.9
  8.2 0.6 %copy-done.9 = f32[128,128]{0,1:T(8,128)} copy-done((f32[128,128]{0,1:T(8,128)}, f32[128,128]{0,1:T(8,128)S(1)}, u32[]{:S(2)}) %copy-start.9) | copy-done | bytes 65560
  8.8 0.2 convolution_multiply_fusion.1
  9.1 0.0 copy-start.5
  9.1 0.0 copy-start.17
  9.2 0.0 copy-start.3
  9.2 0.1 collective-permute-start
  9.2 0.4 %copy-done.8 = f32[128,128]{1,0:T(8,128)S(1)} copy-done((f32[128,128]{1,0:T(8,128)S(1)}, f32[128,128]{1,0:T(8,128)}, u32[]{:S(2)}) %copy-start.8) | copy-done | bytes 65560
  9.7 0.2 copy-done.17
  9.8 0.4 convolution_bitcast_fusion
  10.2 0.2 fusion.195
  10.5 0.3 fusion.196
  10.8 0.4 fusion.199
  11.2 0.4 fusion.10
  11.5 0.6 %copy-done.1 = bf16[512,256]{1,0:T(8,128)(2,1)S(1)} copy-done((bf16[512,256]{1,0:T(8,128)(2,1)S(1)}, bf16[512,256]{1,0:T(8,128)(2,1)}, u32[]{:S(2)}) %copy-start.1) | copy-done | bytes 262168
  12.1 0.2 convolution_multiply_fusion
  12.4 1.5 %collective-permute-start.4 = (f32[256,128]{1,0:T(8,128)S(1)}, f32[256,128]{1,0:T(8,128)S(1)}, u32[]{:S(2)}, u32[]{:S(2)}) collective-permute-start(f32[256,128]{1,0:T(8,128)S(1)} %pad_maximum_fusion.6), channel_id=1, source_target_pairs={{0,8},{8,0},{16,24},{24,16},{1,9},{9,1},{17,25},{25,17},{2,10},{10... | collective-permute-start | bytes 393224 | tf_op jit(solution)/shard_map/ppermute | solution.py:134
  13.9 1.6 %collective-permute-start.3 = (bf16[1,128,128]{2,1,0:T(8,128)(2,1)S(1)}, bf16[1,128,128]{2,1,0:T(8,128)(2,1)S(1)}, u32[]{:S(2)}, u32[]{:S(2)}) collective-permute-start(bf16[1,128,128]{2,1,0:T(8,128)(2,1)S(1)} %slice_select_fusion.2), channel_id=1, source_target_pairs={{0,16},{8,24},{16,0},{24,8},{1,17},{9,25},{17,1},{25,9},{2,18},{10... | collective-permute-start | bytes 98312 | tf_op jit(solution)/shard_map/ppermute | solution.py:150
  15.5 1.9 %collective-permute-done.4 = f32[256,128]{1,0:T(8,128)S(1)} collective-permute-done((f32[256,128]{1,0:T(8,128)S(1)}, f32[256,128]{1,0:T(8,128)S(1)}, u32[]{:S(2)}, u32[]{:S(2)}) %collective-permute-start.4) | collective-permute-done | bytes 131104 | tf_op jit(solution)/shard_map/ppermute | solution.py:134
  17.4 0.2 fusion.108
  17.6 0.1 copy.20
  17.8 0.6 %copy-done.14 = bf16[1,2]{1,0:T(2,128)(2,1)S(1)} copy-done((bf16[1,2]{1,0:T(2,128)(2,1)S(1)}, bf16[1,2]{1,0:T(2,128)(2,1)}, u32[]{:S(2)}) %copy-start.14) | copy-done | bytes 28
  18.4 0.6 %slice.232 = f32[1]{0:T(128)} slice(f32[2]{0:T(128)S(1)} %compare_select_fusion), slice={[1:2]} | slice | bytes 8 | tf_op jit(solution)/shard_map/slice | solution.py:130
  19.0 0.9 %fusion.63 = f32[128,128]{1,0:T(8,128)S(1)} fusion(f32[256,128]{1,0:T(8,128)S(1)} %collective-permute-done.4, f32[128,128]{0,1:T(8,128)S(1)} %fusion.108, f32[]{:T(128)} %bitcast.3, bf16[4,128,128]{2,1,0:T(8,128)(2,1)S(1)} %collective-permute-done.1, pred[]{:T(512)S(6)} %and.35, f32[128,256]{1,0:T(8,128)S(1)} %convolution_multiply_fusion, ...), kind=kOutput, calls=%fused_computation.80 | convolution fusion | flops 4276224 | bytes 327685 | tf_op jit(solution)/shard_map/dot_general | solution.py:16
  19.9 1.6 %collective-permute-start.5 = (f32[128,128]{1,0:T(8,128)S(1)}, f32[128,128]{1,0:T(8,128)S(1)}, u32[]{:S(2)}, u32[]{:S(2)}) collective-permute-start(f32[128,128]{1,0:T(8,128)S(1)} %fusion.63), channel_id=1, source_target_pairs={{0,16},{8,24},{16,0},{24,8},{1,17},{9,25},{17,1},{25,9},{2,18},{10... | collective-permute-start | bytes 196616 | tf_op jit(solution)/shard_map/ppermute | solution.py:134
  21.5 0.8 %fusion.74 = f32[128,128]{1,0:T(8,128)S(1)} fusion(f32[272,128]{1,0:T(8,128)S(1)} %collective-permute-done, f32[]{:T(128)} %bitcast.3, bf16[4,128,128]{2,1,0:T(8,128)(2,1)S(1)} %collective-permute-done.1, pred[]{:T(512)S(6)} %and.35, f32[128,256]{1,0:T(8,128)S(1)} %convolution_multiply_fusion.1, bf16[2,256,128]{2,1,0:T(8,128)(2,1)S(1)} %copy-done.7), kind=kOutput, calls=%fused_computation.96 | convolution fusion | flops 4308992 | bytes 393221 | tf_op jit(solution)/shard_map/dot_general | solution.py:10
  22.3 0.6 %collective-permute-start.2 = (f32[136,128]{1,0:T(8,128)S(1)}, f32[136,128]{1,0:T(8,128)S(1)}, u32[]{:S(2)}, u32[]{:S(2)}) collective-permute-start(f32[136,128]{1,0:T(8,128)S(1)} %pad_maximum_fusion.7), channel_id=1, source_target_pairs={{0,16},{8,24},{16,0},{24,8},{1,17},{9,25},{17,1},{25,9},{2,18},{10... | collective-permute-start | bytes 208904 | tf_op jit(solution)/shard_map/ppermute | solution.py:134
  22.9 1.7 %collective-permute-done.5 = f32[128,128]{1,0:T(8,128)S(1)} collective-permute-done((f32[128,128]{1,0:T(8,128)S(1)}, f32[128,128]{1,0:T(8,128)S(1)}, u32[]{:S(2)}, u32[]{:S(2)}) %collective-permute-start.5) | collective-permute-done | bytes 65568 | tf_op jit(solution)/shard_map/ppermute | solution.py:134
  24.5 0.1 fusion.102
  24.7 0.8 %fusion.103 = f32[128,128]{1,0:T(8,128)S(1)} fusion(f32[128,128]{1,0:T(8,128)S(1)} %fusion.102, f32[]{:T(128)} %bitcast.3, bf16[4,128,128]{2,1,0:T(8,128)(2,1)S(1)} %collective-permute-done.1, pred[]{:T(512)S(6)} %and.35, bf16[2,256,128]{2,1,0:T(8,128)(2,1)S(1)} %copy-done.7), kind=kOutput, calls=%fused_computation.121 | convolution fusion | flops 4243456 | bytes 196613 | tf_op jit(solution)/shard_map/dot_general | solution.py:16
  25.5 0.7 %copy-done.12 = f32[256]{0:T(256)S(1)} copy-done((f32[256]{0:T(256)S(1)}, f32[256]{0:T(256)}, u32[]{:S(2)}) %copy-start.12) | copy-done | bytes 1048
  26.2 0.3 convolution_subtract_fusion
  26.4 0.2 fusion.204
  26.7 0.2 fusion.205
  26.9 0.2 convolution_subtract_fusion.8
  27.1 0.1 fusion.104
  27.3 1.0 %fusion.13 = f32[128,128]{1,0:T(8,128)S(1)} fusion(f32[128,128]{1,0:T(8,128)S(1)} %fusion.104, f32[]{:T(128)} %bitcast.3, f32[272,128]{1,0:T(8,128)S(1)} %collective-permute-done, bf16[4,128,128]{2,1,0:T(8,128)(2,1)S(1)} %collective-permute-done.1, pred[]{:T(512)S(6)} %and.35, bf16[2,128,128]{2,1,0:T(8,128)(2,1)S(1)} %copy-done.2, ...), kind=kOutput, calls=%fused_computation.33 | convolution fusion | flops 8519680 | bytes 394244 | tf_op jit(solution)/shard_map/dot_general | solution.py:10
  28.3 0.2 convolution_subtract_fusion.1
  28.5 0.1 fusion.186
  28.7 0.3 fusion.187
  29.0 0.3 fusion.190
  29.3 0.3 fusion.7
  29.6 0.1 fusion.14
  29.7 2.6 %collective-permute-start.6 = (f32[4,64]{1,0:T(4,128)S(1)}, f32[4,64]{1,0:T(4,128)S(1)}, u32[]{:S(2)}, u32[]{:S(2)}) collective-permute-start(f32[4,64]{1,0:T(4,128)S(1)} %slice_select_fusion.4), channel_id=1, source_target_pairs={{0,4},{1,5},{2,6},{3,7},{4,0},{5,1},{6,2},{7,3},{8,12},{9,13},{10,... | collective-permute-start | bytes 3080 | tf_op jit(solution)/shard_map/ppermute | solution.py:227
  32.4 1.9 %collective-permute-done.6 = f32[4,64]{1,0:T(4,128)S(1)} collective-permute-done((f32[4,64]{1,0:T(4,128)S(1)}, f32[4,64]{1,0:T(4,128)S(1)}, u32[]{:S(2)}, u32[]{:S(2)}) %collective-permute-start.6) | collective-permute-done | bytes 1056 | tf_op jit(solution)/shard_map/ppermute | solution.py:227
  34.3 1.6 %collective-permute-start.7 = (f32[2,64]{1,0:T(2,128)S(1)}, f32[2,64]{1,0:T(2,128)S(1)}, u32[]{:S(2)}, u32[]{:S(2)}) collective-permute-start(f32[2,64]{1,0:T(2,128)S(1)} %broadcast_select_fusion.3), channel_id=1, source_target_pairs={{0,2},{1,3},{2,0},{3,1},{4,6},{5,7},{6,4},{7,5},{8,10},{9,11},{10,... | collective-permute-start | bytes 1544 | tf_op jit(solution)/shard_map/ppermute | solution.py:227
  35.9 0.8 %copy.24 = f32[128,512]{1,0:T(8,128)} copy(f32[128,512]{0,1:T(8,128)S(1)} %pad_maximum_fusion.3) | data formatting | bytes 524288
  36.8 1.1 %collective-permute-done.7 = f32[2,64]{1,0:T(2,128)S(1)} collective-permute-done((f32[2,64]{1,0:T(2,128)S(1)}, f32[2,64]{1,0:T(2,128)S(1)}, u32[]{:S(2)}, u32[]{:S(2)}) %collective-permute-start.7) | collective-permute-done | bytes 544 | tf_op jit(solution)/shard_map/ppermute | solution.py:227
  37.9 0.1 collective-permute-start.8
  38.0 0.8 %copy.23 = f32[128,512]{1,0:T(8,128)} copy(f32[128,512]{0,1:T(8,128)S(1)} %pad_maximum_fusion.1) | data formatting | bytes 524288
  38.9 0.2 collective-permute-done.8
  39.1 0.5 %fusion.156 = f32[64]{0:T(128)} fusion(f32[1,64]{1,0:T(1,128)S(1)} %collective-permute-done.8, pred[]{:T(512)S(6)} %ne.27, f32[2,64]{1,0:T(2,128)S(1)} %select_add_fusion.1), kind=kLoop, calls=%fused_computation.177 | loop fusion | flops 192 | bytes 1025 | tf_op jit(solution)/shard_map/mul | solution.py:229
  (56 shorter events, 0.3 us)
Async XLA Ops:
  0.6 8.2 %copy-start = (bf16[256,512]{1,0:T(8,128)(2,1)S(1)}, bf16[256,512]{1,0:T(8,128)(2,1)}, u32[]{:S(2)}) copy-start(bf16[256,512]{1,0:T(8,128)(2,1)} %param.19) | copy-start | bytes 786436
  0.6 1.6 %copy-start.2 = (bf16[2,128,128]{2,1,0:T(8,128)(2,1)S(1)}, bf16[2,128,128]{2,1,0:T(8,128)(2,1)}, u32[]{:S(2)}) copy-start(bf16[2,128,128]{2,1,0:T(8,128)(2,1)} %param.21) | copy-start | bytes 196612
  0.7 7.0 %copy-start.6 = (bf16[512,512]{1,0:T(8,128)(2,1)S(1)}, bf16[512,512]{1,0:T(8,128)(2,1)}, u32[]{:S(2)}) copy-start(bf16[512,512]{1,0:T(8,128)(2,1)} %param.16) | copy-start | bytes 1572868
  2.3 11.6 %collective-permute-start.1 = (bf16[4,128,128]{2,1,0:T(8,128)(2,1)S(1)}, bf16[4,128,128]{2,1,0:T(8,128)(2,1)S(1)}, u32[]{:S(2)}, u32[]{:S(2)}) collective-permute-start(bf16[4,128,128]{2,1,0:T(8,128)(2,1)S(1)} %pad_maximum_fusion.5), channel_id=1, source_target_pairs={{0,8},{8,0},{16,24},{24,16},{1,9},{9,1},{17,25},{25,17},{2,10},{10... | collective-permute-start | bytes 393224 | tf_op jit(solution)/shard_map/ppermute | solution.py:150
  7.7 3.9 %copy-start.11 = (f32[256]{0:T(256)}, f32[256]{0:T(256)S(1)}, u32[]{:S(2)}) copy-start(f32[256]{0:T(256)S(1)} %broadcast_bitcast_fusion) | copy-start | bytes 3076
  7.7 1.4 %copy-start.13 = (bf16[1,2]{1,0:T(2,128)(2,1)}, bf16[1,2]{1,0:T(2,128)(2,1)S(1)}, u32[]{:S(2)}) copy-start(bf16[1,2]{1,0:T(2,128)(2,1)S(1)} %get-tuple-element.12) | copy-start | bytes 16
  7.7 1.4 %copy-start.15 = (bf16[1,2]{1,0:T(2,128)(2,1)}, bf16[1,2]{1,0:T(2,128)(2,1)S(1)}, u32[]{:S(2)}) copy-start(bf16[1,2]{1,0:T(2,128)(2,1)S(1)} %get-tuple-element.13) | copy-start | bytes 16
  8.2 0.6 %copy-start.9 = (f32[128,128]{0,1:T(8,128)}, f32[128,128]{0,1:T(8,128)S(1)}, u32[]{:S(2)}) copy-start(f32[128,128]{0,1:T(8,128)S(1)} %convolution_subtract_fusion.5) | copy-start | bytes 196612
  8.8 0.8 %copy-start.8 = (f32[128,128]{1,0:T(8,128)S(1)}, f32[128,128]{1,0:T(8,128)}, u32[]{:S(2)}) copy-start(f32[128,128]{1,0:T(8,128)} %param.14) | copy-start | bytes 196612
  9.1 1.4 %copy-start.5 = (bf16[512,512]{1,0:T(8,128)(2,1)S(1)}, bf16[512,512]{1,0:T(8,128)(2,1)}, u32[]{:S(2)}) copy-start(bf16[512,512]{1,0:T(8,128)(2,1)} %param.17) | copy-start | bytes 1572868
  9.1 0.7 %copy-start.17 = (s32[128]{0:T(128)S(1)}, s32[128]{0:T(128)}, u32[]{:S(2)}) copy-start(s32[128]{0:T(128)} %param.13) | copy-start | bytes 1540
  9.2 1.1 %copy-start.3 = (bf16[4,128,128]{2,1,0:T(8,128)(2,1)S(1)}, bf16[4,128,128]{2,1,0:T(8,128)(2,1)}, u32[]{:S(2)}) copy-start(bf16[4,128,128]{2,1,0:T(8,128)(2,1)} %param.18) | copy-start | bytes 393220
  9.2 8.6 %collective-permute-start = (f32[272,128]{1,0:T(8,128)S(1)}, f32[272,128]{1,0:T(8,128)S(1)}, u32[]{:S(2)}, u32[]{:S(2)}) collective-permute-start(f32[272,128]{1,0:T(8,128)S(1)} %pad_maximum_fusion.4), channel_id=1, source_target_pairs={{0,8},{8,0},{16,24},{24,16},{1,9},{9,1},{17,25},{25,17},{2,10},{10... | collective-permute-start | bytes 417800 | tf_op jit(solution)/shard_map/ppermute | solution.py:134
  11.2 1.0 %copy-start.1 = (bf16[512,256]{1,0:T(8,128)(2,1)S(1)}, bf16[512,256]{1,0:T(8,128)(2,1)}, u32[]{:S(2)}) copy-start(bf16[512,256]{1,0:T(8,128)(2,1)} %param.20) | copy-start | bytes 786436
  12.4 5.0 %collective-permute-start.4 = (f32[256,128]{1,0:T(8,128)S(1)}, f32[256,128]{1,0:T(8,128)S(1)}, u32[]{:S(2)}, u32[]{:S(2)}) collective-permute-start(f32[256,128]{1,0:T(8,128)S(1)} %pad_maximum_fusion.6), channel_id=1, source_target_pairs={{0,8},{8,0},{16,24},{24,16},{1,9},{9,1},{17,25},{25,17},{2,10},{10... | collective-permute-start | bytes 393224 | tf_op jit(solution)/shard_map/ppermute | solution.py:134
  13.9 9.0 %collective-permute-start.3 = (bf16[1,128,128]{2,1,0:T(8,128)(2,1)S(1)}, bf16[1,128,128]{2,1,0:T(8,128)(2,1)S(1)}, u32[]{:S(2)}, u32[]{:S(2)}) collective-permute-start(bf16[1,128,128]{2,1,0:T(8,128)(2,1)S(1)} %slice_select_fusion.2), channel_id=1, source_target_pairs={{0,16},{8,24},{16,0},{24,8},{1,17},{9,25},{17,1},{25,9},{2,18},{10... | collective-permute-start | bytes 98312 | tf_op jit(solution)/shard_map/ppermute | solution.py:150
  17.7 0.7 %copy-start.14 = (bf16[1,2]{1,0:T(2,128)(2,1)S(1)}, bf16[1,2]{1,0:T(2,128)(2,1)}, u32[]{:S(2)}) copy-start(bf16[1,2]{1,0:T(2,128)(2,1)} %copy-done.13) | copy-start | bytes 16
  17.8 0.7 %copy-start.16 = (bf16[1,2]{1,0:T(2,128)(2,1)S(1)}, bf16[1,2]{1,0:T(2,128)(2,1)}, u32[]{:S(2)}) copy-start(bf16[1,2]{1,0:T(2,128)(2,1)} %copy-done.15) | copy-start | bytes 16
  17.8 1.3 %copy-start.4 = (bf16[2,128,256]{2,1,0:T(8,128)(2,1)S(1)}, bf16[2,128,256]{2,1,0:T(8,128)(2,1)}, u32[]{:S(2)}) copy-start(bf16[2,128,256]{2,1,0:T(8,128)(2,1)} %param.23) | copy-start | bytes 393220
  19.0 2.5 %copy-start.7 = (bf16[2,256,128]{2,1,0:T(8,128)(2,1)S(1)}, bf16[2,256,128]{2,1,0:T(8,128)(2,1)}, u32[]{:S(2)}) copy-start(bf16[2,256,128]{2,1,0:T(8,128)(2,1)} %param.22) | copy-start | bytes 393220
  19.9 4.6 %collective-permute-start.5 = (f32[128,128]{1,0:T(8,128)S(1)}, f32[128,128]{1,0:T(8,128)S(1)}, u32[]{:S(2)}, u32[]{:S(2)}) collective-permute-start(f32[128,128]{1,0:T(8,128)S(1)} %fusion.63), channel_id=1, source_target_pairs={{0,16},{8,24},{16,0},{24,8},{1,17},{9,25},{17,1},{25,9},{2,18},{10... | collective-permute-start | bytes 196616 | tf_op jit(solution)/shard_map/ppermute | solution.py:134
  22.3 4.8 %collective-permute-start.2 = (f32[136,128]{1,0:T(8,128)S(1)}, f32[136,128]{1,0:T(8,128)S(1)}, u32[]{:S(2)}, u32[]{:S(2)}) collective-permute-start(f32[136,128]{1,0:T(8,128)S(1)} %pad_maximum_fusion.7), channel_id=1, source_target_pairs={{0,16},{8,24},{16,0},{24,8},{1,17},{9,25},{17,1},{25,9},{2,18},{10... | collective-permute-start | bytes 208904 | tf_op jit(solution)/shard_map/ppermute | solution.py:134
  25.5 0.7 %copy-start.12 = (f32[256]{0:T(256)S(1)}, f32[256]{0:T(256)}, u32[]{:S(2)}) copy-start(f32[256]{0:T(256)} %copy-done.11) | copy-start | bytes 3076
  27.3 1.0 %copy-start.10 = (f32[128,128]{0,1:T(8,128)S(1)}, f32[128,128]{0,1:T(8,128)}, u32[]{:S(2)}) copy-start(f32[128,128]{0,1:T(8,128)} %copy-done.9) | copy-start | bytes 196612
  29.7 4.5 %collective-permute-start.6 = (f32[4,64]{1,0:T(4,128)S(1)}, f32[4,64]{1,0:T(4,128)S(1)}, u32[]{:S(2)}, u32[]{:S(2)}) collective-permute-start(f32[4,64]{1,0:T(4,128)S(1)} %slice_select_fusion.4), channel_id=1, source_target_pairs={{0,4},{1,5},{2,6},{3,7},{4,0},{5,1},{6,2},{7,3},{8,12},{9,13},{10,... | collective-permute-start | bytes 3080 | tf_op jit(solution)/shard_map/ppermute | solution.py:227
  34.3 3.6 %collective-permute-start.7 = (f32[2,64]{1,0:T(2,128)S(1)}, f32[2,64]{1,0:T(2,128)S(1)}, u32[]{:S(2)}, u32[]{:S(2)}) collective-permute-start(f32[2,64]{1,0:T(2,128)S(1)} %broadcast_select_fusion.3), channel_id=1, source_target_pairs={{0,2},{1,3},{2,0},{3,1},{4,6},{5,7},{6,4},{7,5},{8,10},{9,11},{10,... | collective-permute-start | bytes 1544 | tf_op jit(solution)/shard_map/ppermute | solution.py:227
  37.9 1.2 %collective-permute-start.8 = (f32[1,64]{1,0:T(1,128)S(1)}, f32[1,64]{1,0:T(1,128)S(1)}, u32[]{:S(2)}, u32[]{:S(2)}) collective-permute-start(f32[1,64]{1,0:T(1,128)S(1)} %broadcast_select_fusion.4), channel_id=1, source_target_pairs={{0,1},{1,0},{2,3},{3,2},{4,5},{5,4},{6,7},{7,6},{8,9},{9,8},{10,11... | collective-permute-start | bytes 776 | tf_op jit(solution)/shard_map/ppermute | solution.py:227

commit v13 on v4

--- a/solution.py
+++ b/solution.py
@@ -172,29 +172,24 @@
         pattern_rows[height - 1] = panel_buffer[row : row + 8]
         row += 8
 
-    def exchange(values, pairs):
-        incoming = lax.ppermute(jnp.concatenate(values, axis=0), "leaf", pairs)
-        return [incoming[k * source_count : (k + 1) * source_count] for k in range(len(values))]
-
     forward_nodes, adjoint_nodes = [], []
     for height in range(1, levels + 1):
         stride = 1 << (height - 1)
         pairs = [(index, index ^ stride) for index in range(leaves)]
-        count = len(forward_sums)
-        received = exchange(forward_sums + adjoint_sums, pairs)
-        forward_sums = [mine + theirs for mine, theirs in zip(forward_sums, received[:count])]
-        adjoint_sums = [mine + theirs for mine, theirs in zip(adjoint_sums, received[count:])]
+        forward_sums = [mine + theirs for mine, theirs in zip(forward_sums, exchange(forward_sums, pairs))]
         forward_node = -forward_sums[0]
         forward_nodes.append(forward_node)
         forward_sums = forward_sums[1:]
+        if forward_sums:
+            forward_coupling = blocks_of(
+                across(as_half(forward_node), lower_panels[height - 1]) * chain_mask(height)
+            )
+            forward_sums = [total + extra for total, extra in zip(forward_sums, forward_coupling)]
+        adjoint_sums = [mine + theirs for mine, theirs in zip(adjoint_sums, exchange(adjoint_sums, pairs))]
         adjoint_node = plain_dot(as_half(-adjoint_sums[0]), inverse_panels[height - 1])
         adjoint_nodes.append(adjoint_node)
         adjoint_sums = adjoint_sums[1:]
-        if forward_sums:
-            forward_coupling = blocks_of(
-                across(as_half(forward_node), lower_panels[height - 1]) * chain_mask(height)
-            )
-            forward_sums = [total + extra for total, extra in zip(forward_sums, forward_coupling)]
+        if adjoint_sums:
             adjoint_coupling = blocks_of(
                 plain_dot(as_half(adjoint_node), upper_panels[height - 1]) * chain_mask(height)
             )
@@ -223,8 +218,17 @@
     spread = lax.axis_size("src")
     product_field = (forward_field * adjoint_field).reshape(source_count, spread, cell_count // spread)
     partial_gradient = jnp.sum(product_field, axis=0)
-    gathered = lax.all_to_all(partial_gradient, "src", 0, 0, tiled=True)
-    gradient = jnp.sum(gathered, axis=0) * factor
+    place = lax.axis_index("src")
+    bit = spread // 2
+    while bit:
+        half = partial_gradient.shape[0] // 2
+        upper = (place & bit) != 0
+        outgoing = jnp.where(upper, partial_gradient[:half], partial_gradient[half:])
+        kept = jnp.where(upper, partial_gradient[half:], partial_gradient[:half])
+        pairs = [(index, index ^ bit) for index in range(spread)]
+        partial_gradient = kept + lax.ppermute(outgoing, "src", pairs)
+        bit //= 2
+    gradient = partial_gradient.reshape(-1) * factor
     return (forward_field, adjoint_field, gradient)
 
 

time: 46.9 us -> 43.3 us (0.923)
  waiting for transfers between devices: 14.4 us -> 8.06 us
  starting transfers between devices: 10.6 us -> 13.2 us
  local copies, waits for them, and re-layouts: 8.66 us -> 9.37 us
  other arithmetic: 3.04 us -> 2.43 us
    ppermute x2 -> x7, starting transfers between devices: 1.17 us -> 8.18 us  [the longest x3 4.37 us: shards(): partial_gradient = kept + lax.ppermute(outgoing, 'src', pairs)]
    all_to_all x1 -> x0, starting transfers between devices: 4.89 us -> none  [shards(): gathered = lax.all_to_all(partial_gradient, 'src', 0, 0, tiled=True)]
    all_to_all x1 -> x0, waiting for transfers between devices: 3.86 us -> none  [shards(): gathered = lax.all_to_all(partial_gradient, 'src', 0, 0, tiled=True)]
    ppermute x2, waiting for transfers between devices: 2.88 us -> 1.47 us  [shards(): received = lax.ppermute(panel_buffer, 'leaf', pairs)]
    ppermute x2 -> x7, waiting for transfers between devices: 7.7 us -> 6.58 us  [the longest x3 3.86 us: shards(): partial_gradient = kept + lax.ppermute(outgoing, 'src', pairs)]
    unnamed x24 -> x28, local copies, waits for them, and re-layouts: 7.74 us -> 8.44 us
    reduce_sum x1, other arithmetic: 0.74 us -> 0.14 us  [shards(): partial_gradient = jnp.sum(product_field, axis=0)]
  transfers between devices with their start and end apart: 5 -> 9, of which waited for: 4 -> 6; matrix products, arithmetic and copies ran while one was open for 14% -> 24% of each run, Pallas kernels for 0% -> 0%
where the time goes in v13:
time: 43.3 us; the launch traced here: 42.7 us
  starting transfers between devices  13.2 us (30%)
  local copies, waits for them, and re-layouts  9.37 us (22%)
  matrix products  8.63 us (20%)
  waiting for transfers between devices  8.06 us (19%)
  other arithmetic  2.43 us (6%)
  between operations  1.02 us (2%)
    unnamed x28, local copies, waits for them, and re-layouts  8.44 us
    ppermute x2, starting transfers between devices, shards(): received = lax.ppermute(panel_buffer, 'leaf', pairs)  5.05 us
    dot_general x13, matrix products, plain_dot(): return jnp.dot(former, latter, preferred_element_type=jnp.float32)  4.39 us
    ppermute x3, starting transfers between devices, shards(): partial_gradient = kept + lax.ppermute(outgoing, 'src', pairs)  4.37 us
    ppermute x3, waiting for transfers between devices, shards(): partial_gradient = kept + lax.ppermute(outgoing, 'src', pairs)  3.86 us
    dot_general x12, matrix products, across(): lax.dot_general(former, latter, (((1,), (1,)), ((), ())), preferred_eleme...  3.86 us
    ppermute x4, starting transfers between devices, exchange(): incoming = lax.ppermute(jnp.concatenate(pieces, axis=0), 'leaf', pairs)  3.8 us
    ppermute x4, waiting for transfers between devices, exchange(): incoming = lax.ppermute(jnp.concatenate(pieces, axis=0), 'leaf', pairs)  2.72 us
  transfers between devices with their start and end apart: 9, of which 6 were waited for; matrix products, arithmetic and copies ran while one was open for 24% of the time, Pallas kernels for 0%

profile of v13, /device:TPU:0, one launch (start us, length us, event | category | flops | bytes accessed | tf_op | source)
XLA Modules:
  0.0 42.7 jit_solution(7786061584155660801)
XLA Ops:
  0.7 0.8 %copy.18 = s32[3,2]{1,0:T(4,128)S(1)} copy(s32[3,2]{0,1:T(2,128)} %param.18) | data formatting | bytes 48 | tf_op args[3]
  1.5 0.8 %bitcast_dynamic-update-slice_fusion.3 = bf16[528,128]{1,0:T(8,128)(2,1)S(1)} fusion(bf16[2,256,128]{2,1,0:T(8,128)(2,1)} %param.25), kind=kLoop, calls=%fused_computation.135 | loop fusion | bytes 65536
  2.3 0.8 %bitcast_dynamic-update-slice_fusion.2 = bf16[528,128]{1,0:T(8,128)(2,1)S(1)} fusion(bf16[528,128]{1,0:T(8,128)(2,1)S(1)} %bitcast_dynamic-update-slice_fusion.3, bf16[2,128,256]{2,1,0:T(8,128)(2,1)} %param.26), kind=kLoop, calls=%fused_computation.134 | loop fusion | bytes 65536
  3.0 0.8 %bitcast_dynamic-update-slice_fusion.1 = bf16[528,128]{1,0:T(8,128)(2,1)S(1)} fusion(bf16[528,128]{1,0:T(8,128)(2,1)S(1)} %bitcast_dynamic-update-slice_fusion.2, bf16[2,128,128]{2,1,0:T(8,128)(2,1)} %param.24), kind=kLoop, calls=%fused_computation.133 | loop fusion | bytes 65536
  3.8 0.8 %bitcast_dynamic-update-slice_fusion = bf16[528,128]{1,0:T(8,128)(2,1)S(1)} fusion(bf16[528,128]{1,0:T(8,128)(2,1)S(1)} %constant_dynamic-update-slice_fusion.1, bf16[2,128,128]{2,1,0:T(8,128)(2,1)} %param.24), kind=kLoop, calls=%fused_computation.132 | loop fusion | bytes 65536
  4.6 3.0 %collective-permute-start.1 = (bf16[528,128]{1,0:T(8,128)(2,1)S(1)}, bf16[528,128]{1,0:T(8,128)(2,1)S(1)}, u32[]{:S(2)}, u32[]{:S(2)}) collective-permute-start(bf16[528,128]{1,0:T(8,128)(2,1)S(1)} %constant_dynamic-update-slice_fusion), channel_id=1, source_target_pairs={{0,8},{8,0},{16,24},{24,16},{1,9},{9,1},{17,25},{25,17},{2,10},{10... | collective-permute-start | bytes 405512 | tf_op jit(solution)/shard_map/ppermute | solution.py:153
  7.6 0.7 %convert_element_type.107 = f32[3,2]{0,1:T(2,128)S(1)} convert(s32[3,2]{0,1:T(2,128)} %param.18) | non-fusion elementwise | flops 6 | bytes 48 | tf_op jit(solution)/shard_map/convert_element_type | solution.py:98
  8.3 0.7 %broadcast_subtract_fusion = s32[128]{0:T(128)S(1)} fusion(s32[128]{0:T(128)} %param.15, s32[]{:T(128)S(6)} %mul.38), kind=kLoop, calls=%fused_computation.180 | loop fusion | flops 128 | bytes 1028 | tf_op jit(solution)/shard_map/sub | solution.py:108
  9.0 0.1 slice_reduce_fusion
  9.1 0.1 broadcast_bitcast_fusion
  9.2 0.1 fusion.173
  9.3 0.1 fusion.174
  9.5 0.2 convolution_subtract_fusion.5
  9.7 0.6 %copy-done.6 = f32[128,128]{0,1:T(8,128)} copy-done((f32[128,128]{0,1:T(8,128)}, f32[128,128]{0,1:T(8,128)S(1)}, u32[]{:S(2)}) %copy-start.6) | copy-done | bytes 65560
  10.3 0.2 convolution_multiply_fusion.1
  10.6 0.1 collective-permute-start
  10.7 0.4 copy-done.5
  11.2 0.2 copy-done.9
  11.4 0.4 convolution_bitcast_fusion
  11.8 0.5 %copy-done.2 = bf16[4,128,128]{2,1,0:T(8,128)(2,1)S(1)} copy-done((bf16[4,128,128]{2,1,0:T(8,128)(2,1)S(1)}, bf16[4,128,128]{2,1,0:T(8,128)(2,1)}, u32[]{:S(2)}) %copy-start.2) | copy-done | bytes 131096
  12.3 0.2 fusion.184
  12.5 0.3 fusion.185
  12.9 0.4 fusion.188
  13.3 0.4 fusion.10
  13.6 0.6 %copy-done.1 = bf16[512,256]{1,0:T(8,128)(2,1)S(1)} copy-done((bf16[512,256]{1,0:T(8,128)(2,1)S(1)}, bf16[512,256]{1,0:T(8,128)(2,1)}, u32[]{:S(2)}) %copy-start.1) | copy-done | bytes 262168
  14.2 0.2 convolution_multiply_fusion
  14.4 0.4 %copy-done.8 = pred[528]{0:T(1024)(128)(4,1)S(1)} copy-done((pred[528]{0:T(1024)(128)(4,1)S(1)}, pred[528]{0:T(1024)(128)(4,1)}, u32[]{:S(2)}) %copy-start.8) | copy-done | bytes 552
  14.9 0.1 broadcast_select_fusion
  15.0 2.0 %collective-permute-start.2 = (bf16[528,128]{1,0:T(8,128)(2,1)S(1)}, bf16[528,128]{1,0:T(8,128)(2,1)S(1)}, u32[]{:S(2)}, u32[]{:S(2)}) collective-permute-start(bf16[528,128]{1,0:T(8,128)(2,1)S(1)} %broadcast_select_fusion), channel_id=1, source_target_pairs={{0,16},{8,24},{16,0},{24,8},{1,17},{9,25},{17,1},{25,9},{2,18},{10... | collective-permute-start | bytes 405512 | tf_op jit(solution)/shard_map/ppermute | solution.py:153
  17.1 1.6 %collective-permute-start.4 = (f32[256,128]{1,0:T(8,128)S(1)}, f32[256,128]{1,0:T(8,128)S(1)}, u32[]{:S(2)}, u32[]{:S(2)}) collective-permute-start(f32[256,128]{1,0:T(8,128)S(1)} %pad_maximum_fusion.5), channel_id=1, source_target_pairs={{0,8},{8,0},{16,24},{24,16},{1,9},{9,1},{17,25},{25,17},{2,10},{10... | collective-permute-start | bytes 393224 | tf_op jit(solution)/shard_map/ppermute | solution.py:135
  18.7 1.5 %collective-permute-done.2 = bf16[528,128]{1,0:T(8,128)(2,1)S(1)} collective-permute-done((bf16[528,128]{1,0:T(8,128)(2,1)S(1)}, bf16[528,128]{1,0:T(8,128)(2,1)S(1)}, u32[]{:S(2)}, u32[]{:S(2)}) %collective-permute-start.2) | collective-permute-done | bytes 135200 | tf_op jit(solution)/shard_map/ppermute | solution.py:153
  20.1 0.1 broadcast_select_fusion.1
  20.3 0.6 %slice.223 = f32[1]{0:T(128)} slice(f32[2]{0:T(128)S(1)} %compare_select_fusion), slice={[1:2]} | slice | bytes 8 | tf_op jit(solution)/shard_map/slice | solution.py:131
  20.9 1.3 %collective-permute-done.4 = f32[256,128]{1,0:T(8,128)S(1)} collective-permute-done((f32[256,128]{1,0:T(8,128)S(1)}, f32[256,128]{1,0:T(8,128)S(1)}, u32[]{:S(2)}, u32[]{:S(2)}) %collective-permute-start.4) | collective-permute-done | bytes 131104 | tf_op jit(solution)/shard_map/ppermute | solution.py:135
  22.1 0.2 fusion.105
  22.4 0.8 %fusion.63 = f32[128,128]{1,0:T(8,128)S(1)} fusion(f32[256,128]{1,0:T(8,128)S(1)} %collective-permute-done.4, f32[128,128]{0,1:T(8,128)S(1)} %fusion.105, f32[]{:T(128)} %bitcast.6, bf16[528,128]{1,0:T(8,128)(2,1)S(1)} %broadcast_select_fusion.1, f32[128,256]{1,0:T(8,128)S(1)} %convolution_multiply_fusion), kind=kOutput, calls=%fused_computation.80 | convolution fusion | flops 4259840 | bytes 294916 | tf_op jit(solution)/shard_map/dot_general | solution.py:17
  23.2 0.8 %collective-permute-start.5 = (f32[128,128]{1,0:T(8,128)S(1)}, f32[128,128]{1,0:T(8,128)S(1)}, u32[]{:S(2)}, u32[]{:S(2)}) collective-permute-start(f32[128,128]{1,0:T(8,128)S(1)} %fusion.63), channel_id=1, source_target_pairs={{0,16},{8,24},{16,0},{24,8},{1,17},{9,25},{17,1},{25,9},{2,18},{10... | collective-permute-start | bytes 196616 | tf_op jit(solution)/shard_map/ppermute | solution.py:135
  24.0 0.8 %fusion.72 = f32[128,128]{1,0:T(8,128)S(1)} fusion(f32[256,128]{1,0:T(8,128)S(1)} %collective-permute-done, f32[]{:T(128)} %bitcast.6, bf16[528,128]{1,0:T(8,128)(2,1)S(1)} %broadcast_select_fusion.1, f32[128,256]{1,0:T(8,128)S(1)} %convolution_multiply_fusion.1), kind=kOutput, calls=%fused_computation.93 | convolution fusion | flops 4292608 | bytes 360452 | tf_op jit(solution)/shard_map/dot_general | solution.py:11
  24.8 0.1 copy.23
  24.9 1.4 %collective-permute-start.3 = (f32[128,128]{1,0:T(8,128)S(1)}, f32[128,128]{1,0:T(8,128)S(1)}, u32[]{:S(2)}, u32[]{:S(2)}) collective-permute-start(f32[128,128]{1,0:T(8,128)S(1)} %fusion.72), channel_id=1, source_target_pairs={{0,16},{8,24},{16,0},{24,8},{1,17},{9,25},{17,1},{25,9},{2,18},{10... | collective-permute-start | bytes 196616 | tf_op jit(solution)/shard_map/ppermute | solution.py:135
  26.3 1.3 %collective-permute-done.5 = f32[128,128]{1,0:T(8,128)S(1)} collective-permute-done((f32[128,128]{1,0:T(8,128)S(1)}, f32[128,128]{1,0:T(8,128)S(1)}, u32[]{:S(2)}, u32[]{:S(2)}) %collective-permute-start.5) | collective-permute-done | bytes 65568 | tf_op jit(solution)/shard_map/ppermute | solution.py:135
  27.5 0.1 fusion.101
  27.7 0.8 %fusion.102 = f32[128,128]{1,0:T(8,128)S(1)} fusion(f32[128,128]{1,0:T(8,128)S(1)} %fusion.101, f32[]{:T(128)} %bitcast.6, bf16[528,128]{1,0:T(8,128)(2,1)S(1)} %broadcast_select_fusion.1), kind=kOutput, calls=%fused_computation.120 | convolution fusion | flops 4227072 | bytes 163844 | tf_op jit(solution)/shard_map/dot_general | solution.py:17
  28.5 0.3 convolution_subtract_fusion
  28.8 0.2 fusion.193
  29.0 0.2 collective-permute-done.3
  29.2 0.1 fusion.100
  29.3 1.0 %fusion.13 = f32[128,128]{1,0:T(8,128)S(1)} fusion(f32[128,128]{1,0:T(8,128)S(1)} %fusion.100, f32[]{:T(128)} %bitcast.6, bf16[528,128]{1,0:T(8,128)(2,1)S(1)} %broadcast_select_fusion.1, f32[256,128]{1,0:T(8,128)S(1)} %collective-permute-done, f32[128,256]{1,0:T(8,128)S(1)} %convolution_multiply_fusion.1), kind=kOutput, calls=%fused_computation.33 | convolution fusion | flops 8486912 | bytes 327684 | tf_op jit(solution)/shard_map/dot_general | solution.py:11
  30.3 0.2 convolution_subtract_fusion.1
  30.6 0.1 fusion.175
  30.7 0.3 fusion.176
  31.0 0.3 fusion.179
  31.3 0.3 fusion.7
  31.6 0.2 fusion.194
  31.8 0.2 convolution_subtract_fusion.8
  32.1 0.1 fusion.14
  32.2 2.7 %collective-permute-start.6 = (f32[4,64]{1,0:T(4,128)S(1)}, f32[4,64]{1,0:T(4,128)S(1)}, u32[]{:S(2)}, u32[]{:S(2)}) collective-permute-start(f32[4,64]{1,0:T(4,128)S(1)} %slice_select_fusion), channel_id=1, source_target_pairs={{0,4},{1,5},{2,6},{3,7},{4,0},{5,1},{6,2},{7,3},{8,12},{9,13},{10,... | collective-permute-start | bytes 3080 | tf_op jit(solution)/shard_map/ppermute | solution.py:229
  34.9 1.9 %collective-permute-done.6 = f32[4,64]{1,0:T(4,128)S(1)} collective-permute-done((f32[4,64]{1,0:T(4,128)S(1)}, f32[4,64]{1,0:T(4,128)S(1)}, u32[]{:S(2)}, u32[]{:S(2)}) %collective-permute-start.6) | collective-permute-done | bytes 1056 | tf_op jit(solution)/shard_map/ppermute | solution.py:229
  36.8 1.6 %collective-permute-start.7 = (f32[2,64]{1,0:T(2,128)S(1)}, f32[2,64]{1,0:T(2,128)S(1)}, u32[]{:S(2)}, u32[]{:S(2)}) collective-permute-start(f32[2,64]{1,0:T(2,128)S(1)} %broadcast_select_fusion.4), channel_id=1, source_target_pairs={{0,2},{1,3},{2,0},{3,1},{4,6},{5,7},{6,4},{7,5},{8,10},{9,11},{10,... | collective-permute-start | bytes 1544 | tf_op jit(solution)/shard_map/ppermute | solution.py:229
  38.5 2.0 %collective-permute-done.7 = f32[2,64]{1,0:T(2,128)S(1)} collective-permute-done((f32[2,64]{1,0:T(2,128)S(1)}, f32[2,64]{1,0:T(2,128)S(1)}, u32[]{:S(2)}, u32[]{:S(2)}) %collective-permute-start.7) | collective-permute-done | bytes 544 | tf_op jit(solution)/shard_map/ppermute | solution.py:229
  40.4 0.1 collective-permute-start.8
  40.5 0.8 %copy.27 = f32[128,512]{1,0:T(8,128)} copy(f32[128,512]{0,1:T(8,128)S(1)} %pad_maximum_fusion.3) | data formatting | bytes 524288
  41.4 0.8 %copy.26 = f32[128,512]{1,0:T(8,128)} copy(f32[128,512]{0,1:T(8,128)S(1)} %pad_maximum_fusion.1) | data formatting | bytes 524288
  42.2 0.5 %fusion.150 = f32[64]{0:T(128)} fusion(f32[1,64]{1,0:T(1,128)S(1)} %collective-permute-done.8, pred[]{:T(512)S(6)} %ne.23, f32[2,64]{1,0:T(2,128)S(1)} %select_add_fusion.1), kind=kLoop, calls=%fused_computation.178 | loop fusion | flops 192 | bytes 1025 | tf_op jit(solution)/shard_map/mul | solution.py:231
  (41 shorter events, 0.3 us)
Async XLA Ops:
  0.6 9.7 %copy-start = (bf16[256,512]{1,0:T(8,128)(2,1)S(1)}, bf16[256,512]{1,0:T(8,128)(2,1)}, u32[]{:S(2)}) copy-start(bf16[256,512]{1,0:T(8,128)(2,1)} %param.22) | copy-start | bytes 786436
  0.6 8.5 %copy-start.4 = (bf16[512,512]{1,0:T(8,128)(2,1)S(1)}, bf16[512,512]{1,0:T(8,128)(2,1)}, u32[]{:S(2)}) copy-start(bf16[512,512]{1,0:T(8,128)(2,1)} %param.19) | copy-start | bytes 1572868
  4.6 10.3 %collective-permute-start.1 = (bf16[528,128]{1,0:T(8,128)(2,1)S(1)}, bf16[528,128]{1,0:T(8,128)(2,1)S(1)}, u32[]{:S(2)}, u32[]{:S(2)}) collective-permute-start(bf16[528,128]{1,0:T(8,128)(2,1)S(1)} %constant_dynamic-update-slice_fusion), channel_id=1, source_target_pairs={{0,8},{8,0},{16,24},{24,16},{1,9},{9,1},{17,25},{25,17},{2,10},{10... | collective-permute-start | bytes 405512 | tf_op jit(solution)/shard_map/ppermute | solution.py:153
  9.7 0.6 %copy-start.6 = (f32[128,128]{0,1:T(8,128)}, f32[128,128]{0,1:T(8,128)S(1)}, u32[]{:S(2)}) copy-start(f32[128,128]{0,1:T(8,128)S(1)} %convolution_subtract_fusion.5) | copy-start | bytes 196612
  10.3 0.8 %copy-start.5 = (f32[128,128]{1,0:T(8,128)S(1)}, f32[128,128]{1,0:T(8,128)}, u32[]{:S(2)}) copy-start(f32[128,128]{1,0:T(8,128)} %param.17) | copy-start | bytes 196612
  10.6 2.0 %copy-start.3 = (bf16[512,512]{1,0:T(8,128)(2,1)S(1)}, bf16[512,512]{1,0:T(8,128)(2,1)}, u32[]{:S(2)}) copy-start(bf16[512,512]{1,0:T(8,128)(2,1)} %param.20) | copy-start | bytes 1572868
  10.6 13.4 %collective-permute-start = (f32[256,128]{1,0:T(8,128)S(1)}, f32[256,128]{1,0:T(8,128)S(1)}, u32[]{:S(2)}, u32[]{:S(2)}) collective-permute-start(f32[256,128]{1,0:T(8,128)S(1)} %pad_maximum_fusion.4), channel_id=1, source_target_pairs={{0,8},{8,0},{16,24},{24,16},{1,9},{9,1},{17,25},{25,17},{2,10},{10... | collective-permute-start | bytes 393224 | tf_op jit(solution)/shard_map/ppermute | solution.py:135
  10.7 0.7 %copy-start.9 = (s32[128]{0:T(128)S(1)}, s32[128]{0:T(128)}, u32[]{:S(2)}) copy-start(s32[128]{0:T(128)} %param.16) | copy-start | bytes 1540
  11.4 0.9 %copy-start.2 = (bf16[4,128,128]{2,1,0:T(8,128)(2,1)S(1)}, bf16[4,128,128]{2,1,0:T(8,128)(2,1)}, u32[]{:S(2)}) copy-start(bf16[4,128,128]{2,1,0:T(8,128)(2,1)} %param.21) | copy-start | bytes 393220
  13.2 1.0 %copy-start.1 = (bf16[512,256]{1,0:T(8,128)(2,1)S(1)}, bf16[512,256]{1,0:T(8,128)(2,1)}, u32[]{:S(2)}) copy-start(bf16[512,256]{1,0:T(8,128)(2,1)} %param.23) | copy-start | bytes 786436
  14.2 0.7 %copy-start.8 = (pred[528]{0:T(1024)(128)(4,1)S(1)}, pred[528]{0:T(1024)(128)(4,1)}, u32[]{:S(2)}) copy-start(pred[528]{0:T(1024)(128)(4,1)} %constant.76) | copy-start | bytes 1588
  15.0 5.1 %collective-permute-start.2 = (bf16[528,128]{1,0:T(8,128)(2,1)S(1)}, bf16[528,128]{1,0:T(8,128)(2,1)S(1)}, u32[]{:S(2)}, u32[]{:S(2)}) collective-permute-start(bf16[528,128]{1,0:T(8,128)(2,1)S(1)} %broadcast_select_fusion), channel_id=1, source_target_pairs={{0,16},{8,24},{16,0},{24,8},{1,17},{9,25},{17,1},{25,9},{2,18},{10... | collective-permute-start | bytes 405512 | tf_op jit(solution)/shard_map/ppermute | solution.py:153
  17.1 5.0 %collective-permute-start.4 = (f32[256,128]{1,0:T(8,128)S(1)}, f32[256,128]{1,0:T(8,128)S(1)}, u32[]{:S(2)}, u32[]{:S(2)}) collective-permute-start(f32[256,128]{1,0:T(8,128)S(1)} %pad_maximum_fusion.5), channel_id=1, source_target_pairs={{0,8},{8,0},{16,24},{24,16},{1,9},{9,1},{17,25},{25,17},{2,10},{10... | collective-permute-start | bytes 393224 | tf_op jit(solution)/shard_map/ppermute | solution.py:135
  23.2 4.3 %collective-permute-start.5 = (f32[128,128]{1,0:T(8,128)S(1)}, f32[128,128]{1,0:T(8,128)S(1)}, u32[]{:S(2)}, u32[]{:S(2)}) collective-permute-start(f32[128,128]{1,0:T(8,128)S(1)} %fusion.63), channel_id=1, source_target_pairs={{0,16},{8,24},{16,0},{24,8},{1,17},{9,25},{17,1},{25,9},{2,18},{10... | collective-permute-start | bytes 196616 | tf_op jit(solution)/shard_map/ppermute | solution.py:135
  24.9 4.3 %collective-permute-start.3 = (f32[128,128]{1,0:T(8,128)S(1)}, f32[128,128]{1,0:T(8,128)S(1)}, u32[]{:S(2)}, u32[]{:S(2)}) collective-permute-start(f32[128,128]{1,0:T(8,128)S(1)} %fusion.72), channel_id=1, source_target_pairs={{0,16},{8,24},{16,0},{24,8},{1,17},{9,25},{17,1},{25,9},{2,18},{10... | collective-permute-start | bytes 196616 | tf_op jit(solution)/shard_map/ppermute | solution.py:135
  29.3 1.0 %copy-start.7 = (f32[128,128]{0,1:T(8,128)S(1)}, f32[128,128]{0,1:T(8,128)}, u32[]{:S(2)}) copy-start(f32[128,128]{0,1:T(8,128)} %copy-done.6) | copy-start | bytes 196612
  32.2 4.5 %collective-permute-start.6 = (f32[4,64]{1,0:T(4,128)S(1)}, f32[4,64]{1,0:T(4,128)S(1)}, u32[]{:S(2)}, u32[]{:S(2)}) collective-permute-start(f32[4,64]{1,0:T(4,128)S(1)} %slice_select_fusion), channel_id=1, source_target_pairs={{0,4},{1,5},{2,6},{3,7},{4,0},{5,1},{6,2},{7,3},{8,12},{9,13},{10,... | collective-permute-start | bytes 3080 | tf_op jit(solution)/shard_map/ppermute | solution.py:229
  36.8 3.6 %collective-permute-start.7 = (f32[2,64]{1,0:T(2,128)S(1)}, f32[2,64]{1,0:T(2,128)S(1)}, u32[]{:S(2)}, u32[]{:S(2)}) collective-permute-start(f32[2,64]{1,0:T(2,128)S(1)} %broadcast_select_fusion.4), channel_id=1, source_target_pairs={{0,2},{1,3},{2,0},{3,1},{4,6},{5,7},{6,4},{7,5},{8,10},{9,11},{10,... | collective-permute-start | bytes 1544 | tf_op jit(solution)/shard_map/ppermute | solution.py:229
  40.4 1.8 %collective-permute-start.8 = (f32[1,64]{1,0:T(1,128)S(1)}, f32[1,64]{1,0:T(1,128)S(1)}, u32[]{:S(2)}, u32[]{:S(2)}) collective-permute-start(f32[1,64]{1,0:T(1,128)S(1)} %broadcast_select_fusion.5), channel_id=1, source_target_pairs={{0,1},{1,0},{2,3},{3,2},{4,5},{5,4},{6,7},{7,6},{8,9},{9,8},{10,11... | collective-permute-start | bytes 776 | tf_op jit(solution)/shard_map/ppermute | solution.py:229

commit v14 on v2

--- a/solution.py
+++ b/solution.py
@@ -192,10 +192,20 @@
     forward_field = upper_solve(forward_remain, leaf_upper, leaf_inv, block_size, block_count)
     adjoint_remain = z_leaf - plain_dot(as_half(adjoint_above * base_mask), anc_lower)
     adjoint_field = lower_t_solve(adjoint_remain, leaf_lower, block_size, block_count)
-    partial_gradient = jnp.sum(forward_field * adjoint_field, axis=0)
     spread = lax.axis_size("src")
-    gathered = lax.all_to_all(partial_gradient.reshape(spread, -1), "src", 0, 0, tiled=True)
-    gradient = jnp.sum(gathered, axis=0) * factor
+    product_field = (forward_field * adjoint_field).reshape(source_count, spread, cell_count // spread)
+    partial_gradient = jnp.sum(product_field, axis=0)
+    place = lax.axis_index("src")
+    bit = spread // 2
+    while bit:
+        half = partial_gradient.shape[0] // 2
+        upper = (place & bit) != 0
+        outgoing = jnp.where(upper, partial_gradient[:half], partial_gradient[half:])
+        kept = jnp.where(upper, partial_gradient[half:], partial_gradient[:half])
+        pairs = [(index, index ^ bit) for index in range(spread)]
+        partial_gradient = kept + lax.ppermute(outgoing, "src", pairs)
+        bit //= 2
+    gradient = partial_gradient.reshape(-1) * factor
     return (forward_field, adjoint_field, gradient)
 
 

time: 38.4 us -> 37.2 us (0.969)
  local copies, waits for them, and re-layouts: 6.18 us -> 5.51 us
  starting transfers between devices: 13.2 us -> 12.7 us
    all_to_all x1 -> x0, starting transfers between devices: 4.88 us -> none  [shards(): lax.all_to_all(partial_gradient.reshape(spread, -1), 'src', 0, 0, tiled=T...]
    ppermute x0 -> x3, starting transfers between devices: none -> 4.37 us  [shards(): partial_gradient = kept + lax.ppermute(outgoing, 'src', pairs)]
    all_to_all x1 -> x0, waiting for transfers between devices: 3.89 us -> none  [shards(): lax.all_to_all(partial_gradient.reshape(spread, -1), 'src', 0, 0, tiled=T...]
    ppermute x0 -> x3, waiting for transfers between devices: none -> 3.87 us  [shards(): partial_gradient = kept + lax.ppermute(outgoing, 'src', pairs)]
    all_to_all x1 -> x0, local copies, waits for them, and re-layouts: 0.68 us -> none  [shards(): lax.all_to_all(partial_gradient.reshape(spread, -1), 'src', 0, 0, tiled=T...]
  transfers between devices with their start and end apart: 7 -> 9, of which waited for: 4 -> 5; matrix products, arithmetic and copies ran while one was open for 16% -> 17% of each run, Pallas kernels for 0% -> 0%
where the time goes in v14:
time: 37.2 us; the launch traced here: 36.8 us
  starting transfers between devices  12.7 us (34%)
  waiting for transfers between devices  8.51 us (23%)
  matrix products  6.11 us (16%)
  local copies, waits for them, and re-layouts  5.51 us (15%)
  other arithmetic  3 us (8%)
  between operations  1.02 us (3%)
    ppermute x6, starting transfers between devices, exchange(): incoming = lax.ppermute(jnp.concatenate(pieces, axis=0), 'leaf', pairs)  8.33 us
    ppermute x6, waiting for transfers between devices, exchange(): incoming = lax.ppermute(jnp.concatenate(pieces, axis=0), 'leaf', pairs)  4.64 us
    ppermute x3, starting transfers between devices, shards(): partial_gradient = kept + lax.ppermute(outgoing, 'src', pairs)  4.37 us
    ppermute x3, waiting for transfers between devices, shards(): partial_gradient = kept + lax.ppermute(outgoing, 'src', pairs)  3.87 us
    unnamed x20, local copies, waits for them, and re-layouts  3.53 us
    dot_general x13, matrix products, plain_dot(): return jnp.dot(former, latter, preferred_element_type=jnp.float32)  3.21 us
    dot_general x12, matrix products, across(): lax.dot_general(former, latter, (((1,), (1,)), ((), ())), preferred_eleme...  2.52 us
    mul x1, other arithmetic, shards(): sep_upper[height - 1, :, height * block_size:]  1.43 us
  transfers between devices with their start and end apart: 9, of which 5 were waited for; matrix products, arithmetic and copies ran while one was open for 17% of the time, Pallas kernels for 0%

profile of v14, /device:TPU:0, one launch (start us, length us, event | category | flops | bytes accessed | tf_op | source)
XLA Modules:
  0.0 36.8 jit_solution(15502302321194308480)
XLA Ops:
  0.6 0.0 copy-start
  0.7 0.8 %convert_element_type.101 = f32[3,2]{0,1:T(2,128)S(1)} convert(s32[3,2]{0,1:T(2,128)} %param.15) | non-fusion elementwise | flops 6 | bytes 48 | tf_op jit(solution)/shard_map/convert_element_type | solution.py:97
  1.4 0.2 slice_reduce_fusion
  1.6 0.6 %slice.199 = bf16[1]{0:T(256)(128)(2,1)} slice(bf16[2]{0:T(256)(128)(2,1)S(1)} %compare_select_fusion), slice={[1:2]} | slice | bytes 4 | tf_op jit(solution)/shard_map/slice | solution.py:121
  2.2 0.8 %slice_bitcast_fusion.1 = (bf16[128,128]{1,0:T(8,128)(2,1)S(1)}, bf16[128,128]{1,0:T(8,128)(2,1)S(1)}) fusion(bf16[2,128,128]{2,1,0:T(8,128)(2,1)} %param.21), kind=kLoop, calls=%fused_computation.139 | loop fusion | bytes 131072 | tf_op jit(solution)/shard_map/squeeze | solution.py:124
  3.0 1.4 %multiply_bitcast_fusion = (bf16[128,128]{1,0:T(8,128)(2,1)S(1)}, bf16[128,128]{1,0:T(8,128)(2,1)S(1)}) fusion(bf16[2,128,256]{2,1,0:T(8,128)(2,1)} %param.23, bf16[]{:T(256)} %bitcast.1, bf16[2,256,128]{2,1,0:T(8,128)(2,1)} %param.22), kind=kLoop, calls=%fused_computation.140 | loop fusion | flops 32768 | bytes 131074 | tf_op jit(solution)/shard_map/mul | solution.py:123
  4.4 3.0 %collective-permute-start.1 = (bf16[512,128]{1,0:T(8,128)(2,1)S(1)}, bf16[512,128]{1,0:T(8,128)(2,1)S(1)}, u32[]{:S(2)}, u32[]{:S(2)}) collective-permute-start(bf16[512,128]{1,0:T(8,128)(2,1)S(1)} %pad_maximum_fusion.5), channel_id=1, source_target_pairs={{0,8},{8,0},{16,24},{24,16},{1,9},{9,1},{17,25},{25,17},{2,10},{10... | collective-permute-start | bytes 393224 | tf_op jit(solution)/shard_map/ppermute | solution.py:128
  7.4 0.7 %copy-done.8 = s32[128]{0:T(128)S(1)} copy-done((s32[128]{0:T(128)S(1)}, s32[128]{0:T(128)}, u32[]{:S(2)}) %copy-start.8) | copy-done | bytes 536
  8.2 0.1 broadcast_bitcast_fusion
  8.2 0.1 fusion.166
  8.4 0.1 fusion.167
  8.5 0.2 convolution_subtract_fusion.5
  8.7 0.0 copy-start.6
  8.7 0.2 convolution_multiply_fusion.1
  9.0 0.0 copy-start.4
  9.0 0.0 copy-start.7
  9.0 0.0 copy-start.3
  9.0 0.1 collective-permute-start
  9.1 0.4 %copy-done.6 = f32[128,128]{1,0:T(8,128)S(1)} copy-done((f32[128,128]{1,0:T(8,128)S(1)}, f32[128,128]{1,0:T(8,128)}, u32[]{:S(2)}) %copy-start.6) | copy-done | bytes 65560
  9.6 0.2 copy-done.7
  9.7 0.4 %convolution_bitcast_fusion = f32[128,512]{0,1:T(8,128)S(1)} fusion(f32[128,128]{1,0:T(8,128)S(1)} %copy-done.6, s32[128]{0:T(128)S(1)} %copy-done.7), kind=kOutput, calls=%fused_computation.2 | convolution fusion | flops 100794368 | bytes 328192 | tf_op jit(solution)/shard_map/dot_general | solution.py:111
  10.1 0.2 fusion.177
  10.3 0.3 fusion.178
  10.7 0.4 fusion.181
  11.0 0.0 copy-start.1
  11.1 0.4 fusion.10
  11.4 0.6 %copy-done.1 = bf16[512,256]{1,0:T(8,128)(2,1)S(1)} copy-done((bf16[512,256]{1,0:T(8,128)(2,1)S(1)}, bf16[512,256]{1,0:T(8,128)(2,1)}, u32[]{:S(2)}) %copy-start.1) | copy-done | bytes 262168
  12.0 0.2 convolution_multiply_fusion
  12.2 0.0 copy-start.2
  12.3 1.5 %collective-permute-start.4 = (f32[256,128]{1,0:T(8,128)S(1)}, f32[256,128]{1,0:T(8,128)S(1)}, u32[]{:S(2)}, u32[]{:S(2)}) collective-permute-start(f32[256,128]{1,0:T(8,128)S(1)} %pad_maximum_fusion.6), channel_id=1, source_target_pairs={{0,8},{8,0},{16,24},{24,16},{1,9},{9,1},{17,25},{25,17},{2,10},{10... | collective-permute-start | bytes 393224 | tf_op jit(solution)/shard_map/ppermute | solution.py:128
  13.8 1.6 %collective-permute-start.3 = (bf16[128,128]{1,0:T(8,128)(2,1)S(1)}, bf16[128,128]{1,0:T(8,128)(2,1)S(1)}, u32[]{:S(2)}, u32[]{:S(2)}) collective-permute-start(bf16[128,128]{1,0:T(8,128)(2,1)S(1)} %slice_select_fusion.2), channel_id=1, source_target_pairs={{0,16},{8,24},{16,0},{24,8},{1,17},{9,25},{17,1},{25,9},{2,18},{10... | collective-permute-start | bytes 98312 | tf_op jit(solution)/shard_map/ppermute | solution.py:128
  15.4 1.9 %collective-permute-done.4 = f32[256,128]{1,0:T(8,128)S(1)} collective-permute-done((f32[256,128]{1,0:T(8,128)S(1)}, f32[256,128]{1,0:T(8,128)S(1)}, u32[]{:S(2)}, u32[]{:S(2)}) %collective-permute-start.4) | collective-permute-done | bytes 131104 | tf_op jit(solution)/shard_map/ppermute | solution.py:128
  17.3 0.2 fusion.104
  17.5 0.2 fusion.63
  17.7 1.6 %collective-permute-start.5 = (f32[128,128]{1,0:T(8,128)S(1)}, f32[128,128]{1,0:T(8,128)S(1)}, u32[]{:S(2)}, u32[]{:S(2)}) collective-permute-start(f32[128,128]{1,0:T(8,128)S(1)} %fusion.63), channel_id=1, source_target_pairs={{0,16},{8,24},{16,0},{24,8},{1,17},{9,25},{17,1},{25,9},{2,18},{10... | collective-permute-start | bytes 196616 | tf_op jit(solution)/shard_map/ppermute | solution.py:128
  19.3 0.2 fusion.72
  19.5 0.1 copy.17
  19.6 0.6 %collective-permute-start.2 = (f32[128,128]{1,0:T(8,128)S(1)}, f32[128,128]{1,0:T(8,128)S(1)}, u32[]{:S(2)}, u32[]{:S(2)}) collective-permute-start(f32[128,128]{1,0:T(8,128)S(1)} %fusion.72), channel_id=1, source_target_pairs={{0,16},{8,24},{16,0},{24,8},{1,17},{9,25},{17,1},{25,9},{2,18},{10... | collective-permute-start | bytes 196616 | tf_op jit(solution)/shard_map/ppermute | solution.py:128
  20.1 1.9 %collective-permute-done.5 = f32[128,128]{1,0:T(8,128)S(1)} collective-permute-done((f32[128,128]{1,0:T(8,128)S(1)}, f32[128,128]{1,0:T(8,128)S(1)}, u32[]{:S(2)}, u32[]{:S(2)}) %collective-permute-start.5) | collective-permute-done | bytes 65568 | tf_op jit(solution)/shard_map/ppermute | solution.py:128
  22.0 0.2 fusion.101
  22.3 0.1 copy.18
  22.4 0.2 fusion.115
  22.6 0.3 convolution_subtract_fusion
  22.9 0.2 fusion.186
  23.1 0.8 %collective-permute-done.2 = f32[128,128]{1,0:T(8,128)S(1)} collective-permute-done((f32[128,128]{1,0:T(8,128)S(1)}, f32[128,128]{1,0:T(8,128)S(1)}, u32[]{:S(2)}, u32[]{:S(2)}) %collective-permute-start.2) | collective-permute-done | bytes 65568 | tf_op jit(solution)/shard_map/ppermute | solution.py:128
  23.9 0.1 fusion.100
  24.0 0.1 copy.15
  24.1 0.3 fusion.13
  24.5 0.2 convolution_subtract_fusion.1
  24.7 0.1 fusion.168
  24.8 0.3 fusion.169
  25.1 0.3 fusion.172
  25.4 0.3 fusion.7
  25.7 0.2 fusion.187
  25.9 0.2 convolution_subtract_fusion.8
  26.2 0.1 fusion.14
  26.3 2.7 %collective-permute-start.6 = (f32[4,64]{1,0:T(4,128)S(1)}, f32[4,64]{1,0:T(4,128)S(1)}, u32[]{:S(2)}, u32[]{:S(2)}) collective-permute-start(f32[4,64]{1,0:T(4,128)S(1)} %slice_select_fusion.11), channel_id=1, source_target_pairs={{0,4},{1,5},{2,6},{3,7},{4,0},{5,1},{6,2},{7,3},{8,12},{9,13},{10,... | collective-permute-start | bytes 3080 | tf_op jit(solution)/shard_map/ppermute | solution.py:206
  29.0 1.9 %collective-permute-done.6 = f32[4,64]{1,0:T(4,128)S(1)} collective-permute-done((f32[4,64]{1,0:T(4,128)S(1)}, f32[4,64]{1,0:T(4,128)S(1)}, u32[]{:S(2)}, u32[]{:S(2)}) %collective-permute-start.6) | collective-permute-done | bytes 1056 | tf_op jit(solution)/shard_map/ppermute | solution.py:206
  30.9 1.6 %collective-permute-start.7 = (f32[2,64]{1,0:T(2,128)S(1)}, f32[2,64]{1,0:T(2,128)S(1)}, u32[]{:S(2)}, u32[]{:S(2)}) collective-permute-start(f32[2,64]{1,0:T(2,128)S(1)} %broadcast_select_fusion.3), channel_id=1, source_target_pairs={{0,2},{1,3},{2,0},{3,1},{4,6},{5,7},{6,4},{7,5},{8,10},{9,11},{10,... | collective-permute-start | bytes 1544 | tf_op jit(solution)/shard_map/ppermute | solution.py:206
  32.6 2.0 %collective-permute-done.7 = f32[2,64]{1,0:T(2,128)S(1)} collective-permute-done((f32[2,64]{1,0:T(2,128)S(1)}, f32[2,64]{1,0:T(2,128)S(1)}, u32[]{:S(2)}, u32[]{:S(2)}) %collective-permute-start.7) | collective-permute-done | bytes 544 | tf_op jit(solution)/shard_map/ppermute | solution.py:206
  34.5 0.1 collective-permute-start.8
  34.7 0.8 %copy.21 = f32[128,512]{1,0:T(8,128)} copy(f32[128,512]{0,1:T(8,128)S(1)} %pad_maximum_fusion.3) | data formatting | bytes 524288
  35.5 0.8 %copy.20 = f32[128,512]{1,0:T(8,128)} copy(f32[128,512]{0,1:T(8,128)S(1)} %pad_maximum_fusion.1) | data formatting | bytes 524288
  36.3 0.5 %fusion.144 = f32[64]{0:T(128)} fusion(f32[1,64]{1,0:T(1,128)S(1)} %collective-permute-done.8, pred[]{:T(512)S(6)} %ne.23, f32[2,64]{1,0:T(2,128)S(1)} %select_add_fusion.1), kind=kLoop, calls=%fused_computation.167 | loop fusion | flops 192 | bytes 1025 | tf_op jit(solution)/shard_map/mul | solution.py:208
  (33 shorter events, 0.2 us)
Async XLA Ops:
  0.6 8.1 %copy-start = (bf16[256,512]{1,0:T(8,128)(2,1)S(1)}, bf16[256,512]{1,0:T(8,128)(2,1)}, u32[]{:S(2)}) copy-start(bf16[256,512]{1,0:T(8,128)(2,1)} %param.19) | copy-start | bytes 786436
  0.6 7.6 %copy-start.5 = (bf16[512,512]{1,0:T(8,128)(2,1)S(1)}, bf16[512,512]{1,0:T(8,128)(2,1)}, u32[]{:S(2)}) copy-start(bf16[512,512]{1,0:T(8,128)(2,1)} %param.16) | copy-start | bytes 1572868
  4.4 9.4 %collective-permute-start.1 = (bf16[512,128]{1,0:T(8,128)(2,1)S(1)}, bf16[512,128]{1,0:T(8,128)(2,1)S(1)}, u32[]{:S(2)}, u32[]{:S(2)}) collective-permute-start(bf16[512,128]{1,0:T(8,128)(2,1)S(1)} %pad_maximum_fusion.5), channel_id=1, source_target_pairs={{0,8},{8,0},{16,24},{24,16},{1,9},{9,1},{17,25},{25,17},{2,10},{10... | collective-permute-start | bytes 393224 | tf_op jit(solution)/shard_map/ppermute | solution.py:128
  7.4 0.7 %copy-start.8 = (s32[128]{0:T(128)S(1)}, s32[128]{0:T(128)}, u32[]{:S(2)}) copy-start(s32[128]{0:T(128)} %param.12) | copy-start | bytes 1540
  8.7 0.8 %copy-start.6 = (f32[128,128]{1,0:T(8,128)S(1)}, f32[128,128]{1,0:T(8,128)}, u32[]{:S(2)}) copy-start(f32[128,128]{1,0:T(8,128)} %param.14) | copy-start | bytes 196612
  9.0 1.4 %copy-start.4 = (bf16[512,512]{1,0:T(8,128)(2,1)S(1)}, bf16[512,512]{1,0:T(8,128)(2,1)}, u32[]{:S(2)}) copy-start(bf16[512,512]{1,0:T(8,128)(2,1)} %param.17) | copy-start | bytes 1572868
  9.0 0.7 %copy-start.7 = (s32[128]{0:T(128)S(1)}, s32[128]{0:T(128)}, u32[]{:S(2)}) copy-start(s32[128]{0:T(128)} %param.13) | copy-start | bytes 1540
  9.0 1.1 %copy-start.3 = (bf16[4,128,128]{2,1,0:T(8,128)(2,1)S(1)}, bf16[4,128,128]{2,1,0:T(8,128)(2,1)}, u32[]{:S(2)}) copy-start(bf16[4,128,128]{2,1,0:T(8,128)(2,1)} %param.18) | copy-start | bytes 393220
  9.0 10.3 %collective-permute-start = (f32[256,128]{1,0:T(8,128)S(1)}, f32[256,128]{1,0:T(8,128)S(1)}, u32[]{:S(2)}, u32[]{:S(2)}) collective-permute-start(f32[256,128]{1,0:T(8,128)S(1)} %pad_maximum_fusion.4), channel_id=1, source_target_pairs={{0,8},{8,0},{16,24},{24,16},{1,9},{9,1},{17,25},{25,17},{2,10},{10... | collective-permute-start | bytes 393224 | tf_op jit(solution)/shard_map/ppermute | solution.py:128
  11.0 1.0 %copy-start.1 = (bf16[512,256]{1,0:T(8,128)(2,1)S(1)}, bf16[512,256]{1,0:T(8,128)(2,1)}, u32[]{:S(2)}) copy-start(bf16[512,256]{1,0:T(8,128)(2,1)} %param.20) | copy-start | bytes 786436
  12.2 1.5 %copy-start.2 = (bf16[2,128,128]{2,1,0:T(8,128)(2,1)S(1)}, bf16[2,128,128]{2,1,0:T(8,128)(2,1)}, u32[]{:S(2)}) copy-start(bf16[2,128,128]{2,1,0:T(8,128)(2,1)} %param.21) | copy-start | bytes 196612
  12.3 5.0 %collective-permute-start.4 = (f32[256,128]{1,0:T(8,128)S(1)}, f32[256,128]{1,0:T(8,128)S(1)}, u32[]{:S(2)}, u32[]{:S(2)}) collective-permute-start(f32[256,128]{1,0:T(8,128)S(1)} %pad_maximum_fusion.6), channel_id=1, source_target_pairs={{0,8},{8,0},{16,24},{24,16},{1,9},{9,1},{17,25},{25,17},{2,10},{10... | collective-permute-start | bytes 393224 | tf_op jit(solution)/shard_map/ppermute | solution.py:128
  13.8 6.3 %collective-permute-start.3 = (bf16[128,128]{1,0:T(8,128)(2,1)S(1)}, bf16[128,128]{1,0:T(8,128)(2,1)S(1)}, u32[]{:S(2)}, u32[]{:S(2)}) collective-permute-start(bf16[128,128]{1,0:T(8,128)(2,1)S(1)} %slice_select_fusion.2), channel_id=1, source_target_pairs={{0,16},{8,24},{16,0},{24,8},{1,17},{9,25},{17,1},{25,9},{2,18},{10... | collective-permute-start | bytes 98312 | tf_op jit(solution)/shard_map/ppermute | solution.py:128
  17.7 4.3 %collective-permute-start.5 = (f32[128,128]{1,0:T(8,128)S(1)}, f32[128,128]{1,0:T(8,128)S(1)}, u32[]{:S(2)}, u32[]{:S(2)}) collective-permute-start(f32[128,128]{1,0:T(8,128)S(1)} %fusion.63), channel_id=1, source_target_pairs={{0,16},{8,24},{16,0},{24,8},{1,17},{9,25},{17,1},{25,9},{2,18},{10... | collective-permute-start | bytes 196616 | tf_op jit(solution)/shard_map/ppermute | solution.py:128
  19.6 4.3 %collective-permute-start.2 = (f32[128,128]{1,0:T(8,128)S(1)}, f32[128,128]{1,0:T(8,128)S(1)}, u32[]{:S(2)}, u32[]{:S(2)}) collective-permute-start(f32[128,128]{1,0:T(8,128)S(1)} %fusion.72), channel_id=1, source_target_pairs={{0,16},{8,24},{16,0},{24,8},{1,17},{9,25},{17,1},{25,9},{2,18},{10... | collective-permute-start | bytes 196616 | tf_op jit(solution)/shard_map/ppermute | solution.py:128
  26.3 4.5 %collective-permute-start.6 = (f32[4,64]{1,0:T(4,128)S(1)}, f32[4,64]{1,0:T(4,128)S(1)}, u32[]{:S(2)}, u32[]{:S(2)}) collective-permute-start(f32[4,64]{1,0:T(4,128)S(1)} %slice_select_fusion.11), channel_id=1, source_target_pairs={{0,4},{1,5},{2,6},{3,7},{4,0},{5,1},{6,2},{7,3},{8,12},{9,13},{10,... | collective-permute-start | bytes 3080 | tf_op jit(solution)/shard_map/ppermute | solution.py:206
  30.9 3.6 %collective-permute-start.7 = (f32[2,64]{1,0:T(2,128)S(1)}, f32[2,64]{1,0:T(2,128)S(1)}, u32[]{:S(2)}, u32[]{:S(2)}) collective-permute-start(f32[2,64]{1,0:T(2,128)S(1)} %broadcast_select_fusion.3), channel_id=1, source_target_pairs={{0,2},{1,3},{2,0},{3,1},{4,6},{5,7},{6,4},{7,5},{8,10},{9,11},{10,... | collective-permute-start | bytes 1544 | tf_op jit(solution)/shard_map/ppermute | solution.py:206
  34.5 1.8 %collective-permute-start.8 = (f32[1,64]{1,0:T(1,128)S(1)}, f32[1,64]{1,0:T(1,128)S(1)}, u32[]{:S(2)}, u32[]{:S(2)}) collective-permute-start(f32[1,64]{1,0:T(1,128)S(1)} %broadcast_select_fusion.4), channel_id=1, source_target_pairs={{0,1},{1,0},{2,3},{3,2},{4,5},{5,4},{6,7},{7,6},{8,9},{9,8},{10,11... | collective-permute-start | bytes 776 | tf_op jit(solution)/shard_map/ppermute | solution.py:206

commit v15 on v14

--- a/solution.py
+++ b/solution.py
@@ -94,11 +94,12 @@
     cell_count = leaf_lower.shape[1]
     source_count = src_cells.shape[0]
     factor = 1.0 / math.sqrt(source_count * lax.axis_size("src"))
-    present = pattern.astype(jnp.float32)
-
     def level_mask(height):
-        level_row = present[height] * (jnp.arange(1, levels + 1) > height).astype(jnp.float32)
+        level_row = jnp.logical_and(pattern[height] != 0, jnp.arange(1, levels + 1) > height)
         return jnp.repeat(level_row, block_size)
+
+    def masked(values, keep):
+        return jnp.where(keep, values, jnp.zeros_like(values))
 
     def blocks_of(values):
         return [values[:, k * block_size : (k + 1) * block_size] for k in range(values.shape[1] // block_size)]
@@ -113,14 +114,14 @@
     base_mask = level_mask(0)
     y_leaf = lower_solve(forcing, leaf_lower, block_size, block_count)
     z_leaf = upper_t_solve(adjoint_rhs, leaf_upper, leaf_inv, block_size, block_count)
-    forward_sums = blocks_of(across(as_half(y_leaf), anc_lower) * base_mask)
-    adjoint_sums = blocks_of(plain_dot(as_half(z_leaf), anc_upper) * base_mask)
+    forward_sums = blocks_of(masked(across(as_half(y_leaf), anc_lower), base_mask))
+    adjoint_sums = blocks_of(masked(plain_dot(as_half(z_leaf), anc_upper), base_mask))
 
     lower_panels, upper_panels, inverse_panels = [], [], []
     for height in range(1, levels + 1):
         mask = level_mask(height)[height * block_size :]
-        lower_panels.append(sep_lower[height - 1, height * block_size :, :] * mask[:, None].astype(jnp.bfloat16))
-        upper_panels.append(sep_upper[height - 1, :, height * block_size :] * mask[None, :].astype(jnp.bfloat16))
+        lower_panels.append(masked(sep_lower[height - 1, height * block_size :, :], mask[:, None]))
+        upper_panels.append(masked(sep_upper[height - 1, :, height * block_size :], mask[None, :]))
         inverse_panels.append(sep_inv[height - 1])
 
     def exchange(values, pairs):
@@ -188,9 +189,9 @@
     forward_above = jnp.concatenate(forward_above, axis=1)
     adjoint_above = jnp.concatenate(adjoint_above, axis=1)
 
-    forward_remain = y_leaf - across(as_half(forward_above * base_mask), anc_upper)
+    forward_remain = y_leaf - across(as_half(masked(forward_above, base_mask)), anc_upper)
     forward_field = upper_solve(forward_remain, leaf_upper, leaf_inv, block_size, block_count)
-    adjoint_remain = z_leaf - plain_dot(as_half(adjoint_above * base_mask), anc_lower)
+    adjoint_remain = z_leaf - plain_dot(as_half(masked(adjoint_above, base_mask)), anc_lower)
     adjoint_field = lower_t_solve(adjoint_remain, leaf_lower, block_size, block_count)
     spread = lax.axis_size("src")
     product_field = (forward_field * adjoint_field).reshape(source_count, spread, cell_count // spread)

time: 37.2 us -> 36.9 us (level)
  matrix products: 6.11 us -> 7.83 us
  local copies, waits for them, and re-layouts: 5.51 us -> 4.12 us
  other arithmetic: 3 us -> 2.44 us
  waiting for transfers between devices: 8.51 us -> 7.97 us
  starting transfers between devices: 12.7 us -> 13.1 us
    mul x3 -> x0, other arithmetic: 1.44 us -> none  [the longest x1 1.43 us: shards(): sep_upper[height - 1, :, height * block_size:]]
    select_n x0 -> x1, other arithmetic: none -> 1.43 us  [masked(): return jnp.where(keep, values, jnp.zeros_like(values))]
    dot_general x1, matrix products: 0.38 us -> 1.31 us  [shards(): jnp.dot(residual, receiver_hits, precision=lax.Precision.HIGHEST)]
    squeeze x1, local copies, waits for them, and re-layouts: 0.78 us -> 0.01 us  [shards(): inverse_panels.append(sep_inv[height - 1])]
    dot_general x13, matrix products: 3.21 us -> 3.98 us  [plain_dot(): return jnp.dot(former, latter, preferred_element_type=jnp.float32)]
    convert_element_type x1 -> x0, other arithmetic: 0.75 us -> none  [shards(): present = pattern.astype(jnp.float32)]
    ppermute x6, waiting for transfers between devices: 4.64 us -> 4.05 us  [exchange(): incoming = lax.ppermute(jnp.concatenate(pieces, axis=0), 'leaf', pairs)]
    ppermute x6, starting transfers between devices: 8.33 us -> 8.81 us  [exchange(): incoming = lax.ppermute(jnp.concatenate(pieces, axis=0), 'leaf', pairs)]
  transfers between devices with their start and end apart: 9 -> 9, of which waited for: 5 -> 4; matrix products, arithmetic and copies ran while one was open for 17% -> 18% of each run, Pallas kernels for 0% -> 0%
where the time goes in v15:
time: 36.9 us; the launch traced here: 36.5 us
  starting transfers between devices  13.1 us (36%)
  waiting for transfers between devices  7.97 us (22%)
  matrix products  7.83 us (21%)
  local copies, waits for them, and re-layouts  4.12 us (11%)
  other arithmetic  2.44 us (7%)
  between operations  1.03 us (3%)
    ppermute x6, starting transfers between devices, exchange(): incoming = lax.ppermute(jnp.concatenate(pieces, axis=0), 'leaf', pairs)  8.81 us
    ppermute x3, starting transfers between devices, shards(): partial_gradient = kept + lax.ppermute(outgoing, 'src', pairs)  4.32 us
    ppermute x6, waiting for transfers between devices, exchange(): incoming = lax.ppermute(jnp.concatenate(pieces, axis=0), 'leaf', pairs)  4.05 us
    dot_general x13, matrix products, plain_dot(): return jnp.dot(former, latter, preferred_element_type=jnp.float32)  3.98 us
    ppermute x3, waiting for transfers between devices, shards(): partial_gradient = kept + lax.ppermute(outgoing, 'src', pairs)  3.92 us
    unnamed x20, local copies, waits for them, and re-layouts  3.05 us
    dot_general x12, matrix products, across(): lax.dot_general(former, latter, (((1,), (1,)), ((), ())), preferred_eleme...  2.54 us
    select_n x1, other arithmetic, masked(): return jnp.where(keep, values, jnp.zeros_like(values))  1.43 us
  transfers between devices with their start and end apart: 9, of which 4 were waited for; matrix products, arithmetic and copies ran while one was open for 18% of the time, Pallas kernels for 0%

profile of v15, /device:TPU:0, one launch (start us, length us, event | category | flops | bytes accessed | tf_op | source)
XLA Modules:
  0.0 36.5 jit_solution(10820312538429912757)
XLA Ops:
  0.6 0.0 copy-start
  0.7 0.0 copy-start.3
  0.7 1.3 %convolution_bitcast_fusion = f32[128,512]{0,1:T(8,128)S(1)} fusion(f32[128,128]{1,0:T(8,128)} %param.14, s32[128]{0:T(128)} %param.13), kind=kOutput, calls=%fused_computation.2 | convolution fusion | flops 100794368 | bytes 328192 | tf_op jit(solution)/shard_map/dot_general | solution.py:112
  2.0 0.2 fusion.181
  2.2 1.1 %fusion.182 = (bf16[128,128]{0,1:T(8,128)(2,1)S(1)}, f32[128,128]{0,1:T(8,128)S(1)}) fusion(bf16[4,128,128]{2,1,0:T(8,128)(2,1)S(1)} %copy-done.2, bf16[128,128]{0,1:T(8,128)(2,1)S(1)} %get-tuple-element.24, f32[128,512]{0,1:T(8,128)S(1)} %convolution_bitcast_fusion, bf16[512,512]{1,0:T(8,128)(2,1)} %param.17), kind=kOutput, calls=%fused_computation.199 | convolution fusion | flops 8437760 | bytes 262144 | tf_op jit(solution)/shard_map/dot_general | solution.py:16
  3.3 0.4 fusion.185
  3.7 0.0 copy-start.6
  3.7 0.0 copy-start.5
  3.7 0.4 fusion.10
  4.1 0.3 copy-done.5
  4.4 0.2 compare_reduce_fusion
  4.6 0.1 broadcast_bitcast_fusion
  4.7 0.2 convolution_select_fusion
  5.0 0.0 copy-start.1
  5.0 0.0 copy-start.4
  5.0 3.0 %collective-permute-start.4 = (f32[256,128]{1,0:T(8,128)S(1)}, f32[256,128]{1,0:T(8,128)S(1)}, u32[]{:S(2)}, u32[]{:S(2)}) collective-permute-start(f32[256,128]{1,0:T(8,128)S(1)} %pad_maximum_fusion.6), channel_id=1, source_target_pairs={{0,8},{8,0},{16,24},{24,16},{1,9},{9,1},{17,25},{25,17},{2,10},{10... | collective-permute-start | bytes 393224 | tf_op jit(solution)/shard_map/ppermute | solution.py:129
  8.0 0.6 %slice.198 = pred[1]{0:T(512)(128)(4,1)} slice(pred[2]{0:T(512)(128)(4,1)S(1)} %compare_and_fusion), slice={[1:2]} | slice | bytes 2 | tf_op jit(solution)/shard_map/slice | solution.py:122
  8.6 1.4 %select_bitcast_fusion = (bf16[128,128]{1,0:T(8,128)(2,1)S(1)}, bf16[128,128]{1,0:T(8,128)(2,1)S(1)}) fusion(bf16[2,128,256]{2,1,0:T(8,128)(2,1)} %param.23, pred[]{:T(512)} %bitcast.1, bf16[2,256,128]{2,1,0:T(8,128)(2,1)} %param.22), kind=kLoop, calls=%fused_computation.142 | loop fusion | flops 32768 | bytes 131073 | tf_op jit(solution)/shard_map/jit(_where)/select_n | solution.py:102
  10.1 0.2 collective-permute-start.1
  10.3 0.7 %copy-done.8 = s32[128]{0:T(128)S(1)} copy-done((s32[128]{0:T(128)S(1)}, s32[128]{0:T(128)}, u32[]{:S(2)}) %copy-start.8) | copy-done | bytes 536
  11.0 0.1 fusion.170
  11.1 0.1 fusion.171
  11.3 0.2 convolution_subtract_fusion.5
  11.5 0.2 convolution_select_fusion.1
  11.8 2.0 %collective-permute-start = (f32[256,128]{1,0:T(8,128)S(1)}, f32[256,128]{1,0:T(8,128)S(1)}, u32[]{:S(2)}, u32[]{:S(2)}) collective-permute-start(f32[256,128]{1,0:T(8,128)S(1)} %pad_maximum_fusion.4), channel_id=1, source_target_pairs={{0,8},{8,0},{16,24},{24,16},{1,9},{9,1},{17,25},{25,17},{2,10},{10... | collective-permute-start | bytes 393224 | tf_op jit(solution)/shard_map/ppermute | solution.py:129
  13.7 0.0 collective-permute-done.4
  13.7 2.5 %collective-permute-done.1 = bf16[512,128]{1,0:T(8,128)(2,1)S(1)} collective-permute-done((bf16[512,128]{1,0:T(8,128)(2,1)S(1)}, bf16[512,128]{1,0:T(8,128)(2,1)S(1)}, u32[]{:S(2)}, u32[]{:S(2)}) %collective-permute-start.1) | collective-permute-done | bytes 131104 | tf_op jit(solution)/shard_map/ppermute | solution.py:129
  16.2 0.2 fusion.106
  16.4 0.2 fusion.63
  16.6 1.6 %collective-permute-start.5 = (f32[128,128]{1,0:T(8,128)S(1)}, f32[128,128]{1,0:T(8,128)S(1)}, u32[]{:S(2)}, u32[]{:S(2)}) collective-permute-start(f32[128,128]{1,0:T(8,128)S(1)} %fusion.63), channel_id=1, source_target_pairs={{0,16},{8,24},{16,0},{24,8},{1,17},{9,25},{17,1},{25,9},{2,18},{10... | collective-permute-start | bytes 196616 | tf_op jit(solution)/shard_map/ppermute | solution.py:129
  18.2 0.5 %collective-permute-start.3 = (bf16[128,128]{1,0:T(8,128)(2,1)S(1)}, bf16[128,128]{1,0:T(8,128)(2,1)S(1)}, u32[]{:S(2)}, u32[]{:S(2)}) collective-permute-start(bf16[128,128]{1,0:T(8,128)(2,1)S(1)} %slice_select_fusion.2), channel_id=1, source_target_pairs={{0,16},{8,24},{16,0},{24,8},{1,17},{9,25},{17,1},{25,9},{2,18},{10... | collective-permute-start | bytes 98312 | tf_op jit(solution)/shard_map/ppermute | solution.py:129
  18.7 0.0 collective-permute-done
  18.7 0.2 fusion.72
  18.9 0.1 copy.17
  19.0 1.6 %collective-permute-start.2 = (f32[128,128]{1,0:T(8,128)S(1)}, f32[128,128]{1,0:T(8,128)S(1)}, u32[]{:S(2)}, u32[]{:S(2)}) collective-permute-start(f32[128,128]{1,0:T(8,128)S(1)} %fusion.72), channel_id=1, source_target_pairs={{0,16},{8,24},{16,0},{24,8},{1,17},{9,25},{17,1},{25,9},{2,18},{10... | collective-permute-start | bytes 196616 | tf_op jit(solution)/shard_map/ppermute | solution.py:129
  20.5 1.6 %collective-permute-done.3 = bf16[128,128]{1,0:T(8,128)(2,1)S(1)} collective-permute-done((bf16[128,128]{1,0:T(8,128)(2,1)S(1)}, bf16[128,128]{1,0:T(8,128)(2,1)S(1)}, u32[]{:S(2)}, u32[]{:S(2)}) %collective-permute-start.3) | collective-permute-done | bytes 32800 | tf_op jit(solution)/shard_map/ppermute | solution.py:129
  22.1 0.0 collective-permute-done.5
  22.1 0.2 fusion.103
  22.3 0.1 copy.18
  22.4 0.2 fusion.117
  22.6 0.3 convolution_subtract_fusion
  22.9 0.2 fusion.190
  23.2 0.2 fusion.191
  23.4 0.2 convolution_subtract_fusion.8
  23.6 0.0 copy-start.7
  23.6 0.0 collective-permute-done.2
  23.7 0.1 fusion.102
  23.8 0.1 copy.15
  23.9 0.3 fusion.13
  24.3 0.3 copy-done.7
  24.6 0.2 convolution_subtract_fusion.1
  24.8 0.1 fusion.172
  24.9 0.3 fusion.173
  25.2 0.3 fusion.176
  25.5 0.3 fusion.7
  25.9 0.1 fusion.14
  26.0 2.6 %collective-permute-start.6 = (f32[4,64]{1,0:T(4,128)S(1)}, f32[4,64]{1,0:T(4,128)S(1)}, u32[]{:S(2)}, u32[]{:S(2)}) collective-permute-start(f32[4,64]{1,0:T(4,128)S(1)} %slice_select_fusion.11), channel_id=1, source_target_pairs={{0,4},{1,5},{2,6},{3,7},{4,0},{5,1},{6,2},{7,3},{8,12},{9,13},{10,... | collective-permute-start | bytes 3080 | tf_op jit(solution)/shard_map/ppermute | solution.py:207
  28.6 1.9 %collective-permute-done.6 = f32[4,64]{1,0:T(4,128)S(1)} collective-permute-done((f32[4,64]{1,0:T(4,128)S(1)}, f32[4,64]{1,0:T(4,128)S(1)}, u32[]{:S(2)}, u32[]{:S(2)}) %collective-permute-start.6) | collective-permute-done | bytes 1056 | tf_op jit(solution)/shard_map/ppermute | solution.py:207
  30.6 1.6 %collective-permute-start.7 = (f32[2,64]{1,0:T(2,128)S(1)}, f32[2,64]{1,0:T(2,128)S(1)}, u32[]{:S(2)}, u32[]{:S(2)}) collective-permute-start(f32[2,64]{1,0:T(2,128)S(1)} %broadcast_select_fusion.3), channel_id=1, source_target_pairs={{0,2},{1,3},{2,0},{3,1},{4,6},{5,7},{6,4},{7,5},{8,10},{9,11},{10,... | collective-permute-start | bytes 1544 | tf_op jit(solution)/shard_map/ppermute | solution.py:207
  32.2 2.0 %collective-permute-done.7 = f32[2,64]{1,0:T(2,128)S(1)} collective-permute-done((f32[2,64]{1,0:T(2,128)S(1)}, f32[2,64]{1,0:T(2,128)S(1)}, u32[]{:S(2)}, u32[]{:S(2)}) %collective-permute-start.7) | collective-permute-done | bytes 544 | tf_op jit(solution)/shard_map/ppermute | solution.py:207
  34.2 0.1 collective-permute-start.8
  34.3 0.8 %copy.21 = f32[128,512]{1,0:T(8,128)} copy(f32[128,512]{0,1:T(8,128)S(1)} %pad_maximum_fusion.3) | data formatting | bytes 524288
  35.2 0.8 %copy.20 = f32[128,512]{1,0:T(8,128)} copy(f32[128,512]{0,1:T(8,128)S(1)} %pad_maximum_fusion.1) | data formatting | bytes 524288
  36.0 0.5 %fusion.146 = f32[64]{0:T(128)} fusion(f32[1,64]{1,0:T(1,128)S(1)} %collective-permute-done.8, pred[]{:T(512)S(6)} %ne.39, f32[2,64]{1,0:T(2,128)S(1)} %select_add_fusion.1), kind=kLoop, calls=%fused_computation.170 | loop fusion | flops 192 | bytes 1025 | tf_op jit(solution)/shard_map/mul | solution.py:209
  (32 shorter events, 0.2 us)
Async XLA Ops:
  0.6 10.8 %copy-start = (bf16[256,512]{1,0:T(8,128)(2,1)S(1)}, bf16[256,512]{1,0:T(8,128)(2,1)}, u32[]{:S(2)}) copy-start(bf16[256,512]{1,0:T(8,128)(2,1)} %param.19) | copy-start | bytes 786436
  0.6 1.3 %copy-start.2 = (bf16[4,128,128]{2,1,0:T(8,128)(2,1)S(1)}, bf16[4,128,128]{2,1,0:T(8,128)(2,1)}, u32[]{:S(2)}) copy-start(bf16[4,128,128]{2,1,0:T(8,128)(2,1)} %param.18) | copy-start | bytes 393220
  0.7 2.7 %copy-start.3 = (bf16[512,512]{1,0:T(8,128)(2,1)S(1)}, bf16[512,512]{1,0:T(8,128)(2,1)}, u32[]{:S(2)}) copy-start(bf16[512,512]{1,0:T(8,128)(2,1)} %param.17) | copy-start | bytes 1572868
  3.7 1.0 %copy-start.6 = (bf16[512,256]{1,0:T(8,128)(2,1)S(1)}, bf16[512,256]{1,0:T(8,128)(2,1)}, u32[]{:S(2)}) copy-start(bf16[512,256]{1,0:T(8,128)(2,1)} %param.20) | copy-start | bytes 786436
  3.7 0.7 %copy-start.5 = (s32[3,2]{0,1:T(2,128)S(1)}, s32[3,2]{0,1:T(2,128)}, u32[]{:S(2)}) copy-start(s32[3,2]{0,1:T(2,128)} %param.15) | copy-start | bytes 76
  5.0 3.6 %copy-start.1 = (bf16[2,128,128]{2,1,0:T(8,128)(2,1)S(1)}, bf16[2,128,128]{2,1,0:T(8,128)(2,1)}, u32[]{:S(2)}) copy-start(bf16[2,128,128]{2,1,0:T(8,128)(2,1)} %param.21) | copy-start | bytes 196612
  5.0 6.0 %copy-start.4 = (bf16[512,512]{1,0:T(8,128)(2,1)S(1)}, bf16[512,512]{1,0:T(8,128)(2,1)}, u32[]{:S(2)}) copy-start(bf16[512,512]{1,0:T(8,128)(2,1)} %param.16) | copy-start | bytes 1572868
  5.0 8.7 %collective-permute-start.4 = (f32[256,128]{1,0:T(8,128)S(1)}, f32[256,128]{1,0:T(8,128)S(1)}, u32[]{:S(2)}, u32[]{:S(2)}) collective-permute-start(f32[256,128]{1,0:T(8,128)S(1)} %pad_maximum_fusion.6), channel_id=1, source_target_pairs={{0,8},{8,0},{16,24},{24,16},{1,9},{9,1},{17,25},{25,17},{2,10},{10... | collective-permute-start | bytes 393224 | tf_op jit(solution)/shard_map/ppermute | solution.py:129
  10.1 6.1 %collective-permute-start.1 = (bf16[512,128]{1,0:T(8,128)(2,1)S(1)}, bf16[512,128]{1,0:T(8,128)(2,1)S(1)}, u32[]{:S(2)}, u32[]{:S(2)}) collective-permute-start(bf16[512,128]{1,0:T(8,128)(2,1)S(1)} %pad_maximum_fusion.5), channel_id=1, source_target_pairs={{0,8},{8,0},{16,24},{24,16},{1,9},{9,1},{17,25},{25,17},{2,10},{10... | collective-permute-start | bytes 393224 | tf_op jit(solution)/shard_map/ppermute | solution.py:129
  10.2 0.7 %copy-start.8 = (s32[128]{0:T(128)S(1)}, s32[128]{0:T(128)}, u32[]{:S(2)}) copy-start(s32[128]{0:T(128)} %param.12) | copy-start | bytes 1540
  11.8 6.9 %collective-permute-start = (f32[256,128]{1,0:T(8,128)S(1)}, f32[256,128]{1,0:T(8,128)S(1)}, u32[]{:S(2)}, u32[]{:S(2)}) collective-permute-start(f32[256,128]{1,0:T(8,128)S(1)} %pad_maximum_fusion.4), channel_id=1, source_target_pairs={{0,8},{8,0},{16,24},{24,16},{1,9},{9,1},{17,25},{25,17},{2,10},{10... | collective-permute-start | bytes 393224 | tf_op jit(solution)/shard_map/ppermute | solution.py:129
  16.6 5.5 %collective-permute-start.5 = (f32[128,128]{1,0:T(8,128)S(1)}, f32[128,128]{1,0:T(8,128)S(1)}, u32[]{:S(2)}, u32[]{:S(2)}) collective-permute-start(f32[128,128]{1,0:T(8,128)S(1)} %fusion.63), channel_id=1, source_target_pairs={{0,16},{8,24},{16,0},{24,8},{1,17},{9,25},{17,1},{25,9},{2,18},{10... | collective-permute-start | bytes 196616 | tf_op jit(solution)/shard_map/ppermute | solution.py:129
  18.2 3.9 %collective-permute-start.3 = (bf16[128,128]{1,0:T(8,128)(2,1)S(1)}, bf16[128,128]{1,0:T(8,128)(2,1)S(1)}, u32[]{:S(2)}, u32[]{:S(2)}) collective-permute-start(bf16[128,128]{1,0:T(8,128)(2,1)S(1)} %slice_select_fusion.2), channel_id=1, source_target_pairs={{0,16},{8,24},{16,0},{24,8},{1,17},{9,25},{17,1},{25,9},{2,18},{10... | collective-permute-start | bytes 98312 | tf_op jit(solution)/shard_map/ppermute | solution.py:129
  19.0 4.7 %collective-permute-start.2 = (f32[128,128]{1,0:T(8,128)S(1)}, f32[128,128]{1,0:T(8,128)S(1)}, u32[]{:S(2)}, u32[]{:S(2)}) collective-permute-start(f32[128,128]{1,0:T(8,128)S(1)} %fusion.72), channel_id=1, source_target_pairs={{0,16},{8,24},{16,0},{24,8},{1,17},{9,25},{17,1},{25,9},{2,18},{10... | collective-permute-start | bytes 196616 | tf_op jit(solution)/shard_map/ppermute | solution.py:129
  23.6 1.0 %copy-start.7 = (bf16[512,256]{1,0:T(8,128)(2,1)S(1)}, bf16[512,256]{1,0:T(8,128)(2,1)}, u32[]{:S(2)}) copy-start(bf16[512,256]{1,0:T(8,128)(2,1)} %param.20) | copy-start | bytes 786436
  26.0 4.5 %collective-permute-start.6 = (f32[4,64]{1,0:T(4,128)S(1)}, f32[4,64]{1,0:T(4,128)S(1)}, u32[]{:S(2)}, u32[]{:S(2)}) collective-permute-start(f32[4,64]{1,0:T(4,128)S(1)} %slice_select_fusion.11), channel_id=1, source_target_pairs={{0,4},{1,5},{2,6},{3,7},{4,0},{5,1},{6,2},{7,3},{8,12},{9,13},{10,... | collective-permute-start | bytes 3080 | tf_op jit(solution)/shard_map/ppermute | solution.py:207
  30.6 3.6 %collective-permute-start.7 = (f32[2,64]{1,0:T(2,128)S(1)}, f32[2,64]{1,0:T(2,128)S(1)}, u32[]{:S(2)}, u32[]{:S(2)}) collective-permute-start(f32[2,64]{1,0:T(2,128)S(1)} %broadcast_select_fusion.3), channel_id=1, source_target_pairs={{0,2},{1,3},{2,0},{3,1},{4,6},{5,7},{6,4},{7,5},{8,10},{9,11},{10,... | collective-permute-start | bytes 1544 | tf_op jit(solution)/shard_map/ppermute | solution.py:207
  34.2 1.8 %collective-permute-start.8 = (f32[1,64]{1,0:T(1,128)S(1)}, f32[1,64]{1,0:T(1,128)S(1)}, u32[]{:S(2)}, u32[]{:S(2)}) collective-permute-start(f32[1,64]{1,0:T(1,128)S(1)} %broadcast_select_fusion.4), channel_id=1, source_target_pairs={{0,1},{1,0},{2,3},{3,2},{4,5},{5,4},{6,7},{7,6},{8,9},{9,8},{10,11... | collective-permute-start | bytes 776 | tf_op jit(solution)/shard_map/ppermute | solution.py:207

commit v16 on v15

--- a/solution.py
+++ b/solution.py
@@ -126,33 +126,39 @@
 
     def exchange(values, pairs):
         pieces = [piece for piece in values]
-        incoming = lax.ppermute(jnp.concatenate(pieces, axis=0), "leaf", pairs)
+        joined = pieces[0] if len(pieces) == 1 else jnp.concatenate(pieces, axis=0)
+        incoming = lax.ppermute(joined, "leaf", pairs)
         received, row = [], 0
         for piece in pieces:
             received.append(incoming[row : row + piece.shape[0]])
             row += piece.shape[0]
         return received
 
+    def level_pieces(height):
+        pieces = [lower_panels[height - 1]] + blocks_of(upper_panels[height - 1]) + [inverse_panels[height - 1]]
+        return [piece for piece in pieces if piece.shape[0]]
+
+    arrivals = {}
+    for offset in range(1, leaves):
+        lowest = offset.bit_length()
+        pairs = [(index, index ^ offset) for index in range(leaves)]
+        received = exchange([piece for height in range(lowest, levels + 1) for piece in level_pieces(height)], pairs)
+        for height in range(lowest, levels + 1):
+            count = len(level_pieces(height))
+            arrivals[offset, height] = received[:count]
+            received = received[count:]
     for height in range(1, levels + 1):
-        stride = 1 << (height - 1)
-        pairs = [(index, index ^ stride) for index in range(leaves)]
-        pieces = []
-        for upper_level in range(height, levels + 1):
-            pieces.append(lower_panels[upper_level - 1])
-            pieces.extend(blocks_of(upper_panels[upper_level - 1]))
-            pieces.append(inverse_panels[upper_level - 1])
-        received = exchange(pieces, pairs)
-        for upper_level in range(height, levels + 1):
-            place = device % (1 << upper_level)
-            take = jnp.logical_and(place >= stride, place < 2 * stride)
-            width = levels - upper_level
-            lower_in = received[0]
-            upper_in = jnp.concatenate(received[1 : 1 + width] or [upper_panels[upper_level - 1]], axis=1)
-            inverse_in = received[1 + width]
-            received = received[2 + width :]
-            lower_panels[upper_level - 1] = jnp.where(take, lower_in, lower_panels[upper_level - 1])
-            upper_panels[upper_level - 1] = jnp.where(take, upper_in, upper_panels[upper_level - 1])
-            inverse_panels[upper_level - 1] = jnp.where(take, inverse_in, inverse_panels[upper_level - 1])
+        place = device % (1 << height)
+        width = levels - height
+        for offset in range(1, 1 << height):
+            arrived = arrivals[offset, height]
+            take = place == offset
+            if width:
+                lower_in = arrived[0]
+                upper_in = jnp.concatenate(arrived[1 : 1 + width], axis=1)
+                lower_panels[height - 1] = jnp.where(take, lower_in, lower_panels[height - 1])
+                upper_panels[height - 1] = jnp.where(take, upper_in, upper_panels[height - 1])
+            inverse_panels[height - 1] = jnp.where(take, arrived[-1], inverse_panels[height - 1])
 
     forward_nodes, adjoint_nodes = [], []
     for height in range(1, levels + 1):

time: 36.9 us -> 37.5 us (1.016)
  starting transfers between devices: 13.1 us -> 14.6 us
  matrix products: 7.83 us -> 6.89 us
  local copies, waits for them, and re-layouts: 4.12 us -> 4.72 us
  waiting for transfers between devices: 7.97 us -> 7.46 us
    ppermute x6 -> x7, starting transfers between devices: 8.81 us -> 10 us  [exchange(): incoming = lax.ppermute(joined, 'leaf', pairs)]
    dot_general x1, matrix products: 1.31 us -> 0.38 us  [shards(): jnp.dot(residual, receiver_hits, precision=lax.Precision.HIGHEST)]
    squeeze x1, local copies, waits for them, and re-layouts: 0.01 us -> 0.84 us  [shards(): inverse_panels.append(sep_inv[height - 1])]
    unnamed x20 -> x24, local copies, waits for them, and re-layouts: 3.05 us -> 2.82 us
    ppermute x6 -> x7, waiting for transfers between devices: 4.05 us -> 3.82 us  [exchange(): incoming = lax.ppermute(joined, 'leaf', pairs)]
  transfers between devices with their start and end apart: 9 -> 10, of which waited for: 4 -> 5; matrix products, arithmetic and copies ran while one was open for 18% -> 26% of each run, Pallas kernels for 0% -> 0%
where the time goes in v16:
time: 37.5 us; the launch traced here: 37.2 us
  starting transfers between devices  14.6 us (39%)
  waiting for transfers between devices  7.46 us (20%)
  matrix products  6.89 us (18%)
  local copies, waits for them, and re-layouts  4.72 us (13%)
  other arithmetic  2.43 us (6%)
  between operations  1.04 us (3%)
    ppermute x7, starting transfers between devices, exchange(): incoming = lax.ppermute(joined, 'leaf', pairs)  10 us
    ppermute x3, starting transfers between devices, shards(): partial_gradient = kept + lax.ppermute(outgoing, 'src', pairs)  4.59 us
    dot_general x13, matrix products, plain_dot(): return jnp.dot(former, latter, preferred_element_type=jnp.float32)  3.98 us
    ppermute x7, waiting for transfers between devices, exchange(): incoming = lax.ppermute(joined, 'leaf', pairs)  3.82 us
    ppermute x3, waiting for transfers between devices, shards(): partial_gradient = kept + lax.ppermute(outgoing, 'src', pairs)  3.64 us
    unnamed x24, local copies, waits for them, and re-layouts  2.82 us
    dot_general x12, matrix products, across(): lax.dot_general(former, latter, (((1,), (1,)), ((), ())), preferred_eleme...  2.54 us
    select_n x1, other arithmetic, masked(): return jnp.where(keep, values, jnp.zeros_like(values))  1.43 us
  transfers between devices with their start and end apart: 10, of which 5 were waited for; matrix products, arithmetic and copies ran while one was open for 26% of the time, Pallas kernels for 0%

profile of v16, /device:TPU:0, one launch (start us, length us, event | category | flops | bytes accessed | tf_op | source)
XLA Modules:
  0.0 37.2 jit_solution(15984446168263146176)
XLA Ops:
  0.6 0.0 copy-start
  0.7 0.8 %slice_bitcast_fusion.1 = (bf16[128,128]{1,0:T(8,128)(2,1)S(1)}, bf16[128,128]{1,0:T(8,128)(2,1)S(1)}) fusion(bf16[2,128,128]{2,1,0:T(8,128)(2,1)} %param.21), kind=kLoop, calls=%fused_computation.143 | loop fusion | bytes 131072 | tf_op jit(solution)/shard_map/squeeze | solution.py:125
  1.5 0.0 copy-start.3
  1.5 4.0 %collective-permute-start.3 = (bf16[128,128]{1,0:T(8,128)(2,1)S(1)}, bf16[128,128]{1,0:T(8,128)(2,1)S(1)}, u32[]{:S(2)}, u32[]{:S(2)}) collective-permute-start(bf16[128,128]{1,0:T(8,128)(2,1)S(1)} %get-tuple-element.13), channel_id=1, source_target_pairs={{0,24},{8,16},{16,8},{24,0},{1,25},{9,17},{17,9},{25,1},{2,26},{10... | collective-permute-start | bytes 98312 | tf_op jit(solution)/shard_map/ppermute | solution.py:130
  5.5 0.5 %collective-permute-start.4 = (bf16[128,128]{1,0:T(8,128)(2,1)S(1)}, bf16[128,128]{1,0:T(8,128)(2,1)S(1)}, u32[]{:S(2)}, u32[]{:S(2)}) collective-permute-start(bf16[128,128]{1,0:T(8,128)(2,1)S(1)} %get-tuple-element.13), channel_id=1, source_target_pairs={{0,16},{8,24},{16,0},{24,8},{1,17},{9,25},{17,1},{25,9},{2,18},{10... | collective-permute-start | bytes 98312 | tf_op jit(solution)/shard_map/ppermute | solution.py:130
  6.0 0.4 %convolution_bitcast_fusion = f32[128,512]{0,1:T(8,128)S(1)} fusion(f32[128,128]{1,0:T(8,128)S(1)} %copy-done.5, s32[128]{0:T(128)S(1)} %copy-done.7), kind=kOutput, calls=%fused_computation.2 | convolution fusion | flops 100794368 | bytes 328192 | tf_op jit(solution)/shard_map/dot_general | solution.py:112
  6.4 0.2 fusion.183
  6.6 1.1 %fusion.184 = (bf16[128,128]{0,1:T(8,128)(2,1)S(1)}, f32[128,128]{0,1:T(8,128)S(1)}) fusion(bf16[4,128,128]{2,1,0:T(8,128)(2,1)S(1)} %copy-done.2, bf16[128,128]{0,1:T(8,128)(2,1)S(1)} %get-tuple-element.24, f32[128,512]{0,1:T(8,128)S(1)} %convolution_bitcast_fusion, bf16[512,512]{1,0:T(8,128)(2,1)} %param.17), kind=kOutput, calls=%fused_computation.200 | convolution fusion | flops 8437760 | bytes 262144 | tf_op jit(solution)/shard_map/dot_general | solution.py:16
  7.7 0.4 fusion.187
  8.1 0.0 copy-start.8
  8.1 0.0 copy-start.6
  8.1 0.4 fusion.10
  8.5 0.3 copy-done.6
  8.8 0.2 compare_reduce_fusion.1
  9.0 0.1 broadcast_bitcast_fusion
  9.1 0.2 convolution_select_fusion
  9.3 0.0 copy-start.4
  9.4 0.2 collective-permute-start.5
  9.6 0.6 %slice.198 = pred[1]{0:T(512)(128)(4,1)} slice(pred[2]{0:T(512)(128)(4,1)S(1)} %compare_and_fusion), slice={[1:2]} | slice | bytes 2 | tf_op jit(solution)/shard_map/slice | solution.py:122
  10.2 1.4 %select_bitcast_fusion = (bf16[128,128]{1,0:T(8,128)(2,1)S(1)}, bf16[128,128]{1,0:T(8,128)(2,1)S(1)}) fusion(bf16[2,128,256]{2,1,0:T(8,128)(2,1)} %param.23, pred[]{:T(512)} %bitcast.1, bf16[2,256,128]{2,1,0:T(8,128)(2,1)} %param.22), kind=kLoop, calls=%fused_computation.144 | loop fusion | flops 32768 | bytes 131073 | tf_op jit(solution)/shard_map/jit(_where)/select_n | solution.py:102
  11.6 2.0 %collective-permute-start.1 = (bf16[512,128]{1,0:T(8,128)(2,1)S(1)}, bf16[512,128]{1,0:T(8,128)(2,1)S(1)}, u32[]{:S(2)}, u32[]{:S(2)}) collective-permute-start(bf16[512,128]{1,0:T(8,128)(2,1)S(1)} %pad_maximum_fusion.5), channel_id=1, source_target_pairs={{0,8},{8,0},{16,24},{24,16},{1,9},{9,1},{17,25},{25,17},{2,10},{10... | collective-permute-start | bytes 393224 | tf_op jit(solution)/shard_map/ppermute | solution.py:130
  13.6 0.7 %copy-done.10 = s32[128]{0:T(128)S(1)} copy-done((s32[128]{0:T(128)S(1)}, s32[128]{0:T(128)}, u32[]{:S(2)}) %copy-start.10) | copy-done | bytes 536
  14.3 0.1 fusion.172
  14.5 0.2 fusion.173
  14.6 0.2 convolution_subtract_fusion.5
  14.8 0.2 convolution_select_fusion.1
  15.1 0.2 collective-permute-start
  15.3 0.0 collective-permute-done.5
  15.3 2.6 %collective-permute-done.1 = bf16[512,128]{1,0:T(8,128)(2,1)S(1)} collective-permute-done((bf16[512,128]{1,0:T(8,128)(2,1)S(1)}, bf16[512,128]{1,0:T(8,128)(2,1)S(1)}, u32[]{:S(2)}, u32[]{:S(2)}) %collective-permute-start.1) | collective-permute-done | bytes 131104 | tf_op jit(solution)/shard_map/ppermute | solution.py:130
  17.9 0.2 fusion.106
  18.1 0.1 copy.17
  18.2 0.2 fusion.63
  18.4 1.7 %collective-permute-start.6 = (f32[128,128]{1,0:T(8,128)S(1)}, f32[128,128]{1,0:T(8,128)S(1)}, u32[]{:S(2)}, u32[]{:S(2)}) collective-permute-start(f32[128,128]{1,0:T(8,128)S(1)} %fusion.63), channel_id=1, source_target_pairs={{0,16},{8,24},{16,0},{24,8},{1,17},{9,25},{17,1},{25,9},{2,18},{10... | collective-permute-start | bytes 196616 | tf_op jit(solution)/shard_map/ppermute | solution.py:130
  20.1 0.0 collective-permute-done
  20.1 0.2 fusion.72
  20.3 1.5 %collective-permute-start.2 = (f32[128,128]{1,0:T(8,128)S(1)}, f32[128,128]{1,0:T(8,128)S(1)}, u32[]{:S(2)}, u32[]{:S(2)}) collective-permute-start(f32[128,128]{1,0:T(8,128)S(1)} %fusion.72), channel_id=1, source_target_pairs={{0,16},{8,24},{16,0},{24,8},{1,17},{9,25},{17,1},{25,9},{2,18},{10... | collective-permute-start | bytes 196616 | tf_op jit(solution)/shard_map/ppermute | solution.py:130
  21.8 0.9 %collective-permute-done.6 = f32[128,128]{1,0:T(8,128)S(1)} collective-permute-done((f32[128,128]{1,0:T(8,128)S(1)}, f32[128,128]{1,0:T(8,128)S(1)}, u32[]{:S(2)}, u32[]{:S(2)}) %collective-permute-start.6) | collective-permute-done | bytes 65568 | tf_op jit(solution)/shard_map/ppermute | solution.py:130
  22.7 0.2 fusion.103
  23.0 0.1 copy.18
  23.1 0.2 fusion.119
  23.3 0.3 convolution_subtract_fusion
  23.6 0.2 fusion.192
  23.8 0.2 fusion.193
  24.0 0.2 convolution_subtract_fusion.8
  24.3 0.0 copy-start.9
  24.3 0.3 collective-permute-done.2
  24.6 0.1 fusion.102
  24.7 0.1 copy.15
  24.8 0.3 fusion.13
  25.1 0.1 copy-done.9
  25.2 0.2 convolution_subtract_fusion.1
  25.5 0.1 fusion.174
  25.6 0.3 fusion.175
  25.9 0.3 fusion.178
  26.2 0.3 fusion.7
  26.5 0.1 fusion.14
  26.7 2.8 %collective-permute-start.7 = (f32[4,64]{1,0:T(4,128)S(1)}, f32[4,64]{1,0:T(4,128)S(1)}, u32[]{:S(2)}, u32[]{:S(2)}) collective-permute-start(f32[4,64]{1,0:T(4,128)S(1)} %slice_select_fusion.11), channel_id=1, source_target_pairs={{0,4},{1,5},{2,6},{3,7},{4,0},{5,1},{6,2},{7,3},{8,12},{9,13},{10,... | collective-permute-start | bytes 3080 | tf_op jit(solution)/shard_map/ppermute | solution.py:213
  29.4 1.8 %collective-permute-done.7 = f32[4,64]{1,0:T(4,128)S(1)} collective-permute-done((f32[4,64]{1,0:T(4,128)S(1)}, f32[4,64]{1,0:T(4,128)S(1)}, u32[]{:S(2)}, u32[]{:S(2)}) %collective-permute-start.7) | collective-permute-done | bytes 1056 | tf_op jit(solution)/shard_map/ppermute | solution.py:213
  31.2 1.8 %collective-permute-start.8 = (f32[2,64]{1,0:T(2,128)S(1)}, f32[2,64]{1,0:T(2,128)S(1)}, u32[]{:S(2)}, u32[]{:S(2)}) collective-permute-start(f32[2,64]{1,0:T(2,128)S(1)} %broadcast_select_fusion), channel_id=1, source_target_pairs={{0,2},{1,3},{2,0},{3,1},{4,6},{5,7},{6,4},{7,5},{8,10},{9,11},{10,... | collective-permute-start | bytes 1544 | tf_op jit(solution)/shard_map/ppermute | solution.py:213
  33.0 1.9 %collective-permute-done.8 = f32[2,64]{1,0:T(2,128)S(1)} collective-permute-done((f32[2,64]{1,0:T(2,128)S(1)}, f32[2,64]{1,0:T(2,128)S(1)}, u32[]{:S(2)}, u32[]{:S(2)}) %collective-permute-start.8) | collective-permute-done | bytes 544 | tf_op jit(solution)/shard_map/ppermute | solution.py:213
  34.9 0.1 collective-permute-start.9
  35.0 0.8 %copy.21 = f32[128,512]{1,0:T(8,128)} copy(f32[128,512]{0,1:T(8,128)S(1)} %pad_maximum_fusion.3) | data formatting | bytes 524288
  35.8 0.8 %copy.20 = f32[128,512]{1,0:T(8,128)} copy(f32[128,512]{0,1:T(8,128)S(1)} %pad_maximum_fusion.1) | data formatting | bytes 524288
  36.7 0.5 %fusion.148 = f32[64]{0:T(128)} fusion(f32[1,64]{1,0:T(1,128)S(1)} %collective-permute-done.9, pred[]{:T(512)S(6)} %ne.37, f32[2,64]{1,0:T(2,128)S(1)} %select_add_fusion.1), kind=kLoop, calls=%fused_computation.171 | loop fusion | flops 192 | bytes 1025 | tf_op jit(solution)/shard_map/mul | solution.py:215
  (38 shorter events, 0.3 us)
Async XLA Ops:
  0.6 14.2 %copy-start = (bf16[256,512]{1,0:T(8,128)(2,1)S(1)}, bf16[256,512]{1,0:T(8,128)(2,1)}, u32[]{:S(2)}) copy-start(bf16[256,512]{1,0:T(8,128)(2,1)} %param.19) | copy-start | bytes 786436
  0.6 5.3 %copy-start.5 = (f32[128,128]{1,0:T(8,128)S(1)}, f32[128,128]{1,0:T(8,128)}, u32[]{:S(2)}) copy-start(f32[128,128]{1,0:T(8,128)} %param.14) | copy-start | bytes 196612
  1.5 4.5 %copy-start.7 = (s32[128]{0:T(128)S(1)}, s32[128]{0:T(128)}, u32[]{:S(2)}) copy-start(s32[128]{0:T(128)} %param.13) | copy-start | bytes 1540
  1.5 4.9 %copy-start.2 = (bf16[4,128,128]{2,1,0:T(8,128)(2,1)S(1)}, bf16[4,128,128]{2,1,0:T(8,128)(2,1)}, u32[]{:S(2)}) copy-start(bf16[4,128,128]{2,1,0:T(8,128)(2,1)} %param.18) | copy-start | bytes 393220
  1.5 6.2 %copy-start.3 = (bf16[512,512]{1,0:T(8,128)(2,1)S(1)}, bf16[512,512]{1,0:T(8,128)(2,1)}, u32[]{:S(2)}) copy-start(bf16[512,512]{1,0:T(8,128)(2,1)} %param.17) | copy-start | bytes 1572868
  1.5 20.3 %collective-permute-start.3 = (bf16[128,128]{1,0:T(8,128)(2,1)S(1)}, bf16[128,128]{1,0:T(8,128)(2,1)S(1)}, u32[]{:S(2)}, u32[]{:S(2)}) collective-permute-start(bf16[128,128]{1,0:T(8,128)(2,1)S(1)} %get-tuple-element.13), channel_id=1, source_target_pairs={{0,24},{8,16},{16,8},{24,0},{1,25},{9,17},{17,9},{25,1},{2,26},{10... | collective-permute-start | bytes 98312 | tf_op jit(solution)/shard_map/ppermute | solution.py:130
  5.5 16.3 %collective-permute-start.4 = (bf16[128,128]{1,0:T(8,128)(2,1)S(1)}, bf16[128,128]{1,0:T(8,128)(2,1)S(1)}, u32[]{:S(2)}, u32[]{:S(2)}) collective-permute-start(bf16[128,128]{1,0:T(8,128)(2,1)S(1)} %get-tuple-element.13), channel_id=1, source_target_pairs={{0,16},{8,24},{16,0},{24,8},{1,17},{9,25},{17,1},{25,9},{2,18},{10... | collective-permute-start | bytes 98312 | tf_op jit(solution)/shard_map/ppermute | solution.py:130
  8.1 1.0 %copy-start.8 = (bf16[512,256]{1,0:T(8,128)(2,1)S(1)}, bf16[512,256]{1,0:T(8,128)(2,1)}, u32[]{:S(2)}) copy-start(bf16[512,256]{1,0:T(8,128)(2,1)} %param.20) | copy-start | bytes 786436
  8.1 0.7 %copy-start.6 = (s32[3,2]{0,1:T(2,128)S(1)}, s32[3,2]{0,1:T(2,128)}, u32[]{:S(2)}) copy-start(s32[3,2]{0,1:T(2,128)} %param.15) | copy-start | bytes 76
  9.3 5.0 %copy-start.4 = (bf16[512,512]{1,0:T(8,128)(2,1)S(1)}, bf16[512,512]{1,0:T(8,128)(2,1)}, u32[]{:S(2)}) copy-start(bf16[512,512]{1,0:T(8,128)(2,1)} %param.16) | copy-start | bytes 1572868
  9.4 6.0 %collective-permute-start.5 = (f32[256,128]{1,0:T(8,128)S(1)}, f32[256,128]{1,0:T(8,128)S(1)}, u32[]{:S(2)}, u32[]{:S(2)}) collective-permute-start(f32[256,128]{1,0:T(8,128)S(1)} %pad_maximum_fusion.6), channel_id=1, source_target_pairs={{0,8},{8,0},{16,24},{24,16},{1,9},{9,1},{17,25},{25,17},{2,10},{10... | collective-permute-start | bytes 393224 | tf_op jit(solution)/shard_map/ppermute | solution.py:130
  11.6 6.3 %collective-permute-start.1 = (bf16[512,128]{1,0:T(8,128)(2,1)S(1)}, bf16[512,128]{1,0:T(8,128)(2,1)S(1)}, u32[]{:S(2)}, u32[]{:S(2)}) collective-permute-start(bf16[512,128]{1,0:T(8,128)(2,1)S(1)} %pad_maximum_fusion.5), channel_id=1, source_target_pairs={{0,8},{8,0},{16,24},{24,16},{1,9},{9,1},{17,25},{25,17},{2,10},{10... | collective-permute-start | bytes 393224 | tf_op jit(solution)/shard_map/ppermute | solution.py:130
  13.6 0.7 %copy-start.10 = (s32[128]{0:T(128)S(1)}, s32[128]{0:T(128)}, u32[]{:S(2)}) copy-start(s32[128]{0:T(128)} %param.12) | copy-start | bytes 1540
  15.1 2.8 %copy-start.1 = (bf16[2,128,128]{2,1,0:T(8,128)(2,1)S(1)}, bf16[2,128,128]{2,1,0:T(8,128)(2,1)}, u32[]{:S(2)}) copy-start(bf16[2,128,128]{2,1,0:T(8,128)(2,1)} %param.21) | copy-start | bytes 196612
  15.1 5.0 %collective-permute-start = (f32[256,128]{1,0:T(8,128)S(1)}, f32[256,128]{1,0:T(8,128)S(1)}, u32[]{:S(2)}, u32[]{:S(2)}) collective-permute-start(f32[256,128]{1,0:T(8,128)S(1)} %pad_maximum_fusion.4), channel_id=1, source_target_pairs={{0,8},{8,0},{16,24},{24,16},{1,9},{9,1},{17,25},{25,17},{2,10},{10... | collective-permute-start | bytes 393224 | tf_op jit(solution)/shard_map/ppermute | solution.py:130
  18.4 4.3 %collective-permute-start.6 = (f32[128,128]{1,0:T(8,128)S(1)}, f32[128,128]{1,0:T(8,128)S(1)}, u32[]{:S(2)}, u32[]{:S(2)}) collective-permute-start(f32[128,128]{1,0:T(8,128)S(1)} %fusion.63), channel_id=1, source_target_pairs={{0,16},{8,24},{16,0},{24,8},{1,17},{9,25},{17,1},{25,9},{2,18},{10... | collective-permute-start | bytes 196616 | tf_op jit(solution)/shard_map/ppermute | solution.py:130
  20.3 4.3 %collective-permute-start.2 = (f32[128,128]{1,0:T(8,128)S(1)}, f32[128,128]{1,0:T(8,128)S(1)}, u32[]{:S(2)}, u32[]{:S(2)}) collective-permute-start(f32[128,128]{1,0:T(8,128)S(1)} %fusion.72), channel_id=1, source_target_pairs={{0,16},{8,24},{16,0},{24,8},{1,17},{9,25},{17,1},{25,9},{2,18},{10... | collective-permute-start | bytes 196616 | tf_op jit(solution)/shard_map/ppermute | solution.py:130
  24.3 1.0 %copy-start.9 = (bf16[512,256]{1,0:T(8,128)(2,1)S(1)}, bf16[512,256]{1,0:T(8,128)(2,1)}, u32[]{:S(2)}) copy-start(bf16[512,256]{1,0:T(8,128)(2,1)} %param.20) | copy-start | bytes 786436
  26.7 4.5 %collective-permute-start.7 = (f32[4,64]{1,0:T(4,128)S(1)}, f32[4,64]{1,0:T(4,128)S(1)}, u32[]{:S(2)}, u32[]{:S(2)}) collective-permute-start(f32[4,64]{1,0:T(4,128)S(1)} %slice_select_fusion.11), channel_id=1, source_target_pairs={{0,4},{1,5},{2,6},{3,7},{4,0},{5,1},{6,2},{7,3},{8,12},{9,13},{10,... | collective-permute-start | bytes 3080 | tf_op jit(solution)/shard_map/ppermute | solution.py:213
  31.2 3.6 %collective-permute-start.8 = (f32[2,64]{1,0:T(2,128)S(1)}, f32[2,64]{1,0:T(2,128)S(1)}, u32[]{:S(2)}, u32[]{:S(2)}) collective-permute-start(f32[2,64]{1,0:T(2,128)S(1)} %broadcast_select_fusion), channel_id=1, source_target_pairs={{0,2},{1,3},{2,0},{3,1},{4,6},{5,7},{6,4},{7,5},{8,10},{9,11},{10,... | collective-permute-start | bytes 1544 | tf_op jit(solution)/shard_map/ppermute | solution.py:213
  34.9 1.8 %collective-permute-start.9 = (f32[1,64]{1,0:T(1,128)S(1)}, f32[1,64]{1,0:T(1,128)S(1)}, u32[]{:S(2)}, u32[]{:S(2)}) collective-permute-start(f32[1,64]{1,0:T(1,128)S(1)} %broadcast_select_fusion.1), channel_id=1, source_target_pairs={{0,1},{1,0},{2,3},{3,2},{4,5},{5,4},{6,7},{7,6},{8,9},{9,8},{10,11... | collective-permute-start | bytes 776 | tf_op jit(solution)/shard_map/ppermute | solution.py:213

commit v17 on v15

--- a/solution.py
+++ b/solution.py
@@ -113,8 +113,9 @@
 
     base_mask = level_mask(0)
     y_leaf = lower_solve(forcing, leaf_lower, block_size, block_count)
+    forward_sums = blocks_of(masked(across(as_half(y_leaf), anc_lower), base_mask))
+    forward_sums, adjoint_rhs = lax.optimization_barrier((forward_sums, adjoint_rhs))
     z_leaf = upper_t_solve(adjoint_rhs, leaf_upper, leaf_inv, block_size, block_count)
-    forward_sums = blocks_of(masked(across(as_half(y_leaf), anc_lower), base_mask))
     adjoint_sums = blocks_of(masked(plain_dot(as_half(z_leaf), anc_upper), base_mask))
 
     lower_panels, upper_panels, inverse_panels = [], [], []

time: 36.9 us -> 40.5 us (1.098)
  local copies, waits for them, and re-layouts: 4.12 us -> 6.06 us
  waiting for transfers between devices: 7.97 us -> 9.69 us
  matrix products: 7.83 us -> 6.9 us
  other arithmetic: 2.44 us -> 3.17 us
    unnamed x20 -> x24, local copies, waits for them, and re-layouts: 3.05 us -> 4.99 us
    ppermute x6, waiting for transfers between devices: 4.05 us -> 5.83 us  [exchange(): incoming = lax.ppermute(jnp.concatenate(pieces, axis=0), 'leaf', pairs)]
    dot_general x1, matrix products: 1.31 us -> 0.38 us  [shards(): jnp.dot(residual, receiver_hits, precision=lax.Precision.HIGHEST)]
    dot_general x13, matrix products: 3.98 us -> 3.22 us  [plain_dot(): return jnp.dot(former, latter, preferred_element_type=jnp.float32)]
    dot_general x12, matrix products: 2.54 us -> 3.29 us  [across(): lax.dot_general(former, latter, (((1,), (1,)), ((), ())), preferred_eleme...]
    sub x1, other arithmetic: 0.01 us -> 0.73 us  [shards(): src_cells[:, None] - device * cell_count == columns]
  transfers between devices with their start and end apart: 9 -> 9, of which waited for: 4 -> 4; matrix products, arithmetic and copies ran while one was open for 18% -> 15% of each run, Pallas kernels for 0% -> 0%
where the time goes in v17:
time: 40.5 us; the launch traced here: 40 us
  starting transfers between devices  13.2 us (33%)
  waiting for transfers between devices  9.69 us (24%)
  matrix products  6.9 us (17%)
  local copies, waits for them, and re-layouts  6.06 us (15%)
  other arithmetic  3.17 us (8%)
  between operations  1.02 us (3%)
    ppermute x6, starting transfers between devices, exchange(): incoming = lax.ppermute(jnp.concatenate(pieces, axis=0), 'leaf', pairs)  8.84 us
    ppermute x6, waiting for transfers between devices, exchange(): incoming = lax.ppermute(jnp.concatenate(pieces, axis=0), 'leaf', pairs)  5.83 us
    unnamed x24, local copies, waits for them, and re-layouts  4.99 us
    ppermute x3, starting transfers between devices, shards(): partial_gradient = kept + lax.ppermute(outgoing, 'src', pairs)  4.37 us
    ppermute x3, waiting for transfers between devices, shards(): partial_gradient = kept + lax.ppermute(outgoing, 'src', pairs)  3.87 us
    dot_general x12, matrix products, across(): lax.dot_general(former, latter, (((1,), (1,)), ((), ())), preferred_eleme...  3.29 us
    dot_general x13, matrix products, plain_dot(): return jnp.dot(former, latter, preferred_element_type=jnp.float32)  3.22 us
    select_n x1, other arithmetic, masked(): return jnp.where(keep, values, jnp.zeros_like(values))  1.43 us
  transfers between devices with their start and end apart: 9, of which 4 were waited for; matrix products, arithmetic and copies ran while one was open for 15% of the time, Pallas kernels for 0%

profile of v17, /device:TPU:0, one launch (start us, length us, event | category | flops | bytes accessed | tf_op | source)
XLA Modules:
  0.0 40.0 jit_solution(16445253711591558450)
XLA Ops:
  0.6 0.0 copy-start
  0.6 0.0 copy-start.4
  0.7 0.7 %broadcast_subtract_fusion = s32[128]{0:T(128)S(1)} fusion(s32[128]{0:T(128)} %param.12, s32[]{:T(128)S(6)} %mul.16), kind=kLoop, calls=%fused_computation.171 | loop fusion | flops 128 | bytes 1028 | tf_op jit(solution)/shard_map/sub | solution.py:108
  1.5 0.9 %fusion.168 = (bf16[128,128]{0,1:T(8,128)(2,1)S(1)}, f32[128,128]{0,1:T(8,128)S(1)}) fusion(bf16[512,512]{1,0:T(8,128)(2,1)} %param.16, f32[128,512]{0,1:T(8,128)S(1)} %fusion.15), kind=kOutput, calls=%fused_computation.191 | convolution fusion | flops 4227072 | bytes 229376 | tf_op jit(solution)/shard_map/dot_general | solution.py:10
  2.4 0.2 fusion.169
  2.5 0.0 copy-start.6
  2.5 0.2 convolution_subtract_fusion.5
  2.7 0.5 %copy-done.6 = s32[3,2]{0,1:T(2,128)S(1)} copy-done((s32[3,2]{0,1:T(2,128)S(1)}, s32[3,2]{0,1:T(2,128)}, u32[]{:S(2)}) %copy-start.6) | copy-done | bytes 48
  3.2 0.2 compare_reduce_fusion
  3.4 0.1 broadcast_bitcast_fusion
  3.5 0.4 copy-done.9
  3.8 0.2 convolution_select_fusion.1
  4.1 0.0 copy-start.5
  4.1 0.0 copy-start.7
  4.1 0.8 %copy-done.5 = f32[128,128]{1,0:T(8,128)S(1)} copy-done((f32[128,128]{1,0:T(8,128)S(1)}, f32[128,128]{1,0:T(8,128)}, u32[]{:S(2)}) %copy-start.5) | copy-done | bytes 65560
  4.9 0.4 convolution_bitcast_fusion
  5.3 0.5 %copy-done.2 = bf16[4,128,128]{2,1,0:T(8,128)(2,1)S(1)} copy-done((bf16[4,128,128]{2,1,0:T(8,128)(2,1)S(1)}, bf16[4,128,128]{2,1,0:T(8,128)(2,1)}, u32[]{:S(2)}) %copy-start.2) | copy-done | bytes 131096
  5.8 0.2 fusion.179
  6.1 0.3 fusion.180
  6.4 0.4 fusion.183
  6.8 0.4 fusion.10
  7.1 0.6 %copy-done.8 = bf16[512,256]{1,0:T(8,128)(2,1)S(1)} copy-done((bf16[512,256]{1,0:T(8,128)(2,1)S(1)}, bf16[512,256]{1,0:T(8,128)(2,1)}, u32[]{:S(2)}) %copy-start.8) | copy-done | bytes 262168
  7.7 0.2 convolution_select_fusion
  8.0 0.0 copy-start.1
  8.0 3.0 %collective-permute-start.4 = (f32[256,128]{1,0:T(8,128)S(1)}, f32[256,128]{1,0:T(8,128)S(1)}, u32[]{:S(2)}, u32[]{:S(2)}) collective-permute-start(f32[256,128]{1,0:T(8,128)S(1)} %pad_maximum_fusion.6), channel_id=1, source_target_pairs={{0,8},{8,0},{16,24},{24,16},{1,9},{9,1},{17,25},{25,17},{2,10},{10... | collective-permute-start | bytes 393224 | tf_op jit(solution)/shard_map/ppermute | solution.py:130
  11.0 0.6 %slice.198 = pred[1]{0:T(512)(128)(4,1)} slice(pred[2]{0:T(512)(128)(4,1)S(1)} %compare_and_fusion), slice={[1:2]} | slice | bytes 2 | tf_op jit(solution)/shard_map/slice | solution.py:123
  11.6 1.4 %select_bitcast_fusion = (bf16[128,128]{1,0:T(8,128)(2,1)S(1)}, bf16[128,128]{1,0:T(8,128)(2,1)S(1)}) fusion(bf16[2,128,256]{2,1,0:T(8,128)(2,1)} %param.23, pred[]{:T(512)} %bitcast.2, bf16[2,256,128]{2,1,0:T(8,128)(2,1)} %param.22), kind=kLoop, calls=%fused_computation.142 | loop fusion | flops 32768 | bytes 131073 | tf_op jit(solution)/shard_map/jit(_where)/select_n | solution.py:102
  13.1 0.2 collective-permute-start.1
  13.3 1.9 %collective-permute-start = (f32[256,128]{1,0:T(8,128)S(1)}, f32[256,128]{1,0:T(8,128)S(1)}, u32[]{:S(2)}, u32[]{:S(2)}) collective-permute-start(f32[256,128]{1,0:T(8,128)S(1)} %pad_maximum_fusion.4), channel_id=1, source_target_pairs={{0,8},{8,0},{16,24},{24,16},{1,9},{9,1},{17,25},{25,17},{2,10},{10... | collective-permute-start | bytes 393224 | tf_op jit(solution)/shard_map/ppermute | solution.py:130
  15.2 4.3 %collective-permute-done.1 = bf16[512,128]{1,0:T(8,128)(2,1)S(1)} collective-permute-done((bf16[512,128]{1,0:T(8,128)(2,1)S(1)}, bf16[512,128]{1,0:T(8,128)(2,1)S(1)}, u32[]{:S(2)}, u32[]{:S(2)}) %collective-permute-start.1) | collective-permute-done | bytes 131104 | tf_op jit(solution)/shard_map/ppermute | solution.py:130
  19.5 0.2 fusion.106
  19.7 0.2 fusion.63
  19.9 1.6 %collective-permute-start.5 = (f32[128,128]{1,0:T(8,128)S(1)}, f32[128,128]{1,0:T(8,128)S(1)}, u32[]{:S(2)}, u32[]{:S(2)}) collective-permute-start(f32[128,128]{1,0:T(8,128)S(1)} %fusion.63), channel_id=1, source_target_pairs={{0,16},{8,24},{16,0},{24,8},{1,17},{9,25},{17,1},{25,9},{2,18},{10... | collective-permute-start | bytes 196616 | tf_op jit(solution)/shard_map/ppermute | solution.py:130
  21.5 0.5 %collective-permute-start.3 = (bf16[128,128]{1,0:T(8,128)(2,1)S(1)}, bf16[128,128]{1,0:T(8,128)(2,1)S(1)}, u32[]{:S(2)}, u32[]{:S(2)}) collective-permute-start(bf16[128,128]{1,0:T(8,128)(2,1)S(1)} %slice_select_fusion.2), channel_id=1, source_target_pairs={{0,16},{8,24},{16,0},{24,8},{1,17},{9,25},{17,1},{25,9},{2,18},{10... | collective-permute-start | bytes 98312 | tf_op jit(solution)/shard_map/ppermute | solution.py:130
  22.0 0.2 fusion.69
  22.2 0.1 copy.17
  22.3 1.6 %collective-permute-start.2 = (f32[128,128]{1,0:T(8,128)S(1)}, f32[128,128]{1,0:T(8,128)S(1)}, u32[]{:S(2)}, u32[]{:S(2)}) collective-permute-start(f32[128,128]{1,0:T(8,128)S(1)} %fusion.69), channel_id=1, source_target_pairs={{0,16},{8,24},{16,0},{24,8},{1,17},{9,25},{17,1},{25,9},{2,18},{10... | collective-permute-start | bytes 196616 | tf_op jit(solution)/shard_map/ppermute | solution.py:130
  23.8 1.6 %collective-permute-done.3 = bf16[128,128]{1,0:T(8,128)(2,1)S(1)} collective-permute-done((bf16[128,128]{1,0:T(8,128)(2,1)S(1)}, bf16[128,128]{1,0:T(8,128)(2,1)S(1)}, u32[]{:S(2)}, u32[]{:S(2)}) %collective-permute-start.3) | collective-permute-done | bytes 32800 | tf_op jit(solution)/shard_map/ppermute | solution.py:130
  25.4 0.2 fusion.103
  25.6 0.1 copy.18
  25.7 0.2 fusion.117
  26.0 0.3 convolution_subtract_fusion
  26.2 0.2 fusion.188
  26.5 0.2 fusion.189
  26.7 0.2 convolution_subtract_fusion.8
  27.0 0.1 fusion.102
  27.1 0.1 copy.15
  27.2 0.0 copy-start.10
  27.3 0.3 fusion.13
  27.6 0.5 %copy-done.10 = f32[128,128]{0,1:T(8,128)S(1)} copy-done((f32[128,128]{0,1:T(8,128)S(1)}, f32[128,128]{0,1:T(8,128)}, u32[]{:S(2)}) %copy-start.10) | copy-done | bytes 65560
  28.1 0.2 convolution_subtract_fusion.1
  28.3 0.1 fusion.170
  28.5 0.3 fusion.171
  28.8 0.3 fusion.174
  29.1 0.3 fusion.7
  29.4 0.1 fusion.14
  29.5 2.7 %collective-permute-start.6 = (f32[4,64]{1,0:T(4,128)S(1)}, f32[4,64]{1,0:T(4,128)S(1)}, u32[]{:S(2)}, u32[]{:S(2)}) collective-permute-start(f32[4,64]{1,0:T(4,128)S(1)} %slice_select_fusion.11), channel_id=1, source_target_pairs={{0,4},{1,5},{2,6},{3,7},{4,0},{5,1},{6,2},{7,3},{8,12},{9,13},{10,... | collective-permute-start | bytes 3080 | tf_op jit(solution)/shard_map/ppermute | solution.py:208
  32.2 1.9 %collective-permute-done.6 = f32[4,64]{1,0:T(4,128)S(1)} collective-permute-done((f32[4,64]{1,0:T(4,128)S(1)}, f32[4,64]{1,0:T(4,128)S(1)}, u32[]{:S(2)}, u32[]{:S(2)}) %collective-permute-start.6) | collective-permute-done | bytes 1056 | tf_op jit(solution)/shard_map/ppermute | solution.py:208
  34.1 1.6 %collective-permute-start.7 = (f32[2,64]{1,0:T(2,128)S(1)}, f32[2,64]{1,0:T(2,128)S(1)}, u32[]{:S(2)}, u32[]{:S(2)}) collective-permute-start(f32[2,64]{1,0:T(2,128)S(1)} %broadcast_select_fusion.3), channel_id=1, source_target_pairs={{0,2},{1,3},{2,0},{3,1},{4,6},{5,7},{6,4},{7,5},{8,10},{9,11},{10,... | collective-permute-start | bytes 1544 | tf_op jit(solution)/shard_map/ppermute | solution.py:208
  35.8 2.0 %collective-permute-done.7 = f32[2,64]{1,0:T(2,128)S(1)} collective-permute-done((f32[2,64]{1,0:T(2,128)S(1)}, f32[2,64]{1,0:T(2,128)S(1)}, u32[]{:S(2)}, u32[]{:S(2)}) %collective-permute-start.7) | collective-permute-done | bytes 544 | tf_op jit(solution)/shard_map/ppermute | solution.py:208
  37.7 0.1 collective-permute-start.8
  37.8 0.8 %copy.21 = f32[128,512]{1,0:T(8,128)} copy(f32[128,512]{0,1:T(8,128)S(1)} %pad_maximum_fusion.3) | data formatting | bytes 524288
  38.7 0.8 %copy.20 = f32[128,512]{1,0:T(8,128)} copy(f32[128,512]{0,1:T(8,128)S(1)} %pad_maximum_fusion.1) | data formatting | bytes 524288
  39.5 0.5 %fusion.146 = f32[64]{0:T(128)} fusion(f32[1,64]{1,0:T(1,128)S(1)} %collective-permute-done.8, pred[]{:T(512)S(6)} %ne.39, f32[2,64]{1,0:T(2,128)S(1)} %select_add_fusion.1), kind=kLoop, calls=%fused_computation.170 | loop fusion | flops 192 | bytes 1025 | tf_op jit(solution)/shard_map/mul | solution.py:210
  (36 shorter events, 0.2 us)
Async XLA Ops:
  0.6 3.2 %copy-start = (bf16[256,512]{1,0:T(8,128)(2,1)S(1)}, bf16[256,512]{1,0:T(8,128)(2,1)}, u32[]{:S(2)}) copy-start(bf16[256,512]{1,0:T(8,128)(2,1)} %param.19) | copy-start | bytes 786436
  0.6 1.7 %copy-start.4 = (bf16[512,512]{1,0:T(8,128)(2,1)S(1)}, bf16[512,512]{1,0:T(8,128)(2,1)}, u32[]{:S(2)}) copy-start(bf16[512,512]{1,0:T(8,128)(2,1)} %param.16) | copy-start | bytes 1572868
  2.5 0.7 %copy-start.6 = (s32[3,2]{0,1:T(2,128)S(1)}, s32[3,2]{0,1:T(2,128)}, u32[]{:S(2)}) copy-start(s32[3,2]{0,1:T(2,128)} %param.15) | copy-start | bytes 76
  3.2 0.6 %copy-start.9 = (f32[128,128]{0,1:T(8,128)}, f32[128,128]{0,1:T(8,128)S(1)}, u32[]{:S(2)}) copy-start(f32[128,128]{0,1:T(8,128)S(1)} %convolution_subtract_fusion.5) | copy-start | bytes 196612
  3.8 2.2 %copy-start.3 = (bf16[512,512]{1,0:T(8,128)(2,1)S(1)}, bf16[512,512]{1,0:T(8,128)(2,1)}, u32[]{:S(2)}) copy-start(bf16[512,512]{1,0:T(8,128)(2,1)} %param.17) | copy-start | bytes 1572868
  4.1 0.8 %copy-start.5 = (f32[128,128]{1,0:T(8,128)S(1)}, f32[128,128]{1,0:T(8,128)}, u32[]{:S(2)}) copy-start(f32[128,128]{1,0:T(8,128)} %param.14) | copy-start | bytes 196612
  4.1 0.8 %copy-start.7 = (s32[128]{0:T(128)S(1)}, s32[128]{0:T(128)}, u32[]{:S(2)}) copy-start(s32[128]{0:T(128)} %param.13) | copy-start | bytes 1540
  4.9 0.9 %copy-start.2 = (bf16[4,128,128]{2,1,0:T(8,128)(2,1)S(1)}, bf16[4,128,128]{2,1,0:T(8,128)(2,1)}, u32[]{:S(2)}) copy-start(bf16[4,128,128]{2,1,0:T(8,128)(2,1)} %param.18) | copy-start | bytes 393220
  6.8 1.0 %copy-start.8 = (bf16[512,256]{1,0:T(8,128)(2,1)S(1)}, bf16[512,256]{1,0:T(8,128)(2,1)}, u32[]{:S(2)}) copy-start(bf16[512,256]{1,0:T(8,128)(2,1)} %param.20) | copy-start | bytes 786436
  8.0 3.6 %copy-start.1 = (bf16[2,128,128]{2,1,0:T(8,128)(2,1)S(1)}, bf16[2,128,128]{2,1,0:T(8,128)(2,1)}, u32[]{:S(2)}) copy-start(bf16[2,128,128]{2,1,0:T(8,128)(2,1)} %param.21) | copy-start | bytes 196612
  8.0 7.2 %collective-permute-start.4 = (f32[256,128]{1,0:T(8,128)S(1)}, f32[256,128]{1,0:T(8,128)S(1)}, u32[]{:S(2)}, u32[]{:S(2)}) collective-permute-start(f32[256,128]{1,0:T(8,128)S(1)} %pad_maximum_fusion.6), channel_id=1, source_target_pairs={{0,8},{8,0},{16,24},{24,16},{1,9},{9,1},{17,25},{25,17},{2,10},{10... | collective-permute-start | bytes 393224 | tf_op jit(solution)/shard_map/ppermute | solution.py:130
  13.1 6.4 %collective-permute-start.1 = (bf16[512,128]{1,0:T(8,128)(2,1)S(1)}, bf16[512,128]{1,0:T(8,128)(2,1)S(1)}, u32[]{:S(2)}, u32[]{:S(2)}) collective-permute-start(bf16[512,128]{1,0:T(8,128)(2,1)S(1)} %pad_maximum_fusion.5), channel_id=1, source_target_pairs={{0,8},{8,0},{16,24},{24,16},{1,9},{9,1},{17,25},{25,17},{2,10},{10... | collective-permute-start | bytes 393224 | tf_op jit(solution)/shard_map/ppermute | solution.py:130
  13.3 8.7 %collective-permute-start = (f32[256,128]{1,0:T(8,128)S(1)}, f32[256,128]{1,0:T(8,128)S(1)}, u32[]{:S(2)}, u32[]{:S(2)}) collective-permute-start(f32[256,128]{1,0:T(8,128)S(1)} %pad_maximum_fusion.4), channel_id=1, source_target_pairs={{0,8},{8,0},{16,24},{24,16},{1,9},{9,1},{17,25},{25,17},{2,10},{10... | collective-permute-start | bytes 393224 | tf_op jit(solution)/shard_map/ppermute | solution.py:130
  19.9 5.5 %collective-permute-start.5 = (f32[128,128]{1,0:T(8,128)S(1)}, f32[128,128]{1,0:T(8,128)S(1)}, u32[]{:S(2)}, u32[]{:S(2)}) collective-permute-start(f32[128,128]{1,0:T(8,128)S(1)} %fusion.63), channel_id=1, source_target_pairs={{0,16},{8,24},{16,0},{24,8},{1,17},{9,25},{17,1},{25,9},{2,18},{10... | collective-permute-start | bytes 196616 | tf_op jit(solution)/shard_map/ppermute | solution.py:130
  21.5 3.9 %collective-permute-start.3 = (bf16[128,128]{1,0:T(8,128)(2,1)S(1)}, bf16[128,128]{1,0:T(8,128)(2,1)S(1)}, u32[]{:S(2)}, u32[]{:S(2)}) collective-permute-start(bf16[128,128]{1,0:T(8,128)(2,1)S(1)} %slice_select_fusion.2), channel_id=1, source_target_pairs={{0,16},{8,24},{16,0},{24,8},{1,17},{9,25},{17,1},{25,9},{2,18},{10... | collective-permute-start | bytes 98312 | tf_op jit(solution)/shard_map/ppermute | solution.py:130
  22.3 4.7 %collective-permute-start.2 = (f32[128,128]{1,0:T(8,128)S(1)}, f32[128,128]{1,0:T(8,128)S(1)}, u32[]{:S(2)}, u32[]{:S(2)}) collective-permute-start(f32[128,128]{1,0:T(8,128)S(1)} %fusion.69), channel_id=1, source_target_pairs={{0,16},{8,24},{16,0},{24,8},{1,17},{9,25},{17,1},{25,9},{2,18},{10... | collective-permute-start | bytes 196616 | tf_op jit(solution)/shard_map/ppermute | solution.py:130
  27.2 0.9 %copy-start.10 = (f32[128,128]{0,1:T(8,128)S(1)}, f32[128,128]{0,1:T(8,128)}, u32[]{:S(2)}) copy-start(f32[128,128]{0,1:T(8,128)} %copy-done.9) | copy-start | bytes 196612
  29.5 4.5 %collective-permute-start.6 = (f32[4,64]{1,0:T(4,128)S(1)}, f32[4,64]{1,0:T(4,128)S(1)}, u32[]{:S(2)}, u32[]{:S(2)}) collective-permute-start(f32[4,64]{1,0:T(4,128)S(1)} %slice_select_fusion.11), channel_id=1, source_target_pairs={{0,4},{1,5},{2,6},{3,7},{4,0},{5,1},{6,2},{7,3},{8,12},{9,13},{10,... | collective-permute-start | bytes 3080 | tf_op jit(solution)/shard_map/ppermute | solution.py:208
  34.1 3.6 %collective-permute-start.7 = (f32[2,64]{1,0:T(2,128)S(1)}, f32[2,64]{1,0:T(2,128)S(1)}, u32[]{:S(2)}, u32[]{:S(2)}) collective-permute-start(f32[2,64]{1,0:T(2,128)S(1)} %broadcast_select_fusion.3), channel_id=1, source_target_pairs={{0,2},{1,3},{2,0},{3,1},{4,6},{5,7},{6,4},{7,5},{8,10},{9,11},{10,... | collective-permute-start | bytes 1544 | tf_op jit(solution)/shard_map/ppermute | solution.py:208
  37.7 1.8 %collective-permute-start.8 = (f32[1,64]{1,0:T(1,128)S(1)}, f32[1,64]{1,0:T(1,128)S(1)}, u32[]{:S(2)}, u32[]{:S(2)}) collective-permute-start(f32[1,64]{1,0:T(1,128)S(1)} %broadcast_select_fusion.4), channel_id=1, source_target_pairs={{0,1},{1,0},{2,3},{3,2},{4,5},{5,4},{6,7},{7,6},{8,9},{9,8},{10,11... | collective-permute-start | bytes 776 | tf_op jit(solution)/shard_map/ppermute | solution.py:208

commit v18 on v15

--- a/solution.py
+++ b/solution.py
@@ -125,11 +125,12 @@
         inverse_panels.append(sep_inv[height - 1])
 
     def exchange(values, pairs):
-        pieces = [piece for piece in values]
-        incoming = lax.ppermute(jnp.concatenate(pieces, axis=0), "leaf", pairs)
+        pieces = [piece for piece in values if piece.shape[0]]
+        joined = pieces[0] if len(pieces) == 1 else jnp.concatenate(pieces, axis=0)
+        incoming = lax.ppermute(joined, "leaf", pairs)
         received, row = [], 0
-        for piece in pieces:
-            received.append(incoming[row : row + piece.shape[0]])
+        for piece in values:
+            received.append(incoming[row : row + piece.shape[0]] if piece.shape[0] else piece)
             row += piece.shape[0]
         return received
 

time: 36.9 us -> 36.9 us (level)
  no operation moved by 1% of the time
where the time goes in v18:
time: 36.9 us; the launch traced here: 36.5 us
  starting transfers between devices  13.1 us (36%)
  waiting for transfers between devices  7.97 us (22%)
  matrix products  7.83 us (21%)
  local copies, waits for them, and re-layouts  4.12 us (11%)
  other arithmetic  2.44 us (7%)
  between operations  1.03 us (3%)
    ppermute x6, starting transfers between devices, exchange(): incoming = lax.ppermute(joined, 'leaf', pairs)  8.81 us
    ppermute x3, starting transfers between devices, shards(): partial_gradient = kept + lax.ppermute(outgoing, 'src', pairs)  4.32 us
    ppermute x6, waiting for transfers between devices, exchange(): incoming = lax.ppermute(joined, 'leaf', pairs)  4.05 us
    dot_general x13, matrix products, plain_dot(): return jnp.dot(former, latter, preferred_element_type=jnp.float32)  3.98 us
    ppermute x3, waiting for transfers between devices, shards(): partial_gradient = kept + lax.ppermute(outgoing, 'src', pairs)  3.92 us
    unnamed x20, local copies, waits for them, and re-layouts  3.05 us
    dot_general x12, matrix products, across(): lax.dot_general(former, latter, (((1,), (1,)), ((), ())), preferred_eleme...  2.54 us
    select_n x1, other arithmetic, masked(): return jnp.where(keep, values, jnp.zeros_like(values))  1.43 us
  transfers between devices with their start and end apart: 9, of which 4 were waited for; matrix products, arithmetic and copies ran while one was open for 18% of the time, Pallas kernels for 0%

profile of v18, /device:TPU:0, one launch (start us, length us, event | category | flops | bytes accessed | tf_op | source)
XLA Modules:
  0.0 36.5 jit_solution(10820312538429912757)
XLA Ops:
  0.6 0.0 copy-start
  0.7 0.0 copy-start.3
  0.7 1.3 %convolution_bitcast_fusion = f32[128,512]{0,1:T(8,128)S(1)} fusion(f32[128,128]{1,0:T(8,128)} %param.14, s32[128]{0:T(128)} %param.13), kind=kOutput, calls=%fused_computation.2 | convolution fusion | flops 100794368 | bytes 328192 | tf_op jit(solution)/shard_map/dot_general | solution.py:112
  2.0 0.2 fusion.181
  2.2 1.1 %fusion.182 = (bf16[128,128]{0,1:T(8,128)(2,1)S(1)}, f32[128,128]{0,1:T(8,128)S(1)}) fusion(bf16[4,128,128]{2,1,0:T(8,128)(2,1)S(1)} %copy-done.2, bf16[128,128]{0,1:T(8,128)(2,1)S(1)} %get-tuple-element.24, f32[128,512]{0,1:T(8,128)S(1)} %convolution_bitcast_fusion, bf16[512,512]{1,0:T(8,128)(2,1)} %param.17), kind=kOutput, calls=%fused_computation.199 | convolution fusion | flops 8437760 | bytes 262144 | tf_op jit(solution)/shard_map/dot_general | solution.py:16
  3.3 0.4 fusion.185
  3.7 0.0 copy-start.6
  3.7 0.0 copy-start.5
  3.7 0.4 fusion.10
  4.1 0.3 copy-done.5
  4.4 0.2 compare_reduce_fusion
  4.6 0.1 broadcast_bitcast_fusion
  4.7 0.2 convolution_select_fusion
  5.0 0.0 copy-start.1
  5.0 0.0 copy-start.4
  5.0 3.0 %collective-permute-start.4 = (f32[256,128]{1,0:T(8,128)S(1)}, f32[256,128]{1,0:T(8,128)S(1)}, u32[]{:S(2)}, u32[]{:S(2)}) collective-permute-start(f32[256,128]{1,0:T(8,128)S(1)} %pad_maximum_fusion.6), channel_id=1, source_target_pairs={{0,8},{8,0},{16,24},{24,16},{1,9},{9,1},{17,25},{25,17},{2,10},{10... | collective-permute-start | bytes 393224 | tf_op jit(solution)/shard_map/ppermute | solution.py:130
  8.0 0.6 %slice.198 = pred[1]{0:T(512)(128)(4,1)} slice(pred[2]{0:T(512)(128)(4,1)S(1)} %compare_and_fusion), slice={[1:2]} | slice | bytes 2 | tf_op jit(solution)/shard_map/slice | solution.py:122
  8.6 1.4 %select_bitcast_fusion = (bf16[128,128]{1,0:T(8,128)(2,1)S(1)}, bf16[128,128]{1,0:T(8,128)(2,1)S(1)}) fusion(bf16[2,128,256]{2,1,0:T(8,128)(2,1)} %param.23, pred[]{:T(512)} %bitcast.1, bf16[2,256,128]{2,1,0:T(8,128)(2,1)} %param.22), kind=kLoop, calls=%fused_computation.142 | loop fusion | flops 32768 | bytes 131073 | tf_op jit(solution)/shard_map/jit(_where)/select_n | solution.py:102
  10.1 0.2 collective-permute-start.1
  10.3 0.7 %copy-done.8 = s32[128]{0:T(128)S(1)} copy-done((s32[128]{0:T(128)S(1)}, s32[128]{0:T(128)}, u32[]{:S(2)}) %copy-start.8) | copy-done | bytes 536
  11.0 0.1 fusion.170
  11.1 0.1 fusion.171
  11.3 0.2 convolution_subtract_fusion.5
  11.5 0.2 convolution_select_fusion.1
  11.8 2.0 %collective-permute-start = (f32[256,128]{1,0:T(8,128)S(1)}, f32[256,128]{1,0:T(8,128)S(1)}, u32[]{:S(2)}, u32[]{:S(2)}) collective-permute-start(f32[256,128]{1,0:T(8,128)S(1)} %pad_maximum_fusion.4), channel_id=1, source_target_pairs={{0,8},{8,0},{16,24},{24,16},{1,9},{9,1},{17,25},{25,17},{2,10},{10... | collective-permute-start | bytes 393224 | tf_op jit(solution)/shard_map/ppermute | solution.py:130
  13.7 0.0 collective-permute-done.4
  13.7 2.5 %collective-permute-done.1 = bf16[512,128]{1,0:T(8,128)(2,1)S(1)} collective-permute-done((bf16[512,128]{1,0:T(8,128)(2,1)S(1)}, bf16[512,128]{1,0:T(8,128)(2,1)S(1)}, u32[]{:S(2)}, u32[]{:S(2)}) %collective-permute-start.1) | collective-permute-done | bytes 131104 | tf_op jit(solution)/shard_map/ppermute | solution.py:130
  16.2 0.2 fusion.106
  16.4 0.2 fusion.63
  16.6 1.6 %collective-permute-start.5 = (f32[128,128]{1,0:T(8,128)S(1)}, f32[128,128]{1,0:T(8,128)S(1)}, u32[]{:S(2)}, u32[]{:S(2)}) collective-permute-start(f32[128,128]{1,0:T(8,128)S(1)} %fusion.63), channel_id=1, source_target_pairs={{0,16},{8,24},{16,0},{24,8},{1,17},{9,25},{17,1},{25,9},{2,18},{10... | collective-permute-start | bytes 196616 | tf_op jit(solution)/shard_map/ppermute | solution.py:130
  18.2 0.5 %collective-permute-start.3 = (bf16[128,128]{1,0:T(8,128)(2,1)S(1)}, bf16[128,128]{1,0:T(8,128)(2,1)S(1)}, u32[]{:S(2)}, u32[]{:S(2)}) collective-permute-start(bf16[128,128]{1,0:T(8,128)(2,1)S(1)} %slice_select_fusion.2), channel_id=1, source_target_pairs={{0,16},{8,24},{16,0},{24,8},{1,17},{9,25},{17,1},{25,9},{2,18},{10... | collective-permute-start | bytes 98312 | tf_op jit(solution)/shard_map/ppermute | solution.py:130
  18.7 0.0 collective-permute-done
  18.7 0.2 fusion.72
  18.9 0.1 copy.17
  19.0 1.6 %collective-permute-start.2 = (f32[128,128]{1,0:T(8,128)S(1)}, f32[128,128]{1,0:T(8,128)S(1)}, u32[]{:S(2)}, u32[]{:S(2)}) collective-permute-start(f32[128,128]{1,0:T(8,128)S(1)} %fusion.72), channel_id=1, source_target_pairs={{0,16},{8,24},{16,0},{24,8},{1,17},{9,25},{17,1},{25,9},{2,18},{10... | collective-permute-start | bytes 196616 | tf_op jit(solution)/shard_map/ppermute | solution.py:130
  20.5 1.6 %collective-permute-done.3 = bf16[128,128]{1,0:T(8,128)(2,1)S(1)} collective-permute-done((bf16[128,128]{1,0:T(8,128)(2,1)S(1)}, bf16[128,128]{1,0:T(8,128)(2,1)S(1)}, u32[]{:S(2)}, u32[]{:S(2)}) %collective-permute-start.3) | collective-permute-done | bytes 32800 | tf_op jit(solution)/shard_map/ppermute | solution.py:130
  22.1 0.0 collective-permute-done.5
  22.1 0.2 fusion.103
  22.3 0.1 copy.18
  22.4 0.2 fusion.117
  22.6 0.3 convolution_subtract_fusion
  22.9 0.2 fusion.190
  23.2 0.2 fusion.191
  23.4 0.2 convolution_subtract_fusion.8
  23.6 0.0 copy-start.7
  23.6 0.0 collective-permute-done.2
  23.7 0.1 fusion.102
  23.8 0.1 copy.15
  23.9 0.3 fusion.13
  24.3 0.3 copy-done.7
  24.6 0.2 convolution_subtract_fusion.1
  24.8 0.1 fusion.172
  24.9 0.3 fusion.173
  25.2 0.3 fusion.176
  25.5 0.3 fusion.7
  25.9 0.1 fusion.14
  26.0 2.6 %collective-permute-start.6 = (f32[4,64]{1,0:T(4,128)S(1)}, f32[4,64]{1,0:T(4,128)S(1)}, u32[]{:S(2)}, u32[]{:S(2)}) collective-permute-start(f32[4,64]{1,0:T(4,128)S(1)} %slice_select_fusion.11), channel_id=1, source_target_pairs={{0,4},{1,5},{2,6},{3,7},{4,0},{5,1},{6,2},{7,3},{8,12},{9,13},{10,... | collective-permute-start | bytes 3080 | tf_op jit(solution)/shard_map/ppermute | solution.py:208
  28.6 1.9 %collective-permute-done.6 = f32[4,64]{1,0:T(4,128)S(1)} collective-permute-done((f32[4,64]{1,0:T(4,128)S(1)}, f32[4,64]{1,0:T(4,128)S(1)}, u32[]{:S(2)}, u32[]{:S(2)}) %collective-permute-start.6) | collective-permute-done | bytes 1056 | tf_op jit(solution)/shard_map/ppermute | solution.py:208
  30.6 1.6 %collective-permute-start.7 = (f32[2,64]{1,0:T(2,128)S(1)}, f32[2,64]{1,0:T(2,128)S(1)}, u32[]{:S(2)}, u32[]{:S(2)}) collective-permute-start(f32[2,64]{1,0:T(2,128)S(1)} %broadcast_select_fusion.3), channel_id=1, source_target_pairs={{0,2},{1,3},{2,0},{3,1},{4,6},{5,7},{6,4},{7,5},{8,10},{9,11},{10,... | collective-permute-start | bytes 1544 | tf_op jit(solution)/shard_map/ppermute | solution.py:208
  32.2 2.0 %collective-permute-done.7 = f32[2,64]{1,0:T(2,128)S(1)} collective-permute-done((f32[2,64]{1,0:T(2,128)S(1)}, f32[2,64]{1,0:T(2,128)S(1)}, u32[]{:S(2)}, u32[]{:S(2)}) %collective-permute-start.7) | collective-permute-done | bytes 544 | tf_op jit(solution)/shard_map/ppermute | solution.py:208
  34.2 0.1 collective-permute-start.8
  34.3 0.8 %copy.21 = f32[128,512]{1,0:T(8,128)} copy(f32[128,512]{0,1:T(8,128)S(1)} %pad_maximum_fusion.3) | data formatting | bytes 524288
  35.2 0.8 %copy.20 = f32[128,512]{1,0:T(8,128)} copy(f32[128,512]{0,1:T(8,128)S(1)} %pad_maximum_fusion.1) | data formatting | bytes 524288
  36.0 0.5 %fusion.146 = f32[64]{0:T(128)} fusion(f32[1,64]{1,0:T(1,128)S(1)} %collective-permute-done.8, pred[]{:T(512)S(6)} %ne.39, f32[2,64]{1,0:T(2,128)S(1)} %select_add_fusion.1), kind=kLoop, calls=%fused_computation.170 | loop fusion | flops 192 | bytes 1025 | tf_op jit(solution)/shard_map/mul | solution.py:210
  (32 shorter events, 0.2 us)
Async XLA Ops:
  0.6 10.8 %copy-start = (bf16[256,512]{1,0:T(8,128)(2,1)S(1)}, bf16[256,512]{1,0:T(8,128)(2,1)}, u32[]{:S(2)}) copy-start(bf16[256,512]{1,0:T(8,128)(2,1)} %param.19) | copy-start | bytes 786436
  0.6 1.3 %copy-start.2 = (bf16[4,128,128]{2,1,0:T(8,128)(2,1)S(1)}, bf16[4,128,128]{2,1,0:T(8,128)(2,1)}, u32[]{:S(2)}) copy-start(bf16[4,128,128]{2,1,0:T(8,128)(2,1)} %param.18) | copy-start | bytes 393220
  0.7 2.7 %copy-start.3 = (bf16[512,512]{1,0:T(8,128)(2,1)S(1)}, bf16[512,512]{1,0:T(8,128)(2,1)}, u32[]{:S(2)}) copy-start(bf16[512,512]{1,0:T(8,128)(2,1)} %param.17) | copy-start | bytes 1572868
  3.7 1.0 %copy-start.6 = (bf16[512,256]{1,0:T(8,128)(2,1)S(1)}, bf16[512,256]{1,0:T(8,128)(2,1)}, u32[]{:S(2)}) copy-start(bf16[512,256]{1,0:T(8,128)(2,1)} %param.20) | copy-start | bytes 786436
  3.7 0.7 %copy-start.5 = (s32[3,2]{0,1:T(2,128)S(1)}, s32[3,2]{0,1:T(2,128)}, u32[]{:S(2)}) copy-start(s32[3,2]{0,1:T(2,128)} %param.15) | copy-start | bytes 76
  5.0 3.6 %copy-start.1 = (bf16[2,128,128]{2,1,0:T(8,128)(2,1)S(1)}, bf16[2,128,128]{2,1,0:T(8,128)(2,1)}, u32[]{:S(2)}) copy-start(bf16[2,128,128]{2,1,0:T(8,128)(2,1)} %param.21) | copy-start | bytes 196612
  5.0 6.0 %copy-start.4 = (bf16[512,512]{1,0:T(8,128)(2,1)S(1)}, bf16[512,512]{1,0:T(8,128)(2,1)}, u32[]{:S(2)}) copy-start(bf16[512,512]{1,0:T(8,128)(2,1)} %param.16) | copy-start | bytes 1572868
  5.0 8.7 %collective-permute-start.4 = (f32[256,128]{1,0:T(8,128)S(1)}, f32[256,128]{1,0:T(8,128)S(1)}, u32[]{:S(2)}, u32[]{:S(2)}) collective-permute-start(f32[256,128]{1,0:T(8,128)S(1)} %pad_maximum_fusion.6), channel_id=1, source_target_pairs={{0,8},{8,0},{16,24},{24,16},{1,9},{9,1},{17,25},{25,17},{2,10},{10... | collective-permute-start | bytes 393224 | tf_op jit(solution)/shard_map/ppermute | solution.py:130
  10.1 6.1 %collective-permute-start.1 = (bf16[512,128]{1,0:T(8,128)(2,1)S(1)}, bf16[512,128]{1,0:T(8,128)(2,1)S(1)}, u32[]{:S(2)}, u32[]{:S(2)}) collective-permute-start(bf16[512,128]{1,0:T(8,128)(2,1)S(1)} %pad_maximum_fusion.5), channel_id=1, source_target_pairs={{0,8},{8,0},{16,24},{24,16},{1,9},{9,1},{17,25},{25,17},{2,10},{10... | collective-permute-start | bytes 393224 | tf_op jit(solution)/shard_map/ppermute | solution.py:130
  10.2 0.7 %copy-start.8 = (s32[128]{0:T(128)S(1)}, s32[128]{0:T(128)}, u32[]{:S(2)}) copy-start(s32[128]{0:T(128)} %param.12) | copy-start | bytes 1540
  11.8 6.9 %collective-permute-start = (f32[256,128]{1,0:T(8,128)S(1)}, f32[256,128]{1,0:T(8,128)S(1)}, u32[]{:S(2)}, u32[]{:S(2)}) collective-permute-start(f32[256,128]{1,0:T(8,128)S(1)} %pad_maximum_fusion.4), channel_id=1, source_target_pairs={{0,8},{8,0},{16,24},{24,16},{1,9},{9,1},{17,25},{25,17},{2,10},{10... | collective-permute-start | bytes 393224 | tf_op jit(solution)/shard_map/ppermute | solution.py:130
  16.6 5.5 %collective-permute-start.5 = (f32[128,128]{1,0:T(8,128)S(1)}, f32[128,128]{1,0:T(8,128)S(1)}, u32[]{:S(2)}, u32[]{:S(2)}) collective-permute-start(f32[128,128]{1,0:T(8,128)S(1)} %fusion.63), channel_id=1, source_target_pairs={{0,16},{8,24},{16,0},{24,8},{1,17},{9,25},{17,1},{25,9},{2,18},{10... | collective-permute-start | bytes 196616 | tf_op jit(solution)/shard_map/ppermute | solution.py:130
  18.2 3.9 %collective-permute-start.3 = (bf16[128,128]{1,0:T(8,128)(2,1)S(1)}, bf16[128,128]{1,0:T(8,128)(2,1)S(1)}, u32[]{:S(2)}, u32[]{:S(2)}) collective-permute-start(bf16[128,128]{1,0:T(8,128)(2,1)S(1)} %slice_select_fusion.2), channel_id=1, source_target_pairs={{0,16},{8,24},{16,0},{24,8},{1,17},{9,25},{17,1},{25,9},{2,18},{10... | collective-permute-start | bytes 98312 | tf_op jit(solution)/shard_map/ppermute | solution.py:130
  19.0 4.7 %collective-permute-start.2 = (f32[128,128]{1,0:T(8,128)S(1)}, f32[128,128]{1,0:T(8,128)S(1)}, u32[]{:S(2)}, u32[]{:S(2)}) collective-permute-start(f32[128,128]{1,0:T(8,128)S(1)} %fusion.72), channel_id=1, source_target_pairs={{0,16},{8,24},{16,0},{24,8},{1,17},{9,25},{17,1},{25,9},{2,18},{10... | collective-permute-start | bytes 196616 | tf_op jit(solution)/shard_map/ppermute | solution.py:130
  23.6 1.0 %copy-start.7 = (bf16[512,256]{1,0:T(8,128)(2,1)S(1)}, bf16[512,256]{1,0:T(8,128)(2,1)}, u32[]{:S(2)}) copy-start(bf16[512,256]{1,0:T(8,128)(2,1)} %param.20) | copy-start | bytes 786436
  26.0 4.5 %collective-permute-start.6 = (f32[4,64]{1,0:T(4,128)S(1)}, f32[4,64]{1,0:T(4,128)S(1)}, u32[]{:S(2)}, u32[]{:S(2)}) collective-permute-start(f32[4,64]{1,0:T(4,128)S(1)} %slice_select_fusion.11), channel_id=1, source_target_pairs={{0,4},{1,5},{2,6},{3,7},{4,0},{5,1},{6,2},{7,3},{8,12},{9,13},{10,... | collective-permute-start | bytes 3080 | tf_op jit(solution)/shard_map/ppermute | solution.py:208
  30.6 3.6 %collective-permute-start.7 = (f32[2,64]{1,0:T(2,128)S(1)}, f32[2,64]{1,0:T(2,128)S(1)}, u32[]{:S(2)}, u32[]{:S(2)}) collective-permute-start(f32[2,64]{1,0:T(2,128)S(1)} %broadcast_select_fusion.3), channel_id=1, source_target_pairs={{0,2},{1,3},{2,0},{3,1},{4,6},{5,7},{6,4},{7,5},{8,10},{9,11},{10,... | collective-permute-start | bytes 1544 | tf_op jit(solution)/shard_map/ppermute | solution.py:208
  34.2 1.8 %collective-permute-start.8 = (f32[1,64]{1,0:T(1,128)S(1)}, f32[1,64]{1,0:T(1,128)S(1)}, u32[]{:S(2)}, u32[]{:S(2)}) collective-permute-start(f32[1,64]{1,0:T(1,128)S(1)} %broadcast_select_fusion.4), channel_id=1, source_target_pairs={{0,1},{1,0},{2,3},{3,2},{4,5},{5,4},{6,7},{7,6},{8,9},{9,8},{10,11... | collective-permute-start | bytes 776 | tf_op jit(solution)/shard_map/ppermute | solution.py:208

commit v19 on v15

--- a/solution.py
+++ b/solution.py
@@ -197,15 +197,21 @@
     product_field = (forward_field * adjoint_field).reshape(source_count, spread, cell_count // spread)
     partial_gradient = jnp.sum(product_field, axis=0)
     place = lax.axis_index("src")
-    bit = spread // 2
-    while bit:
-        half = partial_gradient.shape[0] // 2
+    bits = [1 << k for k in reversed(range(spread.bit_length() - 1))]
+    if len(bits) > 2:
+        bits[0], bits[1] = bits[1], bits[0]
+    axes = [1 << k for k in reversed(range(spread.bit_length() - 1))]
+    partial_gradient = partial_gradient.reshape([2] * len(axes) + [cell_count // spread])
+    for bit in bits:
+        axis = axes.index(bit)
         upper = (place & bit) != 0
-        outgoing = jnp.where(upper, partial_gradient[:half], partial_gradient[half:])
-        kept = jnp.where(upper, partial_gradient[half:], partial_gradient[:half])
+        lower_half = lax.index_in_dim(partial_gradient, 0, axis, keepdims=False)
+        upper_half = lax.index_in_dim(partial_gradient, 1, axis, keepdims=False)
+        outgoing = jnp.where(upper, lower_half, upper_half)
+        kept = jnp.where(upper, upper_half, lower_half)
         pairs = [(index, index ^ bit) for index in range(spread)]
         partial_gradient = kept + lax.ppermute(outgoing, "src", pairs)
-        bit //= 2
+        axes.remove(bit)
     gradient = partial_gradient.reshape(-1) * factor
     return (forward_field, adjoint_field, gradient)
 

time: 36.9 us -> 36.9 us (level)
  no operation moved by 1% of the time
where the time goes in v19:
time: 36.9 us; the launch traced here: 36.5 us
  starting transfers between devices  13.1 us (36%)
  waiting for transfers between devices  7.97 us (22%)
  matrix products  7.83 us (21%)
  local copies, waits for them, and re-layouts  4.12 us (11%)
  other arithmetic  2.44 us (7%)
  between operations  1.03 us (3%)
    ppermute x6, starting transfers between devices, exchange(): incoming = lax.ppermute(jnp.concatenate(pieces, axis=0), 'leaf', pairs)  8.81 us
    ppermute x3, starting transfers between devices, shards(): partial_gradient = kept + lax.ppermute(outgoing, 'src', pairs)  4.31 us
    ppermute x6, waiting for transfers between devices, exchange(): incoming = lax.ppermute(jnp.concatenate(pieces, axis=0), 'leaf', pairs)  4.05 us
    dot_general x13, matrix products, plain_dot(): return jnp.dot(former, latter, preferred_element_type=jnp.float32)  3.98 us
    ppermute x3, waiting for transfers between devices, shards(): partial_gradient = kept + lax.ppermute(outgoing, 'src', pairs)  3.92 us
    unnamed x20, local copies, waits for them, and re-layouts  3.05 us
    dot_general x12, matrix products, across(): lax.dot_general(former, latter, (((1,), (1,)), ((), ())), preferred_eleme...  2.54 us
    select_n x1, other arithmetic, masked(): return jnp.where(keep, values, jnp.zeros_like(values))  1.43 us
  transfers between devices with their start and end apart: 9, of which 4 were waited for; matrix products, arithmetic and copies ran while one was open for 18% of the time, Pallas kernels for 0%

profile of v19, /device:TPU:0, one launch (start us, length us, event | category | flops | bytes accessed | tf_op | source)
XLA Modules:
  0.0 36.5 jit_solution(3652371919893724515)
XLA Ops:
  0.6 0.0 copy-start
  0.7 0.0 copy-start.3
  0.7 1.3 %convolution_bitcast_fusion = f32[128,512]{0,1:T(8,128)S(1)} fusion(f32[128,128]{1,0:T(8,128)} %param.14, s32[128]{0:T(128)} %param.13), kind=kOutput, calls=%fused_computation.2 | convolution fusion | flops 100794368 | bytes 328192 | tf_op jit(solution)/shard_map/dot_general | solution.py:112
  2.0 0.2 fusion.185
  2.2 1.1 %fusion.186 = (bf16[128,128]{0,1:T(8,128)(2,1)S(1)}, f32[128,128]{0,1:T(8,128)S(1)}) fusion(bf16[4,128,128]{2,1,0:T(8,128)(2,1)S(1)} %copy-done.2, bf16[128,128]{0,1:T(8,128)(2,1)S(1)} %get-tuple-element.27, f32[128,512]{0,1:T(8,128)S(1)} %convolution_bitcast_fusion, bf16[512,512]{1,0:T(8,128)(2,1)} %param.17), kind=kOutput, calls=%fused_computation.203 | convolution fusion | flops 8437760 | bytes 262144 | tf_op jit(solution)/shard_map/dot_general | solution.py:16
  3.3 0.4 fusion.189
  3.7 0.0 copy-start.6
  3.7 0.0 copy-start.5
  3.7 0.4 fusion.10
  4.1 0.3 copy-done.5
  4.4 0.2 compare_reduce_fusion
  4.6 0.1 broadcast_bitcast_fusion
  4.7 0.2 convolution_select_fusion
  5.0 0.0 copy-start.1
  5.0 0.0 copy-start.4
  5.0 3.0 %collective-permute-start.4 = (f32[256,128]{1,0:T(8,128)S(1)}, f32[256,128]{1,0:T(8,128)S(1)}, u32[]{:S(2)}, u32[]{:S(2)}) collective-permute-start(f32[256,128]{1,0:T(8,128)S(1)} %pad_maximum_fusion.6), channel_id=1, source_target_pairs={{0,8},{8,0},{16,24},{24,16},{1,9},{9,1},{17,25},{25,17},{2,10},{10... | collective-permute-start | bytes 393224 | tf_op jit(solution)/shard_map/ppermute | solution.py:129
  8.0 0.6 %slice.192 = pred[1]{0:T(512)(128)(4,1)} slice(pred[2]{0:T(512)(128)(4,1)S(1)} %compare_and_fusion), slice={[1:2]} | slice | bytes 2 | tf_op jit(solution)/shard_map/slice | solution.py:122
  8.6 1.4 %select_bitcast_fusion = (bf16[128,128]{1,0:T(8,128)(2,1)S(1)}, bf16[128,128]{1,0:T(8,128)(2,1)S(1)}) fusion(bf16[2,128,256]{2,1,0:T(8,128)(2,1)} %param.23, pred[]{:T(512)} %bitcast.1, bf16[2,256,128]{2,1,0:T(8,128)(2,1)} %param.22), kind=kLoop, calls=%fused_computation.142 | loop fusion | flops 32768 | bytes 131073 | tf_op jit(solution)/shard_map/jit(_where)/select_n | solution.py:102
  10.1 0.2 collective-permute-start.1
  10.3 0.7 %copy-done.8 = s32[128]{0:T(128)S(1)} copy-done((s32[128]{0:T(128)S(1)}, s32[128]{0:T(128)}, u32[]{:S(2)}) %copy-start.8) | copy-done | bytes 536
  11.0 0.1 fusion.174
  11.1 0.1 fusion.175
  11.3 0.2 convolution_subtract_fusion.5
  11.5 0.2 convolution_select_fusion.1
  11.8 2.0 %collective-permute-start = (f32[256,128]{1,0:T(8,128)S(1)}, f32[256,128]{1,0:T(8,128)S(1)}, u32[]{:S(2)}, u32[]{:S(2)}) collective-permute-start(f32[256,128]{1,0:T(8,128)S(1)} %pad_maximum_fusion.4), channel_id=1, source_target_pairs={{0,8},{8,0},{16,24},{24,16},{1,9},{9,1},{17,25},{25,17},{2,10},{10... | collective-permute-start | bytes 393224 | tf_op jit(solution)/shard_map/ppermute | solution.py:129
  13.7 0.0 collective-permute-done.4
  13.7 2.5 %collective-permute-done.1 = bf16[512,128]{1,0:T(8,128)(2,1)S(1)} collective-permute-done((bf16[512,128]{1,0:T(8,128)(2,1)S(1)}, bf16[512,128]{1,0:T(8,128)(2,1)S(1)}, u32[]{:S(2)}, u32[]{:S(2)}) %collective-permute-start.1) | collective-permute-done | bytes 131104 | tf_op jit(solution)/shard_map/ppermute | solution.py:129
  16.2 0.2 fusion.106
  16.4 0.2 fusion.63
  16.6 1.6 %collective-permute-start.5 = (f32[128,128]{1,0:T(8,128)S(1)}, f32[128,128]{1,0:T(8,128)S(1)}, u32[]{:S(2)}, u32[]{:S(2)}) collective-permute-start(f32[128,128]{1,0:T(8,128)S(1)} %fusion.63), channel_id=1, source_target_pairs={{0,16},{8,24},{16,0},{24,8},{1,17},{9,25},{17,1},{25,9},{2,18},{10... | collective-permute-start | bytes 196616 | tf_op jit(solution)/shard_map/ppermute | solution.py:129
  18.2 0.5 %collective-permute-start.3 = (bf16[128,128]{1,0:T(8,128)(2,1)S(1)}, bf16[128,128]{1,0:T(8,128)(2,1)S(1)}, u32[]{:S(2)}, u32[]{:S(2)}) collective-permute-start(bf16[128,128]{1,0:T(8,128)(2,1)S(1)} %slice_select_fusion.2), channel_id=1, source_target_pairs={{0,16},{8,24},{16,0},{24,8},{1,17},{9,25},{17,1},{25,9},{2,18},{10... | collective-permute-start | bytes 98312 | tf_op jit(solution)/shard_map/ppermute | solution.py:129
  18.7 0.0 collective-permute-done
  18.7 0.2 fusion.72
  18.9 0.1 copy.24
  19.0 1.6 %collective-permute-start.2 = (f32[128,128]{1,0:T(8,128)S(1)}, f32[128,128]{1,0:T(8,128)S(1)}, u32[]{:S(2)}, u32[]{:S(2)}) collective-permute-start(f32[128,128]{1,0:T(8,128)S(1)} %fusion.72), channel_id=1, source_target_pairs={{0,16},{8,24},{16,0},{24,8},{1,17},{9,25},{17,1},{25,9},{2,18},{10... | collective-permute-start | bytes 196616 | tf_op jit(solution)/shard_map/ppermute | solution.py:129
  20.5 1.6 %collective-permute-done.3 = bf16[128,128]{1,0:T(8,128)(2,1)S(1)} collective-permute-done((bf16[128,128]{1,0:T(8,128)(2,1)S(1)}, bf16[128,128]{1,0:T(8,128)(2,1)S(1)}, u32[]{:S(2)}, u32[]{:S(2)}) %collective-permute-start.3) | collective-permute-done | bytes 32800 | tf_op jit(solution)/shard_map/ppermute | solution.py:129
  22.1 0.0 collective-permute-done.5
  22.1 0.2 fusion.103
  22.3 0.1 copy.25
  22.4 0.2 fusion.117
  22.6 0.3 convolution_subtract_fusion
  22.9 0.2 fusion.194
  23.2 0.2 fusion.195
  23.4 0.2 convolution_subtract_fusion.8
  23.6 0.0 copy-start.7
  23.6 0.0 collective-permute-done.2
  23.7 0.1 fusion.102
  23.8 0.1 copy.22
  23.9 0.3 fusion.13
  24.3 0.3 copy-done.7
  24.6 0.2 convolution_subtract_fusion.1
  24.8 0.1 fusion.176
  24.9 0.3 fusion.177
  25.2 0.3 fusion.180
  25.5 0.3 fusion.7
  25.9 0.1 fusion.14
  26.0 1.6 %collective-permute-start.6 = (f32[2,2,64]{2,1,0:T(2,128)S(1)}, f32[2,2,64]{2,1,0:T(2,128)S(1)}, u32[]{:S(2)}, u32[]{:S(2)}) collective-permute-start(f32[2,2,64]{2,1,0:T(2,128)S(1)} %fusion.144), channel_id=1, source_target_pairs={{0,2},{1,3},{2,0},{3,1},{4,6},{5,7},{6,4},{7,5},{8,10},{9,11},{10,... | collective-permute-start | bytes 3080 | tf_op jit(solution)/shard_map/ppermute | solution.py:213
  27.6 2.0 %collective-permute-done.6 = f32[2,2,64]{2,1,0:T(2,128)S(1)} collective-permute-done((f32[2,2,64]{2,1,0:T(2,128)S(1)}, f32[2,2,64]{2,1,0:T(2,128)S(1)}, u32[]{:S(2)}, u32[]{:S(2)}) %collective-permute-start.6) | collective-permute-done | bytes 1056 | tf_op jit(solution)/shard_map/ppermute | solution.py:213
  29.7 2.6 %collective-permute-start.7 = (f32[2,64]{1,0:T(2,128)S(1)}, f32[2,64]{1,0:T(2,128)S(1)}, u32[]{:S(2)}, u32[]{:S(2)}) collective-permute-start(f32[2,64]{1,0:T(2,128)S(1)} %select_bitcast_fusion.2), channel_id=1, source_target_pairs={{0,4},{1,5},{2,6},{3,7},{4,0},{5,1},{6,2},{7,3},{8,12},{9,13},{10,... | collective-permute-start | bytes 1544 | tf_op jit(solution)/shard_map/ppermute | solution.py:213
  32.3 1.9 %collective-permute-done.7 = f32[2,64]{1,0:T(2,128)S(1)} collective-permute-done((f32[2,64]{1,0:T(2,128)S(1)}, f32[2,64]{1,0:T(2,128)S(1)}, u32[]{:S(2)}, u32[]{:S(2)}) %collective-permute-start.7) | collective-permute-done | bytes 544 | tf_op jit(solution)/shard_map/ppermute | solution.py:213
  34.2 0.1 collective-permute-start.8
  34.3 0.8 %copy.32 = f32[128,512]{1,0:T(8,128)} copy(f32[128,512]{0,1:T(8,128)S(1)} %pad_maximum_fusion.3) | data formatting | bytes 524288
  35.2 0.8 %copy.31 = f32[128,512]{1,0:T(8,128)} copy(f32[128,512]{0,1:T(8,128)S(1)} %pad_maximum_fusion.1) | data formatting | bytes 524288
  36.0 0.5 %fusion.149 = f32[64]{0:T(128)} fusion(f32[64]{0:T(128)S(1)} %collective-permute-done.8, pred[]{:T(512)S(6)} %ne.39, f32[2,64]{1,0:T(2,128)S(1)} %bitcast_add_fusion), kind=kLoop, calls=%fused_computation.172 | loop fusion | flops 192 | bytes 1025 | tf_op jit(solution)/shard_map/mul | solution.py:215
  (32 shorter events, 0.2 us)
Async XLA Ops:
  0.6 10.8 %copy-start = (bf16[256,512]{1,0:T(8,128)(2,1)S(1)}, bf16[256,512]{1,0:T(8,128)(2,1)}, u32[]{:S(2)}) copy-start(bf16[256,512]{1,0:T(8,128)(2,1)} %param.19) | copy-start | bytes 786436
  0.6 1.3 %copy-start.2 = (bf16[4,128,128]{2,1,0:T(8,128)(2,1)S(1)}, bf16[4,128,128]{2,1,0:T(8,128)(2,1)}, u32[]{:S(2)}) copy-start(bf16[4,128,128]{2,1,0:T(8,128)(2,1)} %param.18) | copy-start | bytes 393220
  0.7 2.7 %copy-start.3 = (bf16[512,512]{1,0:T(8,128)(2,1)S(1)}, bf16[512,512]{1,0:T(8,128)(2,1)}, u32[]{:S(2)}) copy-start(bf16[512,512]{1,0:T(8,128)(2,1)} %param.17) | copy-start | bytes 1572868
  3.7 1.0 %copy-start.6 = (bf16[512,256]{1,0:T(8,128)(2,1)S(1)}, bf16[512,256]{1,0:T(8,128)(2,1)}, u32[]{:S(2)}) copy-start(bf16[512,256]{1,0:T(8,128)(2,1)} %param.20) | copy-start | bytes 786436
  3.7 0.7 %copy-start.5 = (s32[3,2]{0,1:T(2,128)S(1)}, s32[3,2]{0,1:T(2,128)}, u32[]{:S(2)}) copy-start(s32[3,2]{0,1:T(2,128)} %param.15) | copy-start | bytes 76
  5.0 3.6 %copy-start.1 = (bf16[2,128,128]{2,1,0:T(8,128)(2,1)S(1)}, bf16[2,128,128]{2,1,0:T(8,128)(2,1)}, u32[]{:S(2)}) copy-start(bf16[2,128,128]{2,1,0:T(8,128)(2,1)} %param.21) | copy-start | bytes 196612
  5.0 6.0 %copy-start.4 = (bf16[512,512]{1,0:T(8,128)(2,1)S(1)}, bf16[512,512]{1,0:T(8,128)(2,1)}, u32[]{:S(2)}) copy-start(bf16[512,512]{1,0:T(8,128)(2,1)} %param.16) | copy-start | bytes 1572868
  5.0 8.7 %collective-permute-start.4 = (f32[256,128]{1,0:T(8,128)S(1)}, f32[256,128]{1,0:T(8,128)S(1)}, u32[]{:S(2)}, u32[]{:S(2)}) collective-permute-start(f32[256,128]{1,0:T(8,128)S(1)} %pad_maximum_fusion.6), channel_id=1, source_target_pairs={{0,8},{8,0},{16,24},{24,16},{1,9},{9,1},{17,25},{25,17},{2,10},{10... | collective-permute-start | bytes 393224 | tf_op jit(solution)/shard_map/ppermute | solution.py:129
  10.1 6.1 %collective-permute-start.1 = (bf16[512,128]{1,0:T(8,128)(2,1)S(1)}, bf16[512,128]{1,0:T(8,128)(2,1)S(1)}, u32[]{:S(2)}, u32[]{:S(2)}) collective-permute-start(bf16[512,128]{1,0:T(8,128)(2,1)S(1)} %pad_maximum_fusion.5), channel_id=1, source_target_pairs={{0,8},{8,0},{16,24},{24,16},{1,9},{9,1},{17,25},{25,17},{2,10},{10... | collective-permute-start | bytes 393224 | tf_op jit(solution)/shard_map/ppermute | solution.py:129
  10.2 0.7 %copy-start.8 = (s32[128]{0:T(128)S(1)}, s32[128]{0:T(128)}, u32[]{:S(2)}) copy-start(s32[128]{0:T(128)} %param.12) | copy-start | bytes 1540
  11.8 6.9 %collective-permute-start = (f32[256,128]{1,0:T(8,128)S(1)}, f32[256,128]{1,0:T(8,128)S(1)}, u32[]{:S(2)}, u32[]{:S(2)}) collective-permute-start(f32[256,128]{1,0:T(8,128)S(1)} %pad_maximum_fusion.4), channel_id=1, source_target_pairs={{0,8},{8,0},{16,24},{24,16},{1,9},{9,1},{17,25},{25,17},{2,10},{10... | collective-permute-start | bytes 393224 | tf_op jit(solution)/shard_map/ppermute | solution.py:129
  16.6 5.5 %collective-permute-start.5 = (f32[128,128]{1,0:T(8,128)S(1)}, f32[128,128]{1,0:T(8,128)S(1)}, u32[]{:S(2)}, u32[]{:S(2)}) collective-permute-start(f32[128,128]{1,0:T(8,128)S(1)} %fusion.63), channel_id=1, source_target_pairs={{0,16},{8,24},{16,0},{24,8},{1,17},{9,25},{17,1},{25,9},{2,18},{10... | collective-permute-start | bytes 196616 | tf_op jit(solution)/shard_map/ppermute | solution.py:129
  18.2 3.9 %collective-permute-start.3 = (bf16[128,128]{1,0:T(8,128)(2,1)S(1)}, bf16[128,128]{1,0:T(8,128)(2,1)S(1)}, u32[]{:S(2)}, u32[]{:S(2)}) collective-permute-start(bf16[128,128]{1,0:T(8,128)(2,1)S(1)} %slice_select_fusion.2), channel_id=1, source_target_pairs={{0,16},{8,24},{16,0},{24,8},{1,17},{9,25},{17,1},{25,9},{2,18},{10... | collective-permute-start | bytes 98312 | tf_op jit(solution)/shard_map/ppermute | solution.py:129
  19.0 4.7 %collective-permute-start.2 = (f32[128,128]{1,0:T(8,128)S(1)}, f32[128,128]{1,0:T(8,128)S(1)}, u32[]{:S(2)}, u32[]{:S(2)}) collective-permute-start(f32[128,128]{1,0:T(8,128)S(1)} %fusion.72), channel_id=1, source_target_pairs={{0,16},{8,24},{16,0},{24,8},{1,17},{9,25},{17,1},{25,9},{2,18},{10... | collective-permute-start | bytes 196616 | tf_op jit(solution)/shard_map/ppermute | solution.py:129
  23.6 1.0 %copy-start.7 = (bf16[512,256]{1,0:T(8,128)(2,1)S(1)}, bf16[512,256]{1,0:T(8,128)(2,1)}, u32[]{:S(2)}) copy-start(bf16[512,256]{1,0:T(8,128)(2,1)} %param.20) | copy-start | bytes 786436
  26.0 3.7 %collective-permute-start.6 = (f32[2,2,64]{2,1,0:T(2,128)S(1)}, f32[2,2,64]{2,1,0:T(2,128)S(1)}, u32[]{:S(2)}, u32[]{:S(2)}) collective-permute-start(f32[2,2,64]{2,1,0:T(2,128)S(1)} %fusion.144), channel_id=1, source_target_pairs={{0,2},{1,3},{2,0},{3,1},{4,6},{5,7},{6,4},{7,5},{8,10},{9,11},{10,... | collective-permute-start | bytes 3080 | tf_op jit(solution)/shard_map/ppermute | solution.py:213
  29.7 4.5 %collective-permute-start.7 = (f32[2,64]{1,0:T(2,128)S(1)}, f32[2,64]{1,0:T(2,128)S(1)}, u32[]{:S(2)}, u32[]{:S(2)}) collective-permute-start(f32[2,64]{1,0:T(2,128)S(1)} %select_bitcast_fusion.2), channel_id=1, source_target_pairs={{0,4},{1,5},{2,6},{3,7},{4,0},{5,1},{6,2},{7,3},{8,12},{9,13},{10,... | collective-permute-start | bytes 1544 | tf_op jit(solution)/shard_map/ppermute | solution.py:213
  34.2 1.8 %collective-permute-start.8 = (f32[64]{0:T(128)S(1)}, f32[64]{0:T(128)S(1)}, u32[]{:S(2)}, u32[]{:S(2)}) collective-permute-start(f32[64]{0:T(128)S(1)} %fusion.150), channel_id=1, source_target_pairs={{0,1},{1,0},{2,3},{3,2},{4,5},{5,4},{6,7},{7,6},{8,9},{9,8},{10,11... | collective-permute-start | bytes 776 | tf_op jit(solution)/shard_map/ppermute | solution.py:213

commit v20 on v15

--- a/solution.py
+++ b/solution.py
@@ -108,8 +108,14 @@
     forcing = (src_cells[:, None] - device * cell_count == columns).astype(jnp.float32)
     receiver_hits = (
         rec_cells[:, None] == lax.broadcasted_iota(jnp.int32, (rec_cells.shape[0], cell_count), 1)
-    ).astype(jnp.float32)
-    adjoint_rhs = jnp.dot(residual, receiver_hits, precision=lax.Precision.HIGHEST)
+    ).astype(jnp.bfloat16)
+    leading = residual.astype(jnp.bfloat16)
+    rest = residual - leading.astype(jnp.float32)
+    middle = rest.astype(jnp.bfloat16)
+    trailing = (rest - middle.astype(jnp.float32)).astype(jnp.bfloat16)
+    adjoint_rhs = (
+        plain_dot(leading, receiver_hits) + plain_dot(middle, receiver_hits)
+    ) + plain_dot(trailing, receiver_hits)
 
     base_mask = level_mask(0)
     y_leaf = lower_solve(forcing, leaf_lower, block_size, block_count)

time: 36.9 us -> 37.3 us (1.011)
  local copies, waits for them, and re-layouts: 4.12 us -> 4.73 us
    dot_general x1 -> x0, matrix products: 1.31 us -> none  [shards(): jnp.dot(residual, receiver_hits, precision=lax.Precision.HIGHEST)]
    dot_general x13 -> x16, matrix products: 3.98 us -> 5.08 us  [plain_dot(): return jnp.dot(former, latter, preferred_element_type=jnp.float32)]
    unnamed x20 -> x24, local copies, waits for them, and re-layouts: 3.05 us -> 3.66 us
where the time goes in v20:
time: 37.3 us; the launch traced here: 36.9 us
  starting transfers between devices  13.1 us (35%)
  waiting for transfers between devices  7.93 us (21%)
  matrix products  7.62 us (20%)
  local copies, waits for them, and re-layouts  4.73 us (13%)
  other arithmetic  2.44 us (7%)
  between operations  1.05 us (3%)
    ppermute x6, starting transfers between devices, exchange(): incoming = lax.ppermute(jnp.concatenate(pieces, axis=0), 'leaf', pairs)  8.79 us
    dot_general x16, matrix products, plain_dot(): return jnp.dot(former, latter, preferred_element_type=jnp.float32)  5.08 us
    ppermute x3, starting transfers between devices, shards(): partial_gradient = kept + lax.ppermute(outgoing, 'src', pairs)  4.35 us
    ppermute x6, waiting for transfers between devices, exchange(): incoming = lax.ppermute(jnp.concatenate(pieces, axis=0), 'leaf', pairs)  4.05 us
    ppermute x3, waiting for transfers between devices, shards(): partial_gradient = kept + lax.ppermute(outgoing, 'src', pairs)  3.88 us
    unnamed x24, local copies, waits for them, and re-layouts  3.66 us
    dot_general x12, matrix products, across(): lax.dot_general(former, latter, (((1,), (1,)), ((), ())), preferred_eleme...  2.54 us
    select_n x1, other arithmetic, masked(): return jnp.where(keep, values, jnp.zeros_like(values))  1.43 us
  transfers between devices with their start and end apart: 9, of which 4 were waited for; matrix products, arithmetic and copies ran while one was open for 18% of the time, Pallas kernels for 0%

profile of v20, /device:TPU:0, one launch (start us, length us, event | category | flops | bytes accessed | tf_op | source)
XLA Modules:
  0.0 36.9 jit_solution(16187624154365904062)
XLA Ops:
  0.6 0.0 copy-start
  0.7 1.3 %fusion.17 = f32[128,512]{0,1:T(8,128)S(1)} fusion(s32[128]{0:T(128)} %param.13, f32[128,128]{1,0:T(8,128)} %param.14), kind=kOutput, calls=%fused_computation.41 | convolution fusion | flops 16957440 | bytes 328192 | tf_op jit(solution)/shard_map/dot_general | solution.py:16
  1.9 0.3 fusion.18
  2.3 0.0 copy-start.4
  2.3 0.3 fusion.1
  2.6 0.6 %copy-done.3 = bf16[4,128,128]{2,1,0:T(8,128)(2,1)S(1)} copy-done((bf16[4,128,128]{2,1,0:T(8,128)(2,1)S(1)}, bf16[4,128,128]{2,1,0:T(8,128)(2,1)}, u32[]{:S(2)}) %copy-start.3) | copy-done | bytes 131096
  3.2 0.2 fusion.190
  3.4 0.3 fusion.191
  3.7 0.4 fusion.194
  4.1 0.0 copy-start.8
  4.1 0.0 copy-start.7
  4.1 0.4 fusion.12
  4.5 0.3 copy-done.7
  4.8 0.2 compare_reduce_fusion
  5.0 0.1 broadcast_bitcast_fusion
  5.1 0.2 convolution_select_fusion
  5.4 0.0 copy-start.2
  5.4 0.0 copy-start.5
  5.4 3.0 %collective-permute-start.4 = (f32[256,128]{1,0:T(8,128)S(1)}, f32[256,128]{1,0:T(8,128)S(1)}, u32[]{:S(2)}, u32[]{:S(2)}) collective-permute-start(f32[256,128]{1,0:T(8,128)S(1)} %pad_maximum_fusion.6), channel_id=1, source_target_pairs={{0,8},{8,0},{16,24},{24,16},{1,9},{9,1},{17,25},{25,17},{2,10},{10... | collective-permute-start | bytes 393224 | tf_op jit(solution)/shard_map/ppermute | solution.py:135
  8.4 0.6 %slice.198 = pred[1]{0:T(512)(128)(4,1)} slice(pred[2]{0:T(512)(128)(4,1)S(1)} %compare_and_fusion), slice={[1:2]} | slice | bytes 2 | tf_op jit(solution)/shard_map/slice | solution.py:128
  9.0 1.4 %select_bitcast_fusion = (bf16[128,128]{1,0:T(8,128)(2,1)S(1)}, bf16[128,128]{1,0:T(8,128)(2,1)S(1)}) fusion(bf16[2,128,256]{2,1,0:T(8,128)(2,1)} %param.23, pred[]{:T(512)} %bitcast.1, bf16[2,256,128]{2,1,0:T(8,128)(2,1)} %param.22), kind=kLoop, calls=%fused_computation.152 | loop fusion | flops 32768 | bytes 131073 | tf_op jit(solution)/shard_map/jit(_where)/select_n | solution.py:102
  10.5 0.2 collective-permute-start.1
  10.7 0.7 %copy-done.10 = s32[128]{0:T(128)S(1)} copy-done((s32[128]{0:T(128)S(1)}, s32[128]{0:T(128)}, u32[]{:S(2)}) %copy-start.10) | copy-done | bytes 536
  11.4 0.1 fusion.179
  11.5 0.1 fusion.180
  11.7 0.2 convolution_subtract_fusion.5
  11.9 0.2 convolution_select_fusion.1
  12.2 2.0 %collective-permute-start = (f32[256,128]{1,0:T(8,128)S(1)}, f32[256,128]{1,0:T(8,128)S(1)}, u32[]{:S(2)}, u32[]{:S(2)}) collective-permute-start(f32[256,128]{1,0:T(8,128)S(1)} %pad_maximum_fusion.4), channel_id=1, source_target_pairs={{0,8},{8,0},{16,24},{24,16},{1,9},{9,1},{17,25},{25,17},{2,10},{10... | collective-permute-start | bytes 393224 | tf_op jit(solution)/shard_map/ppermute | solution.py:135
  14.1 0.0 collective-permute-done.4
  14.1 2.5 %collective-permute-done.1 = bf16[512,128]{1,0:T(8,128)(2,1)S(1)} collective-permute-done((bf16[512,128]{1,0:T(8,128)(2,1)S(1)}, bf16[512,128]{1,0:T(8,128)(2,1)S(1)}, u32[]{:S(2)}, u32[]{:S(2)}) %collective-permute-start.1) | collective-permute-done | bytes 131104 | tf_op jit(solution)/shard_map/ppermute | solution.py:135
  16.6 0.2 fusion.115
  16.8 0.2 fusion.69
  17.0 1.5 %collective-permute-start.5 = (f32[128,128]{1,0:T(8,128)S(1)}, f32[128,128]{1,0:T(8,128)S(1)}, u32[]{:S(2)}, u32[]{:S(2)}) collective-permute-start(f32[128,128]{1,0:T(8,128)S(1)} %fusion.69), channel_id=1, source_target_pairs={{0,16},{8,24},{16,0},{24,8},{1,17},{9,25},{17,1},{25,9},{2,18},{10... | collective-permute-start | bytes 196616 | tf_op jit(solution)/shard_map/ppermute | solution.py:135
  18.6 0.6 %collective-permute-start.3 = (bf16[128,128]{1,0:T(8,128)(2,1)S(1)}, bf16[128,128]{1,0:T(8,128)(2,1)S(1)}, u32[]{:S(2)}, u32[]{:S(2)}) collective-permute-start(bf16[128,128]{1,0:T(8,128)(2,1)S(1)} %slice_select_fusion.2), channel_id=1, source_target_pairs={{0,16},{8,24},{16,0},{24,8},{1,17},{9,25},{17,1},{25,9},{2,18},{10... | collective-permute-start | bytes 98312 | tf_op jit(solution)/shard_map/ppermute | solution.py:135
  19.1 0.2 fusion.78
  19.3 0.1 copy.19
  19.4 1.5 %collective-permute-start.2 = (f32[128,128]{1,0:T(8,128)S(1)}, f32[128,128]{1,0:T(8,128)S(1)}, u32[]{:S(2)}, u32[]{:S(2)}) collective-permute-start(f32[128,128]{1,0:T(8,128)S(1)} %fusion.78), channel_id=1, source_target_pairs={{0,16},{8,24},{16,0},{24,8},{1,17},{9,25},{17,1},{25,9},{2,18},{10... | collective-permute-start | bytes 196616 | tf_op jit(solution)/shard_map/ppermute | solution.py:135
  20.9 1.6 %collective-permute-done.3 = bf16[128,128]{1,0:T(8,128)(2,1)S(1)} collective-permute-done((bf16[128,128]{1,0:T(8,128)(2,1)S(1)}, bf16[128,128]{1,0:T(8,128)(2,1)S(1)}, u32[]{:S(2)}, u32[]{:S(2)}) %collective-permute-start.3) | collective-permute-done | bytes 32800 | tf_op jit(solution)/shard_map/ppermute | solution.py:135
  22.5 0.2 fusion.112
  22.7 0.1 copy.20
  22.8 0.2 fusion.126
  23.0 0.3 convolution_subtract_fusion
  23.3 0.2 fusion.199
  23.6 0.2 fusion.200
  23.8 0.2 convolution_subtract_fusion.8
  24.0 0.0 copy-start.9
  24.0 0.1 fusion.111
  24.2 0.1 copy.15
  24.3 0.3 fusion.15
  24.6 0.3 copy-done.9
  25.0 0.2 convolution_subtract_fusion.1
  25.2 0.1 fusion.181
  25.3 0.3 fusion.182
  25.6 0.3 fusion.185
  25.9 0.3 fusion.9
  26.3 0.1 fusion.16
  26.4 2.6 %collective-permute-start.6 = (f32[4,64]{1,0:T(4,128)S(1)}, f32[4,64]{1,0:T(4,128)S(1)}, u32[]{:S(2)}, u32[]{:S(2)}) collective-permute-start(f32[4,64]{1,0:T(4,128)S(1)} %slice_select_fusion.11), channel_id=1, source_target_pairs={{0,4},{1,5},{2,6},{3,7},{4,0},{5,1},{6,2},{7,3},{8,12},{9,13},{10,... | collective-permute-start | bytes 3080 | tf_op jit(solution)/shard_map/ppermute | solution.py:213
  29.1 1.9 %collective-permute-done.6 = f32[4,64]{1,0:T(4,128)S(1)} collective-permute-done((f32[4,64]{1,0:T(4,128)S(1)}, f32[4,64]{1,0:T(4,128)S(1)}, u32[]{:S(2)}, u32[]{:S(2)}) %collective-permute-start.6) | collective-permute-done | bytes 1056 | tf_op jit(solution)/shard_map/ppermute | solution.py:213
  31.0 1.6 %collective-permute-start.7 = (f32[2,64]{1,0:T(2,128)S(1)}, f32[2,64]{1,0:T(2,128)S(1)}, u32[]{:S(2)}, u32[]{:S(2)}) collective-permute-start(f32[2,64]{1,0:T(2,128)S(1)} %broadcast_select_fusion.3), channel_id=1, source_target_pairs={{0,2},{1,3},{2,0},{3,1},{4,6},{5,7},{6,4},{7,5},{8,10},{9,11},{10,... | collective-permute-start | bytes 1544 | tf_op jit(solution)/shard_map/ppermute | solution.py:213
  32.6 2.0 %collective-permute-done.7 = f32[2,64]{1,0:T(2,128)S(1)} collective-permute-done((f32[2,64]{1,0:T(2,128)S(1)}, f32[2,64]{1,0:T(2,128)S(1)}, u32[]{:S(2)}, u32[]{:S(2)}) %collective-permute-start.7) | collective-permute-done | bytes 544 | tf_op jit(solution)/shard_map/ppermute | solution.py:213
  34.6 0.1 collective-permute-start.8
  34.7 0.8 %copy.23 = f32[128,512]{1,0:T(8,128)} copy(f32[128,512]{0,1:T(8,128)S(1)} %pad_maximum_fusion.3) | data formatting | bytes 524288
  35.6 0.8 %copy.22 = f32[128,512]{1,0:T(8,128)} copy(f32[128,512]{0,1:T(8,128)S(1)} %pad_maximum_fusion.1) | data formatting | bytes 524288
  36.4 0.5 %fusion.155 = f32[64]{0:T(128)} fusion(f32[1,64]{1,0:T(1,128)S(1)} %collective-permute-done.8, pred[]{:T(512)S(6)} %ne.39, f32[2,64]{1,0:T(2,128)S(1)} %select_add_fusion.1), kind=kLoop, calls=%fused_computation.180 | loop fusion | flops 192 | bytes 1025 | tf_op jit(solution)/shard_map/mul | solution.py:215
  (38 shorter events, 0.3 us)
Async XLA Ops:
  0.6 11.2 %copy-start = (bf16[256,512]{1,0:T(8,128)(2,1)S(1)}, bf16[256,512]{1,0:T(8,128)(2,1)}, u32[]{:S(2)}) copy-start(bf16[256,512]{1,0:T(8,128)(2,1)} %param.19) | copy-start | bytes 786436
  0.6 1.3 %copy-start.6 = (s32[128]{0:T(128)S(1)}, s32[128]{0:T(128)}, u32[]{:S(2)}) copy-start(s32[128]{0:T(128)} %param.13) | copy-start | bytes 1540
  0.7 1.3 %copy-start.1 = (f32[128,128]{1,0:T(8,128)S(1)}, f32[128,128]{1,0:T(8,128)}, u32[]{:S(2)}) copy-start(f32[128,128]{1,0:T(8,128)} %param.14) | copy-start | bytes 196612
  2.3 0.9 %copy-start.3 = (bf16[4,128,128]{2,1,0:T(8,128)(2,1)S(1)}, bf16[4,128,128]{2,1,0:T(8,128)(2,1)}, u32[]{:S(2)}) copy-start(bf16[4,128,128]{2,1,0:T(8,128)(2,1)} %param.18) | copy-start | bytes 393220
  2.3 1.1 %copy-start.4 = (bf16[512,512]{1,0:T(8,128)(2,1)S(1)}, bf16[512,512]{1,0:T(8,128)(2,1)}, u32[]{:S(2)}) copy-start(bf16[512,512]{1,0:T(8,128)(2,1)} %param.17) | copy-start | bytes 1572868
  4.1 1.0 %copy-start.8 = (bf16[512,256]{1,0:T(8,128)(2,1)S(1)}, bf16[512,256]{1,0:T(8,128)(2,1)}, u32[]{:S(2)}) copy-start(bf16[512,256]{1,0:T(8,128)(2,1)} %param.20) | copy-start | bytes 786436
  4.1 0.7 %copy-start.7 = (s32[3,2]{0,1:T(2,128)S(1)}, s32[3,2]{0,1:T(2,128)}, u32[]{:S(2)}) copy-start(s32[3,2]{0,1:T(2,128)} %param.15) | copy-start | bytes 76
  5.4 3.6 %copy-start.2 = (bf16[2,128,128]{2,1,0:T(8,128)(2,1)S(1)}, bf16[2,128,128]{2,1,0:T(8,128)(2,1)}, u32[]{:S(2)}) copy-start(bf16[2,128,128]{2,1,0:T(8,128)(2,1)} %param.21) | copy-start | bytes 196612
  5.4 6.0 %copy-start.5 = (bf16[512,512]{1,0:T(8,128)(2,1)S(1)}, bf16[512,512]{1,0:T(8,128)(2,1)}, u32[]{:S(2)}) copy-start(bf16[512,512]{1,0:T(8,128)(2,1)} %param.16) | copy-start | bytes 1572868
  5.4 8.7 %collective-permute-start.4 = (f32[256,128]{1,0:T(8,128)S(1)}, f32[256,128]{1,0:T(8,128)S(1)}, u32[]{:S(2)}, u32[]{:S(2)}) collective-permute-start(f32[256,128]{1,0:T(8,128)S(1)} %pad_maximum_fusion.6), channel_id=1, source_target_pairs={{0,8},{8,0},{16,24},{24,16},{1,9},{9,1},{17,25},{25,17},{2,10},{10... | collective-permute-start | bytes 393224 | tf_op jit(solution)/shard_map/ppermute | solution.py:135
  10.5 6.1 %collective-permute-start.1 = (bf16[512,128]{1,0:T(8,128)(2,1)S(1)}, bf16[512,128]{1,0:T(8,128)(2,1)S(1)}, u32[]{:S(2)}, u32[]{:S(2)}) collective-permute-start(bf16[512,128]{1,0:T(8,128)(2,1)S(1)} %pad_maximum_fusion.5), channel_id=1, source_target_pairs={{0,8},{8,0},{16,24},{24,16},{1,9},{9,1},{17,25},{25,17},{2,10},{10... | collective-permute-start | bytes 393224 | tf_op jit(solution)/shard_map/ppermute | solution.py:135
  10.7 0.7 %copy-start.10 = (s32[128]{0:T(128)S(1)}, s32[128]{0:T(128)}, u32[]{:S(2)}) copy-start(s32[128]{0:T(128)} %param.12) | copy-start | bytes 1540
  12.2 7.0 %collective-permute-start = (f32[256,128]{1,0:T(8,128)S(1)}, f32[256,128]{1,0:T(8,128)S(1)}, u32[]{:S(2)}, u32[]{:S(2)}) collective-permute-start(f32[256,128]{1,0:T(8,128)S(1)} %pad_maximum_fusion.4), channel_id=1, source_target_pairs={{0,8},{8,0},{16,24},{24,16},{1,9},{9,1},{17,25},{25,17},{2,10},{10... | collective-permute-start | bytes 393224 | tf_op jit(solution)/shard_map/ppermute | solution.py:135
  17.0 5.5 %collective-permute-start.5 = (f32[128,128]{1,0:T(8,128)S(1)}, f32[128,128]{1,0:T(8,128)S(1)}, u32[]{:S(2)}, u32[]{:S(2)}) collective-permute-start(f32[128,128]{1,0:T(8,128)S(1)} %fusion.69), channel_id=1, source_target_pairs={{0,16},{8,24},{16,0},{24,8},{1,17},{9,25},{17,1},{25,9},{2,18},{10... | collective-permute-start | bytes 196616 | tf_op jit(solution)/shard_map/ppermute | solution.py:135
  18.6 3.9 %collective-permute-start.3 = (bf16[128,128]{1,0:T(8,128)(2,1)S(1)}, bf16[128,128]{1,0:T(8,128)(2,1)S(1)}, u32[]{:S(2)}, u32[]{:S(2)}) collective-permute-start(bf16[128,128]{1,0:T(8,128)(2,1)S(1)} %slice_select_fusion.2), channel_id=1, source_target_pairs={{0,16},{8,24},{16,0},{24,8},{1,17},{9,25},{17,1},{25,9},{2,18},{10... | collective-permute-start | bytes 98312 | tf_op jit(solution)/shard_map/ppermute | solution.py:135
  19.4 4.7 %collective-permute-start.2 = (f32[128,128]{1,0:T(8,128)S(1)}, f32[128,128]{1,0:T(8,128)S(1)}, u32[]{:S(2)}, u32[]{:S(2)}) collective-permute-start(f32[128,128]{1,0:T(8,128)S(1)} %fusion.78), channel_id=1, source_target_pairs={{0,16},{8,24},{16,0},{24,8},{1,17},{9,25},{17,1},{25,9},{2,18},{10... | collective-permute-start | bytes 196616 | tf_op jit(solution)/shard_map/ppermute | solution.py:135
  24.0 1.0 %copy-start.9 = (bf16[512,256]{1,0:T(8,128)(2,1)S(1)}, bf16[512,256]{1,0:T(8,128)(2,1)}, u32[]{:S(2)}) copy-start(bf16[512,256]{1,0:T(8,128)(2,1)} %param.20) | copy-start | bytes 786436
  26.4 4.5 %collective-permute-start.6 = (f32[4,64]{1,0:T(4,128)S(1)}, f32[4,64]{1,0:T(4,128)S(1)}, u32[]{:S(2)}, u32[]{:S(2)}) collective-permute-start(f32[4,64]{1,0:T(4,128)S(1)} %slice_select_fusion.11), channel_id=1, source_target_pairs={{0,4},{1,5},{2,6},{3,7},{4,0},{5,1},{6,2},{7,3},{8,12},{9,13},{10,... | collective-permute-start | bytes 3080 | tf_op jit(solution)/shard_map/ppermute | solution.py:213
  31.0 3.6 %collective-permute-start.7 = (f32[2,64]{1,0:T(2,128)S(1)}, f32[2,64]{1,0:T(2,128)S(1)}, u32[]{:S(2)}, u32[]{:S(2)}) collective-permute-start(f32[2,64]{1,0:T(2,128)S(1)} %broadcast_select_fusion.3), channel_id=1, source_target_pairs={{0,2},{1,3},{2,0},{3,1},{4,6},{5,7},{6,4},{7,5},{8,10},{9,11},{10,... | collective-permute-start | bytes 1544 | tf_op jit(solution)/shard_map/ppermute | solution.py:213
  34.6 1.8 %collective-permute-start.8 = (f32[1,64]{1,0:T(1,128)S(1)}, f32[1,64]{1,0:T(1,128)S(1)}, u32[]{:S(2)}, u32[]{:S(2)}) collective-permute-start(f32[1,64]{1,0:T(1,128)S(1)} %broadcast_select_fusion.4), channel_id=1, source_target_pairs={{0,1},{1,0},{2,3},{3,2},{4,5},{5,4},{6,7},{7,6},{8,9},{9,8},{10,11... | collective-permute-start | bytes 776 | tf_op jit(solution)/shard_map/ppermute | solution.py:213

commit v21 on v15

--- a/solution.py
+++ b/solution.py
@@ -195,7 +195,7 @@
     adjoint_field = lower_t_solve(adjoint_remain, leaf_lower, block_size, block_count)
     spread = lax.axis_size("src")
     product_field = (forward_field * adjoint_field).reshape(source_count, spread, cell_count // spread)
-    partial_gradient = jnp.sum(product_field, axis=0)
+    partial_gradient = jnp.sum(product_field, axis=0) * factor
     place = lax.axis_index("src")
     bit = spread // 2
     while bit:
@@ -206,7 +206,7 @@
         pairs = [(index, index ^ bit) for index in range(spread)]
         partial_gradient = kept + lax.ppermute(outgoing, "src", pairs)
         bit //= 2
-    gradient = partial_gradient.reshape(-1) * factor
+    gradient = partial_gradient.reshape(-1)
     return (forward_field, adjoint_field, gradient)
 
 

time: 36.9 us -> 36.9 us (level)
    reshape x0 -> x1, other arithmetic: none -> 0.52 us  [shards(): gradient = partial_gradient.reshape(-1)]
    mul x1, other arithmetic: 0.52 us -> 0.01 us  [shards(): partial_gradient = jnp.sum(product_field, axis=0) * factor]
where the time goes in v21:
time: 36.9 us; the launch traced here: 36.5 us
  starting transfers between devices  13.1 us (36%)
  waiting for transfers between devices  7.97 us (22%)
  matrix products  7.83 us (21%)
  local copies, waits for them, and re-layouts  4.12 us (11%)
  other arithmetic  2.45 us (7%)
  between operations  1.04 us (3%)
    ppermute x6, starting transfers between devices, exchange(): incoming = lax.ppermute(jnp.concatenate(pieces, axis=0), 'leaf', pairs)  8.81 us
    ppermute x3, starting transfers between devices, shards(): partial_gradient = kept + lax.ppermute(outgoing, 'src', pairs)  4.32 us
    ppermute x6, waiting for transfers between devices, exchange(): incoming = lax.ppermute(jnp.concatenate(pieces, axis=0), 'leaf', pairs)  4.05 us
    dot_general x13, matrix products, plain_dot(): return jnp.dot(former, latter, preferred_element_type=jnp.float32)  3.98 us
    ppermute x3, waiting for transfers between devices, shards(): partial_gradient = kept + lax.ppermute(outgoing, 'src', pairs)  3.92 us
    unnamed x20, local copies, waits for them, and re-layouts  3.05 us
    dot_general x12, matrix products, across(): lax.dot_general(former, latter, (((1,), (1,)), ((), ())), preferred_eleme...  2.54 us
    select_n x1, other arithmetic, masked(): return jnp.where(keep, values, jnp.zeros_like(values))  1.43 us
  transfers between devices with their start and end apart: 9, of which 4 were waited for; matrix products, arithmetic and copies ran while one was open for 18% of the time, Pallas kernels for 0%

profile of v21, /device:TPU:0, one launch (start us, length us, event | category | flops | bytes accessed | tf_op | source)
XLA Modules:
  0.0 36.5 jit_solution(4164087529001774768)
XLA Ops:
  0.6 0.0 copy-start
  0.7 0.0 copy-start.3
  0.7 1.3 %convolution_bitcast_fusion = f32[128,512]{0,1:T(8,128)S(1)} fusion(f32[128,128]{1,0:T(8,128)} %param.14, s32[128]{0:T(128)} %param.13), kind=kOutput, calls=%fused_computation.2 | convolution fusion | flops 100794368 | bytes 328192 | tf_op jit(solution)/shard_map/dot_general | solution.py:112
  2.0 0.2 fusion.180
  2.2 1.1 %fusion.181 = (bf16[128,128]{0,1:T(8,128)(2,1)S(1)}, f32[128,128]{0,1:T(8,128)S(1)}) fusion(bf16[4,128,128]{2,1,0:T(8,128)(2,1)S(1)} %copy-done.2, bf16[128,128]{0,1:T(8,128)(2,1)S(1)} %get-tuple-element.24, f32[128,512]{0,1:T(8,128)S(1)} %convolution_bitcast_fusion, bf16[512,512]{1,0:T(8,128)(2,1)} %param.17), kind=kOutput, calls=%fused_computation.199 | convolution fusion | flops 8437760 | bytes 262144 | tf_op jit(solution)/shard_map/dot_general | solution.py:16
  3.3 0.4 fusion.184
  3.7 0.0 copy-start.6
  3.7 0.0 copy-start.5
  3.7 0.4 fusion.10
  4.1 0.3 copy-done.5
  4.4 0.2 compare_reduce_fusion
  4.6 0.1 broadcast_bitcast_fusion
  4.7 0.2 convolution_select_fusion
  5.0 0.0 copy-start.1
  5.0 0.0 copy-start.4
  5.0 3.0 %collective-permute-start.4 = (f32[256,128]{1,0:T(8,128)S(1)}, f32[256,128]{1,0:T(8,128)S(1)}, u32[]{:S(2)}, u32[]{:S(2)}) collective-permute-start(f32[256,128]{1,0:T(8,128)S(1)} %pad_maximum_fusion.6), channel_id=1, source_target_pairs={{0,8},{8,0},{16,24},{24,16},{1,9},{9,1},{17,25},{25,17},{2,10},{10... | collective-permute-start | bytes 393224 | tf_op jit(solution)/shard_map/ppermute | solution.py:129
  8.0 0.6 %slice.198 = pred[1]{0:T(512)(128)(4,1)} slice(pred[2]{0:T(512)(128)(4,1)S(1)} %compare_and_fusion), slice={[1:2]} | slice | bytes 2 | tf_op jit(solution)/shard_map/slice | solution.py:122
  8.6 1.4 %select_bitcast_fusion = (bf16[128,128]{1,0:T(8,128)(2,1)S(1)}, bf16[128,128]{1,0:T(8,128)(2,1)S(1)}) fusion(bf16[2,128,256]{2,1,0:T(8,128)(2,1)} %param.23, pred[]{:T(512)} %bitcast.1, bf16[2,256,128]{2,1,0:T(8,128)(2,1)} %param.22), kind=kLoop, calls=%fused_computation.142 | loop fusion | flops 32768 | bytes 131073 | tf_op jit(solution)/shard_map/jit(_where)/select_n | solution.py:102
  10.1 0.2 collective-permute-start.1
  10.3 0.7 %copy-done.8 = s32[128]{0:T(128)S(1)} copy-done((s32[128]{0:T(128)S(1)}, s32[128]{0:T(128)}, u32[]{:S(2)}) %copy-start.8) | copy-done | bytes 536
  11.0 0.1 fusion.169
  11.1 0.1 fusion.170
  11.3 0.2 convolution_subtract_fusion.5
  11.5 0.2 convolution_select_fusion.1
  11.8 2.0 %collective-permute-start = (f32[256,128]{1,0:T(8,128)S(1)}, f32[256,128]{1,0:T(8,128)S(1)}, u32[]{:S(2)}, u32[]{:S(2)}) collective-permute-start(f32[256,128]{1,0:T(8,128)S(1)} %pad_maximum_fusion.4), channel_id=1, source_target_pairs={{0,8},{8,0},{16,24},{24,16},{1,9},{9,1},{17,25},{25,17},{2,10},{10... | collective-permute-start | bytes 393224 | tf_op jit(solution)/shard_map/ppermute | solution.py:129
  13.7 0.0 collective-permute-done.4
  13.7 2.5 %collective-permute-done.1 = bf16[512,128]{1,0:T(8,128)(2,1)S(1)} collective-permute-done((bf16[512,128]{1,0:T(8,128)(2,1)S(1)}, bf16[512,128]{1,0:T(8,128)(2,1)S(1)}, u32[]{:S(2)}, u32[]{:S(2)}) %collective-permute-start.1) | collective-permute-done | bytes 131104 | tf_op jit(solution)/shard_map/ppermute | solution.py:129
  16.2 0.2 fusion.106
  16.4 0.2 fusion.63
  16.6 1.6 %collective-permute-start.5 = (f32[128,128]{1,0:T(8,128)S(1)}, f32[128,128]{1,0:T(8,128)S(1)}, u32[]{:S(2)}, u32[]{:S(2)}) collective-permute-start(f32[128,128]{1,0:T(8,128)S(1)} %fusion.63), channel_id=1, source_target_pairs={{0,16},{8,24},{16,0},{24,8},{1,17},{9,25},{17,1},{25,9},{2,18},{10... | collective-permute-start | bytes 196616 | tf_op jit(solution)/shard_map/ppermute | solution.py:129
  18.2 0.5 %collective-permute-start.3 = (bf16[128,128]{1,0:T(8,128)(2,1)S(1)}, bf16[128,128]{1,0:T(8,128)(2,1)S(1)}, u32[]{:S(2)}, u32[]{:S(2)}) collective-permute-start(bf16[128,128]{1,0:T(8,128)(2,1)S(1)} %slice_select_fusion.2), channel_id=1, source_target_pairs={{0,16},{8,24},{16,0},{24,8},{1,17},{9,25},{17,1},{25,9},{2,18},{10... | collective-permute-start | bytes 98312 | tf_op jit(solution)/shard_map/ppermute | solution.py:129
  18.7 0.0 collective-permute-done
  18.7 0.2 fusion.72
  18.9 0.1 copy.17
  19.0 1.6 %collective-permute-start.2 = (f32[128,128]{1,0:T(8,128)S(1)}, f32[128,128]{1,0:T(8,128)S(1)}, u32[]{:S(2)}, u32[]{:S(2)}) collective-permute-start(f32[128,128]{1,0:T(8,128)S(1)} %fusion.72), channel_id=1, source_target_pairs={{0,16},{8,24},{16,0},{24,8},{1,17},{9,25},{17,1},{25,9},{2,18},{10... | collective-permute-start | bytes 196616 | tf_op jit(solution)/shard_map/ppermute | solution.py:129
  20.5 1.6 %collective-permute-done.3 = bf16[128,128]{1,0:T(8,128)(2,1)S(1)} collective-permute-done((bf16[128,128]{1,0:T(8,128)(2,1)S(1)}, bf16[128,128]{1,0:T(8,128)(2,1)S(1)}, u32[]{:S(2)}, u32[]{:S(2)}) %collective-permute-start.3) | collective-permute-done | bytes 32800 | tf_op jit(solution)/shard_map/ppermute | solution.py:129
  22.1 0.0 collective-permute-done.5
  22.1 0.2 fusion.103
  22.3 0.1 copy.18
  22.4 0.2 fusion.117
  22.6 0.3 convolution_subtract_fusion
  22.9 0.2 fusion.189
  23.2 0.2 fusion.190
  23.4 0.2 convolution_subtract_fusion.8
  23.6 0.0 copy-start.7
  23.6 0.0 collective-permute-done.2
  23.7 0.1 fusion.102
  23.8 0.1 copy.15
  23.9 0.3 fusion.13
  24.3 0.3 copy-done.7
  24.6 0.2 convolution_subtract_fusion.1
  24.8 0.1 fusion.171
  24.9 0.3 fusion.172
  25.2 0.3 fusion.175
  25.5 0.3 fusion.7
  25.9 0.1 fusion.14
  26.0 2.6 %collective-permute-start.6 = (f32[4,64]{1,0:T(4,128)S(1)}, f32[4,64]{1,0:T(4,128)S(1)}, u32[]{:S(2)}, u32[]{:S(2)}) collective-permute-start(f32[4,64]{1,0:T(4,128)S(1)} %slice_select_fusion.11), channel_id=1, source_target_pairs={{0,4},{1,5},{2,6},{3,7},{4,0},{5,1},{6,2},{7,3},{8,12},{9,13},{10,... | collective-permute-start | bytes 3080 | tf_op jit(solution)/shard_map/ppermute | solution.py:207
  28.7 1.9 %collective-permute-done.6 = f32[4,64]{1,0:T(4,128)S(1)} collective-permute-done((f32[4,64]{1,0:T(4,128)S(1)}, f32[4,64]{1,0:T(4,128)S(1)}, u32[]{:S(2)}, u32[]{:S(2)}) %collective-permute-start.6) | collective-permute-done | bytes 1056 | tf_op jit(solution)/shard_map/ppermute | solution.py:207
  30.6 1.6 %collective-permute-start.7 = (f32[2,64]{1,0:T(2,128)S(1)}, f32[2,64]{1,0:T(2,128)S(1)}, u32[]{:S(2)}, u32[]{:S(2)}) collective-permute-start(f32[2,64]{1,0:T(2,128)S(1)} %broadcast_select_fusion.3), channel_id=1, source_target_pairs={{0,2},{1,3},{2,0},{3,1},{4,6},{5,7},{6,4},{7,5},{8,10},{9,11},{10,... | collective-permute-start | bytes 1544 | tf_op jit(solution)/shard_map/ppermute | solution.py:207
  32.2 2.0 %collective-permute-done.7 = f32[2,64]{1,0:T(2,128)S(1)} collective-permute-done((f32[2,64]{1,0:T(2,128)S(1)}, f32[2,64]{1,0:T(2,128)S(1)}, u32[]{:S(2)}, u32[]{:S(2)}) %collective-permute-start.7) | collective-permute-done | bytes 544 | tf_op jit(solution)/shard_map/ppermute | solution.py:207
  34.2 0.1 collective-permute-start.8
  34.3 0.8 %copy.21 = f32[128,512]{1,0:T(8,128)} copy(f32[128,512]{0,1:T(8,128)S(1)} %pad_maximum_fusion.3) | data formatting | bytes 524288
  35.2 0.8 %copy.20 = f32[128,512]{1,0:T(8,128)} copy(f32[128,512]{0,1:T(8,128)S(1)} %pad_maximum_fusion.1) | data formatting | bytes 524288
  36.0 0.5 %fusion.145 = f32[64]{0:T(128)} fusion(f32[1,64]{1,0:T(1,128)S(1)} %collective-permute-done.8, pred[]{:T(512)S(6)} %ne.39, f32[2,64]{1,0:T(2,128)S(1)} %select_add_fusion.1), kind=kLoop, calls=%fused_computation.169 | loop fusion | flops 128 | bytes 1025 | tf_op jit(solution)/shard_map/reshape | solution.py:209
  (33 shorter events, 0.2 us)
Async XLA Ops:
  0.6 10.8 %copy-start = (bf16[256,512]{1,0:T(8,128)(2,1)S(1)}, bf16[256,512]{1,0:T(8,128)(2,1)}, u32[]{:S(2)}) copy-start(bf16[256,512]{1,0:T(8,128)(2,1)} %param.19) | copy-start | bytes 786436
  0.6 1.3 %copy-start.2 = (bf16[4,128,128]{2,1,0:T(8,128)(2,1)S(1)}, bf16[4,128,128]{2,1,0:T(8,128)(2,1)}, u32[]{:S(2)}) copy-start(bf16[4,128,128]{2,1,0:T(8,128)(2,1)} %param.18) | copy-start | bytes 393220
  0.7 2.7 %copy-start.3 = (bf16[512,512]{1,0:T(8,128)(2,1)S(1)}, bf16[512,512]{1,0:T(8,128)(2,1)}, u32[]{:S(2)}) copy-start(bf16[512,512]{1,0:T(8,128)(2,1)} %param.17) | copy-start | bytes 1572868
  3.7 1.0 %copy-start.6 = (bf16[512,256]{1,0:T(8,128)(2,1)S(1)}, bf16[512,256]{1,0:T(8,128)(2,1)}, u32[]{:S(2)}) copy-start(bf16[512,256]{1,0:T(8,128)(2,1)} %param.20) | copy-start | bytes 786436
  3.7 0.7 %copy-start.5 = (s32[3,2]{0,1:T(2,128)S(1)}, s32[3,2]{0,1:T(2,128)}, u32[]{:S(2)}) copy-start(s32[3,2]{0,1:T(2,128)} %param.15) | copy-start | bytes 76
  5.0 3.6 %copy-start.1 = (bf16[2,128,128]{2,1,0:T(8,128)(2,1)S(1)}, bf16[2,128,128]{2,1,0:T(8,128)(2,1)}, u32[]{:S(2)}) copy-start(bf16[2,128,128]{2,1,0:T(8,128)(2,1)} %param.21) | copy-start | bytes 196612
  5.0 6.0 %copy-start.4 = (bf16[512,512]{1,0:T(8,128)(2,1)S(1)}, bf16[512,512]{1,0:T(8,128)(2,1)}, u32[]{:S(2)}) copy-start(bf16[512,512]{1,0:T(8,128)(2,1)} %param.16) | copy-start | bytes 1572868
  5.0 8.7 %collective-permute-start.4 = (f32[256,128]{1,0:T(8,128)S(1)}, f32[256,128]{1,0:T(8,128)S(1)}, u32[]{:S(2)}, u32[]{:S(2)}) collective-permute-start(f32[256,128]{1,0:T(8,128)S(1)} %pad_maximum_fusion.6), channel_id=1, source_target_pairs={{0,8},{8,0},{16,24},{24,16},{1,9},{9,1},{17,25},{25,17},{2,10},{10... | collective-permute-start | bytes 393224 | tf_op jit(solution)/shard_map/ppermute | solution.py:129
  10.1 6.1 %collective-permute-start.1 = (bf16[512,128]{1,0:T(8,128)(2,1)S(1)}, bf16[512,128]{1,0:T(8,128)(2,1)S(1)}, u32[]{:S(2)}, u32[]{:S(2)}) collective-permute-start(bf16[512,128]{1,0:T(8,128)(2,1)S(1)} %pad_maximum_fusion.5), channel_id=1, source_target_pairs={{0,8},{8,0},{16,24},{24,16},{1,9},{9,1},{17,25},{25,17},{2,10},{10... | collective-permute-start | bytes 393224 | tf_op jit(solution)/shard_map/ppermute | solution.py:129
  10.2 0.7 %copy-start.8 = (s32[128]{0:T(128)S(1)}, s32[128]{0:T(128)}, u32[]{:S(2)}) copy-start(s32[128]{0:T(128)} %param.12) | copy-start | bytes 1540
  11.8 6.9 %collective-permute-start = (f32[256,128]{1,0:T(8,128)S(1)}, f32[256,128]{1,0:T(8,128)S(1)}, u32[]{:S(2)}, u32[]{:S(2)}) collective-permute-start(f32[256,128]{1,0:T(8,128)S(1)} %pad_maximum_fusion.4), channel_id=1, source_target_pairs={{0,8},{8,0},{16,24},{24,16},{1,9},{9,1},{17,25},{25,17},{2,10},{10... | collective-permute-start | bytes 393224 | tf_op jit(solution)/shard_map/ppermute | solution.py:129
  16.6 5.5 %collective-permute-start.5 = (f32[128,128]{1,0:T(8,128)S(1)}, f32[128,128]{1,0:T(8,128)S(1)}, u32[]{:S(2)}, u32[]{:S(2)}) collective-permute-start(f32[128,128]{1,0:T(8,128)S(1)} %fusion.63), channel_id=1, source_target_pairs={{0,16},{8,24},{16,0},{24,8},{1,17},{9,25},{17,1},{25,9},{2,18},{10... | collective-permute-start | bytes 196616 | tf_op jit(solution)/shard_map/ppermute | solution.py:129
  18.2 3.9 %collective-permute-start.3 = (bf16[128,128]{1,0:T(8,128)(2,1)S(1)}, bf16[128,128]{1,0:T(8,128)(2,1)S(1)}, u32[]{:S(2)}, u32[]{:S(2)}) collective-permute-start(bf16[128,128]{1,0:T(8,128)(2,1)S(1)} %slice_select_fusion.2), channel_id=1, source_target_pairs={{0,16},{8,24},{16,0},{24,8},{1,17},{9,25},{17,1},{25,9},{2,18},{10... | collective-permute-start | bytes 98312 | tf_op jit(solution)/shard_map/ppermute | solution.py:129
  19.0 4.7 %collective-permute-start.2 = (f32[128,128]{1,0:T(8,128)S(1)}, f32[128,128]{1,0:T(8,128)S(1)}, u32[]{:S(2)}, u32[]{:S(2)}) collective-permute-start(f32[128,128]{1,0:T(8,128)S(1)} %fusion.72), channel_id=1, source_target_pairs={{0,16},{8,24},{16,0},{24,8},{1,17},{9,25},{17,1},{25,9},{2,18},{10... | collective-permute-start | bytes 196616 | tf_op jit(solution)/shard_map/ppermute | solution.py:129
  23.6 1.0 %copy-start.7 = (bf16[512,256]{1,0:T(8,128)(2,1)S(1)}, bf16[512,256]{1,0:T(8,128)(2,1)}, u32[]{:S(2)}) copy-start(bf16[512,256]{1,0:T(8,128)(2,1)} %param.20) | copy-start | bytes 786436
  26.0 4.5 %collective-permute-start.6 = (f32[4,64]{1,0:T(4,128)S(1)}, f32[4,64]{1,0:T(4,128)S(1)}, u32[]{:S(2)}, u32[]{:S(2)}) collective-permute-start(f32[4,64]{1,0:T(4,128)S(1)} %slice_select_fusion.11), channel_id=1, source_target_pairs={{0,4},{1,5},{2,6},{3,7},{4,0},{5,1},{6,2},{7,3},{8,12},{9,13},{10,... | collective-permute-start | bytes 3080 | tf_op jit(solution)/shard_map/ppermute | solution.py:207
  30.6 3.6 %collective-permute-start.7 = (f32[2,64]{1,0:T(2,128)S(1)}, f32[2,64]{1,0:T(2,128)S(1)}, u32[]{:S(2)}, u32[]{:S(2)}) collective-permute-start(f32[2,64]{1,0:T(2,128)S(1)} %broadcast_select_fusion.3), channel_id=1, source_target_pairs={{0,2},{1,3},{2,0},{3,1},{4,6},{5,7},{6,4},{7,5},{8,10},{9,11},{10,... | collective-permute-start | bytes 1544 | tf_op jit(solution)/shard_map/ppermute | solution.py:207
  34.2 1.8 %collective-permute-start.8 = (f32[1,64]{1,0:T(1,128)S(1)}, f32[1,64]{1,0:T(1,128)S(1)}, u32[]{:S(2)}, u32[]{:S(2)}) collective-permute-start(f32[1,64]{1,0:T(1,128)S(1)} %broadcast_select_fusion.4), channel_id=1, source_target_pairs={{0,1},{1,0},{2,3},{3,2},{4,5},{5,4},{6,7},{7,6},{8,9},{9,8},{10,11... | collective-permute-start | bytes 776 | tf_op jit(solution)/shard_map/ppermute | solution.py:207

commit v22 on v19

--- a/solution.py
+++ b/solution.py
@@ -197,9 +197,7 @@
     product_field = (forward_field * adjoint_field).reshape(source_count, spread, cell_count // spread)
     partial_gradient = jnp.sum(product_field, axis=0)
     place = lax.axis_index("src")
-    bits = [1 << k for k in reversed(range(spread.bit_length() - 1))]
-    if len(bits) > 2:
-        bits[0], bits[1] = bits[1], bits[0]
+    bits = [1 << k for k in range(spread.bit_length() - 1)]
     axes = [1 << k for k in reversed(range(spread.bit_length() - 1))]
     partial_gradient = partial_gradient.reshape([2] * len(axes) + [cell_count // spread])
     for bit in bits:

time: 36.9 us -> 36.3 us (0.984)
  waiting for transfers between devices: 7.97 us -> 7.36 us
    ppermute x3, waiting for transfers between devices: 3.92 us -> 3.31 us  [shards(): partial_gradient = kept + lax.ppermute(outgoing, 'src', pairs)]
  transfers between devices with their start and end apart: 9 -> 9, of which waited for: 4 -> 5; matrix products, arithmetic and copies ran while one was open for 18% -> 19% of each run, Pallas kernels for 0% -> 0%
where the time goes in v22:
time: 36.3 us; the launch traced here: 35.9 us
  starting transfers between devices  13.1 us (36%)
  matrix products  7.83 us (22%)
  waiting for transfers between devices  7.36 us (20%)
  local copies, waits for them, and re-layouts  4.12 us (11%)
  other arithmetic  2.44 us (7%)
  between operations  1.04 us (3%)
    ppermute x6, starting transfers between devices, exchange(): incoming = lax.ppermute(jnp.concatenate(pieces, axis=0), 'leaf', pairs)  8.81 us
    ppermute x3, starting transfers between devices, shards(): partial_gradient = kept + lax.ppermute(outgoing, 'src', pairs)  4.32 us
    ppermute x6, waiting for transfers between devices, exchange(): incoming = lax.ppermute(jnp.concatenate(pieces, axis=0), 'leaf', pairs)  4.05 us
    dot_general x13, matrix products, plain_dot(): return jnp.dot(former, latter, preferred_element_type=jnp.float32)  3.98 us
    ppermute x3, waiting for transfers between devices, shards(): partial_gradient = kept + lax.ppermute(outgoing, 'src', pairs)  3.31 us
    unnamed x20, local copies, waits for them, and re-layouts  3.05 us
    dot_general x12, matrix products, across(): lax.dot_general(former, latter, (((1,), (1,)), ((), ())), preferred_eleme...  2.54 us
    select_n x1, other arithmetic, masked(): return jnp.where(keep, values, jnp.zeros_like(values))  1.43 us
  transfers between devices with their start and end apart: 9, of which 5 were waited for; matrix products, arithmetic and copies ran while one was open for 19% of the time, Pallas kernels for 0%

profile of v22, /device:TPU:0, one launch (start us, length us, event | category | flops | bytes accessed | tf_op | source)
XLA Modules:
  0.0 35.9 jit_solution(14688696904833682903)
XLA Ops:
  0.6 0.0 copy-start
  0.7 0.0 copy-start.3
  0.7 1.3 %convolution_bitcast_fusion = f32[128,512]{0,1:T(8,128)S(1)} fusion(f32[128,128]{1,0:T(8,128)} %param.14, s32[128]{0:T(128)} %param.13), kind=kOutput, calls=%fused_computation.2 | convolution fusion | flops 100794368 | bytes 328192 | tf_op jit(solution)/shard_map/dot_general | solution.py:112
  2.0 0.2 fusion.183
  2.2 1.1 %fusion.184 = (bf16[128,128]{0,1:T(8,128)(2,1)S(1)}, f32[128,128]{0,1:T(8,128)S(1)}) fusion(bf16[4,128,128]{2,1,0:T(8,128)(2,1)S(1)} %copy-done.2, bf16[128,128]{0,1:T(8,128)(2,1)S(1)} %get-tuple-element.32, f32[128,512]{0,1:T(8,128)S(1)} %convolution_bitcast_fusion, bf16[512,512]{1,0:T(8,128)(2,1)} %param.17), kind=kOutput, calls=%fused_computation.201 | convolution fusion | flops 8437760 | bytes 262144 | tf_op jit(solution)/shard_map/dot_general | solution.py:16
  3.3 0.4 fusion.187
  3.7 0.0 copy-start.6
  3.7 0.0 copy-start.5
  3.7 0.4 fusion.10
  4.1 0.3 copy-done.5
  4.4 0.2 compare_reduce_fusion
  4.6 0.1 broadcast_bitcast_fusion
  4.7 0.2 convolution_select_fusion
  5.0 0.0 copy-start.1
  5.0 0.0 copy-start.4
  5.0 3.0 %collective-permute-start.4 = (f32[256,128]{1,0:T(8,128)S(1)}, f32[256,128]{1,0:T(8,128)S(1)}, u32[]{:S(2)}, u32[]{:S(2)}) collective-permute-start(f32[256,128]{1,0:T(8,128)S(1)} %pad_maximum_fusion.6), channel_id=1, source_target_pairs={{0,8},{8,0},{16,24},{24,16},{1,9},{9,1},{17,25},{25,17},{2,10},{10... | collective-permute-start | bytes 393224 | tf_op jit(solution)/shard_map/ppermute | solution.py:129
  8.0 0.6 %slice.192 = pred[1]{0:T(512)(128)(4,1)} slice(pred[2]{0:T(512)(128)(4,1)S(1)} %compare_and_fusion), slice={[1:2]} | slice | bytes 2 | tf_op jit(solution)/shard_map/slice | solution.py:122
  8.6 1.4 %select_bitcast_fusion = (bf16[128,128]{1,0:T(8,128)(2,1)S(1)}, bf16[128,128]{1,0:T(8,128)(2,1)S(1)}) fusion(bf16[2,128,256]{2,1,0:T(8,128)(2,1)} %param.23, pred[]{:T(512)} %bitcast.1, bf16[2,256,128]{2,1,0:T(8,128)(2,1)} %param.22), kind=kLoop, calls=%fused_computation.142 | loop fusion | flops 32768 | bytes 131073 | tf_op jit(solution)/shard_map/jit(_where)/select_n | solution.py:102
  10.1 0.2 collective-permute-start.1
  10.3 0.7 %copy-done.8 = s32[128]{0:T(128)S(1)} copy-done((s32[128]{0:T(128)S(1)}, s32[128]{0:T(128)}, u32[]{:S(2)}) %copy-start.8) | copy-done | bytes 536
  11.0 0.1 fusion.172
  11.1 0.1 fusion.173
  11.3 0.2 convolution_subtract_fusion.5
  11.5 0.2 convolution_select_fusion.1
  11.8 2.0 %collective-permute-start = (f32[256,128]{1,0:T(8,128)S(1)}, f32[256,128]{1,0:T(8,128)S(1)}, u32[]{:S(2)}, u32[]{:S(2)}) collective-permute-start(f32[256,128]{1,0:T(8,128)S(1)} %pad_maximum_fusion.4), channel_id=1, source_target_pairs={{0,8},{8,0},{16,24},{24,16},{1,9},{9,1},{17,25},{25,17},{2,10},{10... | collective-permute-start | bytes 393224 | tf_op jit(solution)/shard_map/ppermute | solution.py:129
  13.7 0.0 collective-permute-done.4
  13.7 2.5 %collective-permute-done.1 = bf16[512,128]{1,0:T(8,128)(2,1)S(1)} collective-permute-done((bf16[512,128]{1,0:T(8,128)(2,1)S(1)}, bf16[512,128]{1,0:T(8,128)(2,1)S(1)}, u32[]{:S(2)}, u32[]{:S(2)}) %collective-permute-start.1) | collective-permute-done | bytes 131104 | tf_op jit(solution)/shard_map/ppermute | solution.py:129
  16.2 0.2 fusion.106
  16.4 0.2 fusion.63
  16.6 1.6 %collective-permute-start.5 = (f32[128,128]{1,0:T(8,128)S(1)}, f32[128,128]{1,0:T(8,128)S(1)}, u32[]{:S(2)}, u32[]{:S(2)}) collective-permute-start(f32[128,128]{1,0:T(8,128)S(1)} %fusion.63), channel_id=1, source_target_pairs={{0,16},{8,24},{16,0},{24,8},{1,17},{9,25},{17,1},{25,9},{2,18},{10... | collective-permute-start | bytes 196616 | tf_op jit(solution)/shard_map/ppermute | solution.py:129
  18.2 0.5 %collective-permute-start.3 = (bf16[128,128]{1,0:T(8,128)(2,1)S(1)}, bf16[128,128]{1,0:T(8,128)(2,1)S(1)}, u32[]{:S(2)}, u32[]{:S(2)}) collective-permute-start(bf16[128,128]{1,0:T(8,128)(2,1)S(1)} %slice_select_fusion.2), channel_id=1, source_target_pairs={{0,16},{8,24},{16,0},{24,8},{1,17},{9,25},{17,1},{25,9},{2,18},{10... | collective-permute-start | bytes 98312 | tf_op jit(solution)/shard_map/ppermute | solution.py:129
  18.7 0.0 collective-permute-done
  18.7 0.2 fusion.72
  18.9 0.1 copy.24
  19.0 1.6 %collective-permute-start.2 = (f32[128,128]{1,0:T(8,128)S(1)}, f32[128,128]{1,0:T(8,128)S(1)}, u32[]{:S(2)}, u32[]{:S(2)}) collective-permute-start(f32[128,128]{1,0:T(8,128)S(1)} %fusion.72), channel_id=1, source_target_pairs={{0,16},{8,24},{16,0},{24,8},{1,17},{9,25},{17,1},{25,9},{2,18},{10... | collective-permute-start | bytes 196616 | tf_op jit(solution)/shard_map/ppermute | solution.py:129
  20.5 1.6 %collective-permute-done.3 = bf16[128,128]{1,0:T(8,128)(2,1)S(1)} collective-permute-done((bf16[128,128]{1,0:T(8,128)(2,1)S(1)}, bf16[128,128]{1,0:T(8,128)(2,1)S(1)}, u32[]{:S(2)}, u32[]{:S(2)}) %collective-permute-start.3) | collective-permute-done | bytes 32800 | tf_op jit(solution)/shard_map/ppermute | solution.py:129
  22.1 0.2 fusion.103
  22.3 0.1 copy.25
  22.4 0.2 fusion.117
  22.6 0.3 convolution_subtract_fusion
  22.9 0.2 fusion.192
  23.2 0.2 fusion.193
  23.4 0.2 convolution_subtract_fusion.8
  23.6 0.0 copy-start.7
  23.6 0.0 collective-permute-done.2
  23.7 0.1 fusion.102
  23.8 0.1 copy.22
  23.9 0.3 fusion.13
  24.3 0.3 copy-done.7
  24.6 0.2 convolution_subtract_fusion.1
  24.8 0.1 fusion.174
  24.9 0.3 fusion.175
  25.2 0.3 fusion.178
  25.5 0.3 fusion.7
  25.9 0.1 fusion.14
  26.0 0.1 collective-permute-start.6
  26.1 1.1 %collective-permute-done.6 = f32[2,2,64]{2,1,0:T(2,128)S(1)} collective-permute-done((f32[2,2,64]{2,1,0:T(2,128)S(1)}, f32[2,2,64]{2,1,0:T(2,128)S(1)}, u32[]{:S(2)}, u32[]{:S(2)}) %collective-permute-start.6) | collective-permute-done | bytes 1056 | tf_op jit(solution)/shard_map/ppermute | solution.py:211
  27.3 1.6 %collective-permute-start.7 = (f32[2,64]{1,0:T(2,128)S(1)}, f32[2,64]{1,0:T(2,128)S(1)}, u32[]{:S(2)}, u32[]{:S(2)}) collective-permute-start(f32[2,64]{1,0:T(2,128)S(1)} %bitcast.101), channel_id=1, source_target_pairs={{0,2},{1,3},{2,0},{3,1},{4,6},{5,7},{6,4},{7,5},{8,10},{9,11},{10,... | collective-permute-start | bytes 1544 | tf_op jit(solution)/shard_map/ppermute | solution.py:211
  28.9 2.0 %collective-permute-done.7 = f32[2,64]{1,0:T(2,128)S(1)} collective-permute-done((f32[2,64]{1,0:T(2,128)S(1)}, f32[2,64]{1,0:T(2,128)S(1)}, u32[]{:S(2)}, u32[]{:S(2)}) %collective-permute-start.7) | collective-permute-done | bytes 544 | tf_op jit(solution)/shard_map/ppermute | solution.py:211
  30.9 2.6 %collective-permute-start.8 = (f32[64]{0:T(128)S(1)}, f32[64]{0:T(128)S(1)}, u32[]{:S(2)}, u32[]{:S(2)}) collective-permute-start(f32[64]{0:T(128)S(1)} %fusion.147), channel_id=1, source_target_pairs={{0,4},{1,5},{2,6},{3,7},{4,0},{5,1},{6,2},{7,3},{8,12},{9,13},{10,... | collective-permute-start | bytes 776 | tf_op jit(solution)/shard_map/ppermute | solution.py:211
  33.6 0.8 %copy.32 = f32[128,512]{1,0:T(8,128)} copy(f32[128,512]{0,1:T(8,128)S(1)} %pad_maximum_fusion.3) | data formatting | bytes 524288
  34.4 0.8 %copy.31 = f32[128,512]{1,0:T(8,128)} copy(f32[128,512]{0,1:T(8,128)S(1)} %pad_maximum_fusion.1) | data formatting | bytes 524288
  35.2 0.2 collective-permute-done.8
  35.4 0.5 %fusion.146 = f32[64]{0:T(128)} fusion(f32[64]{0:T(128)S(1)} %collective-permute-done.8, pred[]{:T(512)S(6)} %ne.39, f32[2,64]{1,0:T(2,128)S(1)} %add.59), kind=kLoop, calls=%fused_computation.169 | loop fusion | flops 192 | bytes 1025 | tf_op jit(solution)/shard_map/mul | solution.py:213
  (32 shorter events, 0.2 us)
Async XLA Ops:
  0.6 10.8 %copy-start = (bf16[256,512]{1,0:T(8,128)(2,1)S(1)}, bf16[256,512]{1,0:T(8,128)(2,1)}, u32[]{:S(2)}) copy-start(bf16[256,512]{1,0:T(8,128)(2,1)} %param.19) | copy-start | bytes 786436
  0.6 1.3 %copy-start.2 = (bf16[4,128,128]{2,1,0:T(8,128)(2,1)S(1)}, bf16[4,128,128]{2,1,0:T(8,128)(2,1)}, u32[]{:S(2)}) copy-start(bf16[4,128,128]{2,1,0:T(8,128)(2,1)} %param.18) | copy-start | bytes 393220
  0.7 2.7 %copy-start.3 = (bf16[512,512]{1,0:T(8,128)(2,1)S(1)}, bf16[512,512]{1,0:T(8,128)(2,1)}, u32[]{:S(2)}) copy-start(bf16[512,512]{1,0:T(8,128)(2,1)} %param.17) | copy-start | bytes 1572868
  3.7 1.0 %copy-start.6 = (bf16[512,256]{1,0:T(8,128)(2,1)S(1)}, bf16[512,256]{1,0:T(8,128)(2,1)}, u32[]{:S(2)}) copy-start(bf16[512,256]{1,0:T(8,128)(2,1)} %param.20) | copy-start | bytes 786436
  3.7 0.7 %copy-start.5 = (s32[3,2]{0,1:T(2,128)S(1)}, s32[3,2]{0,1:T(2,128)}, u32[]{:S(2)}) copy-start(s32[3,2]{0,1:T(2,128)} %param.15) | copy-start | bytes 76
  5.0 3.6 %copy-start.1 = (bf16[2,128,128]{2,1,0:T(8,128)(2,1)S(1)}, bf16[2,128,128]{2,1,0:T(8,128)(2,1)}, u32[]{:S(2)}) copy-start(bf16[2,128,128]{2,1,0:T(8,128)(2,1)} %param.21) | copy-start | bytes 196612
  5.0 6.0 %copy-start.4 = (bf16[512,512]{1,0:T(8,128)(2,1)S(1)}, bf16[512,512]{1,0:T(8,128)(2,1)}, u32[]{:S(2)}) copy-start(bf16[512,512]{1,0:T(8,128)(2,1)} %param.16) | copy-start | bytes 1572868
  5.0 8.7 %collective-permute-start.4 = (f32[256,128]{1,0:T(8,128)S(1)}, f32[256,128]{1,0:T(8,128)S(1)}, u32[]{:S(2)}, u32[]{:S(2)}) collective-permute-start(f32[256,128]{1,0:T(8,128)S(1)} %pad_maximum_fusion.6), channel_id=1, source_target_pairs={{0,8},{8,0},{16,24},{24,16},{1,9},{9,1},{17,25},{25,17},{2,10},{10... | collective-permute-start | bytes 393224 | tf_op jit(solution)/shard_map/ppermute | solution.py:129
  10.1 6.1 %collective-permute-start.1 = (bf16[512,128]{1,0:T(8,128)(2,1)S(1)}, bf16[512,128]{1,0:T(8,128)(2,1)S(1)}, u32[]{:S(2)}, u32[]{:S(2)}) collective-permute-start(bf16[512,128]{1,0:T(8,128)(2,1)S(1)} %pad_maximum_fusion.5), channel_id=1, source_target_pairs={{0,8},{8,0},{16,24},{24,16},{1,9},{9,1},{17,25},{25,17},{2,10},{10... | collective-permute-start | bytes 393224 | tf_op jit(solution)/shard_map/ppermute | solution.py:129
  10.2 0.7 %copy-start.8 = (s32[128]{0:T(128)S(1)}, s32[128]{0:T(128)}, u32[]{:S(2)}) copy-start(s32[128]{0:T(128)} %param.12) | copy-start | bytes 1540
  11.8 6.9 %collective-permute-start = (f32[256,128]{1,0:T(8,128)S(1)}, f32[256,128]{1,0:T(8,128)S(1)}, u32[]{:S(2)}, u32[]{:S(2)}) collective-permute-start(f32[256,128]{1,0:T(8,128)S(1)} %pad_maximum_fusion.4), channel_id=1, source_target_pairs={{0,8},{8,0},{16,24},{24,16},{1,9},{9,1},{17,25},{25,17},{2,10},{10... | collective-permute-start | bytes 393224 | tf_op jit(solution)/shard_map/ppermute | solution.py:129
  16.6 5.5 %collective-permute-start.5 = (f32[128,128]{1,0:T(8,128)S(1)}, f32[128,128]{1,0:T(8,128)S(1)}, u32[]{:S(2)}, u32[]{:S(2)}) collective-permute-start(f32[128,128]{1,0:T(8,128)S(1)} %fusion.63), channel_id=1, source_target_pairs={{0,16},{8,24},{16,0},{24,8},{1,17},{9,25},{17,1},{25,9},{2,18},{10... | collective-permute-start | bytes 196616 | tf_op jit(solution)/shard_map/ppermute | solution.py:129
  18.2 3.9 %collective-permute-start.3 = (bf16[128,128]{1,0:T(8,128)(2,1)S(1)}, bf16[128,128]{1,0:T(8,128)(2,1)S(1)}, u32[]{:S(2)}, u32[]{:S(2)}) collective-permute-start(bf16[128,128]{1,0:T(8,128)(2,1)S(1)} %slice_select_fusion.2), channel_id=1, source_target_pairs={{0,16},{8,24},{16,0},{24,8},{1,17},{9,25},{17,1},{25,9},{2,18},{10... | collective-permute-start | bytes 98312 | tf_op jit(solution)/shard_map/ppermute | solution.py:129
  19.0 4.7 %collective-permute-start.2 = (f32[128,128]{1,0:T(8,128)S(1)}, f32[128,128]{1,0:T(8,128)S(1)}, u32[]{:S(2)}, u32[]{:S(2)}) collective-permute-start(f32[128,128]{1,0:T(8,128)S(1)} %fusion.72), channel_id=1, source_target_pairs={{0,16},{8,24},{16,0},{24,8},{1,17},{9,25},{17,1},{25,9},{2,18},{10... | collective-permute-start | bytes 196616 | tf_op jit(solution)/shard_map/ppermute | solution.py:129
  23.6 1.0 %copy-start.7 = (bf16[512,256]{1,0:T(8,128)(2,1)S(1)}, bf16[512,256]{1,0:T(8,128)(2,1)}, u32[]{:S(2)}) copy-start(bf16[512,256]{1,0:T(8,128)(2,1)} %param.20) | copy-start | bytes 786436
  26.0 1.2 %collective-permute-start.6 = (f32[2,2,64]{2,1,0:T(2,128)S(1)}, f32[2,2,64]{2,1,0:T(2,128)S(1)}, u32[]{:S(2)}, u32[]{:S(2)}) collective-permute-start(f32[2,2,64]{2,1,0:T(2,128)S(1)} %bitcast.100), channel_id=1, source_target_pairs={{0,1},{1,0},{2,3},{3,2},{4,5},{5,4},{6,7},{7,6},{8,9},{9,8},{10,11... | collective-permute-start | bytes 3080 | tf_op jit(solution)/shard_map/ppermute | solution.py:211
  27.3 3.6 %collective-permute-start.7 = (f32[2,64]{1,0:T(2,128)S(1)}, f32[2,64]{1,0:T(2,128)S(1)}, u32[]{:S(2)}, u32[]{:S(2)}) collective-permute-start(f32[2,64]{1,0:T(2,128)S(1)} %bitcast.101), channel_id=1, source_target_pairs={{0,2},{1,3},{2,0},{3,1},{4,6},{5,7},{6,4},{7,5},{8,10},{9,11},{10,... | collective-permute-start | bytes 1544 | tf_op jit(solution)/shard_map/ppermute | solution.py:211
  30.9 4.5 %collective-permute-start.8 = (f32[64]{0:T(128)S(1)}, f32[64]{0:T(128)S(1)}, u32[]{:S(2)}, u32[]{:S(2)}) collective-permute-start(f32[64]{0:T(128)S(1)} %fusion.147), channel_id=1, source_target_pairs={{0,4},{1,5},{2,6},{3,7},{4,0},{5,1},{6,2},{7,3},{8,12},{9,13},{10,... | collective-permute-start | bytes 776 | tf_op jit(solution)/shard_map/ppermute | solution.py:211

commit v23 on v22

--- a/solution.py
+++ b/solution.py
@@ -198,6 +198,7 @@
     partial_gradient = jnp.sum(product_field, axis=0)
     place = lax.axis_index("src")
     bits = [1 << k for k in range(spread.bit_length() - 1)]
+    bits = bits[:1] + bits[1:][::-1]
     axes = [1 << k for k in reversed(range(spread.bit_length() - 1))]
     partial_gradient = partial_gradient.reshape([2] * len(axes) + [cell_count // spread])
     for bit in bits:

time: 36.3 us -> 36.3 us (level)
  no operation moved by 1% of the time
where the time goes in v23:
time: 36.3 us; the launch traced here: 35.9 us
  starting transfers between devices  13.1 us (36%)
  matrix products  7.83 us (22%)
  waiting for transfers between devices  7.36 us (20%)
  local copies, waits for them, and re-layouts  4.12 us (11%)
  other arithmetic  2.45 us (7%)
  between operations  1.04 us (3%)
    ppermute x6, starting transfers between devices, exchange(): incoming = lax.ppermute(jnp.concatenate(pieces, axis=0), 'leaf', pairs)  8.81 us
    ppermute x3, starting transfers between devices, shards(): partial_gradient = kept + lax.ppermute(outgoing, 'src', pairs)  4.31 us
    ppermute x6, waiting for transfers between devices, exchange(): incoming = lax.ppermute(jnp.concatenate(pieces, axis=0), 'leaf', pairs)  4.05 us
    dot_general x13, matrix products, plain_dot(): return jnp.dot(former, latter, preferred_element_type=jnp.float32)  3.98 us
    ppermute x3, waiting for transfers between devices, shards(): partial_gradient = kept + lax.ppermute(outgoing, 'src', pairs)  3.31 us
    unnamed x20, local copies, waits for them, and re-layouts  3.05 us
    dot_general x12, matrix products, across(): lax.dot_general(former, latter, (((1,), (1,)), ((), ())), preferred_eleme...  2.54 us
    select_n x1, other arithmetic, masked(): return jnp.where(keep, values, jnp.zeros_like(values))  1.43 us
  transfers between devices with their start and end apart: 9, of which 5 were waited for; matrix products, arithmetic and copies ran while one was open for 19% of the time, Pallas kernels for 0%

profile of v23, /device:TPU:0, one launch (start us, length us, event | category | flops | bytes accessed | tf_op | source)
XLA Modules:
  0.0 35.9 jit_solution(6086554182799612399)
XLA Ops:
  0.6 0.0 copy-start
  0.7 0.0 copy-start.3
  0.7 1.3 %convolution_bitcast_fusion = f32[128,512]{0,1:T(8,128)S(1)} fusion(f32[128,128]{1,0:T(8,128)} %param.14, s32[128]{0:T(128)} %param.13), kind=kOutput, calls=%fused_computation.2 | convolution fusion | flops 100794368 | bytes 328192 | tf_op jit(solution)/shard_map/dot_general | solution.py:112
  2.0 0.2 fusion.183
  2.2 1.1 %fusion.184 = (bf16[128,128]{0,1:T(8,128)(2,1)S(1)}, f32[128,128]{0,1:T(8,128)S(1)}) fusion(bf16[4,128,128]{2,1,0:T(8,128)(2,1)S(1)} %copy-done.2, bf16[128,128]{0,1:T(8,128)(2,1)S(1)} %get-tuple-element.30, f32[128,512]{0,1:T(8,128)S(1)} %convolution_bitcast_fusion, bf16[512,512]{1,0:T(8,128)(2,1)} %param.17), kind=kOutput, calls=%fused_computation.201 | convolution fusion | flops 8437760 | bytes 262144 | tf_op jit(solution)/shard_map/dot_general | solution.py:16
  3.3 0.4 fusion.187
  3.7 0.0 copy-start.6
  3.7 0.0 copy-start.5
  3.7 0.4 fusion.10
  4.1 0.3 copy-done.5
  4.4 0.2 compare_reduce_fusion
  4.6 0.1 broadcast_bitcast_fusion
  4.7 0.2 convolution_select_fusion
  5.0 0.0 copy-start.1
  5.0 0.0 copy-start.4
  5.0 3.0 %collective-permute-start.4 = (f32[256,128]{1,0:T(8,128)S(1)}, f32[256,128]{1,0:T(8,128)S(1)}, u32[]{:S(2)}, u32[]{:S(2)}) collective-permute-start(f32[256,128]{1,0:T(8,128)S(1)} %pad_maximum_fusion.6), channel_id=1, source_target_pairs={{0,8},{8,0},{16,24},{24,16},{1,9},{9,1},{17,25},{25,17},{2,10},{10... | collective-permute-start | bytes 393224 | tf_op jit(solution)/shard_map/ppermute | solution.py:129
  8.0 0.6 %slice.192 = pred[1]{0:T(512)(128)(4,1)} slice(pred[2]{0:T(512)(128)(4,1)S(1)} %compare_and_fusion), slice={[1:2]} | slice | bytes 2 | tf_op jit(solution)/shard_map/slice | solution.py:122
  8.6 1.4 %select_bitcast_fusion = (bf16[128,128]{1,0:T(8,128)(2,1)S(1)}, bf16[128,128]{1,0:T(8,128)(2,1)S(1)}) fusion(bf16[2,128,256]{2,1,0:T(8,128)(2,1)} %param.23, pred[]{:T(512)} %bitcast.1, bf16[2,256,128]{2,1,0:T(8,128)(2,1)} %param.22), kind=kLoop, calls=%fused_computation.142 | loop fusion | flops 32768 | bytes 131073 | tf_op jit(solution)/shard_map/jit(_where)/select_n | solution.py:102
  10.1 0.2 collective-permute-start.1
  10.3 0.7 %copy-done.8 = s32[128]{0:T(128)S(1)} copy-done((s32[128]{0:T(128)S(1)}, s32[128]{0:T(128)}, u32[]{:S(2)}) %copy-start.8) | copy-done | bytes 536
  11.0 0.1 fusion.172
  11.1 0.1 fusion.173
  11.3 0.2 convolution_subtract_fusion.5
  11.5 0.2 convolution_select_fusion.1
  11.8 2.0 %collective-permute-start = (f32[256,128]{1,0:T(8,128)S(1)}, f32[256,128]{1,0:T(8,128)S(1)}, u32[]{:S(2)}, u32[]{:S(2)}) collective-permute-start(f32[256,128]{1,0:T(8,128)S(1)} %pad_maximum_fusion.4), channel_id=1, source_target_pairs={{0,8},{8,0},{16,24},{24,16},{1,9},{9,1},{17,25},{25,17},{2,10},{10... | collective-permute-start | bytes 393224 | tf_op jit(solution)/shard_map/ppermute | solution.py:129
  13.7 0.0 collective-permute-done.4
  13.7 2.5 %collective-permute-done.1 = bf16[512,128]{1,0:T(8,128)(2,1)S(1)} collective-permute-done((bf16[512,128]{1,0:T(8,128)(2,1)S(1)}, bf16[512,128]{1,0:T(8,128)(2,1)S(1)}, u32[]{:S(2)}, u32[]{:S(2)}) %collective-permute-start.1) | collective-permute-done | bytes 131104 | tf_op jit(solution)/shard_map/ppermute | solution.py:129
  16.2 0.2 fusion.106
  16.4 0.2 fusion.63
  16.6 1.6 %collective-permute-start.5 = (f32[128,128]{1,0:T(8,128)S(1)}, f32[128,128]{1,0:T(8,128)S(1)}, u32[]{:S(2)}, u32[]{:S(2)}) collective-permute-start(f32[128,128]{1,0:T(8,128)S(1)} %fusion.63), channel_id=1, source_target_pairs={{0,16},{8,24},{16,0},{24,8},{1,17},{9,25},{17,1},{25,9},{2,18},{10... | collective-permute-start | bytes 196616 | tf_op jit(solution)/shard_map/ppermute | solution.py:129
  18.2 0.5 %collective-permute-start.3 = (bf16[128,128]{1,0:T(8,128)(2,1)S(1)}, bf16[128,128]{1,0:T(8,128)(2,1)S(1)}, u32[]{:S(2)}, u32[]{:S(2)}) collective-permute-start(bf16[128,128]{1,0:T(8,128)(2,1)S(1)} %slice_select_fusion.2), channel_id=1, source_target_pairs={{0,16},{8,24},{16,0},{24,8},{1,17},{9,25},{17,1},{25,9},{2,18},{10... | collective-permute-start | bytes 98312 | tf_op jit(solution)/shard_map/ppermute | solution.py:129
  18.7 0.0 collective-permute-done
  18.7 0.2 fusion.72
  18.9 0.1 copy.24
  19.0 1.6 %collective-permute-start.2 = (f32[128,128]{1,0:T(8,128)S(1)}, f32[128,128]{1,0:T(8,128)S(1)}, u32[]{:S(2)}, u32[]{:S(2)}) collective-permute-start(f32[128,128]{1,0:T(8,128)S(1)} %fusion.72), channel_id=1, source_target_pairs={{0,16},{8,24},{16,0},{24,8},{1,17},{9,25},{17,1},{25,9},{2,18},{10... | collective-permute-start | bytes 196616 | tf_op jit(solution)/shard_map/ppermute | solution.py:129
  20.5 1.6 %collective-permute-done.3 = bf16[128,128]{1,0:T(8,128)(2,1)S(1)} collective-permute-done((bf16[128,128]{1,0:T(8,128)(2,1)S(1)}, bf16[128,128]{1,0:T(8,128)(2,1)S(1)}, u32[]{:S(2)}, u32[]{:S(2)}) %collective-permute-start.3) | collective-permute-done | bytes 32800 | tf_op jit(solution)/shard_map/ppermute | solution.py:129
  22.1 0.2 fusion.103
  22.3 0.1 copy.25
  22.4 0.2 fusion.117
  22.6 0.3 convolution_subtract_fusion
  22.9 0.2 fusion.192
  23.2 0.2 fusion.193
  23.4 0.2 convolution_subtract_fusion.8
  23.6 0.0 copy-start.7
  23.6 0.0 collective-permute-done.2
  23.7 0.1 fusion.102
  23.8 0.1 copy.22
  23.9 0.3 fusion.13
  24.3 0.3 copy-done.7
  24.6 0.2 convolution_subtract_fusion.1
  24.8 0.1 fusion.174
  24.9 0.3 fusion.175
  25.2 0.3 fusion.178
  25.5 0.3 fusion.7
  25.9 0.1 fusion.14
  26.0 0.1 collective-permute-start.6
  26.1 1.1 %collective-permute-done.6 = f32[2,2,64]{2,1,0:T(2,128)S(1)} collective-permute-done((f32[2,2,64]{2,1,0:T(2,128)S(1)}, f32[2,2,64]{2,1,0:T(2,128)S(1)}, u32[]{:S(2)}, u32[]{:S(2)}) %collective-permute-start.6) | collective-permute-done | bytes 1056 | tf_op jit(solution)/shard_map/ppermute | solution.py:212
  27.3 2.6 %collective-permute-start.7 = (f32[2,64]{1,0:T(2,128)S(1)}, f32[2,64]{1,0:T(2,128)S(1)}, u32[]{:S(2)}, u32[]{:S(2)}) collective-permute-start(f32[2,64]{1,0:T(2,128)S(1)} %select_bitcast_fusion.2), channel_id=1, source_target_pairs={{0,4},{1,5},{2,6},{3,7},{4,0},{5,1},{6,2},{7,3},{8,12},{9,13},{10,... | collective-permute-start | bytes 1544 | tf_op jit(solution)/shard_map/ppermute | solution.py:212
  29.9 1.9 %collective-permute-done.7 = f32[2,64]{1,0:T(2,128)S(1)} collective-permute-done((f32[2,64]{1,0:T(2,128)S(1)}, f32[2,64]{1,0:T(2,128)S(1)}, u32[]{:S(2)}, u32[]{:S(2)}) %collective-permute-start.7) | collective-permute-done | bytes 544 | tf_op jit(solution)/shard_map/ppermute | solution.py:212
  31.8 1.6 %collective-permute-start.8 = (f32[64]{0:T(128)S(1)}, f32[64]{0:T(128)S(1)}, u32[]{:S(2)}, u32[]{:S(2)}) collective-permute-start(f32[64]{0:T(128)S(1)} %fusion.147), channel_id=1, source_target_pairs={{0,2},{1,3},{2,0},{3,1},{4,6},{5,7},{6,4},{7,5},{8,10},{9,11},{10,... | collective-permute-start | bytes 776 | tf_op jit(solution)/shard_map/ppermute | solution.py:212
  33.4 0.8 %copy.32 = f32[128,512]{1,0:T(8,128)} copy(f32[128,512]{0,1:T(8,128)S(1)} %pad_maximum_fusion.3) | data formatting | bytes 524288
  34.3 0.8 %copy.31 = f32[128,512]{1,0:T(8,128)} copy(f32[128,512]{0,1:T(8,128)S(1)} %pad_maximum_fusion.1) | data formatting | bytes 524288
  35.1 0.3 collective-permute-done.8
  35.4 0.5 %fusion.146 = f32[64]{0:T(128)} fusion(f32[64]{0:T(128)S(1)} %collective-permute-done.8, pred[]{:T(512)S(6)} %ne.39, f32[2,64]{1,0:T(2,128)S(1)} %bitcast_add_fusion.1), kind=kLoop, calls=%fused_computation.169 | loop fusion | flops 192 | bytes 1025 | tf_op jit(solution)/shard_map/mul | solution.py:214
  (32 shorter events, 0.2 us)
Async XLA Ops:
  0.6 10.8 %copy-start = (bf16[256,512]{1,0:T(8,128)(2,1)S(1)}, bf16[256,512]{1,0:T(8,128)(2,1)}, u32[]{:S(2)}) copy-start(bf16[256,512]{1,0:T(8,128)(2,1)} %param.19) | copy-start | bytes 786436
  0.6 1.3 %copy-start.2 = (bf16[4,128,128]{2,1,0:T(8,128)(2,1)S(1)}, bf16[4,128,128]{2,1,0:T(8,128)(2,1)}, u32[]{:S(2)}) copy-start(bf16[4,128,128]{2,1,0:T(8,128)(2,1)} %param.18) | copy-start | bytes 393220
  0.7 2.7 %copy-start.3 = (bf16[512,512]{1,0:T(8,128)(2,1)S(1)}, bf16[512,512]{1,0:T(8,128)(2,1)}, u32[]{:S(2)}) copy-start(bf16[512,512]{1,0:T(8,128)(2,1)} %param.17) | copy-start | bytes 1572868
  3.7 1.0 %copy-start.6 = (bf16[512,256]{1,0:T(8,128)(2,1)S(1)}, bf16[512,256]{1,0:T(8,128)(2,1)}, u32[]{:S(2)}) copy-start(bf16[512,256]{1,0:T(8,128)(2,1)} %param.20) | copy-start | bytes 786436
  3.7 0.7 %copy-start.5 = (s32[3,2]{0,1:T(2,128)S(1)}, s32[3,2]{0,1:T(2,128)}, u32[]{:S(2)}) copy-start(s32[3,2]{0,1:T(2,128)} %param.15) | copy-start | bytes 76
  5.0 3.6 %copy-start.1 = (bf16[2,128,128]{2,1,0:T(8,128)(2,1)S(1)}, bf16[2,128,128]{2,1,0:T(8,128)(2,1)}, u32[]{:S(2)}) copy-start(bf16[2,128,128]{2,1,0:T(8,128)(2,1)} %param.21) | copy-start | bytes 196612
  5.0 6.0 %copy-start.4 = (bf16[512,512]{1,0:T(8,128)(2,1)S(1)}, bf16[512,512]{1,0:T(8,128)(2,1)}, u32[]{:S(2)}) copy-start(bf16[512,512]{1,0:T(8,128)(2,1)} %param.16) | copy-start | bytes 1572868
  5.0 8.7 %collective-permute-start.4 = (f32[256,128]{1,0:T(8,128)S(1)}, f32[256,128]{1,0:T(8,128)S(1)}, u32[]{:S(2)}, u32[]{:S(2)}) collective-permute-start(f32[256,128]{1,0:T(8,128)S(1)} %pad_maximum_fusion.6), channel_id=1, source_target_pairs={{0,8},{8,0},{16,24},{24,16},{1,9},{9,1},{17,25},{25,17},{2,10},{10... | collective-permute-start | bytes 393224 | tf_op jit(solution)/shard_map/ppermute | solution.py:129
  10.1 6.1 %collective-permute-start.1 = (bf16[512,128]{1,0:T(8,128)(2,1)S(1)}, bf16[512,128]{1,0:T(8,128)(2,1)S(1)}, u32[]{:S(2)}, u32[]{:S(2)}) collective-permute-start(bf16[512,128]{1,0:T(8,128)(2,1)S(1)} %pad_maximum_fusion.5), channel_id=1, source_target_pairs={{0,8},{8,0},{16,24},{24,16},{1,9},{9,1},{17,25},{25,17},{2,10},{10... | collective-permute-start | bytes 393224 | tf_op jit(solution)/shard_map/ppermute | solution.py:129
  10.2 0.7 %copy-start.8 = (s32[128]{0:T(128)S(1)}, s32[128]{0:T(128)}, u32[]{:S(2)}) copy-start(s32[128]{0:T(128)} %param.12) | copy-start | bytes 1540
  11.8 6.9 %collective-permute-start = (f32[256,128]{1,0:T(8,128)S(1)}, f32[256,128]{1,0:T(8,128)S(1)}, u32[]{:S(2)}, u32[]{:S(2)}) collective-permute-start(f32[256,128]{1,0:T(8,128)S(1)} %pad_maximum_fusion.4), channel_id=1, source_target_pairs={{0,8},{8,0},{16,24},{24,16},{1,9},{9,1},{17,25},{25,17},{2,10},{10... | collective-permute-start | bytes 393224 | tf_op jit(solution)/shard_map/ppermute | solution.py:129
  16.6 5.5 %collective-permute-start.5 = (f32[128,128]{1,0:T(8,128)S(1)}, f32[128,128]{1,0:T(8,128)S(1)}, u32[]{:S(2)}, u32[]{:S(2)}) collective-permute-start(f32[128,128]{1,0:T(8,128)S(1)} %fusion.63), channel_id=1, source_target_pairs={{0,16},{8,24},{16,0},{24,8},{1,17},{9,25},{17,1},{25,9},{2,18},{10... | collective-permute-start | bytes 196616 | tf_op jit(solution)/shard_map/ppermute | solution.py:129
  18.2 3.9 %collective-permute-start.3 = (bf16[128,128]{1,0:T(8,128)(2,1)S(1)}, bf16[128,128]{1,0:T(8,128)(2,1)S(1)}, u32[]{:S(2)}, u32[]{:S(2)}) collective-permute-start(bf16[128,128]{1,0:T(8,128)(2,1)S(1)} %slice_select_fusion.2), channel_id=1, source_target_pairs={{0,16},{8,24},{16,0},{24,8},{1,17},{9,25},{17,1},{25,9},{2,18},{10... | collective-permute-start | bytes 98312 | tf_op jit(solution)/shard_map/ppermute | solution.py:129
  19.0 4.7 %collective-permute-start.2 = (f32[128,128]{1,0:T(8,128)S(1)}, f32[128,128]{1,0:T(8,128)S(1)}, u32[]{:S(2)}, u32[]{:S(2)}) collective-permute-start(f32[128,128]{1,0:T(8,128)S(1)} %fusion.72), channel_id=1, source_target_pairs={{0,16},{8,24},{16,0},{24,8},{1,17},{9,25},{17,1},{25,9},{2,18},{10... | collective-permute-start | bytes 196616 | tf_op jit(solution)/shard_map/ppermute | solution.py:129
  23.6 1.0 %copy-start.7 = (bf16[512,256]{1,0:T(8,128)(2,1)S(1)}, bf16[512,256]{1,0:T(8,128)(2,1)}, u32[]{:S(2)}) copy-start(bf16[512,256]{1,0:T(8,128)(2,1)} %param.20) | copy-start | bytes 786436
  26.0 1.2 %collective-permute-start.6 = (f32[2,2,64]{2,1,0:T(2,128)S(1)}, f32[2,2,64]{2,1,0:T(2,128)S(1)}, u32[]{:S(2)}, u32[]{:S(2)}) collective-permute-start(f32[2,2,64]{2,1,0:T(2,128)S(1)} %bitcast.101), channel_id=1, source_target_pairs={{0,1},{1,0},{2,3},{3,2},{4,5},{5,4},{6,7},{7,6},{8,9},{9,8},{10,11... | collective-permute-start | bytes 3080 | tf_op jit(solution)/shard_map/ppermute | solution.py:212
  27.3 4.5 %collective-permute-start.7 = (f32[2,64]{1,0:T(2,128)S(1)}, f32[2,64]{1,0:T(2,128)S(1)}, u32[]{:S(2)}, u32[]{:S(2)}) collective-permute-start(f32[2,64]{1,0:T(2,128)S(1)} %select_bitcast_fusion.2), channel_id=1, source_target_pairs={{0,4},{1,5},{2,6},{3,7},{4,0},{5,1},{6,2},{7,3},{8,12},{9,13},{10,... | collective-permute-start | bytes 1544 | tf_op jit(solution)/shard_map/ppermute | solution.py:212
  31.8 3.6 %collective-permute-start.8 = (f32[64]{0:T(128)S(1)}, f32[64]{0:T(128)S(1)}, u32[]{:S(2)}, u32[]{:S(2)}) collective-permute-start(f32[64]{0:T(128)S(1)} %fusion.147), channel_id=1, source_target_pairs={{0,2},{1,3},{2,0},{3,1},{4,6},{5,7},{6,4},{7,5},{8,10},{9,11},{10,... | collective-permute-start | bytes 776 | tf_op jit(solution)/shard_map/ppermute | solution.py:212
